TPU v7x, 32 devices: a whole 2x2x4 slice. The times are simulated.
32 devices in a mesh: real: 4 (over y, x), strike: 8 (over z, core).
Axes of the slice: x: 2, y: 2, z: 4, core: 2. Of those that a mesh axis runs over, the one named last changes fastest.
Arguments:
- grades: bfloat16 [4, 32, 16, 32, 128], P('real', None, 'strike'), may hold values from -6 to 6
- cotangent: bfloat16 [4, 32, 16, 32, 128], P('real', None, 'strike'), may hold values from -6 to 6
- weight: bfloat16 [32, 864], P('real'), may hold values from -0.21875 to 0.21875
- bias: bfloat16 [32], P('real'), may hold values from -3 to 3
Outputs:
- activation: bfloat16 [4, 32, 16, 32, 128], P('real', None, 'strike')
- grad_input: bfloat16 [4, 32, 16, 32, 128], P('real', None, 'strike')
- grad_weight: float32 [32, 864], P('real')
- grad_bias: float32 [32], P('real')
All inputs are finite; a program needn't handle non-finite values.
Results may differ from a plain program's by a relative error of at most 0.0095.
Values may be sent and summed in bfloat16 or wider, within the bound.
No kernel may reach another device: no remote copies, remote signals or barrier semaphores. Data moves between devices by JAX's collectives and lax.ppermute only.
A program may use at most 128 MiB of HBM per device.

v0:
```python
import jax
import jax.numpy as jnp
from jax import lax
from jax.sharding import PartitionSpec as P


def padded(value, sides, width):
    for axis, dim in sides:
        peers, length = (lax.axis_size(axis), value.shape[dim])
        up = [(i, (i + 1) % peers) for i in range(peers - 1)]
        down = [(j, i) for i, j in up]
        last = lax.slice_in_dim(value, length - width, length, axis=dim)
        leading = lax.slice_in_dim(value, 0, width, axis=dim)
        before = lax.ppermute(last, axis, up)
        after = lax.ppermute(leading, axis, down)
        value = jnp.concatenate([before, value, after], axis=dim)
    return value


def tap_list():
    listing = []
    for shift_x in (-1, 0, 1):
        for shift_y in (-1, 0, 1):
            for shift_z in (-1, 0, 1):
                listing.append(
                    (
                        shift_x,
                        shift_y,
                        shift_z,
                        9 * (shift_x + 1) + 3 * (shift_y + 1) + (shift_z + 1),
                    )
                )
    return listing


def transposed_stencil(padded_grad, kernel3, planes, rows, depth):
    total = jnp.zeros((kernel3.shape[2], planes, rows, depth), jnp.float32)
    for shift_x, shift_y, shift_z, column in tap_list():
        window = padded_grad[
            :,
            1 - shift_x : 1 - shift_x + planes,
            1 - shift_y : 1 - shift_y + rows,
            1 - shift_z : 1 - shift_z + depth,
        ]
        total = total + jnp.einsum(
            "oi,oxyz->ixyz", kernel3[:, column, :], window, preferred_element_type=jnp.float32
        )
    return total


def local(grades, cotangent, weight, bias):
    field = grades[0]
    cot = cotangent[0]
    in_chan, planes, rows, depth = field.shape
    whole_weight, whole_bias = (
        lax.all_gather(weight, "real", axis=0, tiled=True),
        lax.all_gather(bias, "real", axis=0, tiled=True),
    )
    out_chan = whole_weight.shape[0]
    kernel3 = whole_weight.reshape(out_chan, 27, in_chan)
    haloed = padded(field, (("strike", 1),), 1)
    padded_in = jnp.pad(haloed, ((0, 0), (0, 0), (1, 1), (1, 1)))
    total = jnp.zeros((out_chan, planes, rows, depth), jnp.float32)
    for shift_x, shift_y, shift_z, column in tap_list():
        window = padded_in[
            :,
            1 + shift_x : 1 + shift_x + planes,
            1 + shift_y : 1 + shift_y + rows,
            1 + shift_z : 1 + shift_z + depth,
        ]
        total = total + jnp.einsum(
            "oi,ixyz->oxyz", kernel3[:, column, :], window, preferred_element_type=jnp.float32
        )
    pre = total + whole_bias.astype(jnp.float32)[:, None, None, None]
    sig = jax.nn.sigmoid(pre)
    activation = (pre * sig).astype(jnp.bfloat16)
    dpre = (cot.astype(jnp.float32) * sig * (1.0 + pre * (1.0 - sig))).astype(jnp.bfloat16)
    grad_haloed = padded(dpre, (("strike", 1),), 1)
    padded_grad = jnp.pad(grad_haloed, ((0, 0), (0, 0), (1, 1), (1, 1)))
    grad_field = transposed_stencil(padded_grad, kernel3, planes, rows, depth)
    grad_input = grad_field.astype(jnp.bfloat16)
    columns = []
    for shift_x, shift_y, shift_z, column in tap_list():
        window = padded_in[
            :,
            1 + shift_x : 1 + shift_x + planes,
            1 + shift_y : 1 + shift_y + rows,
            1 + shift_z : 1 + shift_z + depth,
        ]
        columns.append(
            jnp.einsum("oxyz,ixyz->oi", dpre, window, preferred_element_type=jnp.float32)
        )
    local_weight = jnp.stack(columns, axis=1).reshape(out_chan, 27 * in_chan)
    local_bias = jnp.sum(dpre.astype(jnp.float32), axis=(1, 2, 3))
    summed = lax.psum((local_weight, local_bias), "strike")
    owned_weight, owned_bias = (
        lax.psum_scatter(summed[0], "real", scatter_dimension=0, tiled=True),
        lax.psum_scatter(summed[1], "real", scatter_dimension=0, tiled=True),
    )
    cells = lax.axis_size("real") * lax.axis_size("strike") * planes * rows * depth
    factor = 1.0 / cells**0.5
    return (activation[None], grad_input[None], owned_weight * factor, owned_bias * factor)


def solution(mesh):
    in_specs = (
        P("real", None, "strike", None, None),
        P("real", None, "strike", None, None),
        P("real", None),
        P("real"),
    )
    out_specs = (
        P("real", None, "strike", None, None),
        P("real", None, "strike", None, None),
        P("real", None),
        P("real"),
    )
    return jax.shard_map(local, mesh=mesh, in_specs=in_specs, out_specs=out_specs, check_vma=False)
```

profile of v0, /device:TPU:0, one launch (start us, length us, event | category | flops | bytes accessed | tf_op | source)
XLA Modules:
  0.0 152.9 jit_solution(3832669373383652591)
XLA Ops:
  7.2 1.4 copy.380
  8.7 2.4 %collective-permute-start = (bf16[32,1,32,128]{3,0,2,1:T(8,128)(2,1)S(1)}, bf16[32,1,32,128]{3,0,2,1:T(8,128)(2,1)S(1)}, u32[]{:S(2)}, u32[]{:S(2)}) collective-permute-start(bf16[32,1,32,128]{3,0,2,1:T(8,128)(2,1)S(1)} %get-tuple-element.23), channel_id=1, source_target_pairs={{0,1},{1,2},{2,3},{3,4},{4,5},{5,6},{6,7},{8,9},{9,10},{10,11},{11... | collective-permute-start | bytes 786440 | tf_op jit(solution)/shard_map/ppermute | solution.py:14
  11.1 1.3 collective-permute-start.1
  12.4 9.2 %all_gather.6 = bf16[32,864]{1,0:T(8,128)(2,1)S(1)} all-gather(bf16[8,864]{1,0:T(8,128)(2,1)} %param.6), channel_id=1, replica_groups=mesh['real'=4,'strike'=8] {'real'}, dimensions={0}, use_global_device_ids=true | all-gather | bytes 69120 | tf_op jit(solution)/shard_map/all_gather | solution.py:56
  22.3 0.6 fusion.205
  24.0 8.9 %all-reduce.2 = bf16[32]{0:T(256)(128)(2,1)S(1)} all-reduce(bf16[32]{0:T(256)(128)(2,1)S(1)} %dynamic-update-slice), channel_id=1, replica_groups=mesh['real'=4,'strike'=8] {'real'}, use_global_device_ids=true, to_apply=%add.2 | all-reduce | flops 32 | bytes 128
  33.0 0.5 convert_element_type.24
  34.1 0.4 fusion.193
  34.6 1.6 %select_maximum_fusion.2 = bf16[32,4,34,130]{3,0,2,1:T(8,128)(2,1)S(1)} fusion(bf16[32,1,32,128]{3,0,2,1:T(8,128)(2,1)S(1)} %collective-permute-done.1, bf16[32,2,32,128]{3,0,2,1:T(8,128)(2,1)S(1)} %bitcast.638, bf16[32,1,32,128]{3,0,2,1:T(8,128)(2,1)S(1)} %collective-permute-done), kind=kLoop, calls=%fused_computation.9 | loop fusion | flops 10749440 | bytes 2180096 | tf_op jit(solution)/shard_map/concatenate | solution.py:16
  36.5 0.4 fusion.160
  36.9 0.4 fusion.163
  37.5 0.4 fusion.169
  37.9 0.4 fusion.172
  38.6 0.4 fusion.178
  40.3 0.4 convolution_bitcast_fusion.10
  41.2 0.4 convolution_bitcast_fusion.3
  41.9 0.4 convolution_bitcast_fusion.6
  42.3 0.4 convolution_bitcast_fusion.7
  43.9 1.3 fusion.53
  45.5 2.0 %convert_reduce_fusion = (f32[32]{0:T(128)}, bf16[32,2,32,128]{3,0,2,1:T(8,128)(2,1)S(1)}, bf16[1,32,2,32,128]{4,1,3,2,0:T(8,128)(2,1)S(1)}) fusion(bf16[1,32,2,32,128]{4,3,2,1,0:T(8,128)(2,1)S(1)} %copy-done.3, f32[32]{0:T(128)S(1)} %copy-done.42, f32[32,2,32,128]{3,0,2,1:T(8,128)S(1)} %convolution_bitcast_fusion, ...), kind=kOutput, calls=%fused_computation.149 | convolution fusion | flops 24117216 | bytes 15745664 | tf_op jit(solution)/shard_map/oi,ixyz->oxyz/dot_general | solution.py:71
  48.2 0.4 fusion.83
  48.6 0.4 fusion.82
  49.5 0.4 fusion.79
  50.1 0.4 fusion.77
  50.5 0.4 fusion.76
  51.2 0.4 fusion.74
  51.5 0.4 fusion.73
  52.2 0.7 fusion.71
  52.8 0.4 fusion.70
  53.5 0.4 fusion.68
  53.9 0.4 fusion.67
  54.5 0.4 fusion.65
  54.9 0.4 fusion.64
  55.8 0.4 fusion.61
  56.5 0.4 fusion.59
  56.8 0.4 fusion.58
  57.5 0.8 reshape.18
  58.4 1.3 collective-permute-start.3
  59.7 3.0 %collective-permute-start.2 = (bf16[32,1,32,128]{3,0,2,1:T(8,128)(2,1)S(1)}, bf16[32,1,32,128]{3,0,2,1:T(8,128)(2,1)S(1)}, u32[]{:S(2)}, u32[]{:S(2)}) collective-permute-start(bf16[32,1,32,128]{3,0,2,1:T(8,128)(2,1)S(1)} %get-tuple-element.21), channel_id=1, source_target_pairs={{0,1},{1,2},{2,3},{3,4},{4,5},{5,6},{6,7},{8,9},{9,10},{10,11},{11... | collective-permute-start | bytes 786440 | tf_op jit(solution)/shard_map/ppermute | solution.py:14
  62.7 1.0 copy.155
  63.7 8.7 %all-reduce.4 = f32[32]{0:T(128)S(1)} all-reduce(f32[32]{0:T(128)S(1)} %copy-done.41), channel_id=3, replica_groups=mesh['real'=4,'strike'=8] {'real'}, use_global_device_ids=true, to_apply=%region_4.5.clone | all-reduce | flops 32 | bytes 256
  72.6 29.9 %all-reduce.8.cloned.1.call-done = f32[32,864]{1,0:T(8,128)} async-done(((f32[32,864]{1,0:T(8,128)}), f32[32,864]{1,0:T(8,128)}) %all-reduce.8.cloned.1.call-update) | async-done | bytes 110608
  102.4 0.8 constant_dynamic-slice_fusion
  103.2 28.1 %all-reduce.5 = (f32[8,864]{1,0:T(8,128)S(1)}, f32[8]{0:T(128)S(1)}) all-reduce(f32[8,864]{1,0:T(8,128)S(1)} %constant_dynamic-slice_fusion, f32[8]{0:T(128)S(1)} %dynamic-slice.4), channel_id=1, replica_groups=mesh['real'=4,'strike'=8] {'strike'}, use_global_device_ids=true, to_apply=%region_0.1 | all-reduce | flops 6920 | bytes 55360 | tf_op jit(solution)/shard_map/psum | solution.py:95
  131.3 0.5 broadcast_multiply_fusion.1
  131.8 0.6 broadcast_multiply_fusion
  132.5 1.4 select_maximum_fusion
  133.9 0.4 fusion.108
  134.7 0.4 fusion.112
  135.1 0.4 fusion.114
  135.9 0.4 fusion.118
  136.3 0.4 fusion.120
  137.0 0.4 fusion.124
  137.8 0.4 fusion.128
  138.2 0.4 convolution_bitcast_fusion.14
  138.6 0.4 convolution_bitcast_fusion.15
  139.3 0.4 convolution_bitcast_fusion.17
  140.1 0.4 convolution_bitcast_fusion.19
  140.5 0.4 convolution_bitcast_fusion.20
  141.2 0.4 fusion.103
  141.6 0.4 fusion.105
  142.7 1.0 fusion.51
  144.0 1.0 fusion.57
  145.1 1.0 copy.156
  (140 shorter events, 12.8 us)
Async XLA Ops:
  7.2 15.2 %copy-start.40 = (u32[32]{0:T(128)S(1)}, u32[32]{0:T(128)}, u32[]{:S(2)}) copy-start(u32[32]{0:T(128)} %constant.18) | copy-start | bytes 388
  7.2 27.0 %copy-start = (bf16[1,32,2,32,128]{4,3,2,1,0:T(8,128)(2,1)S(1)}, bf16[1,32,2,32,128]{4,3,2,1,0:T(8,128)(2,1)}, u32[]{:S(2)}) copy-start(bf16[1,32,2,32,128]{4,3,2,1,0:T(8,128)(2,1)} %param.4) | copy-start | bytes 1572868
  7.2 16.4 %copy-start.43 = (bf16[8]{0:T(256)(128)(2,1)S(1)}, bf16[8]{0:T(256)(128)(2,1)}, u32[]{:S(2)}) copy-start(bf16[8]{0:T(256)(128)(2,1)} %param.7) | copy-start | bytes 52
  7.2 95.3 %all-reduce.8.cloned.1.call-start = ((), (), s32[]{:S(2)}) async-start(), calls=%async_computation | async-start | bytes 229376
  8.7 25.8 %collective-permute-start = (bf16[32,1,32,128]{3,0,2,1:T(8,128)(2,1)S(1)}, bf16[32,1,32,128]{3,0,2,1:T(8,128)(2,1)S(1)}, u32[]{:S(2)}, u32[]{:S(2)}) collective-permute-start(bf16[32,1,32,128]{3,0,2,1:T(8,128)(2,1)S(1)} %get-tuple-element.23), channel_id=1, source_target_pairs={{0,1},{1,2},{2,3},{3,4},{4,5},{5,6},{6,7},{8,9},{9,10},{10,11},{11... | collective-permute-start | bytes 786440 | tf_op jit(solution)/shard_map/ppermute | solution.py:14
  11.1 23.5 %collective-permute-start.1 = (bf16[32,1,32,128]{3,0,2,1:T(8,128)(2,1)S(1)}, bf16[32,1,32,128]{3,0,2,1:T(8,128)(2,1)S(1)}, u32[]{:S(2)}, u32[]{:S(2)}) collective-permute-start(bf16[32,1,32,128]{3,0,2,1:T(8,128)(2,1)S(1)} %get-tuple-element.24), channel_id=1, source_target_pairs={{1,0},{2,1},{3,2},{4,3},{5,4},{6,5},{7,6},{9,8},{10,9},{11,10},{12... | collective-permute-start | bytes 786440 | tf_op jit(solution)/shard_map/ppermute | solution.py:15
  22.2 14.0 %copy-start.38 = (bf16[32,1,32]{2,1,0:T(2,128)(2,1)}, bf16[32,1,32]{2,1,0:T(2,128)(2,1)S(1)}, u32[]{:S(2)}) copy-start(bf16[32,1,32]{2,1,0:T(2,128)(2,1)S(1)} %get-tuple-element.37) | copy-start | bytes 6148
  22.2 14.0 %copy-start.22 = (bf16[32,1,32]{2,1,0:T(2,128)(2,1)}, bf16[32,1,32]{2,1,0:T(2,128)(2,1)S(1)}, u32[]{:S(2)}) copy-start(bf16[32,1,32]{2,1,0:T(2,128)(2,1)S(1)} %get-tuple-element.38) | copy-start | bytes 6148
  22.2 14.3 %copy-start.20 = (bf16[32,1,32]{2,1,0:T(2,128)(2,1)}, bf16[32,1,32]{2,1,0:T(2,128)(2,1)S(1)}, u32[]{:S(2)}) copy-start(bf16[32,1,32]{2,1,0:T(2,128)(2,1)S(1)} %get-tuple-element.39) | copy-start | bytes 6148
  22.2 14.6 %copy-start.18 = (bf16[32,1,32]{2,1,0:T(2,128)(2,1)}, bf16[32,1,32]{2,1,0:T(2,128)(2,1)S(1)}, u32[]{:S(2)}) copy-start(bf16[32,1,32]{2,1,0:T(2,128)(2,1)S(1)} %get-tuple-element.40) | copy-start | bytes 6148
  22.3 15.0 %copy-start.16 = (bf16[32,1,32]{2,1,0:T(2,128)(2,1)}, bf16[32,1,32]{2,1,0:T(2,128)(2,1)S(1)}, u32[]{:S(2)}) copy-start(bf16[32,1,32]{2,1,0:T(2,128)(2,1)S(1)} %get-tuple-element.41) | copy-start | bytes 6148
  22.3 15.3 %copy-start.14 = (bf16[32,1,32]{2,1,0:T(2,128)(2,1)}, bf16[32,1,32]{2,1,0:T(2,128)(2,1)S(1)}, u32[]{:S(2)}) copy-start(bf16[32,1,32]{2,1,0:T(2,128)(2,1)S(1)} %get-tuple-element.42) | copy-start | bytes 6148
  22.3 15.6 %copy-start.12 = (bf16[32,1,32]{2,1,0:T(2,128)(2,1)}, bf16[32,1,32]{2,1,0:T(2,128)(2,1)S(1)}, u32[]{:S(2)}) copy-start(bf16[32,1,32]{2,1,0:T(2,128)(2,1)S(1)} %get-tuple-element.43) | copy-start | bytes 6148
  22.3 17.7 %copy-start.10 = (bf16[32,1,32]{2,1,0:T(2,128)(2,1)}, bf16[32,1,32]{2,1,0:T(2,128)(2,1)S(1)}, u32[]{:S(2)}) copy-start(bf16[32,1,32]{2,1,0:T(2,128)(2,1)S(1)} %get-tuple-element.26) | copy-start | bytes 6148
  22.3 18.7 %copy-start.8 = (bf16[32,1,32]{2,1,0:T(2,128)(2,1)}, bf16[32,1,32]{2,1,0:T(2,128)(2,1)S(1)}, u32[]{:S(2)}) copy-start(bf16[32,1,32]{2,1,0:T(2,128)(2,1)S(1)} %get-tuple-element.27) | copy-start | bytes 6148
  22.3 18.9 %copy-start.6 = (bf16[32,1,32]{2,1,0:T(2,128)(2,1)}, bf16[32,1,32]{2,1,0:T(2,128)(2,1)S(1)}, u32[]{:S(2)}) copy-start(bf16[32,1,32]{2,1,0:T(2,128)(2,1)S(1)} %get-tuple-element.28) | copy-start | bytes 6148
  22.3 19.3 %copy-start.4 = (bf16[32,1,32]{2,1,0:T(2,128)(2,1)}, bf16[32,1,32]{2,1,0:T(2,128)(2,1)S(1)}, u32[]{:S(2)}) copy-start(bf16[32,1,32]{2,1,0:T(2,128)(2,1)S(1)} %get-tuple-element.30) | copy-start | bytes 6148
  24.0 14.3 %copy-start.36 = (bf16[32,1,32]{2,1,0:T(2,128)(2,1)}, bf16[32,1,32]{2,1,0:T(2,128)(2,1)S(1)}, u32[]{:S(2)}) copy-start(bf16[32,1,32]{2,1,0:T(2,128)(2,1)S(1)} %get-tuple-element.45) | copy-start | bytes 6148
  24.0 14.6 %copy-start.34 = (bf16[32,1,32]{2,1,0:T(2,128)(2,1)}, bf16[32,1,32]{2,1,0:T(2,128)(2,1)S(1)}, u32[]{:S(2)}) copy-start(bf16[32,1,32]{2,1,0:T(2,128)(2,1)S(1)} %get-tuple-element.46) | copy-start | bytes 6148
  24.0 14.9 %copy-start.32 = (bf16[32,1,32]{2,1,0:T(2,128)(2,1)}, bf16[32,1,32]{2,1,0:T(2,128)(2,1)S(1)}, u32[]{:S(2)}) copy-start(bf16[32,1,32]{2,1,0:T(2,128)(2,1)S(1)} %get-tuple-element.48) | copy-start | bytes 6148
  24.0 15.2 %copy-start.30 = (bf16[32,1,32]{2,1,0:T(2,128)(2,1)}, bf16[32,1,32]{2,1,0:T(2,128)(2,1)S(1)}, u32[]{:S(2)}) copy-start(bf16[32,1,32]{2,1,0:T(2,128)(2,1)S(1)} %get-tuple-element.49) | copy-start | bytes 6148
  24.0 15.6 %copy-start.28 = (bf16[32,1,32]{2,1,0:T(2,128)(2,1)}, bf16[32,1,32]{2,1,0:T(2,128)(2,1)S(1)}, u32[]{:S(2)}) copy-start(bf16[32,1,32]{2,1,0:T(2,128)(2,1)S(1)} %get-tuple-element.50) | copy-start | bytes 6148
  24.0 19.2 %copy-start.26 = (bf16[32,1,32]{2,1,0:T(2,128)(2,1)}, bf16[32,1,32]{2,1,0:T(2,128)(2,1)S(1)}, u32[]{:S(2)}) copy-start(bf16[32,1,32]{2,1,0:T(2,128)(2,1)S(1)} %get-tuple-element.51) | copy-start | bytes 6148
  24.0 19.6 %copy-start.24 = (bf16[32,1,32]{2,1,0:T(2,128)(2,1)}, bf16[32,1,32]{2,1,0:T(2,128)(2,1)S(1)}, u32[]{:S(2)}) copy-start(bf16[32,1,32]{2,1,0:T(2,128)(2,1)S(1)} %get-tuple-element.47) | copy-start | bytes 6148
  34.6 9.1 %copy-start.1 = (bf16[32,1,32,128]{3,0,2,1:T(8,128)(2,1)}, bf16[32,1,32,128]{3,0,2,1:T(8,128)(2,1)S(1)}, u32[]{:S(2)}) copy-start(bf16[32,1,32,128]{3,0,2,1:T(8,128)(2,1)S(1)} %collective-permute-done) | copy-start | bytes 786436
  43.9 1.6 %copy-start.3 = (bf16[1,32,2,32,128]{4,3,2,1,0:T(8,128)(2,1)S(1)}, bf16[1,32,2,32,128]{4,3,2,1,0:T(8,128)(2,1)}, u32[]{:S(2)}) copy-start(bf16[1,32,2,32,128]{4,3,2,1,0:T(8,128)(2,1)} %param.5) | copy-start | bytes 1572868
  43.9 1.6 %copy-start.42 = (f32[32]{0:T(128)S(1)}, f32[32]{0:T(128)}, u32[]{:S(2)}) copy-start(f32[32]{0:T(128)} %convert_element_type.24) | copy-start | bytes 388
  45.5 2.3 %copy-start.39 = (bf16[32,1,32]{2,1,0:T(2,128)(2,1)S(1)}, bf16[32,1,32]{2,1,0:T(2,128)(2,1)}, u32[]{:S(2)}) copy-start(bf16[32,1,32]{2,1,0:T(2,128)(2,1)} %copy-done.38) | copy-start | bytes 6148
  47.8 1.4 copy-start.2
  56.8 6.9 %copy-start.41 = (f32[32]{0:T(128)S(1)}, f32[32]{0:T(128)}, u32[]{:S(2)}) copy-start(f32[32]{0:T(128)} %get-tuple-element.18) | copy-start | bytes 388
  58.4 74.1 %collective-permute-start.3 = (bf16[32,1,32,128]{3,0,2,1:T(8,128)(2,1)S(1)}, bf16[32,1,32,128]{3,0,2,1:T(8,128)(2,1)S(1)}, u32[]{:S(2)}, u32[]{:S(2)}) collective-permute-start(bf16[32,1,32,128]{3,0,2,1:T(8,128)(2,1)S(1)} %get-tuple-element.22), channel_id=1, source_target_pairs={{1,0},{2,1},{3,2},{4,3},{5,4},{6,5},{7,6},{9,8},{10,9},{11,10},{12... | collective-permute-start | bytes 786440 | tf_op jit(solution)/shard_map/ppermute | solution.py:15
  59.7 72.8 %collective-permute-start.2 = (bf16[32,1,32,128]{3,0,2,1:T(8,128)(2,1)S(1)}, bf16[32,1,32,128]{3,0,2,1:T(8,128)(2,1)S(1)}, u32[]{:S(2)}, u32[]{:S(2)}) collective-permute-start(bf16[32,1,32,128]{3,0,2,1:T(8,128)(2,1)S(1)} %get-tuple-element.21), channel_id=1, source_target_pairs={{0,1},{1,2},{2,3},{3,4},{4,5},{5,6},{6,7},{8,9},{9,10},{10,11},{11... | collective-permute-start | bytes 786440 | tf_op jit(solution)/shard_map/ppermute | solution.py:14
  62.7 71.1 %copy-start.23 = (bf16[32,1,32]{2,1,0:T(2,128)(2,1)S(1)}, bf16[32,1,32]{2,1,0:T(2,128)(2,1)}, u32[]{:S(2)}) copy-start(bf16[32,1,32]{2,1,0:T(2,128)(2,1)} %copy-done.22) | copy-start | bytes 6148
  132.5 1.8 %copy-start.21 = (bf16[32,1,32]{2,1,0:T(2,128)(2,1)S(1)}, bf16[32,1,32]{2,1,0:T(2,128)(2,1)}, u32[]{:S(2)}) copy-start(bf16[32,1,32]{2,1,0:T(2,128)(2,1)} %copy-done.20) | copy-start | bytes 6148
  133.9 0.8 copy-start.19
  133.9 1.2 copy-start.17
  134.3 1.2 copy-start.15
  134.7 1.2 copy-start.13
  135.1 1.2 copy-start.37
  135.5 1.2 copy-start.35
  135.9 1.2 copy-start.33
  136.3 1.2 copy-start.31
  136.7 1.1 copy-start.29
  137.0 1.2 copy-start.11
  137.4 1.2 copy-start.9
  137.8 1.2 copy-start.7
  138.2 1.1 copy-start.5
  140.9 1.1 copy-start.27
  141.2 1.1 copy-start.25
Sparse Core Ops, SparseCore 0:
  58.5 43.9 all-reduce.7
where the time goes:
time: 153 us
  blocking collectives  55 us (36%)
  matrix products  31.7 us (21%)
  waiting for transfers between devices  29.9 us (20%)
  between operations  16.4 us (11%)
  starting transfers between devices  8.04 us (5%)
  local copies, waits for them, and re-layouts  7.13 us (5%)
  other arithmetic  4.63 us (3%)
    unnamed x2, waiting for transfers between devices  29.9 us
    psum x1, blocking collectives, local(): summed = lax.psum((local_weight, local_bias), 'strike')  28.1 us
    unnamed x2, blocking collectives  17.7 us
    dot_general x27, matrix products, local(): jnp.einsum('oi,ixyz->oxyz', kernel3[:, column, :], window, preferred_elem...  11.4 us
    dot_general x27, matrix products, transposed_stencil(): jnp.einsum('oi,oxyz->ixyz', kernel3[:, column, :], window, preferred_elem...  11.1 us
    dot_general x27, matrix products, local(): jnp.einsum('oxyz,ixyz->oi', dpre, window, preferred_element_type=jnp.floa...  9.25 us
    all_gather x1, blocking collectives, local(): lax.all_gather(weight, 'real', axis=0, tiled=True)  9.23 us
    ppermute x2, starting transfers between devices, padded(): before = lax.ppermute(last, axis, up)  5.42 us
  transfers between devices with their start and end apart: 5, of which 1 were waited for; matrix products, arithmetic and copies ran while one was open for 4% of the time, Pallas kernels for 0%

commit v1 on v0

--- a/solution.py
+++ b/solution.py
@@ -14,6 +14,44 @@
         before = lax.ppermute(last, axis, up)
         after = lax.ppermute(leading, axis, down)
         value = jnp.concatenate([before, value, after], axis=dim)
+    return value
+
+
+def swap(value, axis, bit):
+    peers = lax.axis_size(axis)
+    return lax.ppermute(value, axis, [(i, i ^ bit) for i in range(peers)])
+
+
+def gather_rows(value, axis):
+    peers = lax.axis_size(axis)
+    me = lax.axis_index(axis)
+    blocks = jnp.zeros((peers,) + value.shape, value.dtype)
+    blocks = lax.dynamic_update_index_in_dim(blocks, value, me, 0)
+    for k in range(1, peers):
+        blocks = lax.dynamic_update_index_in_dim(blocks, swap(value, axis, k), me ^ k, 0)
+    return blocks.reshape((peers * value.shape[0],) + value.shape[1:])
+
+
+def scatter_rows(value, axis):
+    peers = lax.axis_size(axis)
+    me = lax.axis_index(axis)
+    bit = peers // 2
+    while bit >= 1:
+        half = value.shape[0] // 2
+        upper = (me // bit) % 2
+        keep = lax.dynamic_slice_in_dim(value, upper * half, half, 0)
+        send = lax.dynamic_slice_in_dim(value, (1 - upper) * half, half, 0)
+        value = keep + swap(send, axis, bit)
+        bit //= 2
+    return value
+
+
+def sum_over(value, axis):
+    peers = lax.axis_size(axis)
+    bit = 1
+    while bit < peers:
+        value = value + swap(value, axis, bit)
+        bit *= 2
     return value
 
 
@@ -52,10 +90,10 @@
     field = grades[0]
     cot = cotangent[0]
     in_chan, planes, rows, depth = field.shape
-    whole_weight, whole_bias = (
-        lax.all_gather(weight, "real", axis=0, tiled=True),
-        lax.all_gather(bias, "real", axis=0, tiled=True),
-    )
+    taps_in = weight.shape[1]
+    packed = jnp.concatenate([weight, bias[:, None]], axis=1)
+    whole = gather_rows(packed, "real")
+    whole_weight, whole_bias = whole[:, :taps_in], whole[:, taps_in]
     out_chan = whole_weight.shape[0]
     kernel3 = whole_weight.reshape(out_chan, 27, in_chan)
     haloed = padded(field, (("strike", 1),), 1)
@@ -75,10 +113,6 @@
     sig = jax.nn.sigmoid(pre)
     activation = (pre * sig).astype(jnp.bfloat16)
     dpre = (cot.astype(jnp.float32) * sig * (1.0 + pre * (1.0 - sig))).astype(jnp.bfloat16)
-    grad_haloed = padded(dpre, (("strike", 1),), 1)
-    padded_grad = jnp.pad(grad_haloed, ((0, 0), (0, 0), (1, 1), (1, 1)))
-    grad_field = transposed_stencil(padded_grad, kernel3, planes, rows, depth)
-    grad_input = grad_field.astype(jnp.bfloat16)
     columns = []
     for shift_x, shift_y, shift_z, column in tap_list():
         window = padded_in[
@@ -92,14 +126,16 @@
         )
     local_weight = jnp.stack(columns, axis=1).reshape(out_chan, 27 * in_chan)
     local_bias = jnp.sum(dpre.astype(jnp.float32), axis=(1, 2, 3))
-    summed = lax.psum((local_weight, local_bias), "strike")
-    owned_weight, owned_bias = (
-        lax.psum_scatter(summed[0], "real", scatter_dimension=0, tiled=True),
-        lax.psum_scatter(summed[1], "real", scatter_dimension=0, tiled=True),
-    )
+    local_grads = jnp.concatenate([local_weight, local_bias[:, None]], axis=1)
+    owned = sum_over(scatter_rows(local_grads, "real"), "strike")
+    grad_haloed = padded(dpre, (("strike", 1),), 1)
+    padded_grad = jnp.pad(grad_haloed, ((0, 0), (0, 0), (1, 1), (1, 1)))
+    grad_field = transposed_stencil(padded_grad, kernel3, planes, rows, depth)
+    grad_input = grad_field.astype(jnp.bfloat16)
     cells = lax.axis_size("real") * lax.axis_size("strike") * planes * rows * depth
     factor = 1.0 / cells**0.5
-    return (activation[None], grad_input[None], owned_weight * factor, owned_bias * factor)
+    owned = owned * factor
+    return (activation[None], grad_input[None], owned[:, :taps_in], owned[:, taps_in])
 
 
 def solution(mesh):

time: 153 us -> 77.3 us (0.51)
  the two profiles are of different devices: /device:TPU:0 before, /device:TPU:1 now
where the time goes in v1:
time: 77.3 us; the launch traced here: 77 us
  matrix products  30.6 us (40%)
  starting transfers between devices  23.4 us (30%)
  waiting for transfers between devices  11.6 us (15%)
  local copies, waits for them, and re-layouts  6.22 us (8%)
  other arithmetic  4.11 us (5%)
  between operations  1.1 us (1%)
    dot_general x27, matrix products, local(): jnp.einsum('oi,ixyz->oxyz', kernel3[:, column, :], window, preferred_elem...  10.8 us
    dot_general x27, matrix products, transposed_stencil(): jnp.einsum('oi,oxyz->ixyz', kernel3[:, column, :], window, preferred_elem...  10.5 us
    ppermute x8, starting transfers between devices, swap(): return lax.ppermute(value, axis, [(i, i ^ bit) for i in range(peers)])  9.89 us
    dot_general x27, matrix products, local(): jnp.einsum('oxyz,ixyz->oi', dpre, window, preferred_element_type=jnp.floa...  9.25 us
    ppermute x2, starting transfers between devices, padded(): before = lax.ppermute(last, axis, up)  7.86 us
    ppermute x8, waiting for transfers between devices, swap(): return lax.ppermute(value, axis, [(i, i ^ bit) for i in range(peers)])  5.72 us
    ppermute x2, starting transfers between devices, padded(): after = lax.ppermute(leading, axis, down)  5.6 us
    ppermute x2, waiting for transfers between devices, padded(): after = lax.ppermute(leading, axis, down)  4.73 us
  transfers between devices with their start and end apart: 12, of which 7 were waited for; matrix products, arithmetic and copies ran while one was open for 6% of the time, Pallas kernels for 0%

profile of v1, /device:TPU:1, one launch (start us, length us, event | category | flops | bytes accessed | tf_op | source)
XLA Modules:
  0.0 77.0 jit_solution(10087661856360492497)
XLA Ops:
  0.6 0.8 %copy.104 = bf16[8,1]{1,0:T(8,128)(2,1)S(1)} copy(bf16[8,1]{0,1:T(2,128)(2,1)} %bitcast.552) | data formatting | bytes 32 | tf_op jit(solution)/shard_map/broadcast_in_dim | solution.py:94
  1.5 0.8 %bitcast_dynamic-update-slice_fusion.3 = (bf16[4,8,865]{2,1,0:T(8,128)(2,1)S(1)}, bf16[8,865]{1,0:T(8,128)(2,1)S(1)}) fusion(bf16[4,8,865]{2,1,0:T(8,128)(2,1)S(1)} %broadcast_in_dim.29, s32[]{:T(128)S(6)} %select_n.41, bf16[8,1]{1,0:T(8,128)(2,1)S(1)} %copy.104, bf16[8,864]{1,0:T(8,128)(2,1)} %param.6), kind=kLoop, calls=%fused_computation.269 | loop fusion | flops 27680 | bytes 44548 | tf_op jit(solution)/shard_map/jit(dynamic_update_index_in_dim)/dynamic_update_slice | solution.py:29
  2.3 2.0 %collective-permute-start = (bf16[8,865]{1,0:T(8,128)(2,1)S(1)}, bf16[8,865]{1,0:T(8,128)(2,1)S(1)}, u32[]{:S(2)}, u32[]{:S(2)}) collective-permute-start(bf16[8,865]{1,0:T(8,128)(2,1)S(1)} %get-tuple-element.19), channel_id=1, source_target_pairs={{0,8},{8,0},{16,24},{24,16},{1,9},{9,1},{17,25},{25,17},{2,10},{10... | collective-permute-start | bytes 41528 | tf_op jit(solution)/shard_map/ppermute | solution.py:22
  4.3 1.2 %collective-permute-start.1 = (bf16[8,865]{1,0:T(8,128)(2,1)S(1)}, bf16[8,865]{1,0:T(8,128)(2,1)S(1)}, u32[]{:S(2)}, u32[]{:S(2)}) collective-permute-start(bf16[8,865]{1,0:T(8,128)(2,1)S(1)} %get-tuple-element.19), channel_id=1, source_target_pairs={{0,16},{8,24},{16,0},{24,8},{1,17},{9,25},{17,1},{25,9},{2,18},{10... | collective-permute-start | bytes 41528 | tf_op jit(solution)/shard_map/ppermute | solution.py:22
  5.5 1.4 %copy.388 = bf16[1,32,2,32,128]{4,1,3,2,0:T(8,128)(2,1)S(1)} copy(bf16[1,32,2,32,128]{4,3,2,1,0:T(8,128)(2,1)} %param.4) | data formatting | bytes 1048576 | tf_op args[0]
  7.0 4.8 %collective-permute-start.3 = (bf16[32,1,32,128]{3,0,2,1:T(8,128)(2,1)S(1)}, bf16[32,1,32,128]{3,0,2,1:T(8,128)(2,1)S(1)}, u32[]{:S(2)}, u32[]{:S(2)}) collective-permute-start(bf16[32,1,32,128]{3,0,2,1:T(8,128)(2,1)S(1)} %get-tuple-element.23), channel_id=1, source_target_pairs={{0,1},{1,2},{2,3},{3,4},{4,5},{5,6},{6,7},{8,9},{9,10},{10,11},{11... | collective-permute-start | bytes 786440 | tf_op jit(solution)/shard_map/ppermute | solution.py:14
  11.8 1.9 %collective-permute-start.4 = (bf16[32,1,32,128]{3,0,2,1:T(8,128)(2,1)S(1)}, bf16[32,1,32,128]{3,0,2,1:T(8,128)(2,1)S(1)}, u32[]{:S(2)}, u32[]{:S(2)}) collective-permute-start(bf16[32,1,32,128]{3,0,2,1:T(8,128)(2,1)S(1)} %get-tuple-element.24), channel_id=1, source_target_pairs={{1,0},{2,1},{3,2},{4,3},{5,4},{6,5},{7,6},{9,8},{10,9},{11,10},{12... | collective-permute-start | bytes 786440 | tf_op jit(solution)/shard_map/ppermute | solution.py:15
  14.7 0.4 fusion.211
  15.1 4.3 %collective-permute-done.4 = bf16[32,1,32,128]{3,0,2,1:T(8,128)(2,1)S(1)} collective-permute-done((bf16[32,1,32,128]{3,0,2,1:T(8,128)(2,1)S(1)}, bf16[32,1,32,128]{3,0,2,1:T(8,128)(2,1)S(1)}, u32[]{:S(2)}, u32[]{:S(2)}) %collective-permute-start.4) | collective-permute-done | bytes 262176 | tf_op jit(solution)/shard_map/ppermute | solution.py:15
  19.5 1.6 %select_maximum_fusion.2 = bf16[32,4,34,130]{3,0,2,1:T(8,128)(2,1)S(1)} fusion(bf16[32,1,32,128]{3,0,2,1:T(8,128)(2,1)S(1)} %collective-permute-done.4, bf16[32,2,32,128]{3,0,2,1:T(8,128)(2,1)S(1)} %bitcast.543, bf16[32,1,32,128]{3,0,2,1:T(8,128)(2,1)S(1)} %collective-permute-done.3), kind=kLoop, calls=%fused_computation.9 | loop fusion | flops 10749440 | bytes 2180096 | tf_op jit(solution)/shard_map/concatenate | solution.py:16
  21.3 0.4 fusion.174
  21.7 0.4 fusion.177
  22.3 0.4 fusion.183
  22.7 0.4 fusion.186
  23.3 0.4 fusion.192
  24.0 0.4 fusion.198
  24.3 0.4 fusion.201
  24.7 0.4 fusion.139
  25.3 0.4 fusion.145
  26.0 0.4 fusion.151
  26.3 0.4 fusion.154
  27.0 0.4 fusion.160
  27.3 0.4 fusion.163
  28.0 0.4 fusion.136
  28.6 1.2 %fusion.48 = f32[32,2,32,128]{3,0,2,1:T(8,128)S(1)} fusion(f32[32,2,32,128]{3,0,2,1:T(8,128)S(1)} %fusion.211, f32[32,2,32,128]{3,0,2,1:T(8,128)S(1)} %fusion.171, f32[32,2,32,128]{3,0,2,1:T(8,128)S(1)} %fusion.174, f32[32,2,32,128]{3,0,2,1:T(8,128)S(1)} %fusion.177, f32[32,2,32,128]{3,0,2,1:T(8,128)S(1)} %fusion.180, f32[32,2,32,128]{3,0,2,1:T(8,128)S(1)} %fusion.183, ...), kind=kOutput, calls=%fused_computation.60 | convolution fusion | flops 20185088 | bytes 15220736 | tf_op jit(solution)/shard_map/oi,ixyz->oxyz/dot_general | solution.py:109
  30.1 1.5 %convert_reduce_fusion = (f32[32]{0:T(128)S(1)}, bf16[32,2,32,128]{3,0,2,1:T(8,128)(2,1)S(1)}, bf16[1,32,2,32,128]{4,1,3,2,0:T(8,128)(2,1)S(1)}) fusion(bf16[1,32,2,32,128]{4,3,2,1,0:T(8,128)(2,1)S(1)} %copy-done.1, f32[32]{0:T(128)S(1)} %convert_reduce_fusion.1, f32[32,2,32,128]{3,0,2,1:T(8,128)S(1)} %fusion.136, f32[32,2,32,128]{3,0,2,1:T(8,128)S(1)} %fusion.139, ...), kind=kOutput, calls=%fused_computation.124 | convolution fusion | flops 24117216 | bytes 15745664 | tf_op jit(solution)/shard_map/oi,ixyz->oxyz/dot_general | solution.py:109
  31.9 0.4 fusion.80
  32.2 0.4 fusion.79
  33.1 0.4 fusion.76
  33.8 0.4 fusion.74
  34.2 0.4 fusion.73
  34.8 0.4 fusion.71
  35.2 0.4 fusion.70
  35.8 0.4 fusion.68
  36.3 0.6 fusion.67
  37.2 0.4 fusion.65
  37.5 0.4 fusion.64
  38.2 0.4 fusion.62
  38.5 0.4 fusion.61
  39.5 0.4 fusion.58
  40.1 0.4 fusion.56
  40.5 0.4 fusion.55
  41.5 1.2 %collective-permute-start.7 = (f32[16,865]{1,0:T(8,128)S(1)}, f32[16,865]{1,0:T(8,128)S(1)}, u32[]{:S(2)}, u32[]{:S(2)}) collective-permute-start(f32[16,865]{1,0:T(8,128)S(1)} %fusion.207), channel_id=1, source_target_pairs={{0,16},{8,24},{16,0},{24,8},{1,17},{9,25},{17,1},{25,9},{2,18},{10... | collective-permute-start | bytes 166088 | tf_op jit(solution)/shard_map/ppermute | solution.py:22
  42.7 2.1 %collective-permute-done.7 = f32[16,865]{1,0:T(8,128)S(1)} collective-permute-done((f32[16,865]{1,0:T(8,128)S(1)}, f32[16,865]{1,0:T(8,128)S(1)}, u32[]{:S(2)}, u32[]{:S(2)}) %collective-permute-start.7) | collective-permute-done | bytes 55392 | tf_op jit(solution)/shard_map/ppermute | solution.py:22
  44.9 1.2 %collective-permute-start.8 = (f32[8,865]{1,0:T(8,128)S(1)}, f32[8,865]{1,0:T(8,128)S(1)}, u32[]{:S(2)}, u32[]{:S(2)}) collective-permute-start(f32[8,865]{1,0:T(8,128)S(1)} %constant_dynamic-slice_fusion), channel_id=1, source_target_pairs={{0,8},{8,0},{16,24},{24,16},{1,9},{9,1},{17,25},{25,17},{2,10},{10... | collective-permute-start | bytes 83048 | tf_op jit(solution)/shard_map/ppermute | solution.py:22
  46.1 1.5 %collective-permute-done.8 = f32[8,865]{1,0:T(8,128)S(1)} collective-permute-done((f32[8,865]{1,0:T(8,128)S(1)}, f32[8,865]{1,0:T(8,128)S(1)}, u32[]{:S(2)}, u32[]{:S(2)}) %collective-permute-start.8) | collective-permute-done | bytes 27712 | tf_op jit(solution)/shard_map/ppermute | solution.py:22
  47.7 1.2 %collective-permute-done.9 = f32[8,865]{1,0:T(8,128)S(1)} collective-permute-done((f32[8,865]{1,0:T(8,128)S(1)}, f32[8,865]{1,0:T(8,128)S(1)}, u32[]{:S(2)}, u32[]{:S(2)}) %collective-permute-start.9) | collective-permute-done | bytes 27712 | tf_op jit(solution)/shard_map/ppermute | solution.py:22
  48.9 1.7 %collective-permute-start.10 = (f32[8,865]{1,0:T(8,128)S(1)}, f32[8,865]{1,0:T(8,128)S(1)}, u32[]{:S(2)}, u32[]{:S(2)}) collective-permute-start(f32[8,865]{1,0:T(8,128)S(1)} %add.291), channel_id=1, source_target_pairs={{0,2},{1,3},{2,0},{3,1},{4,6},{5,7},{6,4},{7,5},{8,10},{9,11},{10,... | collective-permute-start | bytes 83048 | tf_op jit(solution)/shard_map/ppermute | solution.py:22
  50.8 0.9 %collective-permute-done.10 = f32[8,865]{1,0:T(8,128)S(1)} collective-permute-done((f32[8,865]{1,0:T(8,128)S(1)}, f32[8,865]{1,0:T(8,128)S(1)}, u32[]{:S(2)}, u32[]{:S(2)}) %collective-permute-start.10) | collective-permute-done | bytes 27712 | tf_op jit(solution)/shard_map/ppermute | solution.py:22
  51.8 2.5 %collective-permute-start.11 = (f32[8,865]{1,0:T(8,128)S(1)}, f32[8,865]{1,0:T(8,128)S(1)}, u32[]{:S(2)}, u32[]{:S(2)}) collective-permute-start(f32[8,865]{1,0:T(8,128)S(1)} %add.292), channel_id=1, source_target_pairs={{0,4},{1,5},{2,6},{3,7},{4,0},{5,1},{6,2},{7,3},{8,12},{9,13},{10,... | collective-permute-start | bytes 83048 | tf_op jit(solution)/shard_map/ppermute | solution.py:22
  54.3 3.7 %collective-permute-start.6 = (bf16[32,1,32,128]{3,0,2,1:T(8,128)(2,1)S(1)}, bf16[32,1,32,128]{3,0,2,1:T(8,128)(2,1)S(1)}, u32[]{:S(2)}, u32[]{:S(2)}) collective-permute-start(bf16[32,1,32,128]{3,0,2,1:T(8,128)(2,1)S(1)} %get-tuple-element.22), channel_id=1, source_target_pairs={{1,0},{2,1},{3,2},{4,3},{5,4},{6,5},{7,6},{9,8},{10,9},{11,10},{12... | collective-permute-start | bytes 786440 | tf_op jit(solution)/shard_map/ppermute | solution.py:15
  58.0 3.1 %collective-permute-start.5 = (bf16[32,1,32,128]{3,0,2,1:T(8,128)(2,1)S(1)}, bf16[32,1,32,128]{3,0,2,1:T(8,128)(2,1)S(1)}, u32[]{:S(2)}, u32[]{:S(2)}) collective-permute-start(bf16[32,1,32,128]{3,0,2,1:T(8,128)(2,1)S(1)} %get-tuple-element.21), channel_id=1, source_target_pairs={{0,1},{1,2},{2,3},{3,4},{4,5},{5,6},{6,7},{8,9},{9,10},{10,11},{11... | collective-permute-start | bytes 786440 | tf_op jit(solution)/shard_map/ppermute | solution.py:14
  61.0 1.0 %copy.163 = bf16[1,32,2,32,128]{4,3,2,1,0:T(8,128)(2,1)} copy(bf16[1,32,2,32,128]{4,1,3,2,0:T(8,128)(2,1)S(1)} %get-tuple-element.20) | data formatting | bytes 1048576
  62.1 0.7 slice_reduce_fusion
  62.8 0.4 collective-permute-done.6
  63.2 1.2 %collective-permute-done.5 = bf16[32,1,32,128]{3,0,2,1:T(8,128)(2,1)S(1)} collective-permute-done((bf16[32,1,32,128]{3,0,2,1:T(8,128)(2,1)S(1)}, bf16[32,1,32,128]{3,0,2,1:T(8,128)(2,1)S(1)}, u32[]{:S(2)}, u32[]{:S(2)}) %collective-permute-start.5) | collective-permute-done | bytes 262176 | tf_op jit(solution)/shard_map/ppermute | solution.py:14
  64.3 1.4 %select_maximum_fusion = bf16[32,4,34,130]{3,0,2,1:T(8,128)(2,1)S(1)} fusion(bf16[32,1,32,128]{3,0,2,1:T(8,128)(2,1)S(1)} %collective-permute-done.6, bf16[32,2,32,128]{3,0,2,1:T(8,128)(2,1)S(1)} %get-tuple-element.17, bf16[32,1,32,128]{3,0,2,1:T(8,128)(2,1)S(1)} %collective-permute-done.5), kind=kLoop, calls=%fused_computation.7 | loop fusion | flops 10749440 | bytes 2180096 | tf_op jit(solution)/shard_map/concatenate | solution.py:16
  65.7 0.4 fusion.109
  66.8 0.4 fusion.115
  69.6 0.4 fusion.100
  71.0 0.4 fusion.86
  73.7 1.0 %fusion.50 = f32[32,2,32,128]{3,0,2,1:T(8,128)S(1)} fusion(f32[32,2,32,128]{3,0,2,1:T(8,128)S(1)} %fusion.210, f32[32,2,32,128]{3,0,2,1:T(8,128)S(1)} %fusion.109, f32[32,2,32,128]{3,0,2,1:T(8,128)S(1)} %fusion.111, f32[32,2,32,128]{3,0,2,1:T(8,128)S(1)} %fusion.113, f32[32,2,32,128]{3,0,2,1:T(8,128)S(1)} %fusion.115, f32[32,2,32,128]{3,0,2,1:T(8,128)S(1)} %fusion.117, ...), kind=kOutput, calls=%fused_computation.62 | convolution fusion | flops 20185088 | bytes 15220736 | tf_op jit(solution)/shard_map/oi,oxyz->ixyz/dot_general | solution.py:83
  75.0 1.0 %fusion.54 = bf16[1,32,2,32,128]{4,1,3,2,0:T(8,128)(2,1)S(1)} fusion(f32[32,2,32,128]{3,0,2,1:T(8,128)S(1)} %fusion.84, f32[32,2,32,128]{3,0,2,1:T(8,128)S(1)} %fusion.86, f32[32,2,32,128]{3,0,2,1:T(8,128)S(1)} %fusion.88, f32[32,2,32,128]{3,0,2,1:T(8,128)S(1)} %fusion.90, f32[32,2,32,128]{3,0,2,1:T(8,128)S(1)} %fusion.92, ...), kind=kOutput, calls=%fused_computation.66 | convolution fusion | flops 20447232 | bytes 14696448 | tf_op jit(solution)/shard_map/oi,oxyz->ixyz/dot_general | solution.py:83
  76.0 1.0 %copy.164 = bf16[1,32,2,32,128]{4,3,2,1,0:T(8,128)(2,1)} copy(bf16[1,32,2,32,128]{4,1,3,2,0:T(8,128)(2,1)S(1)} %fusion.54) | data formatting | bytes 1048576
  (75 shorter events, 14.6 us)
Async XLA Ops:
  0.6 14.1 %copy-start = (bf16[1,32,2,32,128]{4,3,2,1,0:T(8,128)(2,1)S(1)}, bf16[1,32,2,32,128]{4,3,2,1,0:T(8,128)(2,1)}, u32[]{:S(2)}) copy-start(bf16[1,32,2,32,128]{4,3,2,1,0:T(8,128)(2,1)} %param.4) | copy-start | bytes 1572868
  2.3 11.5 %collective-permute-start = (bf16[8,865]{1,0:T(8,128)(2,1)S(1)}, bf16[8,865]{1,0:T(8,128)(2,1)S(1)}, u32[]{:S(2)}, u32[]{:S(2)}) collective-permute-start(bf16[8,865]{1,0:T(8,128)(2,1)S(1)} %get-tuple-element.19), channel_id=1, source_target_pairs={{0,8},{8,0},{16,24},{24,16},{1,9},{9,1},{17,25},{25,17},{2,10},{10... | collective-permute-start | bytes 41528 | tf_op jit(solution)/shard_map/ppermute | solution.py:22
  4.3 9.5 %collective-permute-start.1 = (bf16[8,865]{1,0:T(8,128)(2,1)S(1)}, bf16[8,865]{1,0:T(8,128)(2,1)S(1)}, u32[]{:S(2)}, u32[]{:S(2)}) collective-permute-start(bf16[8,865]{1,0:T(8,128)(2,1)S(1)} %get-tuple-element.19), channel_id=1, source_target_pairs={{0,16},{8,24},{16,0},{24,8},{1,17},{9,25},{17,1},{25,9},{2,18},{10... | collective-permute-start | bytes 41528 | tf_op jit(solution)/shard_map/ppermute | solution.py:22
  5.5 8.3 %collective-permute-start.2 = (bf16[8,865]{1,0:T(8,128)(2,1)S(1)}, bf16[8,865]{1,0:T(8,128)(2,1)S(1)}, u32[]{:S(2)}, u32[]{:S(2)}) collective-permute-start(bf16[8,865]{1,0:T(8,128)(2,1)S(1)} %get-tuple-element.19), channel_id=1, source_target_pairs={{0,24},{8,16},{16,8},{24,0},{1,25},{9,17},{17,9},{25,1},{2,26},{10... | collective-permute-start | bytes 41528 | tf_op jit(solution)/shard_map/ppermute | solution.py:22
  7.0 8.2 %collective-permute-start.3 = (bf16[32,1,32,128]{3,0,2,1:T(8,128)(2,1)S(1)}, bf16[32,1,32,128]{3,0,2,1:T(8,128)(2,1)S(1)}, u32[]{:S(2)}, u32[]{:S(2)}) collective-permute-start(bf16[32,1,32,128]{3,0,2,1:T(8,128)(2,1)S(1)} %get-tuple-element.23), channel_id=1, source_target_pairs={{0,1},{1,2},{2,3},{3,4},{4,5},{5,6},{6,7},{8,9},{9,10},{10,11},{11... | collective-permute-start | bytes 786440 | tf_op jit(solution)/shard_map/ppermute | solution.py:14
  11.8 7.7 %collective-permute-start.4 = (bf16[32,1,32,128]{3,0,2,1:T(8,128)(2,1)S(1)}, bf16[32,1,32,128]{3,0,2,1:T(8,128)(2,1)S(1)}, u32[]{:S(2)}, u32[]{:S(2)}) collective-permute-start(bf16[32,1,32,128]{3,0,2,1:T(8,128)(2,1)S(1)} %get-tuple-element.24), channel_id=1, source_target_pairs={{1,0},{2,1},{3,2},{4,3},{5,4},{6,5},{7,6},{9,8},{10,9},{11,10},{12... | collective-permute-start | bytes 786440 | tf_op jit(solution)/shard_map/ppermute | solution.py:15
  28.6 1.5 %copy-start.1 = (bf16[1,32,2,32,128]{4,3,2,1,0:T(8,128)(2,1)S(1)}, bf16[1,32,2,32,128]{4,3,2,1,0:T(8,128)(2,1)}, u32[]{:S(2)}) copy-start(bf16[1,32,2,32,128]{4,3,2,1,0:T(8,128)(2,1)} %param.5) | copy-start | bytes 1572868
  41.5 3.3 %collective-permute-start.7 = (f32[16,865]{1,0:T(8,128)S(1)}, f32[16,865]{1,0:T(8,128)S(1)}, u32[]{:S(2)}, u32[]{:S(2)}) collective-permute-start(f32[16,865]{1,0:T(8,128)S(1)} %fusion.207), channel_id=1, source_target_pairs={{0,16},{8,24},{16,0},{24,8},{1,17},{9,25},{17,1},{25,9},{2,18},{10... | collective-permute-start | bytes 166088 | tf_op jit(solution)/shard_map/ppermute | solution.py:22
  44.9 2.7 %collective-permute-start.8 = (f32[8,865]{1,0:T(8,128)S(1)}, f32[8,865]{1,0:T(8,128)S(1)}, u32[]{:S(2)}, u32[]{:S(2)}) collective-permute-start(f32[8,865]{1,0:T(8,128)S(1)} %constant_dynamic-slice_fusion), channel_id=1, source_target_pairs={{0,8},{8,0},{16,24},{24,16},{1,9},{9,1},{17,25},{25,17},{2,10},{10... | collective-permute-start | bytes 83048 | tf_op jit(solution)/shard_map/ppermute | solution.py:22
  47.7 1.2 %collective-permute-start.9 = (f32[8,865]{1,0:T(8,128)S(1)}, f32[8,865]{1,0:T(8,128)S(1)}, u32[]{:S(2)}, u32[]{:S(2)}) collective-permute-start(f32[8,865]{1,0:T(8,128)S(1)} %dynamic-slice_add_fusion), channel_id=1, source_target_pairs={{0,1},{1,0},{2,3},{3,2},{4,5},{5,4},{6,7},{7,6},{8,9},{9,8},{10,11... | collective-permute-start | bytes 83048 | tf_op jit(solution)/shard_map/ppermute | solution.py:22
  48.9 2.9 %collective-permute-start.10 = (f32[8,865]{1,0:T(8,128)S(1)}, f32[8,865]{1,0:T(8,128)S(1)}, u32[]{:S(2)}, u32[]{:S(2)}) collective-permute-start(f32[8,865]{1,0:T(8,128)S(1)} %add.291), channel_id=1, source_target_pairs={{0,2},{1,3},{2,0},{3,1},{4,6},{5,7},{6,4},{7,5},{8,10},{9,11},{10,... | collective-permute-start | bytes 83048 | tf_op jit(solution)/shard_map/ppermute | solution.py:22
  51.8 10.3 %collective-permute-start.11 = (f32[8,865]{1,0:T(8,128)S(1)}, f32[8,865]{1,0:T(8,128)S(1)}, u32[]{:S(2)}, u32[]{:S(2)}) collective-permute-start(f32[8,865]{1,0:T(8,128)S(1)} %add.292), channel_id=1, source_target_pairs={{0,4},{1,5},{2,6},{3,7},{4,0},{5,1},{6,2},{7,3},{8,12},{9,13},{10,... | collective-permute-start | bytes 83048 | tf_op jit(solution)/shard_map/ppermute | solution.py:22
  54.3 8.9 %collective-permute-start.6 = (bf16[32,1,32,128]{3,0,2,1:T(8,128)(2,1)S(1)}, bf16[32,1,32,128]{3,0,2,1:T(8,128)(2,1)S(1)}, u32[]{:S(2)}, u32[]{:S(2)}) collective-permute-start(bf16[32,1,32,128]{3,0,2,1:T(8,128)(2,1)S(1)} %get-tuple-element.22), channel_id=1, source_target_pairs={{1,0},{2,1},{3,2},{4,3},{5,4},{6,5},{7,6},{9,8},{10,9},{11,10},{12... | collective-permute-start | bytes 786440 | tf_op jit(solution)/shard_map/ppermute | solution.py:15
  58.0 6.4 %collective-permute-start.5 = (bf16[32,1,32,128]{3,0,2,1:T(8,128)(2,1)S(1)}, bf16[32,1,32,128]{3,0,2,1:T(8,128)(2,1)S(1)}, u32[]{:S(2)}, u32[]{:S(2)}) collective-permute-start(bf16[32,1,32,128]{3,0,2,1:T(8,128)(2,1)S(1)} %get-tuple-element.21), channel_id=1, source_target_pairs={{0,1},{1,2},{2,3},{3,4},{4,5},{5,6},{6,7},{8,9},{9,10},{10,11},{11... | collective-permute-start | bytes 786440 | tf_op jit(solution)/shard_map/ppermute | solution.py:14
  62.1 4.0 %copy-start.2 = (f32[8,865]{1,0:T(8,128)}, f32[8,865]{1,0:T(8,128)S(1)}, u32[]{:S(2)}) copy-start(f32[8,865]{1,0:T(8,128)S(1)} %add_multiply_fusion) | copy-start | bytes 83044

commit v2 on v1

--- a/solution.py
+++ b/solution.py
@@ -32,29 +32,6 @@
     return blocks.reshape((peers * value.shape[0],) + value.shape[1:])
 
 
-def scatter_rows(value, axis):
-    peers = lax.axis_size(axis)
-    me = lax.axis_index(axis)
-    bit = peers // 2
-    while bit >= 1:
-        half = value.shape[0] // 2
-        upper = (me // bit) % 2
-        keep = lax.dynamic_slice_in_dim(value, upper * half, half, 0)
-        send = lax.dynamic_slice_in_dim(value, (1 - upper) * half, half, 0)
-        value = keep + swap(send, axis, bit)
-        bit //= 2
-    return value
-
-
-def sum_over(value, axis):
-    peers = lax.axis_size(axis)
-    bit = 1
-    while bit < peers:
-        value = value + swap(value, axis, bit)
-        bit *= 2
-    return value
-
-
 def tap_list():
     listing = []
     for shift_x in (-1, 0, 1):
@@ -71,9 +48,8 @@
     return listing
 
 
-def transposed_stencil(padded_grad, kernel3, planes, rows, depth):
-    total = jnp.zeros((kernel3.shape[2], planes, rows, depth), jnp.float32)
-    for shift_x, shift_y, shift_z, column in tap_list():
+def transposed_taps(total, padded_grad, kernel3, taps, planes, rows, depth):
+    for shift_x, shift_y, shift_z, column in taps:
         window = padded_grad[
             :,
             1 - shift_x : 1 - shift_x + planes,
@@ -84,6 +60,42 @@
             "oi,oxyz->ixyz", kernel3[:, column, :], window, preferred_element_type=jnp.float32
         )
     return total
+
+
+def reduce_beside(local_grads, padded_grad, kernel3, planes, rows, depth):
+    rounds = []
+    bit = lax.axis_size("real") // 2
+    while bit >= 1:
+        rounds.append(("real", bit))
+        bit //= 2
+    bit = 1
+    while bit < lax.axis_size("strike"):
+        rounds.append(("strike", bit))
+        bit *= 2
+    taps = tap_list()
+    bounds = [len(taps) * k // len(rounds) for k in range(len(rounds) + 1)]
+    total = jnp.zeros((kernel3.shape[2], planes, rows, depth), jnp.float32)
+    value = local_grads
+    for k, (axis, bit) in enumerate(rounds):
+        if axis == "real":
+            half = value.shape[0] // 2
+            upper = (lax.axis_index(axis) // bit) % 2
+            keep = lax.dynamic_slice_in_dim(value, upper * half, half, 0)
+            send = lax.dynamic_slice_in_dim(value, (1 - upper) * half, half, 0)
+        else:
+            keep, send = value, value
+        send, total = lax.optimization_barrier((send, total))
+        received = swap(send, axis, bit)
+        chunk = taps[bounds[k] : bounds[k + 1]]
+        total = lax.cond(
+            lax.axis_index("strike") < lax.axis_size("strike"),
+            lambda t, c=chunk: transposed_taps(t, padded_grad, kernel3, c, planes, rows, depth),
+            lambda t: t,
+            total,
+        )
+        received, total = lax.optimization_barrier((received, total))
+        value = keep + received
+    return value, total
 
 
 def local(grades, cotangent, weight, bias):
@@ -113,24 +125,33 @@
     sig = jax.nn.sigmoid(pre)
     activation = (pre * sig).astype(jnp.bfloat16)
     dpre = (cot.astype(jnp.float32) * sig * (1.0 + pre * (1.0 - sig))).astype(jnp.bfloat16)
-    columns = []
-    for shift_x, shift_y, shift_z, column in tap_list():
-        window = padded_in[
-            :,
-            1 + shift_x : 1 + shift_x + planes,
-            1 + shift_y : 1 + shift_y + rows,
-            1 + shift_z : 1 + shift_z + depth,
-        ]
-        columns.append(
-            jnp.einsum("oxyz,ixyz->oi", dpre, window, preferred_element_type=jnp.float32)
-        )
-    local_weight = jnp.stack(columns, axis=1).reshape(out_chan, 27 * in_chan)
+    grad_haloed = padded(dpre, (("strike", 1),), 1)
+    def weight_terms(operands):
+        values, grads = operands
+        columns = []
+        for shift_x, shift_y, shift_z, column in tap_list():
+            window = values[
+                :,
+                1 + shift_x : 1 + shift_x + planes,
+                1 + shift_y : 1 + shift_y + rows,
+                1 + shift_z : 1 + shift_z + depth,
+            ]
+            columns.append(
+                jnp.einsum("oxyz,ixyz->oi", grads, window, preferred_element_type=jnp.float32)
+            )
+        return jnp.stack(columns, axis=1).reshape(out_chan, 27 * in_chan)
+
+    local_weight = lax.cond(
+        lax.axis_index("strike") < lax.axis_size("strike"),
+        weight_terms,
+        lambda operands: jnp.zeros((out_chan, 27 * in_chan), jnp.float32),
+        (padded_in, dpre),
+    )
     local_bias = jnp.sum(dpre.astype(jnp.float32), axis=(1, 2, 3))
     local_grads = jnp.concatenate([local_weight, local_bias[:, None]], axis=1)
-    owned = sum_over(scatter_rows(local_grads, "real"), "strike")
-    grad_haloed = padded(dpre, (("strike", 1),), 1)
+    grad_haloed, local_grads = lax.optimization_barrier((grad_haloed, local_grads))
     padded_grad = jnp.pad(grad_haloed, ((0, 0), (0, 0), (1, 1), (1, 1)))
-    grad_field = transposed_stencil(padded_grad, kernel3, planes, rows, depth)
+    owned, grad_field = reduce_beside(local_grads, padded_grad, kernel3, planes, rows, depth)
     grad_input = grad_field.astype(jnp.bfloat16)
     cells = lax.axis_size("real") * lax.axis_size("strike") * planes * rows * depth
     factor = 1.0 / cells**0.5

time: 77.3 us -> 104 us (1.35)
  the two profiles are of different devices: /device:TPU:1 before, /device:TPU:0 now
where the time goes in v2:
time: 104 us; the launch traced here: 102 us
  matrix products  49.1 us (47%)
  starting transfers between devices  23.1 us (22%)
  local copies, waits for them, and re-layouts  15.9 us (15%)
  other arithmetic  9.41 us (9%)
  waiting for transfers between devices  3.05 us (3%)
  between operations  1.06 us (1%)
    dot_general x27, matrix products, transposed_taps(): jnp.einsum('oi,oxyz->ixyz', kernel3[:, column, :], window, preferred_elem...  28 us
    dot_general x27, matrix products, local(): jnp.einsum('oi,ixyz->oxyz', kernel3[:, column, :], window, preferred_elem...  11.9 us
    ppermute x8, starting transfers between devices, swap(): return lax.ppermute(value, axis, [(i, i ^ bit) for i in range(peers)])  11.7 us
    dot_general x27, matrix products, weight_terms(): jnp.einsum('oxyz,ixyz->oi', grads, window, preferred_element_type=jnp.flo...  9.14 us
    ppermute x2, starting transfers between devices, padded(): before = lax.ppermute(last, axis, up)  8.66 us
    add x4, other arithmetic, reduce_beside(): value = keep + received  5.01 us
    another operation x5, local copies, waits for them, and re-layouts  4.89 us
    unnamed x12, local copies, waits for them, and re-layouts  4.05 us
  transfers between devices with their start and end apart: 12, of which 2 were waited for; matrix products, arithmetic and copies ran while one was open for 48% of the time, Pallas kernels for 0%

profile of v2, /device:TPU:0, one launch (start us, length us, event | category | flops | bytes accessed | tf_op | source)
XLA Modules:
  0.0 101.8 jit_solution(2161104650486854188)
XLA Ops:
  0.6 0.8 copy.61
  1.5 0.8 bitcast_dynamic-update-slice_fusion.3
  2.3 2.9 %collective-permute-start = (bf16[8,865]{1,0:T(8,128)(2,1)S(1)}, bf16[8,865]{1,0:T(8,128)(2,1)S(1)}, u32[]{:S(2)}, u32[]{:S(2)}) collective-permute-start(bf16[8,865]{1,0:T(8,128)(2,1)S(1)} %get-tuple-element.182), channel_id=1, source_target_pairs={{0,8},{8,0},{16,24},{24,16},{1,9},{9,1},{17,25},{25,17},{2,10},{10... | collective-permute-start | bytes 41528 | tf_op jit(solution)/shard_map/ppermute | solution.py:22
  5.2 1.5 %collective-permute-start.1 = (bf16[8,865]{1,0:T(8,128)(2,1)S(1)}, bf16[8,865]{1,0:T(8,128)(2,1)S(1)}, u32[]{:S(2)}, u32[]{:S(2)}) collective-permute-start(bf16[8,865]{1,0:T(8,128)(2,1)S(1)} %get-tuple-element.182), channel_id=1, source_target_pairs={{0,16},{8,24},{16,0},{24,8},{1,17},{9,25},{17,1},{25,9},{2,18},{10... | collective-permute-start | bytes 41528 | tf_op jit(solution)/shard_map/ppermute | solution.py:22
  6.7 1.4 %copy.271 = bf16[1,32,2,32,128]{4,1,3,2,0:T(8,128)(2,1)S(1)} copy(bf16[1,32,2,32,128]{4,3,2,1,0:T(8,128)(2,1)} %param.16) | data formatting | bytes 1048576 | tf_op args[0]
  8.1 1.3 %collective-permute-start.3 = (bf16[32,1,32,128]{3,0,2,1:T(8,128)(2,1)S(1)}, bf16[32,1,32,128]{3,0,2,1:T(8,128)(2,1)S(1)}, u32[]{:S(2)}, u32[]{:S(2)}) collective-permute-start(bf16[32,1,32,128]{3,0,2,1:T(8,128)(2,1)S(1)} %get-tuple-element.186), channel_id=1, source_target_pairs={{0,1},{1,2},{2,3},{3,4},{4,5},{5,6},{6,7},{8,9},{9,10},{10,11},{11... | collective-permute-start | bytes 786440 | tf_op jit(solution)/shard_map/ppermute | solution.py:14
  9.5 1.3 %collective-permute-start.4 = (bf16[32,1,32,128]{3,0,2,1:T(8,128)(2,1)S(1)}, bf16[32,1,32,128]{3,0,2,1:T(8,128)(2,1)S(1)}, u32[]{:S(2)}, u32[]{:S(2)}) collective-permute-start(bf16[32,1,32,128]{3,0,2,1:T(8,128)(2,1)S(1)} %get-tuple-element.187), channel_id=1, source_target_pairs={{1,0},{2,1},{3,2},{4,3},{5,4},{6,5},{7,6},{9,8},{10,9},{11,10},{12... | collective-permute-start | bytes 786440 | tf_op jit(solution)/shard_map/ppermute | solution.py:15
  12.6 2.5 %collective-permute-done.4 = bf16[32,1,32,128]{3,0,2,1:T(8,128)(2,1)S(1)} collective-permute-done((bf16[32,1,32,128]{3,0,2,1:T(8,128)(2,1)S(1)}, bf16[32,1,32,128]{3,0,2,1:T(8,128)(2,1)S(1)}, u32[]{:S(2)}, u32[]{:S(2)}) %collective-permute-start.4) | collective-permute-done | bytes 262176 | tf_op jit(solution)/shard_map/ppermute | solution.py:15
  15.2 1.4 %select_maximum_fusion = bf16[32,4,34,130]{3,0,2,1:T(8,128)(2,1)S(1)} fusion(bf16[32,1,32,128]{3,0,2,1:T(8,128)(2,1)S(1)} %collective-permute-done.4, bf16[32,2,32,128]{3,0,2,1:T(8,128)(2,1)S(1)} %bitcast.650, bf16[32,1,32,128]{3,0,2,1:T(8,128)(2,1)S(1)} %collective-permute-done.3), kind=kLoop, calls=%fused_computation.169 | loop fusion | flops 10749440 | bytes 2180096 | tf_op jit(solution)/shard_map/concatenate | solution.py:16
  24.1 1.0 fusion.109
  25.4 2.8 %convert_reduce_fusion = (f32[32]{0:T(128)}, bf16[32,2,32,128]{3,0,2,1:T(8,128)(2,1)S(1)}, bf16[1,32,2,32,128]{4,1,3,2,0:T(8,128)(2,1)}) fusion(bf16[1,32,2,32,128]{4,3,2,1,0:T(8,128)(2,1)S(1)} %copy-done.1, f32[32]{0:T(128)S(1)} %convert_reduce_fusion.1, f32[32,2,32,128]{3,0,2,1:T(8,128)S(1)} %fusion.115, f32[32,2,32,128]{3,0,2,1:T(8,128)S(1)} %fusion.117, ...), kind=kOutput, calls=%fused_computation.206 | convolution fusion | flops 24117216 | bytes 15745664 | tf_op jit(solution)/shard_map/oi,ixyz->oxyz/dot_general | solution.py:121
  28.2 7.4 %collective-permute-start.5 = (bf16[32,1,32,128]{3,0,2,1:T(8,128)(2,1)S(1)}, bf16[32,1,32,128]{3,0,2,1:T(8,128)(2,1)}, u32[]{:S(2)}, u32[]{:S(2)}) collective-permute-start(bf16[32,1,32,128]{3,0,2,1:T(8,128)(2,1)S(1)} %get-tuple-element.184), channel_id=1, source_target_pairs={{0,1},{1,2},{2,3},{3,4},{4,5},{5,6},{6,7},{8,9},{9,10},{10,11},{11... | collective-permute-start | bytes 786440 | tf_op jit(solution)/shard_map/ppermute | solution.py:14
  35.6 1.5 %collective-permute-start.6 = (bf16[32,1,32,128]{3,0,2,1:T(8,128)(2,1)S(1)}, bf16[32,1,32,128]{3,0,2,1:T(8,128)(2,1)}, u32[]{:S(2)}, u32[]{:S(2)}) collective-permute-start(bf16[32,1,32,128]{3,0,2,1:T(8,128)(2,1)S(1)} %get-tuple-element.185), channel_id=1, source_target_pairs={{1,0},{2,1},{3,2},{4,3},{5,4},{6,5},{7,6},{9,8},{10,9},{11,10},{12... | collective-permute-start | bytes 786440 | tf_op jit(solution)/shard_map/ppermute | solution.py:15
  37.8 9.6 %conditional.6 = (f32[32,864]{1,0:T(8,128)S(1)}) conditional(s32[]{:T(128)} %convert_element_type.45, () %tuple.55, (bf16[32,4,34,130]{3,0,2,1:T(8,128)(2,1)S(1)}, bf16[32,2,32,128]{3,0,2,1:T(8,128)(2,1)S(1)}) %tuple.56), branch_computations={%region_0.1_spmd, %region_1.2_spmd} | conditional | flops 452984832 | bytes 29196296 | solution.py:144
  47.5 1.2 %pad_maximum_fusion = bf16[32,4,32,128]{3,0,2,1:T(8,128)(2,1)S(1)} fusion(bf16[32,1,32,128]{3,0,2,1:T(8,128)(2,1)} %collective-permute-done.6, bf16[32,2,32,128]{3,0,2,1:T(8,128)(2,1)S(1)} %get-tuple-element.180, bf16[32,1,32,128]{3,0,2,1:T(8,128)(2,1)} %collective-permute-done.5), kind=kLoop, calls=%fused_computation.201 | loop fusion | flops 1048576 | bytes 2097152 | tf_op jit(solution)/shard_map/concatenate | solution.py:16
  49.4 1.6 %collective-permute-start.7 = (f32[16,865]{1,0:T(8,128)}, f32[16,865]{1,0:T(8,128)}, u32[]{:S(2)}, u32[]{:S(2)}) collective-permute-start(f32[16,865]{1,0:T(8,128)} %constant_dynamic-slice_fusion.1), channel_id=1, source_target_pairs={{0,16},{8,24},{16,0},{24,8},{1,17},{9,25},{17,1},{25,9},{2,18},{10... | collective-permute-start | bytes 166088 | tf_op jit(solution)/shard_map/ppermute | solution.py:22
  51.0 0.8 pad.8
  51.9 6.2 %conditional.7 = (f32[32,2,32,128]{3,0,2,1:T(8,128)S(1)}) conditional(s32[]{:T(128)} %convert_element_type.45, f32[32,2,32,128]{3,0,2,1:T(8,128)S(1)} %broadcast_in_dim.40, (bf16[32,27,32]{2,1,0:T(8,128)(2,1)S(1)}, bf16[32,4,34,130]{3,0,2,1:T(8,128)(2,1)S(1)}, f32[32,2,32,128]{3,0,2,1:T(8,128)S(1)}) %tuple.59), branch_computations={%region_3.4_spmd, %region_4.5_spmd} | conditional | flops 85196800 | bytes 13258760 | solution.py:90
  51.9 1.0 copy.92
  52.8 1.0 %convolution_add_fusion.4 = f32[32,2,32,128]{3,0,2,1:T(8,128)S(1)} fusion(f32[32,2,32,128]{3,0,2,1:T(8,128)S(1)} %get-tuple-element.59, bf16[32,4,34,130]{3,0,2,1:T(8,128)(2,1)S(1)} %get-tuple-element.61, bf16[32,27,32]{0,2,1:T(8,128)(2,1)} %copy.92), kind=kOutput, calls=%fused_computation.85 | convolution fusion | flops 17039360 | bytes 2629632 | tf_op jit(solution)/shard_map/cond/branch_1_fun/oi,oxyz->ixyz/dot_general | solution.py:59
  53.9 1.1 %convolution_add_fusion.3 = f32[32,2,32,128]{3,0,2,1:T(8,128)S(1)} fusion(f32[32,2,32,128]{3,0,2,1:T(8,128)S(1)} %convolution_add_fusion.4, bf16[32,4,34,130]{3,0,2,1:T(8,128)(2,1)S(1)} %get-tuple-element.61, bf16[32,27,32]{0,2,1:T(8,128)(2,1)} %copy.92), kind=kOutput, calls=%fused_computation.84 | convolution fusion | flops 17039360 | bytes 2629632 | tf_op jit(solution)/shard_map/cond/branch_1_fun/oi,oxyz->ixyz/dot_general | solution.py:59
  55.0 1.0 convolution_add_fusion.2
  55.9 1.1 %convolution_add_fusion.1 = f32[32,2,32,128]{3,0,2,1:T(8,128)S(1)} fusion(f32[32,2,32,128]{3,0,2,1:T(8,128)S(1)} %convolution_add_fusion.2, bf16[32,4,34,130]{3,0,2,1:T(8,128)(2,1)S(1)} %get-tuple-element.61, bf16[32,27,32]{0,2,1:T(8,128)(2,1)} %copy.92), kind=kOutput, calls=%fused_computation.82 | convolution fusion | flops 17039360 | bytes 2629632 | tf_op jit(solution)/shard_map/cond/branch_1_fun/oi,oxyz->ixyz/dot_general | solution.py:59
  57.0 1.1 %convolution_add_fusion = f32[32,2,32,128]{3,0,2,1:T(8,128)S(1)} fusion(f32[32,2,32,128]{3,0,2,1:T(8,128)S(1)} %convolution_add_fusion.1, bf16[32,4,34,130]{3,0,2,1:T(8,128)(2,1)S(1)} %get-tuple-element.61, bf16[32,27,32]{0,2,1:T(8,128)(2,1)} %copy.92), kind=kOutput, calls=%fused_computation.81 | convolution fusion | flops 17039360 | bytes 2629632 | tf_op jit(solution)/shard_map/cond/branch_1_fun/oi,oxyz->ixyz/dot_general | solution.py:59
  58.1 0.9 dynamic-slice_add_fusion
  60.2 1.5 %collective-permute-start.8 = (f32[8,865]{1,0:T(8,128)}, f32[8,865]{1,0:T(8,128)}, u32[]{:S(2)}, u32[]{:S(2)}) collective-permute-start(f32[8,865]{1,0:T(8,128)} %constant_dynamic-slice_fusion), channel_id=1, source_target_pairs={{0,8},{8,0},{16,24},{24,16},{1,9},{9,1},{17,25},{25,17},{2,10},{10... | collective-permute-start | bytes 83048 | tf_op jit(solution)/shard_map/ppermute | solution.py:22
  61.7 6.1 %conditional.8 = (f32[32,2,32,128]{3,0,2,1:T(8,128)S(1)}) conditional(s32[]{:T(128)} %convert_element_type.45, f32[32,2,32,128]{3,0,2,1:T(8,128)S(1)} %get-tuple-element.216, (bf16[32,27,32]{2,1,0:T(8,128)(2,1)S(1)}, bf16[32,4,34,130]{3,0,2,1:T(8,128)(2,1)S(1)}, f32[32,2,32,128]{3,0,2,1:T(8,128)S(1)}) %tuple.62), branch_computations={%region_5.6_spmd, %region_6.7_spmd} | conditional | flops 85196800 | bytes 13258760 | solution.py:90
  61.7 1.0 copy.93
  62.6 1.0 convolution_add_fusion.9
  63.6 1.1 %convolution_add_fusion.8 = f32[32,2,32,128]{3,0,2,1:T(8,128)S(1)} fusion(f32[32,2,32,128]{3,0,2,1:T(8,128)S(1)} %convolution_add_fusion.9, bf16[32,4,34,130]{3,0,2,1:T(8,128)(2,1)S(1)} %get-tuple-element.64, bf16[32,27,32]{0,2,1:T(8,128)(2,1)} %copy.93), kind=kOutput, calls=%fused_computation.99 | convolution fusion | flops 17039360 | bytes 2629632 | tf_op jit(solution)/shard_map/cond/branch_1_fun/oi,oxyz->ixyz/dot_general | solution.py:59
  64.7 1.1 %convolution_add_fusion.7 = f32[32,2,32,128]{3,0,2,1:T(8,128)S(1)} fusion(f32[32,2,32,128]{3,0,2,1:T(8,128)S(1)} %convolution_add_fusion.8, bf16[32,4,34,130]{3,0,2,1:T(8,128)(2,1)S(1)} %get-tuple-element.64, bf16[32,27,32]{0,2,1:T(8,128)(2,1)} %copy.93), kind=kOutput, calls=%fused_computation.98 | convolution fusion | flops 17039360 | bytes 2629632 | tf_op jit(solution)/shard_map/cond/branch_1_fun/oi,oxyz->ixyz/dot_general | solution.py:59
  65.7 1.0 convolution_add_fusion.6
  66.7 1.1 %convolution_add_fusion.5 = f32[32,2,32,128]{3,0,2,1:T(8,128)S(1)} fusion(f32[32,2,32,128]{3,0,2,1:T(8,128)S(1)} %convolution_add_fusion.6, bf16[32,4,34,130]{3,0,2,1:T(8,128)(2,1)S(1)} %get-tuple-element.64, bf16[32,27,32]{0,2,1:T(8,128)(2,1)} %copy.93), kind=kOutput, calls=%fused_computation.96 | convolution fusion | flops 17039360 | bytes 2629632 | tf_op jit(solution)/shard_map/cond/branch_1_fun/oi,oxyz->ixyz/dot_general | solution.py:59
  67.8 1.4 %dynamic-slice_add_fusion.1 = f32[8,865]{1,0:T(8,128)} fusion(f32[8,865]{1,0:T(8,128)} %collective-permute-done.8, f32[16,865]{1,0:T(8,128)} %copy-done.3, s32[]{:T(128)S(6)} %select_n.50), kind=kLoop, calls=%fused_computation.267 | loop fusion | flops 6920 | bytes 83044 | tf_op jit(solution)/shard_map/add | solution.py:97
  69.7 7.4 %conditional.9 = (f32[32,2,32,128]{3,0,2,1:T(8,128)S(1)}) conditional(s32[]{:T(128)} %convert_element_type.45, f32[32,2,32,128]{3,0,2,1:T(8,128)S(1)} %get-tuple-element.217, (bf16[32,27,32]{2,1,0:T(8,128)(2,1)S(1)}, bf16[32,4,34,130]{3,0,2,1:T(8,128)(2,1)S(1)}, f32[32,2,32,128]{3,0,2,1:T(8,128)S(1)}) %tuple.65), branch_computations={%region_7.8_spmd, %region_8.9_spmd} | conditional | flops 102236160 | bytes 15888392 | solution.py:90
  69.7 1.0 copy.94
  70.7 1.0 %convolution_add_fusion.15 = f32[32,2,32,128]{3,0,2,1:T(8,128)S(1)} fusion(f32[32,2,32,128]{3,0,2,1:T(8,128)S(1)} %get-tuple-element.65, bf16[32,4,34,130]{3,0,2,1:T(8,128)(2,1)S(1)} %get-tuple-element.67, bf16[32,27,32]{0,2,1:T(8,128)(2,1)} %copy.94), kind=kOutput, calls=%fused_computation.116 | convolution fusion | flops 17039360 | bytes 2629632 | tf_op jit(solution)/shard_map/cond/branch_1_fun/oi,oxyz->ixyz/dot_general | solution.py:59
  71.7 1.0 convolution_add_fusion.14
  72.7 1.3 %convolution_add_fusion.13 = f32[32,2,32,128]{3,0,2,1:T(8,128)S(1)} fusion(f32[32,2,32,128]{3,0,2,1:T(8,128)S(1)} %convolution_add_fusion.14, bf16[32,4,34,130]{3,0,2,1:T(8,128)(2,1)S(1)} %get-tuple-element.67, bf16[32,27,32]{0,2,1:T(8,128)(2,1)} %copy.94), kind=kOutput, calls=%fused_computation.114 | convolution fusion | flops 17039360 | bytes 2629632 | tf_op jit(solution)/shard_map/cond/branch_1_fun/oi,oxyz->ixyz/dot_general | solution.py:59
  74.0 1.1 %convolution_add_fusion.12 = f32[32,2,32,128]{3,0,2,1:T(8,128)S(1)} fusion(f32[32,2,32,128]{3,0,2,1:T(8,128)S(1)} %convolution_add_fusion.13, bf16[32,4,34,130]{3,0,2,1:T(8,128)(2,1)S(1)} %get-tuple-element.67, bf16[32,27,32]{0,2,1:T(8,128)(2,1)} %copy.94), kind=kOutput, calls=%fused_computation.113 | convolution fusion | flops 17039360 | bytes 2629632 | tf_op jit(solution)/shard_map/cond/branch_1_fun/oi,oxyz->ixyz/dot_general | solution.py:59
  75.1 1.0 convolution_add_fusion.11
  76.1 1.1 %convolution_add_fusion.10 = f32[32,2,32,128]{3,0,2,1:T(8,128)S(1)} fusion(f32[32,2,32,128]{3,0,2,1:T(8,128)S(1)} %convolution_add_fusion.11, bf16[32,4,34,130]{3,0,2,1:T(8,128)(2,1)S(1)} %get-tuple-element.67, bf16[32,27,32]{0,2,1:T(8,128)(2,1)} %copy.94), kind=kOutput, calls=%fused_computation.111 | convolution fusion | flops 17039360 | bytes 2629632 | tf_op jit(solution)/shard_map/cond/branch_1_fun/oi,oxyz->ixyz/dot_general | solution.py:59
  77.1 1.4 %add.268 = f32[8,865]{1,0:T(8,128)} add(f32[8,865]{1,0:T(8,128)} %dynamic-slice_add_fusion.1, f32[8,865]{1,0:T(8,128)} %collective-permute-done.9) | non-fusion elementwise | flops 6920 | bytes 83040 | tf_op jit(solution)/shard_map/add | solution.py:97
  78.5 1.1 %collective-permute-start.10 = (f32[8,865]{1,0:T(8,128)}, f32[8,865]{1,0:T(8,128)}, u32[]{:S(2)}, u32[]{:S(2)}) collective-permute-start(f32[8,865]{1,0:T(8,128)} %add.268), channel_id=1, source_target_pairs={{0,2},{1,3},{2,0},{3,1},{4,6},{5,7},{6,4},{7,5},{8,10},{9,11},{10,... | collective-permute-start | bytes 83048 | tf_op jit(solution)/shard_map/ppermute | solution.py:22
  79.6 6.1 %conditional.10 = (f32[32,2,32,128]{3,0,2,1:T(8,128)S(1)}) conditional(s32[]{:T(128)} %convert_element_type.45, f32[32,2,32,128]{3,0,2,1:T(8,128)S(1)} %get-tuple-element.218, (bf16[32,27,32]{2,1,0:T(8,128)(2,1)S(1)}, bf16[32,4,34,130]{3,0,2,1:T(8,128)(2,1)S(1)}, f32[32,2,32,128]{3,0,2,1:T(8,128)S(1)}) %tuple.68), branch_computations={%region_9.10_spmd, %region_10.11_spmd} | conditional | flops 85196800 | bytes 13258760 | solution.py:90
  79.6 1.0 copy.95
  80.6 1.1 %convolution_add_fusion.20 = f32[32,2,32,128]{3,0,2,1:T(8,128)S(1)} fusion(f32[32,2,32,128]{3,0,2,1:T(8,128)S(1)} %get-tuple-element.68, bf16[32,4,34,130]{3,0,2,1:T(8,128)(2,1)S(1)} %get-tuple-element.70, bf16[32,27,32]{0,2,1:T(8,128)(2,1)} %copy.95), kind=kOutput, calls=%fused_computation.133 | convolution fusion | flops 17039360 | bytes 2629632 | tf_op jit(solution)/shard_map/cond/branch_1_fun/oi,oxyz->ixyz/dot_general | solution.py:59
  81.6 1.0 convolution_add_fusion.19
  82.6 1.1 %convolution_add_fusion.18 = f32[32,2,32,128]{3,0,2,1:T(8,128)S(1)} fusion(f32[32,2,32,128]{3,0,2,1:T(8,128)S(1)} %convolution_add_fusion.19, bf16[32,4,34,130]{3,0,2,1:T(8,128)(2,1)S(1)} %get-tuple-element.70, bf16[32,27,32]{0,2,1:T(8,128)(2,1)} %copy.95), kind=kOutput, calls=%fused_computation.131 | convolution fusion | flops 17039360 | bytes 2629632 | tf_op jit(solution)/shard_map/cond/branch_1_fun/oi,oxyz->ixyz/dot_general | solution.py:59
  83.7 1.1 %convolution_add_fusion.17 = f32[32,2,32,128]{3,0,2,1:T(8,128)S(1)} fusion(f32[32,2,32,128]{3,0,2,1:T(8,128)S(1)} %convolution_add_fusion.18, bf16[32,4,34,130]{3,0,2,1:T(8,128)(2,1)S(1)} %get-tuple-element.70, bf16[32,27,32]{0,2,1:T(8,128)(2,1)} %copy.95), kind=kOutput, calls=%fused_computation.130 | convolution fusion | flops 17039360 | bytes 2629632 | tf_op jit(solution)/shard_map/cond/branch_1_fun/oi,oxyz->ixyz/dot_general | solution.py:59
  84.8 1.0 convolution_add_fusion.16
  85.8 1.4 %add.269 = f32[8,865]{1,0:T(8,128)} add(f32[8,865]{1,0:T(8,128)} %add.268, f32[8,865]{1,0:T(8,128)} %collective-permute-done.10) | non-fusion elementwise | flops 6920 | bytes 83040 | tf_op jit(solution)/shard_map/add | solution.py:97
  87.1 2.6 %collective-permute-start.11 = (f32[8,865]{1,0:T(8,128)}, f32[8,865]{1,0:T(8,128)}, u32[]{:S(2)}, u32[]{:S(2)}) collective-permute-start(f32[8,865]{1,0:T(8,128)} %add.269), channel_id=1, source_target_pairs={{0,4},{1,5},{2,6},{3,7},{4,0},{5,1},{6,2},{7,3},{8,12},{9,13},{10,... | collective-permute-start | bytes 83048 | tf_op jit(solution)/shard_map/ppermute | solution.py:22
  89.7 2.0 %copy.98 = bf16[1,32,2,32,128]{4,3,2,1,0:T(8,128)(2,1)} copy(bf16[1,32,2,32,128]{4,1,3,2,0:T(8,128)(2,1)} %get-tuple-element.183) | data formatting | bytes 1048576
  91.8 7.2 %conditional.11 = (f32[32,2,32,128]{3,0,2,1:T(8,128)S(1)}) conditional(s32[]{:T(128)} %convert_element_type.45, f32[32,2,32,128]{3,0,2,1:T(8,128)S(1)} %get-tuple-element.219, (bf16[32,27,32]{2,1,0:T(8,128)(2,1)S(1)}, bf16[32,4,34,130]{3,0,2,1:T(8,128)(2,1)S(1)}, f32[32,2,32,128]{3,0,2,1:T(8,128)S(1)}) %tuple.71), branch_computations={%region_11.12_spmd, %region_12.13_spmd} | conditional | flops 102236160 | bytes 15888392 | solution.py:90
  91.8 1.0 copy.96
  92.7 1.1 %convolution_add_fusion.26 = f32[32,2,32,128]{3,0,2,1:T(8,128)S(1)} fusion(f32[32,2,32,128]{3,0,2,1:T(8,128)S(1)} %get-tuple-element.71, bf16[32,4,34,130]{3,0,2,1:T(8,128)(2,1)S(1)} %get-tuple-element.73, bf16[32,27,32]{0,2,1:T(8,128)(2,1)} %copy.96), kind=kOutput, calls=%fused_computation.149 | convolution fusion | flops 17039360 | bytes 2629632 | tf_op jit(solution)/shard_map/cond/branch_1_fun/oi,oxyz->ixyz/dot_general | solution.py:59
  93.8 1.1 %convolution_add_fusion.25 = f32[32,2,32,128]{3,0,2,1:T(8,128)S(1)} fusion(f32[32,2,32,128]{3,0,2,1:T(8,128)S(1)} %convolution_add_fusion.26, bf16[32,4,34,130]{3,0,2,1:T(8,128)(2,1)S(1)} %get-tuple-element.73, bf16[32,27,32]{0,2,1:T(8,128)(2,1)} %copy.96), kind=kOutput, calls=%fused_computation.148 | convolution fusion | flops 17039360 | bytes 2629632 | tf_op jit(solution)/shard_map/cond/branch_1_fun/oi,oxyz->ixyz/dot_general | solution.py:59
  94.9 1.0 convolution_add_fusion.24
  95.8 1.1 %convolution_add_fusion.23 = f32[32,2,32,128]{3,0,2,1:T(8,128)S(1)} fusion(f32[32,2,32,128]{3,0,2,1:T(8,128)S(1)} %convolution_add_fusion.24, bf16[32,4,34,130]{3,0,2,1:T(8,128)(2,1)S(1)} %get-tuple-element.73, bf16[32,27,32]{0,2,1:T(8,128)(2,1)} %copy.96), kind=kOutput, calls=%fused_computation.146 | convolution fusion | flops 17039360 | bytes 2629632 | tf_op jit(solution)/shard_map/cond/branch_1_fun/oi,oxyz->ixyz/dot_general | solution.py:59
  96.9 1.1 %convolution_add_fusion.22 = f32[32,2,32,128]{3,0,2,1:T(8,128)S(1)} fusion(f32[32,2,32,128]{3,0,2,1:T(8,128)S(1)} %convolution_add_fusion.23, bf16[32,4,34,130]{3,0,2,1:T(8,128)(2,1)S(1)} %get-tuple-element.73, bf16[32,27,32]{0,2,1:T(8,128)(2,1)} %copy.96), kind=kOutput, calls=%fused_computation.145 | convolution fusion | flops 17039360 | bytes 2629632 | tf_op jit(solution)/shard_map/cond/branch_1_fun/oi,oxyz->ixyz/dot_general | solution.py:59
  98.0 1.0 convolution_add_fusion.21
  99.0 0.8 add_multiply_fusion
  100.4 1.4 %copy.270 = bf16[32,2,32,128]{3,2,1,0:T(8,128)(2,1)} copy(f32[32,2,32,128]{3,0,2,1:T(8,128)S(1)} %get-tuple-element.220) | data formatting | bytes 1572864 | tf_op jit(solution)/shard_map/optimization_barrier | solution.py:96
  (93 shorter events, 23.2 us)
Async XLA Ops:
  0.6 11.6 %copy-start = (bf16[1,32,2,32,128]{4,3,2,1,0:T(8,128)(2,1)S(1)}, bf16[1,32,2,32,128]{4,3,2,1,0:T(8,128)(2,1)}, u32[]{:S(2)}) copy-start(bf16[1,32,2,32,128]{4,3,2,1,0:T(8,128)(2,1)} %param.16) | copy-start | bytes 1572868
  2.3 8.5 %collective-permute-start = (bf16[8,865]{1,0:T(8,128)(2,1)S(1)}, bf16[8,865]{1,0:T(8,128)(2,1)S(1)}, u32[]{:S(2)}, u32[]{:S(2)}) collective-permute-start(bf16[8,865]{1,0:T(8,128)(2,1)S(1)} %get-tuple-element.182), channel_id=1, source_target_pairs={{0,8},{8,0},{16,24},{24,16},{1,9},{9,1},{17,25},{25,17},{2,10},{10... | collective-permute-start | bytes 41528 | tf_op jit(solution)/shard_map/ppermute | solution.py:22
  5.2 5.6 %collective-permute-start.1 = (bf16[8,865]{1,0:T(8,128)(2,1)S(1)}, bf16[8,865]{1,0:T(8,128)(2,1)S(1)}, u32[]{:S(2)}, u32[]{:S(2)}) collective-permute-start(bf16[8,865]{1,0:T(8,128)(2,1)S(1)} %get-tuple-element.182), channel_id=1, source_target_pairs={{0,16},{8,24},{16,0},{24,8},{1,17},{9,25},{17,1},{25,9},{2,18},{10... | collective-permute-start | bytes 41528 | tf_op jit(solution)/shard_map/ppermute | solution.py:22
  6.7 4.6 %collective-permute-start.2 = (bf16[8,865]{1,0:T(8,128)(2,1)S(1)}, bf16[8,865]{1,0:T(8,128)(2,1)S(1)}, u32[]{:S(2)}, u32[]{:S(2)}) collective-permute-start(bf16[8,865]{1,0:T(8,128)(2,1)S(1)} %get-tuple-element.182), channel_id=1, source_target_pairs={{0,24},{8,16},{16,8},{24,0},{1,25},{9,17},{17,9},{25,1},{2,26},{10... | collective-permute-start | bytes 41528 | tf_op jit(solution)/shard_map/ppermute | solution.py:22
  8.1 4.5 %collective-permute-start.3 = (bf16[32,1,32,128]{3,0,2,1:T(8,128)(2,1)S(1)}, bf16[32,1,32,128]{3,0,2,1:T(8,128)(2,1)S(1)}, u32[]{:S(2)}, u32[]{:S(2)}) collective-permute-start(bf16[32,1,32,128]{3,0,2,1:T(8,128)(2,1)S(1)} %get-tuple-element.186), channel_id=1, source_target_pairs={{0,1},{1,2},{2,3},{3,4},{4,5},{5,6},{6,7},{8,9},{9,10},{10,11},{11... | collective-permute-start | bytes 786440 | tf_op jit(solution)/shard_map/ppermute | solution.py:14
  9.5 5.7 %collective-permute-start.4 = (bf16[32,1,32,128]{3,0,2,1:T(8,128)(2,1)S(1)}, bf16[32,1,32,128]{3,0,2,1:T(8,128)(2,1)S(1)}, u32[]{:S(2)}, u32[]{:S(2)}) collective-permute-start(bf16[32,1,32,128]{3,0,2,1:T(8,128)(2,1)S(1)} %get-tuple-element.187), channel_id=1, source_target_pairs={{1,0},{2,1},{3,2},{4,3},{5,4},{6,5},{7,6},{9,8},{10,9},{11,10},{12... | collective-permute-start | bytes 786440 | tf_op jit(solution)/shard_map/ppermute | solution.py:15
  24.1 1.3 %copy-start.1 = (bf16[1,32,2,32,128]{4,3,2,1,0:T(8,128)(2,1)S(1)}, bf16[1,32,2,32,128]{4,3,2,1,0:T(8,128)(2,1)}, u32[]{:S(2)}) copy-start(bf16[1,32,2,32,128]{4,3,2,1,0:T(8,128)(2,1)} %param.17) | copy-start | bytes 1572868
  28.2 19.3 %collective-permute-start.5 = (bf16[32,1,32,128]{3,0,2,1:T(8,128)(2,1)S(1)}, bf16[32,1,32,128]{3,0,2,1:T(8,128)(2,1)}, u32[]{:S(2)}, u32[]{:S(2)}) collective-permute-start(bf16[32,1,32,128]{3,0,2,1:T(8,128)(2,1)S(1)} %get-tuple-element.184), channel_id=1, source_target_pairs={{0,1},{1,2},{2,3},{3,4},{4,5},{5,6},{6,7},{8,9},{9,10},{10,11},{11... | collective-permute-start | bytes 786440 | tf_op jit(solution)/shard_map/ppermute | solution.py:14
  35.6 12.0 %collective-permute-start.6 = (bf16[32,1,32,128]{3,0,2,1:T(8,128)(2,1)S(1)}, bf16[32,1,32,128]{3,0,2,1:T(8,128)(2,1)}, u32[]{:S(2)}, u32[]{:S(2)}) collective-permute-start(bf16[32,1,32,128]{3,0,2,1:T(8,128)(2,1)S(1)} %get-tuple-element.185), channel_id=1, source_target_pairs={{1,0},{2,1},{3,2},{4,3},{5,4},{6,5},{7,6},{9,8},{10,9},{11,10},{12... | collective-permute-start | bytes 786440 | tf_op jit(solution)/shard_map/ppermute | solution.py:15
  47.5 3.4 %copy-start.2 = (f32[32,865]{1,0:T(8,128)}, f32[32,865]{1,0:T(8,128)S(1)}, u32[]{:S(2)}) copy-start(f32[32,865]{1,0:T(8,128)S(1)} %pad_maximum_fusion.5) | copy-start | bytes 332164
  49.4 8.7 %collective-permute-start.7 = (f32[16,865]{1,0:T(8,128)}, f32[16,865]{1,0:T(8,128)}, u32[]{:S(2)}, u32[]{:S(2)}) collective-permute-start(f32[16,865]{1,0:T(8,128)} %constant_dynamic-slice_fusion.1), channel_id=1, source_target_pairs={{0,16},{8,24},{16,0},{24,8},{1,17},{9,25},{17,1},{25,9},{2,18},{10... | collective-permute-start | bytes 166088 | tf_op jit(solution)/shard_map/ppermute | solution.py:22
  59.0 0.6 copy-start.3
  60.2 7.6 %collective-permute-start.8 = (f32[8,865]{1,0:T(8,128)}, f32[8,865]{1,0:T(8,128)}, u32[]{:S(2)}, u32[]{:S(2)}) collective-permute-start(f32[8,865]{1,0:T(8,128)} %constant_dynamic-slice_fusion), channel_id=1, source_target_pairs={{0,8},{8,0},{16,24},{24,16},{1,9},{9,1},{17,25},{25,17},{2,10},{10... | collective-permute-start | bytes 83048 | tf_op jit(solution)/shard_map/ppermute | solution.py:22
  69.2 7.9 %collective-permute-start.9 = (f32[8,865]{1,0:T(8,128)}, f32[8,865]{1,0:T(8,128)}, u32[]{:S(2)}, u32[]{:S(2)}) collective-permute-start(f32[8,865]{1,0:T(8,128)} %dynamic-slice_add_fusion.1), channel_id=1, source_target_pairs={{0,1},{1,0},{2,3},{3,2},{4,5},{5,4},{6,7},{7,6},{8,9},{9,8},{10,11... | collective-permute-start | bytes 83048 | tf_op jit(solution)/shard_map/ppermute | solution.py:22
  78.5 7.2 %collective-permute-start.10 = (f32[8,865]{1,0:T(8,128)}, f32[8,865]{1,0:T(8,128)}, u32[]{:S(2)}, u32[]{:S(2)}) collective-permute-start(f32[8,865]{1,0:T(8,128)} %add.268), channel_id=1, source_target_pairs={{0,2},{1,3},{2,0},{3,1},{4,6},{5,7},{6,4},{7,5},{8,10},{9,11},{10,... | collective-permute-start | bytes 83048 | tf_op jit(solution)/shard_map/ppermute | solution.py:22
  87.1 11.8 %collective-permute-start.11 = (f32[8,865]{1,0:T(8,128)}, f32[8,865]{1,0:T(8,128)}, u32[]{:S(2)}, u32[]{:S(2)}) collective-permute-start(f32[8,865]{1,0:T(8,128)} %add.269), channel_id=1, source_target_pairs={{0,4},{1,5},{2,6},{3,7},{4,0},{5,1},{6,2},{7,3},{8,12},{9,13},{10,... | collective-permute-start | bytes 83048 | tf_op jit(solution)/shard_map/ppermute | solution.py:22
  99.7 2.1 %copy-start.4 = (f32[8,865]{1,0:T(8,128)}, f32[8,865]{1,0:T(8,128)S(1)}, u32[]{:S(2)}) copy-start(f32[8,865]{1,0:T(8,128)S(1)} %add_multiply_fusion) | copy-start | bytes 83044

commit v3 on v2

v3 whole, which is shorter than its diff:
```python
import functools

import jax
import jax.numpy as jnp
from jax import lax
from jax.experimental import pallas as pl
from jax.experimental.pallas import tpu as pltpu
from jax.sharding import PartitionSpec as P

OFFSETS = [(b, c) for b in (-1, 0, 1) for c in (-1, 0, 1)]


def plane_masks(rows, depth):
    y = jnp.arange(rows)[:, None]
    z = jnp.arange(depth)[None, :]
    masks = [((y + b >= 0) & (y + b < rows) & (z + c >= 0) & (z + c < depth)) for b, c in OFFSETS]
    return jnp.stack(masks).reshape(len(OFFSETS), 1, rows * depth).astype(jnp.float32)


def _stacked(lo, mid, hi, h, planes):
    def plane(index):
        if index == 0:
            return lo[0]
        if index == planes + 1:
            return hi[0]
        return mid[index - 1]
    return jnp.concatenate([plane(h), plane(h + 1), plane(h + 2)], axis=0)


def _shifted_sum(y, mask, chans, lanes, depth, sign):
    total = None
    for k, (b, c) in enumerate(OFFSETS):
        off = sign * (b * depth + c)
        block = y[k * chans : (k + 1) * chans]
        if off != 0:
            block = pltpu.roll(block, (-off) % lanes, 1)
            block = jnp.where(mask[k if sign > 0 else len(OFFSETS) - 1 - k] > 0.5, block, 0.0)
        total = block if total is None else total + block
    return total


def _forward_kernel(lo, mid, hi, wall, bias, cot, mask, act_out, dpre_out, *, planes, depth):
    chans, lanes = mid.shape[1], mid.shape[2]
    for p in range(planes):
        y = jnp.dot(wall[...], _stacked(lo, mid, hi, p, planes), preferred_element_type=jnp.float32)
        pre = _shifted_sum(y, mask, chans, lanes, depth, 1) + bias[...]
        sig = 1.0 / (1.0 + jnp.exp(-pre))
        act_out[p] = (pre * sig).astype(act_out.dtype)
        dpre_out[p] = (cot[p].astype(jnp.float32) * sig * (1.0 + pre * (1.0 - sig))).astype(dpre_out.dtype)


def _input_kernel(lo, mid, hi, wall, mask, out, *, planes, first, depth):
    chans, lanes = mid.shape[1], mid.shape[2]
    for n in range(out.shape[0]):
        y = jnp.dot(wall[...], _stacked(lo, mid, hi, first + n, planes), preferred_element_type=jnp.float32)
        out[n] = _shifted_sum(y, mask, chans, lanes, depth, -1).astype(out.dtype)


def _weight_kernel(lo, mid, hi, dpre, mask, gw_out, gb_out, *, planes, depth):
    chans, lanes = dpre.shape[1], dpre.shape[2]
    gw = jnp.zeros(gw_out.shape, jnp.float32)
    gb = jnp.zeros(gb_out.shape, jnp.float32)
    for p in range(planes):
        d = dpre[p].astype(jnp.float32)
        gb = gb + jnp.sum(d, axis=1, keepdims=True)
        parts = []
        for k, (b, c) in enumerate(OFFSETS):
            off = b * depth + c
            e = d
            if off != 0:
                e = pltpu.roll(jnp.where(mask[k] > 0.5, d, 0.0), off % lanes, 1)
            parts.append(e.astype(jnp.bfloat16))
        gw = gw + lax.dot_general(
            jnp.concatenate(parts, axis=0), _stacked(lo, mid, hi, p, planes),
            (((1,), (1,)), ((), ())), preferred_element_type=jnp.float32,
        )
    gw_out[...] = gw
    gb_out[...] = gb


def _vmem(n):
    return [pl.BlockSpec(memory_space=pltpu.VMEM)] * n


def forward_call(lo, mid, hi, wall, bias, cot, mask, depth):
    planes, chans, lanes = mid.shape
    shape = jax.ShapeDtypeStruct(mid.shape, jnp.bfloat16)
    flops = 2 * planes * wall.shape[0] * wall.shape[1] * lanes
    return pl.pallas_call(
        functools.partial(_forward_kernel, planes=planes, depth=depth),
        out_shape=(shape, shape),
        in_specs=_vmem(7),
        out_specs=tuple(_vmem(2)),
        cost_estimate=pl.CostEstimate(flops=flops, transcendentals=planes * chans * lanes, bytes_accessed=5 * mid.size * 2),
    )(lo, mid, hi, wall, bias, cot, mask)


def input_call(lo, mid, hi, wall, mask, depth, first, count):
    planes, chans, lanes = mid.shape
    flops = 2 * count * wall.shape[0] * wall.shape[1] * lanes
    return pl.pallas_call(
        functools.partial(_input_kernel, planes=planes, first=first, depth=depth),
        out_shape=jax.ShapeDtypeStruct((count, chans, lanes), jnp.bfloat16),
        in_specs=_vmem(5),
        out_specs=_vmem(1)[0],
        cost_estimate=pl.CostEstimate(flops=flops, transcendentals=0, bytes_accessed=3 * mid.size * 2),
    )(lo, mid, hi, wall, mask)


def weight_call(lo, mid, hi, dpre, mask, depth):
    planes, chans, lanes = mid.shape
    flops = 2 * planes * 9 * chans * 3 * chans * lanes
    return pl.pallas_call(
        functools.partial(_weight_kernel, planes=planes, depth=depth),
        out_shape=(jax.ShapeDtypeStruct((9 * chans, 3 * chans), jnp.float32), jax.ShapeDtypeStruct((chans, 1), jnp.float32)),
        in_specs=_vmem(5),
        out_specs=tuple(_vmem(2)),
        cost_estimate=pl.CostEstimate(flops=flops, transcendentals=0, bytes_accessed=3 * mid.size * 2),
    )(lo, mid, hi, dpre, mask)


def neighbours(first, last, axis):
    peers = lax.axis_size(axis)
    up = [(i, i + 1) for i in range(peers - 1)]
    down = [(j, i) for i, j in up]
    return lax.ppermute(last, axis, up), lax.ppermute(first, axis, down)


def swap(value, axis, bit):
    peers = lax.axis_size(axis)
    return lax.ppermute(value, axis, [(i, i ^ bit) for i in range(peers)])


def gather_rows(value, axis):
    peers = lax.axis_size(axis)
    me = lax.axis_index(axis)
    blocks = jnp.zeros((peers,) + value.shape, value.dtype)
    blocks = lax.dynamic_update_index_in_dim(blocks, value, me, 0)
    for k in range(1, peers):
        blocks = lax.dynamic_update_index_in_dim(blocks, swap(value, axis, k), me ^ k, 0)
    return blocks.reshape((peers * value.shape[0],) + value.shape[1:])


def reduce_beside(local_grads, work):
    rounds = []
    bit = lax.axis_size("real") // 2
    while bit >= 1:
        rounds.append(("real", bit))
        bit //= 2
    bit = 1
    while bit < lax.axis_size("strike"):
        rounds.append(("strike", bit))
        bit *= 2
    results = []
    value = local_grads
    for k, (axis, bit) in enumerate(rounds):
        if axis == "real":
            half = value.shape[0] // 2
            upper = (lax.axis_index(axis) // bit) % 2
            keep = lax.dynamic_slice_in_dim(value, upper * half, half, 0)
            send = lax.dynamic_slice_in_dim(value, (1 - upper) * half, half, 0)
        else:
            keep, send = value, value
        if k < len(work):
            send, inputs = lax.optimization_barrier((send, work[k][1]))
            received = swap(send, axis, bit)
            result = work[k][0](*inputs)
            received, result = lax.optimization_barrier((received, result))
            results.append(result)
        else:
            received = swap(send, axis, bit)
        value = keep + received
    for job, inputs in work[len(rounds) :]:
        results.append(job(*inputs))
    return value, results


def local(grades, cotangent, weight, bias):
    field = grades[0]
    chans, planes, rows, depth = field.shape
    lanes = rows * depth
    taps_in = weight.shape[1]
    packed = jnp.concatenate([weight, bias[:, None]], axis=1)
    whole = gather_rows(packed, "real")
    whole_weight, whole_bias = whole[:, :taps_in], whole[:, taps_in]
    out_chan = whole_weight.shape[0]
    w5 = whole_weight.reshape(out_chan, 3, 3, 3, chans)
    forward_w = w5.transpose(2, 3, 0, 1, 4).reshape(9 * out_chan, 3 * chans)
    backward_w = w5[:, ::-1].transpose(2, 3, 4, 1, 0).reshape(9 * chans, 3 * out_chan)
    mask = plane_masks(rows, depth)

    def flat(value):
        return value.transpose(1, 0, 2, 3).reshape(planes, value.shape[0], lanes)

    def unflat(value):
        return value.reshape(planes, value.shape[1], rows, depth).transpose(1, 0, 2, 3)

    mid = flat(field)
    lo, hi = neighbours(mid[:1], mid[planes - 1 :], "strike")
    act, dpre = forward_call(
        lo, mid, hi, forward_w, whole_bias.astype(jnp.float32)[:, None], flat(cotangent[0]), mask, depth
    )
    dlo, dhi = neighbours(dpre[:1], dpre[planes - 1 :], "strike")
    g, gb = weight_call(lo, mid, hi, dpre, mask, depth)
    local_weight = g.reshape(3, 3, out_chan, 3, chans).transpose(2, 3, 0, 1, 4).reshape(out_chan, 27 * chans)
    local_grads = jnp.concatenate([local_weight, gb], axis=1)
    work = [
        (functools.partial(input_call, depth=depth, first=p, count=1), (dlo, dpre, dhi, backward_w, mask))
        for p in range(planes)
    ]
    owned, pieces = reduce_beside(local_grads, work)
    grad_input = unflat(jnp.concatenate(pieces, axis=0))
    cells = lax.axis_size("real") * lax.axis_size("strike") * planes * rows * depth
    factor = 1.0 / cells**0.5
    owned = owned * factor
    return (unflat(act)[None], grad_input[None], owned[:, :taps_in], owned[:, taps_in])


def solution(mesh):
    in_specs = (
        P("real", None, "strike", None, None),
        P("real", None, "strike", None, None),
        P("real", None),
        P("real"),
    )
    out_specs = (
        P("real", None, "strike", None, None),
        P("real", None, "strike", None, None),
        P("real", None),
        P("real"),
    )
    return jax.shard_map(local, mesh=mesh, in_specs=in_specs, out_specs=out_specs, check_vma=False)
```

time: 104 us -> 59.8 us (0.57); the launches traced: 102 us -> 59.3 us
  matrix products: 49.1 us -> 0 us
  Pallas kernels: 0 us -> 14.7 us
  other arithmetic: 9.41 us -> 2.04 us
    dot_general x81 -> x0, matrix products: 49.1 us -> none  [the longest x27 28 us: transposed_taps(): jnp.einsum('oi,oxyz->ixyz', kernel3[:, column, :], window, preferred_elem...]
    pallas_call x0 -> x4, Pallas kernels: none -> 14.7 us  [the longest x2 6.11 us: input_call(): pl.pallas_call(functools.partial(_input_kernel, planes=planes, first=firs...]
    reshape x2 -> x9, local copies, waits for them, and re-layouts: 0.41 us -> 5.62 us  [the longest x4 2.41 us: flat(): return value.transpose(1, 0, 2, 3).reshape(planes, value.shape[0], lanes)]
    add x4, other arithmetic: 5.01 us -> 0.1 us  [reduce_beside(): value = keep + received]
    another operation x6 -> x1, local copies, waits for them, and re-layouts: 5.15 us -> 0.25 us  [plane_masks(): jnp.stack(masks).reshape(len(OFFSETS), 1, rows * depth).astype(jnp.float32)]
    ppermute x8, waiting for transfers between devices: 0.51 us -> 3.5 us  [swap(): return lax.ppermute(value, axis, [(i, i ^ bit) for i in range(peers)])]
    concatenate x3 -> x2, other arithmetic: 2.66 us -> 0.13 us  [the longest x1 0.08 us: local(): local_grads = jnp.concatenate([local_weight, gb], axis=1)]
    ppermute x4, waiting for transfers between devices: 2.54 us -> 0.01 us  [neighbours(): return (lax.ppermute(last, axis, up), lax.ppermute(first, axis, down))]
  transfers between devices with their start and end apart: 12 -> 12, of which waited for: 2 -> 2; matrix products, arithmetic and copies ran while one was open for 48% -> 20% of each run, Pallas kernels for 0% -> 17%
where the time goes in v3:
time: 59.8 us; the launch traced here: 59.3 us
  starting transfers between devices  23 us (38%)
  local copies, waits for them, and re-layouts  15.2 us (25%)
  Pallas kernels  14.7 us (25%)
  waiting for transfers between devices  3.51 us (6%)
  other arithmetic  2.04 us (3%)
  between operations  0.95 us (2%)
    ppermute x8, starting transfers between devices, swap(): return lax.ppermute(value, axis, [(i, i ^ bit) for i in range(peers)])  13 us
    ppermute x4, starting transfers between devices, neighbours(): return (lax.ppermute(last, axis, up), lax.ppermute(first, axis, down))  9.93 us
    pallas_call x2, Pallas kernels, input_call(): pl.pallas_call(functools.partial(_input_kernel, planes=planes, first=firs...  6.11 us
    pallas_call x1, Pallas kernels, forward_call(): pl.pallas_call(functools.partial(_forward_kernel, planes=planes, depth=de...  4.89 us
    pallas_call x1, Pallas kernels, weight_call(): pl.pallas_call(functools.partial(_weight_kernel, planes=planes, depth=dep...  3.68 us
    unnamed x34, local copies, waits for them, and re-layouts  3.59 us
    ppermute x8, waiting for transfers between devices, swap(): return lax.ppermute(value, axis, [(i, i ^ bit) for i in range(peers)])  3.5 us
    reshape x4, local copies, waits for them, and re-layouts, flat(): return value.transpose(1, 0, 2, 3).reshape(planes, value.shape[0], lanes)  2.41 us
  transfers between devices with their start and end apart: 12, of which 2 were waited for; matrix products, arithmetic and copies ran while one was open for 20% of the time, Pallas kernels for 17%

profile of v3, /device:TPU:0, one launch (start us, length us, event | category | flops | bytes accessed | tf_op | source)
XLA Modules:
  0.0 59.3 jit_solution(3638506434520535947)
XLA Ops:
  0.6 0.6 %copy-done.12 = bf16[8]{0:T(256)(128)(2,1)S(1)} copy-done((bf16[8]{0:T(256)(128)(2,1)S(1)}, bf16[8]{0:T(256)(128)(2,1)}, u32[]{:S(2)}) %copy-start.12) | copy-done | bytes 40
  1.3 0.1 copy.33
  1.4 0.7 %copy-done.11 = bf16[8,864]{1,0:T(8,128)(2,1)S(1)} copy-done((bf16[8,864]{1,0:T(8,128)(2,1)S(1)}, bf16[8,864]{1,0:T(8,128)(2,1)}, u32[]{:S(2)}) %copy-start.11) | copy-done | bytes 13848
  2.1 0.1 bitcast_dynamic-update-slice_fusion.3
  2.2 3.0 %collective-permute-start.3 = (bf16[8,865]{1,0:T(8,128)(2,1)S(1)}, bf16[8,865]{1,0:T(8,128)(2,1)S(1)}, u32[]{:S(2)}, u32[]{:S(2)}) collective-permute-start(bf16[8,865]{1,0:T(8,128)(2,1)S(1)} %get-tuple-element.45), channel_id=1, source_target_pairs={{0,16},{8,24},{16,0},{24,8},{1,17},{9,25},{17,1},{25,9},{2,18},{10... | collective-permute-start | bytes 41528 | tf_op jit(solution)/shard_map/ppermute | solution.py:131
  5.1 1.5 %collective-permute-start.2 = (bf16[8,865]{1,0:T(8,128)(2,1)S(1)}, bf16[8,865]{1,0:T(8,128)(2,1)S(1)}, u32[]{:S(2)}, u32[]{:S(2)}) collective-permute-start(bf16[8,865]{1,0:T(8,128)(2,1)S(1)} %get-tuple-element.45), channel_id=1, source_target_pairs={{0,8},{8,0},{16,24},{24,16},{1,9},{9,1},{17,25},{25,17},{2,10},{10... | collective-permute-start | bytes 41528 | tf_op jit(solution)/shard_map/ppermute | solution.py:131
  6.6 0.0 collective-permute-start.4
  6.7 1.1 %fusion.23 = (bf16[1,32,32,128]{3,2,0,1:T(8,128)(2,1)S(1)}, bf16[1,32,32,128]{3,2,0,1:T(8,128)(2,1)S(1)}) fusion(bf16[2,32,32,128]{3,2,0,1:T(8,128)(2,1)} %bitcast.165), kind=kLoop, calls=%fused_computation.64 | loop fusion | bytes 1048576 | tf_op jit(solution)/shard_map/slice | solution.py:199
  7.8 0.1 slice.31
  7.9 1.3 %collective-permute-start = (bf16[1,32,4096]{2,1,0:T(8,128)(2,1)S(1)}, bf16[1,32,4096]{2,1,0:T(8,128)(2,1)S(1)}, u32[]{:S(2)}, u32[]{:S(2)}) collective-permute-start(bf16[1,32,4096]{2,1,0:T(8,128)(2,1)S(1)} %slice.31), channel_id=1, source_target_pairs={{0,1},{1,2},{2,3},{3,4},{4,5},{5,6},{6,7},{8,9},{9,10},{10,11},{11... | collective-permute-start | bytes 786440 | tf_op jit(solution)/shard_map/ppermute | solution.py:126
  9.2 0.0 copy-start
  9.2 0.1 slice.33
  9.3 1.4 %collective-permute-start.1 = (bf16[1,32,4096]{2,1,0:T(8,128)(2,1)S(1)}, bf16[1,32,4096]{2,1,0:T(8,128)(2,1)S(1)}, u32[]{:S(2)}, u32[]{:S(2)}) collective-permute-start(bf16[1,32,4096]{2,1,0:T(8,128)(2,1)S(1)} %slice.33), channel_id=1, source_target_pairs={{1,0},{2,1},{3,2},{4,3},{5,4},{6,5},{7,6},{9,8},{10,9},{11,10},{12... | collective-permute-start | bytes 786440 | tf_op jit(solution)/shard_map/ppermute | solution.py:126
  10.8 0.1 broadcast_bitcast_fusion.5
  10.9 0.1 broadcast_bitcast_fusion.6
  11.0 0.2 fusion.6
  11.2 0.2 stack.39
  11.5 0.8 %copy_convert_fusion.mask = f32[9,1,4096]{2,1,0:T(1,128)} fusion(pred[9,1,4096]{2,0,1:T(8,128)(4,1)S(1)} %stack.39), kind=kLoop, calls=%fused_computation | loop fusion | flops 36864 | bytes 184320 | tf_op jit(solution)/shard_map/convert_element_type | solution.py:17
  12.3 0.1 reshape.687
  12.4 0.0 copy-start.7
  12.4 1.1 %copy.41.mid = bf16[2,32,4096]{2,1,0:T(8,128)(2,1)} copy(bf16[2,32,4096]{2,0,1:T(2,128)(2,1)S(1)} %reshape.687) | data formatting | bytes 1048576 | tf_op jit(solution)/shard_map/reshape | solution.py:193
  13.5 0.1 reshape.688
  13.7 1.1 %copy.42.cot = bf16[2,32,4096]{2,1,0:T(8,128)(2,1)} copy(bf16[2,32,4096]{2,0,1:T(2,128)(2,1)S(1)} %reshape.688) | data formatting | bytes 1048576 | tf_op jit(solution)/shard_map/reshape | solution.py:193
  14.7 0.0 collective-permute-done.2
  14.8 0.0 collective-permute-done.3
  14.8 0.2 reshape.679
  15.0 0.1 copy.34
  15.1 0.8 %reshape.680.wall = bf16[288,96]{1,0:T(8,128)(2,1)} reshape(bf16[3,3,32,3,32]{4,3,2,1,0:T(4,128)(2,1)S(1)} %copy.34) | data formatting | bytes 110592 | tf_op jit(solution)/shard_map/reshape | solution.py:188
  15.9 0.7 %slice_convert_fusion.bias = f32[32,1]{1,0:T(8,128)} fusion(bf16[32,865]{1,0:T(8,128)(2,1)S(1)} %bitcast.173), kind=kLoop, calls=%fused_computation.43 | loop fusion | flops 32 | bytes 192 | tf_op jit(solution)/shard_map/convert_element_type | solution.py:201
  16.6 0.0 collective-permute-done.1.hi
  16.6 0.7 %copy-done.1 = bf16[1,32,4096]{2,1,0:T(8,128)(2,1)} copy-done((bf16[1,32,4096]{2,1,0:T(8,128)(2,1)}, bf16[1,32,4096]{2,1,0:T(8,128)(2,1)S(1)}, u32[]{:S(2)}) %copy-start.1) | copy-done | bytes 262168
  17.3 0.7 %copy-done.2 = bf16[1,32,4096]{2,1,0:T(8,128)(2,1)} copy-done((bf16[1,32,4096]{2,1,0:T(8,128)(2,1)}, bf16[1,32,4096]{2,1,0:T(8,128)(2,1)S(1)}, u32[]{:S(2)}) %copy-start.2) | copy-done | bytes 262168
  18.0 4.9 %shard_map.75 = (bf16[2,32,4096]{2,1,0:T(8,128)(2,1)}, bf16[2,32,4096]{2,1,0:T(8,128)(2,1)}) custom-call(bf16[1,32,4096]{2,1,0:T(8,128)(2,1)} %copy-done.1, bf16[2,32,4096]{2,1,0:T(8,128)(2,1)} %copy.41.mid, bf16[1,32,4096]{2,1,0:T(8,128)(2,1)} %copy-done.2, bf16[288,96]{1,0:T(8,128)(2,1)} %reshape.680.wall, f32[32,1]{1,0:T(8,128)} %slice_convert_fusion.bias, ...), custom_call_target="tpu_custom_call" | custom-call | flops 452984832 | bytes 2621440 | tf_op jit(solution)/shard_map/pallas_call | solution.py:89
  22.9 1.1 %fusion.22 = (bf16[1,32,4096]{2,1,0:T(8,128)(2,1)S(1)}, bf16[1,32,4096]{2,1,0:T(8,128)(2,1)S(1)}) fusion(bf16[2,32,4096]{2,1,0:T(8,128)(2,1)} %get-tuple-element.38.dpre.mid), kind=kLoop, calls=%fused_computation.63 | loop fusion | bytes 1048576 | tf_op jit(solution)/shard_map/slice | solution.py:203
  24.0 1.3 %collective-permute-start.6 = (bf16[1,32,4096]{2,1,0:T(8,128)(2,1)S(1)}, bf16[1,32,4096]{2,1,0:T(8,128)(2,1)S(1)}, u32[]{:S(2)}, u32[]{:S(2)}) collective-permute-start(bf16[1,32,4096]{2,1,0:T(8,128)(2,1)S(1)} %get-tuple-element.46), channel_id=1, source_target_pairs={{1,0},{2,1},{3,2},{4,3},{5,4},{6,5},{7,6},{9,8},{10,9},{11,10},{12... | collective-permute-start | bytes 786440 | tf_op jit(solution)/shard_map/ppermute | solution.py:126
  25.3 5.9 %collective-permute-start.5 = (bf16[1,32,4096]{2,1,0:T(8,128)(2,1)S(1)}, bf16[1,32,4096]{2,1,0:T(8,128)(2,1)S(1)}, u32[]{:S(2)}, u32[]{:S(2)}) collective-permute-start(bf16[1,32,4096]{2,1,0:T(8,128)(2,1)S(1)} %get-tuple-element.47), channel_id=1, source_target_pairs={{0,1},{1,2},{2,3},{3,4},{4,5},{5,6},{6,7},{8,9},{9,10},{10,11},{11... | collective-permute-start | bytes 786440 | tf_op jit(solution)/shard_map/ppermute | solution.py:126
  31.2 0.1 reverse_bitcast_fusion
  31.3 0.3 copy.39
  31.6 0.8 %reshape.685.wall = bf16[288,96]{1,0:T(8,128)(2,1)} reshape(bf16[3,3,32,3,32]{4,3,2,1,0:T(4,128)(2,1)S(1)} %copy.39) | data formatting | bytes 110592 | tf_op jit(solution)/shard_map/reshape | solution.py:189
  32.4 3.7 %shard_map.76 = (f32[288,96]{1,0:T(8,128)}, f32[32,1]{1,0:T(8,128)}) custom-call(bf16[1,32,4096]{2,1,0:T(8,128)(2,1)} %copy-done.1, bf16[2,32,4096]{2,1,0:T(8,128)(2,1)} %copy.41.mid, bf16[1,32,4096]{2,1,0:T(8,128)(2,1)} %copy-done.2, bf16[2,32,4096]{2,1,0:T(8,128)(2,1)} %get-tuple-element.38.dpre.mid, f32[9,1,4096]{2,1,0:T(1,128)} %copy_convert_fusion.mask), custom_call_target="tpu_custom_call" | custom-call | flops 452984832 | bytes 1572864 | tf_op jit(solution)/shard_map/pallas_call | solution.py:113
  36.1 1.1 %reshape.683 = f32[3,3,32,3,32]{4,3,2,1,0:T(4,128)S(1)} reshape(f32[288,96]{1,0:T(8,128)} %get-tuple-element.26) | data formatting | bytes 221184 | tf_op jit(solution)/shard_map/reshape | solution.py:205
  37.2 0.3 copy.38
  37.5 0.0 copy-start.9
  37.6 0.3 reshape.684
  37.8 0.4 copy-done.9
  38.3 0.1 fusion.17
  38.4 0.0 collective-permute-done.5.lo
  38.4 0.0 copy-start.4
  38.4 1.6 %collective-permute-start.7 = (f32[16,865]{1,0:T(8,128)S(1)}, f32[16,865]{1,0:T(8,128)S(1)}, u32[]{:S(2)}, u32[]{:S(2)}) collective-permute-start(f32[16,865]{1,0:T(8,128)S(1)} %fusion.17), channel_id=1, source_target_pairs={{0,16},{8,24},{16,0},{24,8},{1,17},{9,25},{17,1},{25,9},{2,18},{10... | collective-permute-start | bytes 166088 | tf_op jit(solution)/shard_map/ppermute | solution.py:131
  40.0 3.1 %shard_map.77 = bf16[1,32,4096]{2,1,0:T(8,128)(2,1)} custom-call(bf16[1,32,4096]{2,1,0:T(8,128)(2,1)} %copy-done.4, bf16[2,32,4096]{2,1,0:T(8,128)(2,1)} %get-tuple-element.38.dpre.mid, bf16[1,32,4096]{2,1,0:T(8,128)(2,1)} %copy-done.3, bf16[288,96]{1,0:T(8,128)(2,1)} %reshape.685.wall, f32[9,1,4096]{2,1,0:T(1,128)} %copy_convert_fusion.mask), custom_call_target="tpu_custom_call" | custom-call | flops 226492416 | bytes 1572864 | tf_op jit(solution)/shard_map/pallas_call | solution.py:101
  43.0 0.1 fusion.16
  43.1 1.5 %collective-permute-start.8 = (f32[8,865]{1,0:T(8,128)S(1)}, f32[8,865]{1,0:T(8,128)S(1)}, u32[]{:S(2)}, u32[]{:S(2)}) collective-permute-start(f32[8,865]{1,0:T(8,128)S(1)} %constant_dynamic-slice_fusion), channel_id=1, source_target_pairs={{0,8},{8,0},{16,24},{24,16},{1,9},{9,1},{17,25},{25,17},{2,10},{10... | collective-permute-start | bytes 83048 | tf_op jit(solution)/shard_map/ppermute | solution.py:131
  44.6 0.1 copy.50
  44.7 3.0 %shard_map.78 = bf16[1,32,4096]{2,1,0:T(8,128)(2,1)} custom-call(bf16[1,32,4096]{2,1,0:T(8,128)(2,1)} %copy-done.4, bf16[2,32,4096]{2,1,0:T(8,128)(2,1)} %get-tuple-element.38.dpre.mid, bf16[1,32,4096]{2,1,0:T(8,128)(2,1)} %copy-done.3, bf16[288,96]{1,0:T(8,128)(2,1)} %reshape.685.wall, f32[9,1,4096]{2,1,0:T(1,128)} %copy_convert_fusion.mask), custom_call_target="tpu_custom_call" | custom-call | flops 226492416 | bytes 1572864 | tf_op jit(solution)/shard_map/pallas_call | solution.py:101
  47.8 1.2 %collective-permute-start.9 = (f32[8,865]{1,0:T(8,128)S(1)}, f32[8,865]{1,0:T(8,128)S(1)}, u32[]{:S(2)}, u32[]{:S(2)}) collective-permute-start(f32[8,865]{1,0:T(8,128)S(1)} %dynamic-slice_add_fusion), channel_id=1, source_target_pairs={{0,1},{1,0},{2,3},{3,2},{4,5},{5,4},{6,7},{7,6},{8,9},{9,8},{10,11... | collective-permute-start | bytes 83048 | tf_op jit(solution)/shard_map/ppermute | solution.py:131
  49.0 0.9 %copy_bitcast_fusion.1 = bf16[1,32,2,32,128]{4,3,2,1,0:T(8,128)(2,1)} fusion(bf16[2,32,32,128]{3,2,1,0:T(8,128)(2,1)S(1)} %bitcast.167), kind=kLoop, calls=%fused_computation.3 | loop fusion | bytes 1048576 | tf_op jit(solution)/shard_map/broadcast_in_dim | solution.py:216
  49.9 1.6 %collective-permute-start.10 = (f32[8,865]{1,0:T(8,128)S(1)}, f32[8,865]{1,0:T(8,128)S(1)}, u32[]{:S(2)}, u32[]{:S(2)}) collective-permute-start(f32[8,865]{1,0:T(8,128)S(1)} %add.139), channel_id=1, source_target_pairs={{0,2},{1,3},{2,0},{3,1},{4,6},{5,7},{6,4},{7,5},{8,10},{9,11},{10,... | collective-permute-start | bytes 83048 | tf_op jit(solution)/shard_map/ppermute | solution.py:131
  51.5 0.1 pad_maximum_fusion
  51.6 0.1 copy.51
  51.7 2.1 %collective-permute-done.10 = f32[8,865]{1,0:T(8,128)S(1)} collective-permute-done((f32[8,865]{1,0:T(8,128)S(1)}, f32[8,865]{1,0:T(8,128)S(1)}, u32[]{:S(2)}, u32[]{:S(2)}) %collective-permute-start.10) | collective-permute-done | bytes 27712 | tf_op jit(solution)/shard_map/ppermute | solution.py:131
  53.9 2.6 %collective-permute-start.11 = (f32[8,865]{1,0:T(8,128)S(1)}, f32[8,865]{1,0:T(8,128)S(1)}, u32[]{:S(2)}, u32[]{:S(2)}) collective-permute-start(f32[8,865]{1,0:T(8,128)S(1)} %add.140), channel_id=1, source_target_pairs={{0,4},{1,5},{2,6},{3,7},{4,0},{5,1},{6,2},{7,3},{8,12},{9,13},{10,... | collective-permute-start | bytes 83048 | tf_op jit(solution)/shard_map/ppermute | solution.py:131
  56.4 0.9 %copy_bitcast_fusion = bf16[1,32,2,32,128]{4,3,2,1,0:T(8,128)(2,1)} fusion(bf16[2,32,32,128]{3,2,1,0:T(8,128)(2,1)S(1)} %bitcast.168), kind=kLoop, calls=%fused_computation.2 | loop fusion | bytes 1048576 | tf_op jit(solution)/shard_map/broadcast_in_dim | solution.py:216
  57.3 1.3 %collective-permute-done.11 = f32[8,865]{1,0:T(8,128)S(1)} collective-permute-done((f32[8,865]{1,0:T(8,128)S(1)}, f32[8,865]{1,0:T(8,128)S(1)}, u32[]{:S(2)}, u32[]{:S(2)}) %collective-permute-start.11) | collective-permute-done | bytes 27712 | tf_op jit(solution)/shard_map/ppermute | solution.py:131
  58.6 0.7 %slice_reduce_fusion = f32[8]{0:T(128)} fusion(f32[8,865]{1,0:T(8,128)S(1)} %add_multiply_fusion), kind=kLoop, calls=%fused_computation.51 | loop fusion | bytes 64 | tf_op jit(solution)/shard_map/slice | solution.py:216
  (42 shorter events, 0.2 us)
Async XLA Ops:
  0.6 0.7 %copy-start.12 = (bf16[8]{0:T(256)(128)(2,1)S(1)}, bf16[8]{0:T(256)(128)(2,1)}, u32[]{:S(2)}) copy-start(bf16[8]{0:T(256)(128)(2,1)} %param.7) | copy-start | bytes 52
  1.4 0.7 %copy-start.11 = (bf16[8,864]{1,0:T(8,128)(2,1)S(1)}, bf16[8,864]{1,0:T(8,128)(2,1)}, u32[]{:S(2)}) copy-start(bf16[8,864]{1,0:T(8,128)(2,1)} %param.6) | copy-start | bytes 41476
  2.2 12.6 %collective-permute-start.3 = (bf16[8,865]{1,0:T(8,128)(2,1)S(1)}, bf16[8,865]{1,0:T(8,128)(2,1)S(1)}, u32[]{:S(2)}, u32[]{:S(2)}) collective-permute-start(bf16[8,865]{1,0:T(8,128)(2,1)S(1)} %get-tuple-element.45), channel_id=1, source_target_pairs={{0,16},{8,24},{16,0},{24,8},{1,17},{9,25},{17,1},{25,9},{2,18},{10... | collective-permute-start | bytes 41528 | tf_op jit(solution)/shard_map/ppermute | solution.py:131
  5.1 9.6 %collective-permute-start.2 = (bf16[8,865]{1,0:T(8,128)(2,1)S(1)}, bf16[8,865]{1,0:T(8,128)(2,1)S(1)}, u32[]{:S(2)}, u32[]{:S(2)}) collective-permute-start(bf16[8,865]{1,0:T(8,128)(2,1)S(1)} %get-tuple-element.45), channel_id=1, source_target_pairs={{0,8},{8,0},{16,24},{24,16},{1,9},{9,1},{17,25},{25,17},{2,10},{10... | collective-permute-start | bytes 41528 | tf_op jit(solution)/shard_map/ppermute | solution.py:131
  6.6 8.1 %collective-permute-start.4 = (bf16[8,865]{1,0:T(8,128)(2,1)S(1)}, bf16[8,865]{1,0:T(8,128)(2,1)S(1)}, u32[]{:S(2)}, u32[]{:S(2)}) collective-permute-start(bf16[8,865]{1,0:T(8,128)(2,1)S(1)} %get-tuple-element.45), channel_id=1, source_target_pairs={{0,24},{8,16},{16,8},{24,0},{1,25},{9,17},{17,9},{25,1},{2,26},{10... | collective-permute-start | bytes 41528 | tf_op jit(solution)/shard_map/ppermute | solution.py:131
  7.9 8.7 %collective-permute-start = (bf16[1,32,4096]{2,1,0:T(8,128)(2,1)S(1)}, bf16[1,32,4096]{2,1,0:T(8,128)(2,1)S(1)}, u32[]{:S(2)}, u32[]{:S(2)}) collective-permute-start(bf16[1,32,4096]{2,1,0:T(8,128)(2,1)S(1)} %slice.31), channel_id=1, source_target_pairs={{0,1},{1,2},{2,3},{3,4},{4,5},{5,6},{6,7},{8,9},{9,10},{10,11},{11... | collective-permute-start | bytes 786440 | tf_op jit(solution)/shard_map/ppermute | solution.py:126
  9.2 3.1 %copy-start = (bf16[1,32,2,32,128]{4,3,2,1,0:T(8,128)(2,1)S(1)}, bf16[1,32,2,32,128]{4,3,2,1,0:T(8,128)(2,1)}, u32[]{:S(2)}) copy-start(bf16[1,32,2,32,128]{4,3,2,1,0:T(8,128)(2,1)} %param.4) | copy-start | bytes 1572868
  9.3 7.3 %collective-permute-start.1 = (bf16[1,32,4096]{2,1,0:T(8,128)(2,1)S(1)}, bf16[1,32,4096]{2,1,0:T(8,128)(2,1)S(1)}, u32[]{:S(2)}, u32[]{:S(2)}) collective-permute-start(bf16[1,32,4096]{2,1,0:T(8,128)(2,1)S(1)} %slice.33), channel_id=1, source_target_pairs={{1,0},{2,1},{3,2},{4,3},{5,4},{6,5},{7,6},{9,8},{10,9},{11,10},{12... | collective-permute-start | bytes 786440 | tf_op jit(solution)/shard_map/ppermute | solution.py:126
  12.4 1.1 %copy-start.7 = (bf16[1,32,2,32,128]{4,3,2,1,0:T(8,128)(2,1)S(1)}, bf16[1,32,2,32,128]{4,3,2,1,0:T(8,128)(2,1)}, u32[]{:S(2)}) copy-start(bf16[1,32,2,32,128]{4,3,2,1,0:T(8,128)(2,1)} %param.5) | copy-start | bytes 1572868
  16.6 0.7 %copy-start.1 = (bf16[1,32,4096]{2,1,0:T(8,128)(2,1)}, bf16[1,32,4096]{2,1,0:T(8,128)(2,1)S(1)}, u32[]{:S(2)}) copy-start(bf16[1,32,4096]{2,1,0:T(8,128)(2,1)S(1)} %collective-permute-done.lo) | copy-start | bytes 786436
  17.3 0.7 %copy-start.2 = (bf16[1,32,4096]{2,1,0:T(8,128)(2,1)}, bf16[1,32,4096]{2,1,0:T(8,128)(2,1)S(1)}, u32[]{:S(2)}) copy-start(bf16[1,32,4096]{2,1,0:T(8,128)(2,1)S(1)} %collective-permute-done.1.hi) | copy-start | bytes 786436
  24.0 14.4 %collective-permute-start.6 = (bf16[1,32,4096]{2,1,0:T(8,128)(2,1)S(1)}, bf16[1,32,4096]{2,1,0:T(8,128)(2,1)S(1)}, u32[]{:S(2)}, u32[]{:S(2)}) collective-permute-start(bf16[1,32,4096]{2,1,0:T(8,128)(2,1)S(1)} %get-tuple-element.46), channel_id=1, source_target_pairs={{1,0},{2,1},{3,2},{4,3},{5,4},{6,5},{7,6},{9,8},{10,9},{11,10},{12... | collective-permute-start | bytes 786440 | tf_op jit(solution)/shard_map/ppermute | solution.py:126
  25.3 13.1 %collective-permute-start.5 = (bf16[1,32,4096]{2,1,0:T(8,128)(2,1)S(1)}, bf16[1,32,4096]{2,1,0:T(8,128)(2,1)S(1)}, u32[]{:S(2)}, u32[]{:S(2)}) collective-permute-start(bf16[1,32,4096]{2,1,0:T(8,128)(2,1)S(1)} %get-tuple-element.47), channel_id=1, source_target_pairs={{0,1},{1,2},{2,3},{3,4},{4,5},{5,6},{6,7},{8,9},{9,10},{10,11},{11... | collective-permute-start | bytes 786440 | tf_op jit(solution)/shard_map/ppermute | solution.py:126
  37.5 0.7 %copy-start.9 = (f32[32,1]{1,0:T(8,128)S(1)}, f32[32,1]{1,0:T(8,128)}, u32[]{:S(2)}) copy-start(f32[32,1]{1,0:T(8,128)} %get-tuple-element.27) | copy-start | bytes 388
  38.4 1.6 %copy-start.3 = (bf16[1,32,4096]{2,1,0:T(8,128)(2,1)}, bf16[1,32,4096]{2,1,0:T(8,128)(2,1)S(1)}, u32[]{:S(2)}) copy-start(bf16[1,32,4096]{2,1,0:T(8,128)(2,1)S(1)} %collective-permute-done.6.hi) | copy-start | bytes 786436
  38.4 1.6 %copy-start.4 = (bf16[1,32,4096]{2,1,0:T(8,128)(2,1)}, bf16[1,32,4096]{2,1,0:T(8,128)(2,1)S(1)}, u32[]{:S(2)}) copy-start(bf16[1,32,4096]{2,1,0:T(8,128)(2,1)S(1)} %collective-permute-done.5.lo) | copy-start | bytes 786436
  38.4 4.7 %collective-permute-start.7 = (f32[16,865]{1,0:T(8,128)S(1)}, f32[16,865]{1,0:T(8,128)S(1)}, u32[]{:S(2)}, u32[]{:S(2)}) collective-permute-start(f32[16,865]{1,0:T(8,128)S(1)} %fusion.17), channel_id=1, source_target_pairs={{0,16},{8,24},{16,0},{24,8},{1,17},{9,25},{17,1},{25,9},{2,18},{10... | collective-permute-start | bytes 166088 | tf_op jit(solution)/shard_map/ppermute | solution.py:131
  40.0 4.7 %copy-start.8 = (bf16[2,32,4096]{2,1,0:T(8,128)(2,1)S(1)}, bf16[2,32,4096]{2,1,0:T(8,128)(2,1)}, u32[]{:S(2)}) copy-start(bf16[2,32,4096]{2,1,0:T(8,128)(2,1)} %get-tuple-element.24) | copy-start | bytes 1572868
  43.1 4.6 %collective-permute-start.8 = (f32[8,865]{1,0:T(8,128)S(1)}, f32[8,865]{1,0:T(8,128)S(1)}, u32[]{:S(2)}, u32[]{:S(2)}) collective-permute-start(f32[8,865]{1,0:T(8,128)S(1)} %constant_dynamic-slice_fusion), channel_id=1, source_target_pairs={{0,8},{8,0},{16,24},{24,16},{1,9},{9,1},{17,25},{25,17},{2,10},{10... | collective-permute-start | bytes 83048 | tf_op jit(solution)/shard_map/ppermute | solution.py:131
  47.8 2.1 %collective-permute-start.9 = (f32[8,865]{1,0:T(8,128)S(1)}, f32[8,865]{1,0:T(8,128)S(1)}, u32[]{:S(2)}, u32[]{:S(2)}) collective-permute-start(f32[8,865]{1,0:T(8,128)S(1)} %dynamic-slice_add_fusion), channel_id=1, source_target_pairs={{0,1},{1,0},{2,3},{3,2},{4,5},{5,4},{6,7},{7,6},{8,9},{9,8},{10,11... | collective-permute-start | bytes 83048 | tf_op jit(solution)/shard_map/ppermute | solution.py:131
  49.0 2.5 %copy-start.5 = (bf16[1,32,4096]{2,1,0:T(8,128)(2,1)S(1)}, bf16[1,32,4096]{2,1,0:T(8,128)(2,1)}, u32[]{:S(2)}) copy-start(bf16[1,32,4096]{2,1,0:T(8,128)(2,1)} %shard_map.77) | copy-start | bytes 786436
  49.0 2.5 %copy-start.6 = (bf16[1,32,4096]{2,1,0:T(8,128)(2,1)S(1)}, bf16[1,32,4096]{2,1,0:T(8,128)(2,1)}, u32[]{:S(2)}) copy-start(bf16[1,32,4096]{2,1,0:T(8,128)(2,1)} %shard_map.78) | copy-start | bytes 786436
  49.9 3.9 %collective-permute-start.10 = (f32[8,865]{1,0:T(8,128)S(1)}, f32[8,865]{1,0:T(8,128)S(1)}, u32[]{:S(2)}, u32[]{:S(2)}) collective-permute-start(f32[8,865]{1,0:T(8,128)S(1)} %add.139), channel_id=1, source_target_pairs={{0,2},{1,3},{2,0},{3,1},{4,6},{5,7},{6,4},{7,5},{8,10},{9,11},{10,... | collective-permute-start | bytes 83048 | tf_op jit(solution)/shard_map/ppermute | solution.py:131
  53.9 4.8 %collective-permute-start.11 = (f32[8,865]{1,0:T(8,128)S(1)}, f32[8,865]{1,0:T(8,128)S(1)}, u32[]{:S(2)}, u32[]{:S(2)}) collective-permute-start(f32[8,865]{1,0:T(8,128)S(1)} %add.140), channel_id=1, source_target_pairs={{0,4},{1,5},{2,6},{3,7},{4,0},{5,1},{6,2},{7,3},{8,12},{9,13},{10,... | collective-permute-start | bytes 83048 | tf_op jit(solution)/shard_map/ppermute | solution.py:131
  58.6 0.7 %copy-start.10 = (f32[8,865]{1,0:T(8,128)}, f32[8,865]{1,0:T(8,128)S(1)}, u32[]{:S(2)}) copy-start(f32[8,865]{1,0:T(8,128)S(1)} %add_multiply_fusion) | copy-start | bytes 83044

commit v4 on v3

--- a/solution.py
+++ b/solution.py
@@ -2,6 +2,7 @@
 
 import jax
 import jax.numpy as jnp
+import numpy as np
 from jax import lax
 from jax.experimental import pallas as pl
 from jax.experimental.pallas import tpu as pltpu
@@ -11,10 +12,10 @@
 
 
 def plane_masks(rows, depth):
-    y = jnp.arange(rows)[:, None]
-    z = jnp.arange(depth)[None, :]
+    y = np.arange(rows)[:, None]
+    z = np.arange(depth)[None, :]
     masks = [((y + b >= 0) & (y + b < rows) & (z + c >= 0) & (z + c < depth)) for b, c in OFFSETS]
-    return jnp.stack(masks).reshape(len(OFFSETS), 1, rows * depth).astype(jnp.float32)
+    return np.stack(masks).reshape(len(OFFSETS), 1, rows * depth).astype(np.float32)
 
 
 def _stacked(lo, mid, hi, h, planes):
@@ -39,14 +40,37 @@
     return total
 
 
-def _forward_kernel(lo, mid, hi, wall, bias, cot, mask, act_out, dpre_out, *, planes, depth):
+def _weight_terms(lo, mid, hi, d, mask, p, planes, depth):
+    lanes = d.shape[1]
+    parts = []
+    for k, (b, c) in enumerate(OFFSETS):
+        off = b * depth + c
+        e = d
+        if off != 0:
+            e = pltpu.roll(jnp.where(mask[k] > 0.5, d, 0.0), off % lanes, 1)
+        parts.append(e.astype(jnp.bfloat16))
+    return lax.dot_general(
+        jnp.concatenate(parts, axis=0), _stacked(lo, mid, hi, p, planes),
+        (((1,), (1,)), ((), ())), preferred_element_type=jnp.float32,
+    )
+
+
+def _forward_kernel(lo, mid, hi, wall, bias, cot, mask, act_out, dpre_out, gw_out, gb_out, *, planes, depth):
     chans, lanes = mid.shape[1], mid.shape[2]
+    gw = jnp.zeros(gw_out.shape, jnp.float32)
+    gb = jnp.zeros(gb_out.shape, jnp.float32)
     for p in range(planes):
         y = jnp.dot(wall[...], _stacked(lo, mid, hi, p, planes), preferred_element_type=jnp.float32)
         pre = _shifted_sum(y, mask, chans, lanes, depth, 1) + bias[...]
         sig = 1.0 / (1.0 + jnp.exp(-pre))
         act_out[p] = (pre * sig).astype(act_out.dtype)
-        dpre_out[p] = (cot[p].astype(jnp.float32) * sig * (1.0 + pre * (1.0 - sig))).astype(dpre_out.dtype)
+        dpre = (cot[p].astype(jnp.float32) * sig * (1.0 + pre * (1.0 - sig))).astype(dpre_out.dtype)
+        dpre_out[p] = dpre
+        d = dpre.astype(jnp.float32)
+        gb = gb + jnp.sum(d, axis=1, keepdims=True)
+        gw = gw + _weight_terms(lo, mid, hi, d, mask, p, planes, depth)
+    gw_out[...] = gw
+    gb_out[...] = gb
 
 
 def _input_kernel(lo, mid, hi, wall, mask, out, *, planes, first, depth):
@@ -56,28 +80,6 @@
         out[n] = _shifted_sum(y, mask, chans, lanes, depth, -1).astype(out.dtype)
 
 
-def _weight_kernel(lo, mid, hi, dpre, mask, gw_out, gb_out, *, planes, depth):
-    chans, lanes = dpre.shape[1], dpre.shape[2]
-    gw = jnp.zeros(gw_out.shape, jnp.float32)
-    gb = jnp.zeros(gb_out.shape, jnp.float32)
-    for p in range(planes):
-        d = dpre[p].astype(jnp.float32)
-        gb = gb + jnp.sum(d, axis=1, keepdims=True)
-        parts = []
-        for k, (b, c) in enumerate(OFFSETS):
-            off = b * depth + c
-            e = d
-            if off != 0:
-                e = pltpu.roll(jnp.where(mask[k] > 0.5, d, 0.0), off % lanes, 1)
-            parts.append(e.astype(jnp.bfloat16))
-        gw = gw + lax.dot_general(
-            jnp.concatenate(parts, axis=0), _stacked(lo, mid, hi, p, planes),
-            (((1,), (1,)), ((), ())), preferred_element_type=jnp.float32,
-        )
-    gw_out[...] = gw
-    gb_out[...] = gb
-
-
 def _vmem(n):
     return [pl.BlockSpec(memory_space=pltpu.VMEM)] * n
 
@@ -85,12 +87,17 @@
 def forward_call(lo, mid, hi, wall, bias, cot, mask, depth):
     planes, chans, lanes = mid.shape
     shape = jax.ShapeDtypeStruct(mid.shape, jnp.bfloat16)
-    flops = 2 * planes * wall.shape[0] * wall.shape[1] * lanes
+    flops = 4 * planes * wall.shape[0] * wall.shape[1] * lanes
     return pl.pallas_call(
         functools.partial(_forward_kernel, planes=planes, depth=depth),
-        out_shape=(shape, shape),
+        out_shape=(
+            shape,
+            shape,
+            jax.ShapeDtypeStruct(wall.shape, jnp.float32),
+            jax.ShapeDtypeStruct((chans, 1), jnp.float32),
+        ),
         in_specs=_vmem(7),
-        out_specs=tuple(_vmem(2)),
+        out_specs=tuple(_vmem(4)),
         cost_estimate=pl.CostEstimate(flops=flops, transcendentals=planes * chans * lanes, bytes_accessed=5 * mid.size * 2),
     )(lo, mid, hi, wall, bias, cot, mask)
 
@@ -105,18 +112,6 @@
         out_specs=_vmem(1)[0],
         cost_estimate=pl.CostEstimate(flops=flops, transcendentals=0, bytes_accessed=3 * mid.size * 2),
     )(lo, mid, hi, wall, mask)
-
-
-def weight_call(lo, mid, hi, dpre, mask, depth):
-    planes, chans, lanes = mid.shape
-    flops = 2 * planes * 9 * chans * 3 * chans * lanes
-    return pl.pallas_call(
-        functools.partial(_weight_kernel, planes=planes, depth=depth),
-        out_shape=(jax.ShapeDtypeStruct((9 * chans, 3 * chans), jnp.float32), jax.ShapeDtypeStruct((chans, 1), jnp.float32)),
-        in_specs=_vmem(5),
-        out_specs=tuple(_vmem(2)),
-        cost_estimate=pl.CostEstimate(flops=flops, transcendentals=0, bytes_accessed=3 * mid.size * 2),
-    )(lo, mid, hi, dpre, mask)
 
 
 def neighbours(first, last, axis):
@@ -187,7 +182,7 @@
     w5 = whole_weight.reshape(out_chan, 3, 3, 3, chans)
     forward_w = w5.transpose(2, 3, 0, 1, 4).reshape(9 * out_chan, 3 * chans)
     backward_w = w5[:, ::-1].transpose(2, 3, 4, 1, 0).reshape(9 * chans, 3 * out_chan)
-    mask = plane_masks(rows, depth)
+    mask = jnp.asarray(plane_masks(rows, depth))
 
     def flat(value):
         return value.transpose(1, 0, 2, 3).reshape(planes, value.shape[0], lanes)
@@ -197,23 +192,23 @@
 
     mid = flat(field)
     lo, hi = neighbours(mid[:1], mid[planes - 1 :], "strike")
-    act, dpre = forward_call(
+    act, dpre, g, gb = forward_call(
         lo, mid, hi, forward_w, whole_bias.astype(jnp.float32)[:, None], flat(cotangent[0]), mask, depth
     )
     dlo, dhi = neighbours(dpre[:1], dpre[planes - 1 :], "strike")
-    g, gb = weight_call(lo, mid, hi, dpre, mask, depth)
     local_weight = g.reshape(3, 3, out_chan, 3, chans).transpose(2, 3, 0, 1, 4).reshape(out_chan, 27 * chans)
     local_grads = jnp.concatenate([local_weight, gb], axis=1)
-    work = [
+    work = [(unflat, (act,))] + [
         (functools.partial(input_call, depth=depth, first=p, count=1), (dlo, dpre, dhi, backward_w, mask))
         for p in range(planes)
     ]
     owned, pieces = reduce_beside(local_grads, work)
-    grad_input = unflat(jnp.concatenate(pieces, axis=0))
+    activation = pieces[0]
+    grad_input = unflat(jnp.concatenate(pieces[1:], axis=0))
     cells = lax.axis_size("real") * lax.axis_size("strike") * planes * rows * depth
     factor = 1.0 / cells**0.5
     owned = owned * factor
-    return (unflat(act)[None], grad_input[None], owned[:, :taps_in], owned[:, taps_in])
+    return (activation[None], grad_input[None], owned[:, :taps_in], owned[:, taps_in])
 
 
 def solution(mesh):

time: 59.8 us -> 61.5 us (1.028)
  starting transfers between devices: 23 us -> 27 us
  local copies, waits for them, and re-layouts: 15.2 us -> 14 us
  waiting for transfers between devices: 3.51 us -> 2.73 us
    ppermute x8, starting transfers between devices: 13 us -> 17.6 us  [swap(): return lax.ppermute(value, axis, [(i, i ^ bit) for i in range(peers)])]
    pallas_call x1 -> x0, Pallas kernels: 3.68 us -> none  [weight_call(): pl.pallas_call(functools.partial(_weight_kernel, planes=planes, depth=dep...]
    pallas_call x1, Pallas kernels: 4.89 us -> 8.32 us  [forward_call(): pl.pallas_call(functools.partial(_forward_kernel, planes=planes, depth=de...]
    ppermute x8, waiting for transfers between devices: 3.5 us -> 1.89 us  [swap(): return lax.ppermute(value, axis, [(i, i ^ bit) for i in range(peers)])]
    slice x1, local copies, waits for them, and re-layouts: 1.06 us -> 0.03 us  [local(): dlo, dhi = neighbours(dpre[:1], dpre[planes - 1:], 'strike')]
    concatenate x1, other arithmetic: 0.05 us -> 1 us  [local(): grad_input = unflat(jnp.concatenate(pieces[1:], axis=0))]
    broadcast_in_dim x1 -> x0, local copies, waits for them, and re-layouts: 0.86 us -> none  [local(): unflat(act)[None]]
    transpose x0 -> x1, local copies, waits for them, and re-layouts: none -> 0.85 us  [unflat(): value.reshape(planes, value.shape[1], rows, depth).transpose(1, 0, 2, 3)]
  transfers between devices with their start and end apart: 12 -> 12, of which waited for: 2 -> 3; matrix products, arithmetic and copies ran while one was open for 20% -> 16% of each run, Pallas kernels for 17% -> 10%
where the time goes in v4:
time: 61.5 us; the launch traced here: 61 us
  starting transfers between devices  27 us (44%)
  Pallas kernels  14.4 us (23%)
  local copies, waits for them, and re-layouts  14 us (23%)
  waiting for transfers between devices  2.73 us (4%)
  other arithmetic  1.95 us (3%)
  between operations  0.95 us (2%)
    ppermute x8, starting transfers between devices, swap(): return lax.ppermute(value, axis, [(i, i ^ bit) for i in range(peers)])  17.6 us
    ppermute x4, starting transfers between devices, neighbours(): return (lax.ppermute(last, axis, up), lax.ppermute(first, axis, down))  9.39 us
    pallas_call x1, Pallas kernels, forward_call(): pl.pallas_call(functools.partial(_forward_kernel, planes=planes, depth=de...  8.32 us
    pallas_call x2, Pallas kernels, input_call(): pl.pallas_call(functools.partial(_input_kernel, planes=planes, first=firs...  6.1 us
    unnamed x28, local copies, waits for them, and re-layouts  3.67 us
    reshape x4, local copies, waits for them, and re-layouts, flat(): return value.transpose(1, 0, 2, 3).reshape(planes, value.shape[0], lanes)  2.41 us
    ppermute x8, waiting for transfers between devices, swap(): return lax.ppermute(value, axis, [(i, i ^ bit) for i in range(peers)])  1.89 us
    reshape x2, local copies, waits for them, and re-layouts, local(): g.reshape(3, 3, out_chan, 3, chans).transpose(2, 3, 0, 1, 4)  1.42 us
  transfers between devices with their start and end apart: 12, of which 3 were waited for; matrix products, arithmetic and copies ran while one was open for 16% of the time, Pallas kernels for 10%

profile of v4, /device:TPU:0, one launch (start us, length us, event | category | flops | bytes accessed | tf_op | source)
XLA Modules:
  0.0 61.0 jit_solution(8650263719093649048)
XLA Ops:
  0.6 0.0 copy-start.10
  0.6 0.6 %copy-done.10 = bf16[8]{0:T(256)(128)(2,1)S(1)} copy-done((bf16[8]{0:T(256)(128)(2,1)S(1)}, bf16[8]{0:T(256)(128)(2,1)}, u32[]{:S(2)}) %copy-start.10) | copy-done | bytes 40
  1.3 0.1 copy.26
  1.4 0.7 %copy-done.9 = bf16[8,864]{1,0:T(8,128)(2,1)S(1)} copy-done((bf16[8,864]{1,0:T(8,128)(2,1)S(1)}, bf16[8,864]{1,0:T(8,128)(2,1)}, u32[]{:S(2)}) %copy-start.9) | copy-done | bytes 13848
  2.1 0.1 bitcast_dynamic-update-slice_fusion.3
  2.2 3.0 %collective-permute-start.3 = (bf16[8,865]{1,0:T(8,128)(2,1)S(1)}, bf16[8,865]{1,0:T(8,128)(2,1)S(1)}, u32[]{:S(2)}, u32[]{:S(2)}) collective-permute-start(bf16[8,865]{1,0:T(8,128)(2,1)S(1)} %get-tuple-element.53), channel_id=1, source_target_pairs={{0,16},{8,24},{16,0},{24,8},{1,17},{9,25},{17,1},{25,9},{2,18},{10... | collective-permute-start | bytes 41528 | tf_op jit(solution)/shard_map/ppermute | solution.py:126
  5.1 1.5 %collective-permute-start.2 = (bf16[8,865]{1,0:T(8,128)(2,1)S(1)}, bf16[8,865]{1,0:T(8,128)(2,1)S(1)}, u32[]{:S(2)}, u32[]{:S(2)}) collective-permute-start(bf16[8,865]{1,0:T(8,128)(2,1)S(1)} %get-tuple-element.53), channel_id=1, source_target_pairs={{0,8},{8,0},{16,24},{24,16},{1,9},{9,1},{17,25},{25,17},{2,10},{10... | collective-permute-start | bytes 41528 | tf_op jit(solution)/shard_map/ppermute | solution.py:126
  6.6 0.0 collective-permute-start.4
  6.7 1.1 %fusion.4 = (bf16[1,32,32,128]{3,2,0,1:T(8,128)(2,1)S(1)}, bf16[1,32,32,128]{3,2,0,1:T(8,128)(2,1)S(1)}) fusion(bf16[2,32,32,128]{3,2,0,1:T(8,128)(2,1)} %bitcast.63), kind=kLoop, calls=%fused_computation.22 | loop fusion | bytes 1048576 | tf_op jit(solution)/shard_map/slice | solution.py:194
  7.8 0.0 copy-start.1
  7.8 0.1 slice.31
  7.9 1.4 %collective-permute-start = (bf16[1,32,4096]{2,1,0:T(8,128)(2,1)S(1)}, bf16[1,32,4096]{2,1,0:T(8,128)(2,1)S(1)}, u32[]{:S(2)}, u32[]{:S(2)}) collective-permute-start(bf16[1,32,4096]{2,1,0:T(8,128)(2,1)S(1)} %slice.31), channel_id=1, source_target_pairs={{0,1},{1,2},{2,3},{3,4},{4,5},{5,6},{6,7},{8,9},{9,10},{10,11},{11... | collective-permute-start | bytes 786440 | tf_op jit(solution)/shard_map/ppermute | solution.py:121
  9.3 0.1 slice.33
  9.5 1.3 %collective-permute-start.1 = (bf16[1,32,4096]{2,1,0:T(8,128)(2,1)S(1)}, bf16[1,32,4096]{2,1,0:T(8,128)(2,1)S(1)}, u32[]{:S(2)}, u32[]{:S(2)}) collective-permute-start(bf16[1,32,4096]{2,1,0:T(8,128)(2,1)S(1)} %slice.33), channel_id=1, source_target_pairs={{1,0},{2,1},{3,2},{4,3},{5,4},{6,5},{7,6},{9,8},{10,9},{11,10},{12... | collective-permute-start | bytes 786440 | tf_op jit(solution)/shard_map/ppermute | solution.py:121
  10.8 0.1 reshape.50
  11.0 0.0 copy-start.5
  11.0 1.1 %copy.33.mid = bf16[2,32,4096]{2,1,0:T(8,128)(2,1)} copy(bf16[2,32,4096]{2,0,1:T(2,128)(2,1)S(1)} %reshape.50) | data formatting | bytes 1048576 | tf_op jit(solution)/shard_map/reshape | solution.py:188
  12.1 0.1 reshape.51
  12.2 1.1 %copy.34.cot = bf16[2,32,4096]{2,1,0:T(8,128)(2,1)} copy(bf16[2,32,4096]{2,0,1:T(2,128)(2,1)S(1)} %reshape.51) | data formatting | bytes 1048576 | tf_op jit(solution)/shard_map/reshape | solution.py:188
  13.3 0.0 collective-permute-done.2
  13.3 0.0 collective-permute-done.3
  13.3 0.0 collective-permute-done.4
  13.3 0.2 reshape.42
  13.5 0.1 reverse_bitcast_fusion
  13.6 0.1 copy.27
  13.8 0.8 %reshape.43.wall = bf16[288,96]{1,0:T(8,128)(2,1)} reshape(bf16[3,3,32,3,32]{4,3,2,1,0:T(4,128)(2,1)S(1)} %copy.27) | data formatting | bytes 110592 | tf_op jit(solution)/shard_map/reshape | solution.py:183
  14.6 0.3 copy.31
  14.9 0.8 %reshape.48.wall = bf16[288,96]{1,0:T(8,128)(2,1)} reshape(bf16[3,3,32,3,32]{4,3,2,1,0:T(4,128)(2,1)S(1)} %copy.31) | data formatting | bytes 110592 | tf_op jit(solution)/shard_map/reshape | solution.py:184
  15.7 0.7 %slice_convert_fusion.bias = f32[32,1]{1,0:T(8,128)} fusion(bf16[32,865]{1,0:T(8,128)(2,1)S(1)} %bitcast.72), kind=kLoop, calls=%fused_computation.18 | loop fusion | flops 32 | bytes 192 | tf_op jit(solution)/shard_map/convert_element_type | solution.py:196
  16.3 0.0 collective-permute-done.lo
  16.3 0.0 collective-permute-done.1.hi
  16.3 0.7 %copy-done.11 = bf16[1,32,4096]{2,1,0:T(8,128)(2,1)} copy-done((bf16[1,32,4096]{2,1,0:T(8,128)(2,1)}, bf16[1,32,4096]{2,1,0:T(8,128)(2,1)S(1)}, u32[]{:S(2)}) %copy-start.11) | copy-done | bytes 262168
  17.1 0.7 %copy-done.12 = bf16[1,32,4096]{2,1,0:T(8,128)(2,1)} copy-done((bf16[1,32,4096]{2,1,0:T(8,128)(2,1)}, bf16[1,32,4096]{2,1,0:T(8,128)(2,1)S(1)}, u32[]{:S(2)}) %copy-start.12) | copy-done | bytes 262168
  17.8 8.3 %shard_map.84 = (bf16[2,32,4096]{2,1,0:T(8,128)(2,1)}, bf16[2,32,4096]{2,1,0:T(8,128)(2,1)}, f32[288,96]{1,0:T(8,128)}, f32[32,1]{1,0:T(8,128)}) custom-call(bf16[1,32,4096]{2,1,0:T(8,128)(2,1)} %copy-done.11, bf16[2,32,4096]{2,1,0:T(8,128)(2,1)} %copy.33.mid, bf16[1,32,4096]{2,1,0:T(8,128)(2,1)} %copy-done.12, bf16[288,96]{1,0:T(8,128)(2,1)} %reshape.43.wall, ...), custom_call_target="tpu_custom_call" | custom-call | flops 905969664 | bytes 2621440 | tf_op jit(solution)/shard_map/pallas_call | solution.py:91
  26.1 1.1 %reshape.45 = f32[3,3,32,3,32]{4,3,2,1,0:T(4,128)S(1)} reshape(f32[288,96]{1,0:T(8,128)} %get-tuple-element.28) | data formatting | bytes 221184 | tf_op jit(solution)/shard_map/reshape | solution.py:199
  27.2 0.3 copy.29
  27.6 0.3 reshape.46
  27.8 0.4 copy-done.7
  28.3 0.1 fusion.2
  28.3 0.3 copy-done.6
  28.6 0.1 copy.35
  28.7 2.0 %collective-permute-start.5 = (f32[16,865]{1,0:T(8,128)S(1)}, f32[16,865]{1,0:T(8,128)S(1)}, u32[]{:S(2)}, u32[]{:S(2)}) collective-permute-start(f32[16,865]{1,0:T(8,128)S(1)} %fusion.2), channel_id=1, source_target_pairs={{0,16},{8,24},{16,0},{24,8},{1,17},{9,25},{17,1},{25,9},{2,18},{10... | collective-permute-start | bytes 166088 | tf_op jit(solution)/shard_map/ppermute | solution.py:126
  30.7 0.0 copy-done
  30.8 0.9 %copy_bitcast_fusion.1 = bf16[32,2,32,128]{3,2,1,0:T(8,128)(2,1)} fusion(bf16[2,32,32,128]{3,2,1,0:T(8,128)(2,1)S(1)} %bitcast.66), kind=kLoop, calls=%fused_computation.2 | loop fusion | bytes 1048576 | tf_op jit(solution)/shard_map/transpose | solution.py:191
  31.6 1.3 %collective-permute-start.7 = (bf16[1,32,4096]{2,1,0:T(8,128)(2,1)S(1)}, bf16[1,32,4096]{2,1,0:T(8,128)(2,1)S(1)}, u32[]{:S(2)}, u32[]{:S(2)}) collective-permute-start(bf16[1,32,4096]{2,1,0:T(8,128)(2,1)S(1)} %get-tuple-element.54), channel_id=1, source_target_pairs={{1,0},{2,1},{3,2},{4,3},{5,4},{6,5},{7,6},{9,8},{10,9},{11,10},{12... | collective-permute-start | bytes 786440 | tf_op jit(solution)/shard_map/ppermute | solution.py:121
  32.9 5.4 %collective-permute-start.6 = (bf16[1,32,4096]{2,1,0:T(8,128)(2,1)S(1)}, bf16[1,32,4096]{2,1,0:T(8,128)(2,1)S(1)}, u32[]{:S(2)}, u32[]{:S(2)}) collective-permute-start(bf16[1,32,4096]{2,1,0:T(8,128)(2,1)S(1)} %get-tuple-element.55), channel_id=1, source_target_pairs={{0,1},{1,2},{2,3},{3,4},{4,5},{5,6},{6,7},{8,9},{9,10},{10,11},{11... | collective-permute-start | bytes 786440 | tf_op jit(solution)/shard_map/ppermute | solution.py:121
  38.3 0.0 collective-permute-done.5
  38.3 0.1 fusion.1
  38.4 0.0 collective-permute-done.7.hi
  38.4 0.8 %collective-permute-done.6.lo = bf16[1,32,4096]{2,1,0:T(8,128)(2,1)S(1)} collective-permute-done((bf16[1,32,4096]{2,1,0:T(8,128)(2,1)S(1)}, bf16[1,32,4096]{2,1,0:T(8,128)(2,1)S(1)}, u32[]{:S(2)}, u32[]{:S(2)}) %collective-permute-start.6) | collective-permute-done | bytes 262176 | tf_op jit(solution)/shard_map/ppermute | solution.py:121
  39.2 1.5 %collective-permute-start.8 = (f32[8,865]{1,0:T(8,128)S(1)}, f32[8,865]{1,0:T(8,128)S(1)}, u32[]{:S(2)}, u32[]{:S(2)}) collective-permute-start(f32[8,865]{1,0:T(8,128)S(1)} %constant_dynamic-slice_fusion), channel_id=1, source_target_pairs={{0,8},{8,0},{16,24},{24,16},{1,9},{9,1},{17,25},{25,17},{2,10},{10... | collective-permute-start | bytes 83048 | tf_op jit(solution)/shard_map/ppermute | solution.py:126
  40.7 3.0 %shard_map.85 = bf16[1,32,4096]{2,1,0:T(8,128)(2,1)} custom-call(bf16[1,32,4096]{2,1,0:T(8,128)(2,1)} %copy-done.3, bf16[2,32,4096]{2,1,0:T(8,128)(2,1)} %get-tuple-element.46.mid, bf16[1,32,4096]{2,1,0:T(8,128)(2,1)} %copy-done.2, bf16[288,96]{1,0:T(8,128)(2,1)} %reshape.48.wall, f32[9,1,4096]{2,1,0:T(1,128)} %constant.68.clone.mask), custom_call_target="tpu_custom_call" | custom-call | flops 226492416 | bytes 1572864 | tf_op jit(solution)/shard_map/pallas_call | solution.py:108
  43.8 0.0 collective-permute-done.8
  43.8 4.0 %collective-permute-start.9 = (f32[8,865]{1,0:T(8,128)S(1)}, f32[8,865]{1,0:T(8,128)S(1)}, u32[]{:S(2)}, u32[]{:S(2)}) collective-permute-start(f32[8,865]{1,0:T(8,128)S(1)} %dynamic-slice_add_fusion), channel_id=1, source_target_pairs={{0,1},{1,0},{2,3},{3,2},{4,5},{5,4},{6,7},{7,6},{8,9},{9,8},{10,11... | collective-permute-start | bytes 83048 | tf_op jit(solution)/shard_map/ppermute | solution.py:126
  47.7 3.1 %shard_map.86 = bf16[1,32,4096]{2,1,0:T(8,128)(2,1)} custom-call(bf16[1,32,4096]{2,1,0:T(8,128)(2,1)} %copy-done.3, bf16[2,32,4096]{2,1,0:T(8,128)(2,1)} %get-tuple-element.46.mid, bf16[1,32,4096]{2,1,0:T(8,128)(2,1)} %copy-done.2, bf16[288,96]{1,0:T(8,128)(2,1)} %reshape.48.wall, f32[9,1,4096]{2,1,0:T(1,128)} %constant.68.clone.mask), custom_call_target="tpu_custom_call" | custom-call | flops 226492416 | bytes 1572864 | tf_op jit(solution)/shard_map/pallas_call | solution.py:108
  50.8 0.0 collective-permute-done.9
  50.8 2.7 %collective-permute-start.10 = (f32[8,865]{1,0:T(8,128)S(1)}, f32[8,865]{1,0:T(8,128)S(1)}, u32[]{:S(2)}, u32[]{:S(2)}) collective-permute-start(f32[8,865]{1,0:T(8,128)S(1)} %add.61), channel_id=1, source_target_pairs={{0,2},{1,3},{2,0},{3,1},{4,6},{5,7},{6,4},{7,5},{8,10},{9,11},{10,... | collective-permute-start | bytes 83048 | tf_op jit(solution)/shard_map/ppermute | solution.py:126
  53.6 1.0 %pad_maximum_fusion = bf16[2,32,4096]{2,1,0:T(8,128)(2,1)S(1)} fusion(bf16[1,32,4096]{2,1,0:T(8,128)(2,1)} %shard_map.86, bf16[1,32,4096]{2,1,0:T(8,128)(2,1)S(1)} %copy-done.4), kind=kLoop, calls=%fused_computation | loop fusion | flops 262144 | bytes 1048576 | tf_op jit(solution)/shard_map/concatenate | solution.py:207
  54.6 0.1 copy.36
  54.7 0.8 %collective-permute-done.10 = f32[8,865]{1,0:T(8,128)S(1)} collective-permute-done((f32[8,865]{1,0:T(8,128)S(1)}, f32[8,865]{1,0:T(8,128)S(1)}, u32[]{:S(2)}, u32[]{:S(2)}) %collective-permute-start.10) | collective-permute-done | bytes 27712 | tf_op jit(solution)/shard_map/ppermute | solution.py:126
  55.5 2.9 %collective-permute-start.11 = (f32[8,865]{1,0:T(8,128)S(1)}, f32[8,865]{1,0:T(8,128)S(1)}, u32[]{:S(2)}, u32[]{:S(2)}) collective-permute-start(f32[8,865]{1,0:T(8,128)S(1)} %add.62), channel_id=1, source_target_pairs={{0,4},{1,5},{2,6},{3,7},{4,0},{5,1},{6,2},{7,3},{8,12},{9,13},{10,... | collective-permute-start | bytes 83048 | tf_op jit(solution)/shard_map/ppermute | solution.py:126
  58.4 0.9 %copy_bitcast_fusion = bf16[1,32,2,32,128]{4,3,2,1,0:T(8,128)(2,1)} fusion(bf16[2,32,32,128]{3,2,1,0:T(8,128)(2,1)S(1)} %bitcast.65), kind=kLoop, calls=%fused_computation.1 | loop fusion | bytes 1048576 | tf_op jit(solution)/shard_map/broadcast_in_dim | solution.py:211
  59.3 1.0 %collective-permute-done.11 = f32[8,865]{1,0:T(8,128)S(1)} collective-permute-done((f32[8,865]{1,0:T(8,128)S(1)}, f32[8,865]{1,0:T(8,128)S(1)}, u32[]{:S(2)}, u32[]{:S(2)}) %collective-permute-start.11) | collective-permute-done | bytes 27712 | tf_op jit(solution)/shard_map/ppermute | solution.py:126
  60.3 0.7 %slice_reduce_fusion = f32[8]{0:T(128)} fusion(f32[8,865]{1,0:T(8,128)S(1)} %add_multiply_fusion), kind=kLoop, calls=%fused_computation.19 | loop fusion | bytes 64 | tf_op jit(solution)/shard_map/slice | solution.py:211
  (26 shorter events, 0.1 us)
Async XLA Ops:
  0.6 0.7 %copy-start.10 = (bf16[8]{0:T(256)(128)(2,1)S(1)}, bf16[8]{0:T(256)(128)(2,1)}, u32[]{:S(2)}) copy-start(bf16[8]{0:T(256)(128)(2,1)} %param.8) | copy-start | bytes 52
  1.4 0.7 %copy-start.9 = (bf16[8,864]{1,0:T(8,128)(2,1)S(1)}, bf16[8,864]{1,0:T(8,128)(2,1)}, u32[]{:S(2)}) copy-start(bf16[8,864]{1,0:T(8,128)(2,1)} %param.7) | copy-start | bytes 41476
  2.2 11.1 %collective-permute-start.3 = (bf16[8,865]{1,0:T(8,128)(2,1)S(1)}, bf16[8,865]{1,0:T(8,128)(2,1)S(1)}, u32[]{:S(2)}, u32[]{:S(2)}) collective-permute-start(bf16[8,865]{1,0:T(8,128)(2,1)S(1)} %get-tuple-element.53), channel_id=1, source_target_pairs={{0,16},{8,24},{16,0},{24,8},{1,17},{9,25},{17,1},{25,9},{2,18},{10... | collective-permute-start | bytes 41528 | tf_op jit(solution)/shard_map/ppermute | solution.py:126
  5.1 8.1 %collective-permute-start.2 = (bf16[8,865]{1,0:T(8,128)(2,1)S(1)}, bf16[8,865]{1,0:T(8,128)(2,1)S(1)}, u32[]{:S(2)}, u32[]{:S(2)}) collective-permute-start(bf16[8,865]{1,0:T(8,128)(2,1)S(1)} %get-tuple-element.53), channel_id=1, source_target_pairs={{0,8},{8,0},{16,24},{24,16},{1,9},{9,1},{17,25},{25,17},{2,10},{10... | collective-permute-start | bytes 41528 | tf_op jit(solution)/shard_map/ppermute | solution.py:126
  6.6 6.7 %collective-permute-start.4 = (bf16[8,865]{1,0:T(8,128)(2,1)S(1)}, bf16[8,865]{1,0:T(8,128)(2,1)S(1)}, u32[]{:S(2)}, u32[]{:S(2)}) collective-permute-start(bf16[8,865]{1,0:T(8,128)(2,1)S(1)} %get-tuple-element.53), channel_id=1, source_target_pairs={{0,24},{8,16},{16,8},{24,0},{1,25},{9,17},{17,9},{25,1},{2,26},{10... | collective-permute-start | bytes 41528 | tf_op jit(solution)/shard_map/ppermute | solution.py:126
  7.8 3.1 %copy-start.1 = (bf16[1,32,2,32,128]{4,3,2,1,0:T(8,128)(2,1)S(1)}, bf16[1,32,2,32,128]{4,3,2,1,0:T(8,128)(2,1)}, u32[]{:S(2)}) copy-start(bf16[1,32,2,32,128]{4,3,2,1,0:T(8,128)(2,1)} %param.5) | copy-start | bytes 1572868
  7.9 8.4 %collective-permute-start = (bf16[1,32,4096]{2,1,0:T(8,128)(2,1)S(1)}, bf16[1,32,4096]{2,1,0:T(8,128)(2,1)S(1)}, u32[]{:S(2)}, u32[]{:S(2)}) collective-permute-start(bf16[1,32,4096]{2,1,0:T(8,128)(2,1)S(1)} %slice.31), channel_id=1, source_target_pairs={{0,1},{1,2},{2,3},{3,4},{4,5},{5,6},{6,7},{8,9},{9,10},{10,11},{11... | collective-permute-start | bytes 786440 | tf_op jit(solution)/shard_map/ppermute | solution.py:121
  9.5 6.9 %collective-permute-start.1 = (bf16[1,32,4096]{2,1,0:T(8,128)(2,1)S(1)}, bf16[1,32,4096]{2,1,0:T(8,128)(2,1)S(1)}, u32[]{:S(2)}, u32[]{:S(2)}) collective-permute-start(bf16[1,32,4096]{2,1,0:T(8,128)(2,1)S(1)} %slice.33), channel_id=1, source_target_pairs={{1,0},{2,1},{3,2},{4,3},{5,4},{6,5},{7,6},{9,8},{10,9},{11,10},{12... | collective-permute-start | bytes 786440 | tf_op jit(solution)/shard_map/ppermute | solution.py:121
  11.0 1.1 %copy-start.5 = (bf16[1,32,2,32,128]{4,3,2,1,0:T(8,128)(2,1)S(1)}, bf16[1,32,2,32,128]{4,3,2,1,0:T(8,128)(2,1)}, u32[]{:S(2)}) copy-start(bf16[1,32,2,32,128]{4,3,2,1,0:T(8,128)(2,1)} %param.6) | copy-start | bytes 1572868
  16.3 0.7 %copy-start.11 = (bf16[1,32,4096]{2,1,0:T(8,128)(2,1)}, bf16[1,32,4096]{2,1,0:T(8,128)(2,1)S(1)}, u32[]{:S(2)}) copy-start(bf16[1,32,4096]{2,1,0:T(8,128)(2,1)S(1)} %collective-permute-done.lo) | copy-start | bytes 786436
  17.0 0.7 %copy-start.12 = (bf16[1,32,4096]{2,1,0:T(8,128)(2,1)}, bf16[1,32,4096]{2,1,0:T(8,128)(2,1)S(1)}, u32[]{:S(2)}) copy-start(bf16[1,32,4096]{2,1,0:T(8,128)(2,1)S(1)} %collective-permute-done.1.hi) | copy-start | bytes 786436
  27.5 0.7 %copy-start.7 = (f32[32,1]{1,0:T(8,128)S(1)}, f32[32,1]{1,0:T(8,128)}, u32[]{:S(2)}) copy-start(f32[32,1]{1,0:T(8,128)} %get-tuple-element.29) | copy-start | bytes 388
  27.6 1.0 %copy-start.6 = (bf16[2,32,4096]{2,1,0:T(8,128)(2,1)S(1)}, bf16[2,32,4096]{2,1,0:T(8,128)(2,1)}, u32[]{:S(2)}) copy-start(bf16[2,32,4096]{2,1,0:T(8,128)(2,1)} %get-tuple-element.32) | copy-start | bytes 1572868
  28.6 2.1 %copy-start = (bf16[2,32,4096]{2,1,0:T(8,128)(2,1)S(1)}, bf16[2,32,4096]{2,1,0:T(8,128)(2,1)}, u32[]{:S(2)}) copy-start(bf16[2,32,4096]{2,1,0:T(8,128)(2,1)} %get-tuple-element.46.mid) | copy-start | bytes 1572868
  28.7 9.6 %collective-permute-start.5 = (f32[16,865]{1,0:T(8,128)S(1)}, f32[16,865]{1,0:T(8,128)S(1)}, u32[]{:S(2)}, u32[]{:S(2)}) collective-permute-start(f32[16,865]{1,0:T(8,128)S(1)} %fusion.2), channel_id=1, source_target_pairs={{0,16},{8,24},{16,0},{24,8},{1,17},{9,25},{17,1},{25,9},{2,18},{10... | collective-permute-start | bytes 166088 | tf_op jit(solution)/shard_map/ppermute | solution.py:126
  31.6 6.8 %collective-permute-start.7 = (bf16[1,32,4096]{2,1,0:T(8,128)(2,1)S(1)}, bf16[1,32,4096]{2,1,0:T(8,128)(2,1)S(1)}, u32[]{:S(2)}, u32[]{:S(2)}) collective-permute-start(bf16[1,32,4096]{2,1,0:T(8,128)(2,1)S(1)} %get-tuple-element.54), channel_id=1, source_target_pairs={{1,0},{2,1},{3,2},{4,3},{5,4},{6,5},{7,6},{9,8},{10,9},{11,10},{12... | collective-permute-start | bytes 786440 | tf_op jit(solution)/shard_map/ppermute | solution.py:121
  32.9 6.3 %collective-permute-start.6 = (bf16[1,32,4096]{2,1,0:T(8,128)(2,1)S(1)}, bf16[1,32,4096]{2,1,0:T(8,128)(2,1)S(1)}, u32[]{:S(2)}, u32[]{:S(2)}) collective-permute-start(bf16[1,32,4096]{2,1,0:T(8,128)(2,1)S(1)} %get-tuple-element.55), channel_id=1, source_target_pairs={{0,1},{1,2},{2,3},{3,4},{4,5},{5,6},{6,7},{8,9},{9,10},{10,11},{11... | collective-permute-start | bytes 786440 | tf_op jit(solution)/shard_map/ppermute | solution.py:121
  38.4 2.3 %copy-start.2 = (bf16[1,32,4096]{2,1,0:T(8,128)(2,1)}, bf16[1,32,4096]{2,1,0:T(8,128)(2,1)S(1)}, u32[]{:S(2)}) copy-start(bf16[1,32,4096]{2,1,0:T(8,128)(2,1)S(1)} %collective-permute-done.7.hi) | copy-start | bytes 786436
  39.2 1.5 %copy-start.3 = (bf16[1,32,4096]{2,1,0:T(8,128)(2,1)}, bf16[1,32,4096]{2,1,0:T(8,128)(2,1)S(1)}, u32[]{:S(2)}) copy-start(bf16[1,32,4096]{2,1,0:T(8,128)(2,1)S(1)} %collective-permute-done.6.lo) | copy-start | bytes 786436
  39.2 4.5 %collective-permute-start.8 = (f32[8,865]{1,0:T(8,128)S(1)}, f32[8,865]{1,0:T(8,128)S(1)}, u32[]{:S(2)}, u32[]{:S(2)}) collective-permute-start(f32[8,865]{1,0:T(8,128)S(1)} %constant_dynamic-slice_fusion), channel_id=1, source_target_pairs={{0,8},{8,0},{16,24},{24,16},{1,9},{9,1},{17,25},{25,17},{2,10},{10... | collective-permute-start | bytes 83048 | tf_op jit(solution)/shard_map/ppermute | solution.py:126
  43.8 7.0 %collective-permute-start.9 = (f32[8,865]{1,0:T(8,128)S(1)}, f32[8,865]{1,0:T(8,128)S(1)}, u32[]{:S(2)}, u32[]{:S(2)}) collective-permute-start(f32[8,865]{1,0:T(8,128)S(1)} %dynamic-slice_add_fusion), channel_id=1, source_target_pairs={{0,1},{1,0},{2,3},{3,2},{4,5},{5,4},{6,7},{7,6},{8,9},{9,8},{10,11... | collective-permute-start | bytes 83048 | tf_op jit(solution)/shard_map/ppermute | solution.py:126
  47.7 5.8 %copy-start.4 = (bf16[1,32,4096]{2,1,0:T(8,128)(2,1)S(1)}, bf16[1,32,4096]{2,1,0:T(8,128)(2,1)}, u32[]{:S(2)}) copy-start(bf16[1,32,4096]{2,1,0:T(8,128)(2,1)} %shard_map.85) | copy-start | bytes 786436
  50.8 4.7 %collective-permute-start.10 = (f32[8,865]{1,0:T(8,128)S(1)}, f32[8,865]{1,0:T(8,128)S(1)}, u32[]{:S(2)}, u32[]{:S(2)}) collective-permute-start(f32[8,865]{1,0:T(8,128)S(1)} %add.61), channel_id=1, source_target_pairs={{0,2},{1,3},{2,0},{3,1},{4,6},{5,7},{6,4},{7,5},{8,10},{9,11},{10,... | collective-permute-start | bytes 83048 | tf_op jit(solution)/shard_map/ppermute | solution.py:126
  55.5 4.8 %collective-permute-start.11 = (f32[8,865]{1,0:T(8,128)S(1)}, f32[8,865]{1,0:T(8,128)S(1)}, u32[]{:S(2)}, u32[]{:S(2)}) collective-permute-start(f32[8,865]{1,0:T(8,128)S(1)} %add.62), channel_id=1, source_target_pairs={{0,4},{1,5},{2,6},{3,7},{4,0},{5,1},{6,2},{7,3},{8,12},{9,13},{10,... | collective-permute-start | bytes 83048 | tf_op jit(solution)/shard_map/ppermute | solution.py:126
  60.3 0.7 %copy-start.8 = (f32[8,865]{1,0:T(8,128)}, f32[8,865]{1,0:T(8,128)S(1)}, u32[]{:S(2)}) copy-start(f32[8,865]{1,0:T(8,128)S(1)} %add_multiply_fusion) | copy-start | bytes 83044

commit v5 on v4

--- a/solution.py
+++ b/solution.py
@@ -136,7 +136,7 @@
     return blocks.reshape((peers * value.shape[0],) + value.shape[1:])
 
 
-def reduce_beside(local_grads, work):
+def reduction_rounds():
     rounds = []
     bit = lax.axis_size("real") // 2
     while bit >= 1:
@@ -146,9 +146,11 @@
     while bit < lax.axis_size("strike"):
         rounds.append(("strike", bit))
         bit *= 2
-    results = []
-    value = local_grads
-    for k, (axis, bit) in enumerate(rounds):
+    return rounds
+
+
+def reduce_beside(value, carry, jobs):
+    for k, (axis, bit) in enumerate(reduction_rounds()):
         if axis == "real":
             half = value.shape[0] // 2
             upper = (lax.axis_index(axis) // bit) % 2
@@ -156,18 +158,17 @@
             send = lax.dynamic_slice_in_dim(value, (1 - upper) * half, half, 0)
         else:
             keep, send = value, value
-        if k < len(work):
-            send, inputs = lax.optimization_barrier((send, work[k][1]))
+        if k < len(jobs):
+            send, carry = lax.optimization_barrier((send, carry))
             received = swap(send, axis, bit)
-            result = work[k][0](*inputs)
-            received, result = lax.optimization_barrier((received, result))
-            results.append(result)
+            carry = jobs[k](carry)
+            received, carry = lax.optimization_barrier((received, carry))
         else:
             received = swap(send, axis, bit)
         value = keep + received
-    for job, inputs in work[len(rounds) :]:
-        results.append(job(*inputs))
-    return value, results
+    for job in jobs[len(reduction_rounds()) :]:
+        carry = job(carry)
+    return value, carry
 
 
 def local(grades, cotangent, weight, bias):
@@ -181,7 +182,6 @@
     out_chan = whole_weight.shape[0]
     w5 = whole_weight.reshape(out_chan, 3, 3, 3, chans)
     forward_w = w5.transpose(2, 3, 0, 1, 4).reshape(9 * out_chan, 3 * chans)
-    backward_w = w5[:, ::-1].transpose(2, 3, 4, 1, 0).reshape(9 * chans, 3 * out_chan)
     mask = jnp.asarray(plane_masks(rows, depth))
 
     def flat(value):
@@ -198,13 +198,24 @@
     dlo, dhi = neighbours(dpre[:1], dpre[planes - 1 :], "strike")
     local_weight = g.reshape(3, 3, out_chan, 3, chans).transpose(2, 3, 0, 1, 4).reshape(out_chan, 27 * chans)
     local_grads = jnp.concatenate([local_weight, gb], axis=1)
-    work = [(unflat, (act,))] + [
-        (functools.partial(input_call, depth=depth, first=p, count=1), (dlo, dpre, dhi, backward_w, mask))
-        for p in range(planes)
-    ]
-    owned, pieces = reduce_beside(local_grads, work)
-    activation = pieces[0]
-    grad_input = unflat(jnp.concatenate(pieces[1:], axis=0))
+    dlo, dhi, local_grads, activation = lax.optimization_barrier((dlo, dhi, local_grads, unflat(act)))
+
+    def backward_weights(carry):
+        weights = carry[3].reshape(out_chan, 3, 3, 3, chans)
+        return carry[:3] + (weights[:, ::-1].transpose(2, 3, 4, 1, 0).reshape(9 * chans, 3 * out_chan),) + carry[4:]
+
+    def plane_job(p):
+        def job(carry):
+            lo_d, mid_d, hi_d, weights = carry[:4]
+            piece = input_call(lo_d, mid_d, hi_d, weights, mask, depth=depth, first=p, count=1)
+            return carry + (piece,)
+        return job
+
+    def finish(carry):
+        return (unflat(jnp.concatenate(carry[4:], axis=0)),)
+
+    jobs = [lambda carry: plane_job(0)(backward_weights(carry))] + [plane_job(p) for p in range(1, planes)] + [finish]
+    owned, (grad_input,) = reduce_beside(local_grads, (dlo, dpre, dhi, whole_weight), jobs)
     cells = lax.axis_size("real") * lax.axis_size("strike") * planes * rows * depth
     factor = 1.0 / cells**0.5
     owned = owned * factor

time: 61.5 us -> 64.4 us (1.047)
  waiting for transfers between devices: 2.73 us -> 5.96 us
    ppermute x8, waiting for transfers between devices: 1.89 us -> 4.49 us  [swap(): return lax.ppermute(value, axis, [(i, i ^ bit) for i in range(peers)])]
    ppermute x8, starting transfers between devices: 17.6 us -> 16.1 us  [swap(): return lax.ppermute(value, axis, [(i, i ^ bit) for i in range(peers)])]
    ppermute x4, starting transfers between devices: 9.39 us -> 10.3 us  [neighbours(): return (lax.ppermute(last, axis, up), lax.ppermute(first, axis, down))]
    transpose x1 -> x2, local copies, waits for them, and re-layouts: 0.85 us -> 1.71 us  [unflat(): value.reshape(planes, value.shape[1], rows, depth).transpose(1, 0, 2, 3)]
    broadcast_in_dim x1 -> x0, local copies, waits for them, and re-layouts: 0.85 us -> none  [local(): grad_input[None]]
  transfers between devices with their start and end apart: 12 -> 12, of which waited for: 3 -> 3; matrix products, arithmetic and copies ran while one was open for 16% -> 13% of each run, Pallas kernels for 10% -> 10%
where the time goes in v5:
time: 64.4 us; the launch traced here: 63.9 us
  starting transfers between devices  26.4 us (41%)
  Pallas kernels  14.4 us (22%)
  local copies, waits for them, and re-layouts  14.3 us (22%)
  waiting for transfers between devices  5.96 us (9%)
  other arithmetic  1.87 us (3%)
  between operations  0.97 us (2%)
    ppermute x8, starting transfers between devices, swap(): return lax.ppermute(value, axis, [(i, i ^ bit) for i in range(peers)])  16.1 us
    ppermute x4, starting transfers between devices, neighbours(): return (lax.ppermute(last, axis, up), lax.ppermute(first, axis, down))  10.3 us
    pallas_call x1, Pallas kernels, forward_call(): pl.pallas_call(functools.partial(_forward_kernel, planes=planes, depth=de...  8.32 us
    pallas_call x2, Pallas kernels, input_call(): pl.pallas_call(functools.partial(_input_kernel, planes=planes, first=firs...  6.09 us
    ppermute x8, waiting for transfers between devices, swap(): return lax.ppermute(value, axis, [(i, i ^ bit) for i in range(peers)])  4.49 us
    unnamed x28, local copies, waits for them, and re-layouts  3.74 us
    reshape x4, local copies, waits for them, and re-layouts, flat(): return value.transpose(1, 0, 2, 3).reshape(planes, value.shape[0], lanes)  2.41 us
    transpose x2, local copies, waits for them, and re-layouts, unflat(): value.reshape(planes, value.shape[1], rows, depth).transpose(1, 0, 2, 3)  1.71 us
  transfers between devices with their start and end apart: 12, of which 3 were waited for; matrix products, arithmetic and copies ran while one was open for 13% of the time, Pallas kernels for 10%

profile of v5, /device:TPU:0, one launch (start us, length us, event | category | flops | bytes accessed | tf_op | source)
XLA Modules:
  0.0 63.9 jit_solution(2591016905880217446)
XLA Ops:
  0.6 0.0 copy-start.10
  0.6 0.6 %copy-done.10 = bf16[8]{0:T(256)(128)(2,1)S(1)} copy-done((bf16[8]{0:T(256)(128)(2,1)S(1)}, bf16[8]{0:T(256)(128)(2,1)}, u32[]{:S(2)}) %copy-start.10) | copy-done | bytes 40
  1.3 0.1 copy.26
  1.4 0.7 %copy-done.9 = bf16[8,864]{1,0:T(8,128)(2,1)S(1)} copy-done((bf16[8,864]{1,0:T(8,128)(2,1)S(1)}, bf16[8,864]{1,0:T(8,128)(2,1)}, u32[]{:S(2)}) %copy-start.9) | copy-done | bytes 13848
  2.1 0.1 bitcast_dynamic-update-slice_fusion.3
  2.2 2.9 %collective-permute-start.2 = (bf16[8,865]{1,0:T(8,128)(2,1)S(1)}, bf16[8,865]{1,0:T(8,128)(2,1)S(1)}, u32[]{:S(2)}, u32[]{:S(2)}) collective-permute-start(bf16[8,865]{1,0:T(8,128)(2,1)S(1)} %get-tuple-element.71), channel_id=1, source_target_pairs={{0,8},{8,0},{16,24},{24,16},{1,9},{9,1},{17,25},{25,17},{2,10},{10... | collective-permute-start | bytes 41528 | tf_op jit(solution)/shard_map/ppermute | solution.py:126
  5.1 1.5 %collective-permute-start.3 = (bf16[8,865]{1,0:T(8,128)(2,1)S(1)}, bf16[8,865]{1,0:T(8,128)(2,1)S(1)}, u32[]{:S(2)}, u32[]{:S(2)}) collective-permute-start(bf16[8,865]{1,0:T(8,128)(2,1)S(1)} %get-tuple-element.71), channel_id=1, source_target_pairs={{0,16},{8,24},{16,0},{24,8},{1,17},{9,25},{17,1},{25,9},{2,18},{10... | collective-permute-start | bytes 41528 | tf_op jit(solution)/shard_map/ppermute | solution.py:126
  6.6 0.0 collective-permute-start.4
  6.7 1.1 %fusion.1 = (bf16[1,32,32,128]{3,2,0,1:T(8,128)(2,1)S(1)}, bf16[1,32,32,128]{3,2,0,1:T(8,128)(2,1)S(1)}) fusion(bf16[2,32,32,128]{3,2,0,1:T(8,128)(2,1)} %bitcast.61), kind=kLoop, calls=%fused_computation.18 | loop fusion | bytes 1048576 | tf_op jit(solution)/shard_map/slice | solution.py:194
  7.7 0.0 copy-start.1
  7.7 0.1 slice.31
  7.9 1.4 %collective-permute-start = (bf16[1,32,4096]{2,1,0:T(8,128)(2,1)S(1)}, bf16[1,32,4096]{2,1,0:T(8,128)(2,1)S(1)}, u32[]{:S(2)}, u32[]{:S(2)}) collective-permute-start(bf16[1,32,4096]{2,1,0:T(8,128)(2,1)S(1)} %slice.31), channel_id=1, source_target_pairs={{0,1},{1,2},{2,3},{3,4},{4,5},{5,6},{6,7},{8,9},{9,10},{10,11},{11... | collective-permute-start | bytes 786440 | tf_op jit(solution)/shard_map/ppermute | solution.py:121
  9.3 0.1 slice.33
  9.4 1.3 %collective-permute-start.1 = (bf16[1,32,4096]{2,1,0:T(8,128)(2,1)S(1)}, bf16[1,32,4096]{2,1,0:T(8,128)(2,1)S(1)}, u32[]{:S(2)}, u32[]{:S(2)}) collective-permute-start(bf16[1,32,4096]{2,1,0:T(8,128)(2,1)S(1)} %slice.33), channel_id=1, source_target_pairs={{1,0},{2,1},{3,2},{4,3},{5,4},{6,5},{7,6},{9,8},{10,9},{11,10},{12... | collective-permute-start | bytes 786440 | tf_op jit(solution)/shard_map/ppermute | solution.py:121
  10.8 0.1 reshape.54
  10.9 0.0 copy-start.5
  10.9 1.1 %copy.33.mid = bf16[2,32,4096]{2,1,0:T(8,128)(2,1)} copy(bf16[2,32,4096]{2,0,1:T(2,128)(2,1)S(1)} %reshape.54) | data formatting | bytes 1048576 | tf_op jit(solution)/shard_map/reshape | solution.py:188
  12.0 0.0 copy-done.5
  12.0 0.1 reshape.55
  12.2 1.1 %copy.34.cot = bf16[2,32,4096]{2,1,0:T(8,128)(2,1)} copy(bf16[2,32,4096]{2,0,1:T(2,128)(2,1)S(1)} %reshape.55) | data formatting | bytes 1048576 | tf_op jit(solution)/shard_map/reshape | solution.py:188
  13.2 0.0 collective-permute-done.2
  13.3 0.0 collective-permute-done.3
  13.3 0.0 collective-permute-done.4
  13.3 0.2 reshape.45
  13.5 0.1 copy.27
  13.6 0.8 %reshape.46.wall = bf16[288,96]{1,0:T(8,128)(2,1)} reshape(bf16[3,3,32,3,32]{4,3,2,1,0:T(4,128)(2,1)S(1)} %copy.27) | data formatting | bytes 110592 | tf_op jit(solution)/shard_map/reshape | solution.py:184
  14.4 0.7 %slice_convert_fusion.bias = f32[32,1]{1,0:T(8,128)} fusion(bf16[32,865]{1,0:T(8,128)(2,1)S(1)} %bitcast.68), kind=kLoop, calls=%fused_computation.13 | loop fusion | flops 32 | bytes 192 | tf_op jit(solution)/shard_map/convert_element_type | solution.py:196
  15.1 0.0 collective-permute-done.lo
  15.1 0.0 collective-permute-done.1.hi
  15.1 0.7 %copy-done.11 = bf16[1,32,4096]{2,1,0:T(8,128)(2,1)} copy-done((bf16[1,32,4096]{2,1,0:T(8,128)(2,1)}, bf16[1,32,4096]{2,1,0:T(8,128)(2,1)S(1)}, u32[]{:S(2)}) %copy-start.11) | copy-done | bytes 262168
  15.8 0.7 %copy-done.12 = bf16[1,32,4096]{2,1,0:T(8,128)(2,1)} copy-done((bf16[1,32,4096]{2,1,0:T(8,128)(2,1)}, bf16[1,32,4096]{2,1,0:T(8,128)(2,1)S(1)}, u32[]{:S(2)}) %copy-start.12) | copy-done | bytes 262168
  16.5 8.3 %shard_map.84 = (bf16[2,32,4096]{2,1,0:T(8,128)(2,1)}, bf16[2,32,4096]{2,1,0:T(8,128)(2,1)}, f32[288,96]{1,0:T(8,128)}, f32[32,1]{1,0:T(8,128)}) custom-call(bf16[1,32,4096]{2,1,0:T(8,128)(2,1)} %copy-done.11, bf16[2,32,4096]{2,1,0:T(8,128)(2,1)} %copy.33.mid, bf16[1,32,4096]{2,1,0:T(8,128)(2,1)} %copy-done.12, bf16[288,96]{1,0:T(8,128)(2,1)} %reshape.46.wall, ...), custom_call_target="tpu_custom_call" | custom-call | flops 905969664 | bytes 2621440 | tf_op jit(solution)/shard_map/pallas_call | solution.py:91
  24.9 1.1 %reshape.48 = f32[3,3,32,3,32]{4,3,2,1,0:T(4,128)S(1)} reshape(f32[288,96]{1,0:T(8,128)} %get-tuple-element.38) | data formatting | bytes 221184 | tf_op jit(solution)/shard_map/reshape | solution.py:199
  26.0 0.3 copy.29
  26.3 0.3 reshape.49
  26.6 0.8 %copy-done = bf16[2,32,4096]{2,1,0:T(8,128)(2,1)S(1)} copy-done((bf16[2,32,4096]{2,1,0:T(8,128)(2,1)S(1)}, bf16[2,32,4096]{2,1,0:T(8,128)(2,1)}, u32[]{:S(2)}) %copy-start) | copy-done | bytes 524312
  27.4 6.1 %collective-permute-start.5 = (bf16[1,32,4096]{2,1,0:T(8,128)(2,1)S(1)}, bf16[1,32,4096]{2,1,0:T(8,128)(2,1)S(1)}, u32[]{:S(2)}, u32[]{:S(2)}) collective-permute-start(bf16[1,32,4096]{2,1,0:T(8,128)(2,1)S(1)} %get-tuple-element.73), channel_id=1, source_target_pairs={{0,1},{1,2},{2,3},{3,4},{4,5},{5,6},{6,7},{8,9},{9,10},{10,11},{11... | collective-permute-start | bytes 786440 | tf_op jit(solution)/shard_map/ppermute | solution.py:121
  33.5 1.5 %collective-permute-start.6 = (bf16[1,32,4096]{2,1,0:T(8,128)(2,1)S(1)}, bf16[1,32,4096]{2,1,0:T(8,128)(2,1)S(1)}, u32[]{:S(2)}, u32[]{:S(2)}) collective-permute-start(bf16[1,32,4096]{2,1,0:T(8,128)(2,1)S(1)} %get-tuple-element.72), channel_id=1, source_target_pairs={{1,0},{2,1},{3,2},{4,3},{5,4},{6,5},{7,6},{9,8},{10,9},{11,10},{12... | collective-permute-start | bytes 786440 | tf_op jit(solution)/shard_map/ppermute | solution.py:121
  35.0 0.1 pad_maximum_fusion.1
  35.1 0.0 copy-done.6
  35.1 0.1 copy.35
  35.2 0.9 %copy_bitcast_fusion.1 = bf16[32,2,32,128]{3,2,1,0:T(8,128)(2,1)} fusion(bf16[2,32,32,128]{3,2,1,0:T(8,128)(2,1)S(1)} %bitcast.65), kind=kLoop, calls=%fused_computation.2 | loop fusion | bytes 1048576 | tf_op jit(solution)/shard_map/transpose | solution.py:191
  36.1 0.0 collective-permute-done.5.lo
  36.1 1.5 %collective-permute-done.6.hi = bf16[1,32,4096]{2,1,0:T(8,128)(2,1)S(1)} collective-permute-done((bf16[1,32,4096]{2,1,0:T(8,128)(2,1)S(1)}, bf16[1,32,4096]{2,1,0:T(8,128)(2,1)S(1)}, u32[]{:S(2)}, u32[]{:S(2)}) %collective-permute-start.6) | collective-permute-done | bytes 262176 | tf_op jit(solution)/shard_map/ppermute | solution.py:121
  37.5 0.2 reshape.51
  37.7 1.6 %collective-permute-start.7 = (f32[16,865]{1,0:T(8,128)S(1)}, f32[16,865]{1,0:T(8,128)S(1)}, u32[]{:S(2)}, u32[]{:S(2)}) collective-permute-start(f32[16,865]{1,0:T(8,128)S(1)} %constant_dynamic-slice_fusion.1), channel_id=1, source_target_pairs={{0,16},{8,24},{16,0},{24,8},{1,17},{9,25},{17,1},{25,9},{2,18},{10... | collective-permute-start | bytes 166088 | tf_op jit(solution)/shard_map/ppermute | solution.py:126
  39.3 0.1 reverse_bitcast_fusion
  39.4 0.3 copy.31
  39.7 0.8 %reshape.52.wall = bf16[288,96]{1,0:T(8,128)(2,1)} reshape(bf16[3,3,32,3,32]{4,3,2,1,0:T(4,128)(2,1)S(1)} %copy.31) | data formatting | bytes 110592 | tf_op jit(solution)/shard_map/reshape | solution.py:205
  40.5 3.0 %shard_map.85 = bf16[1,32,4096]{2,1,0:T(8,128)(2,1)} custom-call(bf16[1,32,4096]{2,1,0:T(8,128)(2,1)} %copy-done.2, bf16[2,32,4096]{2,1,0:T(8,128)(2,1)} %get-tuple-element.58.mid, bf16[1,32,4096]{2,1,0:T(8,128)(2,1)} %copy-done.3, bf16[288,96]{1,0:T(8,128)(2,1)} %reshape.52.wall, f32[9,1,4096]{2,1,0:T(1,128)} %constant.68.clone.mask), custom_call_target="tpu_custom_call" | custom-call | flops 226492416 | bytes 1572864 | tf_op jit(solution)/shard_map/pallas_call | solution.py:108
  43.5 0.0 collective-permute-done.7
  43.6 1.6 %collective-permute-start.8 = (f32[8,865]{1,0:T(8,128)S(1)}, f32[8,865]{1,0:T(8,128)S(1)}, u32[]{:S(2)}, u32[]{:S(2)}) collective-permute-start(f32[8,865]{1,0:T(8,128)S(1)} %constant_dynamic-slice_fusion), channel_id=1, source_target_pairs={{0,8},{8,0},{16,24},{24,16},{1,9},{9,1},{17,25},{25,17},{2,10},{10... | collective-permute-start | bytes 83048 | tf_op jit(solution)/shard_map/ppermute | solution.py:126
  45.1 3.1 %shard_map.86 = bf16[1,32,4096]{2,1,0:T(8,128)(2,1)} custom-call(bf16[1,32,4096]{2,1,0:T(8,128)(2,1)} %copy-done.2, bf16[2,32,4096]{2,1,0:T(8,128)(2,1)} %get-tuple-element.58.mid, bf16[1,32,4096]{2,1,0:T(8,128)(2,1)} %copy-done.3, bf16[288,96]{1,0:T(8,128)(2,1)} %reshape.52.wall, f32[9,1,4096]{2,1,0:T(1,128)} %constant.68.clone.mask), custom_call_target="tpu_custom_call" | custom-call | flops 226492416 | bytes 1572864 | tf_op jit(solution)/shard_map/pallas_call | solution.py:108
  48.2 0.0 collective-permute-done.8
  48.2 1.0 %pad_maximum_fusion = bf16[2,32,4096]{2,1,0:T(8,128)(2,1)S(1)} fusion(bf16[1,32,4096]{2,1,0:T(8,128)(2,1)} %shard_map.86, bf16[1,32,4096]{2,1,0:T(8,128)(2,1)S(1)} %copy-done.4), kind=kLoop, calls=%fused_computation | loop fusion | flops 262144 | bytes 1048576 | tf_op jit(solution)/shard_map/concatenate | solution.py:215
  49.2 0.1 copy.36
  49.3 4.3 %collective-permute-start.9 = (f32[8,865]{1,0:T(8,128)S(1)}, f32[8,865]{1,0:T(8,128)S(1)}, u32[]{:S(2)}, u32[]{:S(2)}) collective-permute-start(f32[8,865]{1,0:T(8,128)S(1)} %dynamic-slice_add_fusion.1), channel_id=1, source_target_pairs={{0,1},{1,0},{2,3},{3,2},{4,5},{5,4},{6,7},{7,6},{8,9},{9,8},{10,11... | collective-permute-start | bytes 83048 | tf_op jit(solution)/shard_map/ppermute | solution.py:126
  53.6 0.9 %copy_bitcast_fusion = bf16[32,2,32,128]{3,2,1,0:T(8,128)(2,1)} fusion(bf16[2,32,32,128]{3,2,1,0:T(8,128)(2,1)S(1)} %bitcast.63), kind=kLoop, calls=%fused_computation.1 | loop fusion | bytes 1048576 | tf_op jit(solution)/shard_map/transpose | solution.py:191
  54.5 0.0 collective-permute-done.9
  54.5 1.6 %collective-permute-start.10 = (f32[8,865]{1,0:T(8,128)S(1)}, f32[8,865]{1,0:T(8,128)S(1)}, u32[]{:S(2)}, u32[]{:S(2)}) collective-permute-start(f32[8,865]{1,0:T(8,128)S(1)} %add.61), channel_id=1, source_target_pairs={{0,2},{1,3},{2,0},{3,1},{4,6},{5,7},{6,4},{7,5},{8,10},{9,11},{10,... | collective-permute-start | bytes 83048 | tf_op jit(solution)/shard_map/ppermute | solution.py:126
  56.1 2.3 %collective-permute-done.10 = f32[8,865]{1,0:T(8,128)S(1)} collective-permute-done((f32[8,865]{1,0:T(8,128)S(1)}, f32[8,865]{1,0:T(8,128)S(1)}, u32[]{:S(2)}, u32[]{:S(2)}) %collective-permute-start.10) | collective-permute-done | bytes 27712 | tf_op jit(solution)/shard_map/ppermute | solution.py:126
  58.4 2.6 %collective-permute-start.11 = (f32[8,865]{1,0:T(8,128)S(1)}, f32[8,865]{1,0:T(8,128)S(1)}, u32[]{:S(2)}, u32[]{:S(2)}) collective-permute-start(f32[8,865]{1,0:T(8,128)S(1)} %add.62), channel_id=1, source_target_pairs={{0,4},{1,5},{2,6},{3,7},{4,0},{5,1},{6,2},{7,3},{8,12},{9,13},{10,... | collective-permute-start | bytes 83048 | tf_op jit(solution)/shard_map/ppermute | solution.py:126
  61.0 2.2 %collective-permute-done.11 = f32[8,865]{1,0:T(8,128)S(1)} collective-permute-done((f32[8,865]{1,0:T(8,128)S(1)}, f32[8,865]{1,0:T(8,128)S(1)}, u32[]{:S(2)}, u32[]{:S(2)}) %collective-permute-start.11) | collective-permute-done | bytes 27712 | tf_op jit(solution)/shard_map/ppermute | solution.py:126
  63.2 0.7 %slice_reduce_fusion = f32[8]{0:T(128)} fusion(f32[8,865]{1,0:T(8,128)S(1)} %add_multiply_fusion), kind=kLoop, calls=%fused_computation.14 | loop fusion | bytes 64 | tf_op jit(solution)/shard_map/slice | solution.py:222
  (28 shorter events, 0.2 us)
Async XLA Ops:
  0.6 0.7 %copy-start.10 = (bf16[8]{0:T(256)(128)(2,1)S(1)}, bf16[8]{0:T(256)(128)(2,1)}, u32[]{:S(2)}) copy-start(bf16[8]{0:T(256)(128)(2,1)} %param.8) | copy-start | bytes 52
  1.4 0.7 %copy-start.9 = (bf16[8,864]{1,0:T(8,128)(2,1)S(1)}, bf16[8,864]{1,0:T(8,128)(2,1)}, u32[]{:S(2)}) copy-start(bf16[8,864]{1,0:T(8,128)(2,1)} %param.7) | copy-start | bytes 41476
  2.2 11.1 %collective-permute-start.2 = (bf16[8,865]{1,0:T(8,128)(2,1)S(1)}, bf16[8,865]{1,0:T(8,128)(2,1)S(1)}, u32[]{:S(2)}, u32[]{:S(2)}) collective-permute-start(bf16[8,865]{1,0:T(8,128)(2,1)S(1)} %get-tuple-element.71), channel_id=1, source_target_pairs={{0,8},{8,0},{16,24},{24,16},{1,9},{9,1},{17,25},{25,17},{2,10},{10... | collective-permute-start | bytes 41528 | tf_op jit(solution)/shard_map/ppermute | solution.py:126
  5.1 8.1 %collective-permute-start.3 = (bf16[8,865]{1,0:T(8,128)(2,1)S(1)}, bf16[8,865]{1,0:T(8,128)(2,1)S(1)}, u32[]{:S(2)}, u32[]{:S(2)}) collective-permute-start(bf16[8,865]{1,0:T(8,128)(2,1)S(1)} %get-tuple-element.71), channel_id=1, source_target_pairs={{0,16},{8,24},{16,0},{24,8},{1,17},{9,25},{17,1},{25,9},{2,18},{10... | collective-permute-start | bytes 41528 | tf_op jit(solution)/shard_map/ppermute | solution.py:126
  6.6 6.6 %collective-permute-start.4 = (bf16[8,865]{1,0:T(8,128)(2,1)S(1)}, bf16[8,865]{1,0:T(8,128)(2,1)S(1)}, u32[]{:S(2)}, u32[]{:S(2)}) collective-permute-start(bf16[8,865]{1,0:T(8,128)(2,1)S(1)} %get-tuple-element.71), channel_id=1, source_target_pairs={{0,24},{8,16},{16,8},{24,0},{1,25},{9,17},{17,9},{25,1},{2,26},{10... | collective-permute-start | bytes 41528 | tf_op jit(solution)/shard_map/ppermute | solution.py:126
  7.7 3.0 %copy-start.1 = (bf16[1,32,2,32,128]{4,3,2,1,0:T(8,128)(2,1)S(1)}, bf16[1,32,2,32,128]{4,3,2,1,0:T(8,128)(2,1)}, u32[]{:S(2)}) copy-start(bf16[1,32,2,32,128]{4,3,2,1,0:T(8,128)(2,1)} %param.5) | copy-start | bytes 1572868
  7.9 7.3 %collective-permute-start = (bf16[1,32,4096]{2,1,0:T(8,128)(2,1)S(1)}, bf16[1,32,4096]{2,1,0:T(8,128)(2,1)S(1)}, u32[]{:S(2)}, u32[]{:S(2)}) collective-permute-start(bf16[1,32,4096]{2,1,0:T(8,128)(2,1)S(1)} %slice.31), channel_id=1, source_target_pairs={{0,1},{1,2},{2,3},{3,4},{4,5},{5,6},{6,7},{8,9},{9,10},{10,11},{11... | collective-permute-start | bytes 786440 | tf_op jit(solution)/shard_map/ppermute | solution.py:121
  9.4 5.7 %collective-permute-start.1 = (bf16[1,32,4096]{2,1,0:T(8,128)(2,1)S(1)}, bf16[1,32,4096]{2,1,0:T(8,128)(2,1)S(1)}, u32[]{:S(2)}, u32[]{:S(2)}) collective-permute-start(bf16[1,32,4096]{2,1,0:T(8,128)(2,1)S(1)} %slice.33), channel_id=1, source_target_pairs={{1,0},{2,1},{3,2},{4,3},{5,4},{6,5},{7,6},{9,8},{10,9},{11,10},{12... | collective-permute-start | bytes 786440 | tf_op jit(solution)/shard_map/ppermute | solution.py:121
  10.9 1.1 %copy-start.5 = (bf16[1,32,2,32,128]{4,3,2,1,0:T(8,128)(2,1)S(1)}, bf16[1,32,2,32,128]{4,3,2,1,0:T(8,128)(2,1)}, u32[]{:S(2)}) copy-start(bf16[1,32,2,32,128]{4,3,2,1,0:T(8,128)(2,1)} %param.6) | copy-start | bytes 1572868
  15.1 0.7 %copy-start.11 = (bf16[1,32,4096]{2,1,0:T(8,128)(2,1)}, bf16[1,32,4096]{2,1,0:T(8,128)(2,1)S(1)}, u32[]{:S(2)}) copy-start(bf16[1,32,4096]{2,1,0:T(8,128)(2,1)S(1)} %collective-permute-done.lo) | copy-start | bytes 786436
  15.8 0.7 %copy-start.12 = (bf16[1,32,4096]{2,1,0:T(8,128)(2,1)}, bf16[1,32,4096]{2,1,0:T(8,128)(2,1)S(1)}, u32[]{:S(2)}) copy-start(bf16[1,32,4096]{2,1,0:T(8,128)(2,1)S(1)} %collective-permute-done.1.hi) | copy-start | bytes 786436
  26.3 1.0 %copy-start = (bf16[2,32,4096]{2,1,0:T(8,128)(2,1)S(1)}, bf16[2,32,4096]{2,1,0:T(8,128)(2,1)}, u32[]{:S(2)}) copy-start(bf16[2,32,4096]{2,1,0:T(8,128)(2,1)} %get-tuple-element.58.mid) | copy-start | bytes 1572868
  27.4 7.6 %copy-start.8 = (f32[32,1]{1,0:T(8,128)S(1)}, f32[32,1]{1,0:T(8,128)}, u32[]{:S(2)}) copy-start(f32[32,1]{1,0:T(8,128)} %get-tuple-element.39) | copy-start | bytes 388
  27.4 7.7 %copy-start.6 = (bf16[2,32,4096]{2,1,0:T(8,128)(2,1)S(1)}, bf16[2,32,4096]{2,1,0:T(8,128)(2,1)}, u32[]{:S(2)}) copy-start(bf16[2,32,4096]{2,1,0:T(8,128)(2,1)} %get-tuple-element.40) | copy-start | bytes 1572868
  27.4 8.6 %collective-permute-start.5 = (bf16[1,32,4096]{2,1,0:T(8,128)(2,1)S(1)}, bf16[1,32,4096]{2,1,0:T(8,128)(2,1)S(1)}, u32[]{:S(2)}, u32[]{:S(2)}) collective-permute-start(bf16[1,32,4096]{2,1,0:T(8,128)(2,1)S(1)} %get-tuple-element.73), channel_id=1, source_target_pairs={{0,1},{1,2},{2,3},{3,4},{4,5},{5,6},{6,7},{8,9},{9,10},{10,11},{11... | collective-permute-start | bytes 786440 | tf_op jit(solution)/shard_map/ppermute | solution.py:121
  33.5 4.0 %collective-permute-start.6 = (bf16[1,32,4096]{2,1,0:T(8,128)(2,1)S(1)}, bf16[1,32,4096]{2,1,0:T(8,128)(2,1)S(1)}, u32[]{:S(2)}, u32[]{:S(2)}) collective-permute-start(bf16[1,32,4096]{2,1,0:T(8,128)(2,1)S(1)} %get-tuple-element.72), channel_id=1, source_target_pairs={{1,0},{2,1},{3,2},{4,3},{5,4},{6,5},{7,6},{9,8},{10,9},{11,10},{12... | collective-permute-start | bytes 786440 | tf_op jit(solution)/shard_map/ppermute | solution.py:121
  36.1 3.4 %copy-start.2 = (bf16[1,32,4096]{2,1,0:T(8,128)(2,1)}, bf16[1,32,4096]{2,1,0:T(8,128)(2,1)S(1)}, u32[]{:S(2)}) copy-start(bf16[1,32,4096]{2,1,0:T(8,128)(2,1)S(1)} %collective-permute-done.5.lo) | copy-start | bytes 786436
  37.5 1.9 %copy-start.3 = (bf16[1,32,4096]{2,1,0:T(8,128)(2,1)}, bf16[1,32,4096]{2,1,0:T(8,128)(2,1)S(1)}, u32[]{:S(2)}) copy-start(bf16[1,32,4096]{2,1,0:T(8,128)(2,1)S(1)} %collective-permute-done.6.hi) | copy-start | bytes 786436
  37.7 5.8 %collective-permute-start.7 = (f32[16,865]{1,0:T(8,128)S(1)}, f32[16,865]{1,0:T(8,128)S(1)}, u32[]{:S(2)}, u32[]{:S(2)}) collective-permute-start(f32[16,865]{1,0:T(8,128)S(1)} %constant_dynamic-slice_fusion.1), channel_id=1, source_target_pairs={{0,16},{8,24},{16,0},{24,8},{1,17},{9,25},{17,1},{25,9},{2,18},{10... | collective-permute-start | bytes 166088 | tf_op jit(solution)/shard_map/ppermute | solution.py:126
  43.6 4.6 %collective-permute-start.8 = (f32[8,865]{1,0:T(8,128)S(1)}, f32[8,865]{1,0:T(8,128)S(1)}, u32[]{:S(2)}, u32[]{:S(2)}) collective-permute-start(f32[8,865]{1,0:T(8,128)S(1)} %constant_dynamic-slice_fusion), channel_id=1, source_target_pairs={{0,8},{8,0},{16,24},{24,16},{1,9},{9,1},{17,25},{25,17},{2,10},{10... | collective-permute-start | bytes 83048 | tf_op jit(solution)/shard_map/ppermute | solution.py:126
  45.1 3.1 %copy-start.4 = (bf16[1,32,4096]{2,1,0:T(8,128)(2,1)S(1)}, bf16[1,32,4096]{2,1,0:T(8,128)(2,1)}, u32[]{:S(2)}) copy-start(bf16[1,32,4096]{2,1,0:T(8,128)(2,1)} %shard_map.85) | copy-start | bytes 786436
  49.3 5.1 %collective-permute-start.9 = (f32[8,865]{1,0:T(8,128)S(1)}, f32[8,865]{1,0:T(8,128)S(1)}, u32[]{:S(2)}, u32[]{:S(2)}) collective-permute-start(f32[8,865]{1,0:T(8,128)S(1)} %dynamic-slice_add_fusion.1), channel_id=1, source_target_pairs={{0,1},{1,0},{2,3},{3,2},{4,5},{5,4},{6,7},{7,6},{8,9},{9,8},{10,11... | collective-permute-start | bytes 83048 | tf_op jit(solution)/shard_map/ppermute | solution.py:126
  54.5 3.9 %collective-permute-start.10 = (f32[8,865]{1,0:T(8,128)S(1)}, f32[8,865]{1,0:T(8,128)S(1)}, u32[]{:S(2)}, u32[]{:S(2)}) collective-permute-start(f32[8,865]{1,0:T(8,128)S(1)} %add.61), channel_id=1, source_target_pairs={{0,2},{1,3},{2,0},{3,1},{4,6},{5,7},{6,4},{7,5},{8,10},{9,11},{10,... | collective-permute-start | bytes 83048 | tf_op jit(solution)/shard_map/ppermute | solution.py:126
  58.4 4.8 %collective-permute-start.11 = (f32[8,865]{1,0:T(8,128)S(1)}, f32[8,865]{1,0:T(8,128)S(1)}, u32[]{:S(2)}, u32[]{:S(2)}) collective-permute-start(f32[8,865]{1,0:T(8,128)S(1)} %add.62), channel_id=1, source_target_pairs={{0,4},{1,5},{2,6},{3,7},{4,0},{5,1},{6,2},{7,3},{8,12},{9,13},{10,... | collective-permute-start | bytes 83048 | tf_op jit(solution)/shard_map/ppermute | solution.py:126
  63.2 0.7 %copy-start.7 = (f32[8,865]{1,0:T(8,128)}, f32[8,865]{1,0:T(8,128)S(1)}, u32[]{:S(2)}) copy-start(f32[8,865]{1,0:T(8,128)S(1)} %add_multiply_fusion) | copy-start | bytes 83044

commit v6 on v3

--- a/solution.py
+++ b/solution.py
@@ -2,6 +2,7 @@
 
 import jax
 import jax.numpy as jnp
+import numpy as np
 from jax import lax
 from jax.experimental import pallas as pl
 from jax.experimental.pallas import tpu as pltpu
@@ -11,13 +12,17 @@
 
 
 def plane_masks(rows, depth):
-    y = jnp.arange(rows)[:, None]
-    z = jnp.arange(depth)[None, :]
+    y = np.arange(rows)[:, None]
+    z = np.arange(depth)[None, :]
     masks = [((y + b >= 0) & (y + b < rows) & (z + c >= 0) & (z + c < depth)) for b, c in OFFSETS]
-    return jnp.stack(masks).reshape(len(OFFSETS), 1, rows * depth).astype(jnp.float32)
-
-
-def _stacked(lo, mid, hi, h, planes):
+    return np.stack(masks).reshape(len(OFFSETS), 1, rows * depth).astype(np.float32)
+
+
+def _stacked(haloed, h):
+    return jnp.concatenate([haloed[h], haloed[h + 1], haloed[h + 2]], axis=0)
+
+
+def _stacked_parts(lo, mid, hi, h, planes):
     def plane(index):
         if index == 0:
             return lo[0]
@@ -39,24 +44,29 @@
     return total
 
 
-def _forward_kernel(lo, mid, hi, wall, bias, cot, mask, act_out, dpre_out, *, planes, depth):
-    chans, lanes = mid.shape[1], mid.shape[2]
+def _forward_kernel(haloed, wall, bias, cot, mask, act_out, dpre_out, first_out, last_out, *, planes, depth):
+    chans, lanes = haloed.shape[1], haloed.shape[2]
     for p in range(planes):
-        y = jnp.dot(wall[...], _stacked(lo, mid, hi, p, planes), preferred_element_type=jnp.float32)
+        y = jnp.dot(wall[...], _stacked(haloed, p), preferred_element_type=jnp.float32)
         pre = _shifted_sum(y, mask, chans, lanes, depth, 1) + bias[...]
         sig = 1.0 / (1.0 + jnp.exp(-pre))
         act_out[p] = (pre * sig).astype(act_out.dtype)
-        dpre_out[p] = (cot[p].astype(jnp.float32) * sig * (1.0 + pre * (1.0 - sig))).astype(dpre_out.dtype)
+        dpre = (cot[p].astype(jnp.float32) * sig * (1.0 + pre * (1.0 - sig))).astype(dpre_out.dtype)
+        dpre_out[p] = dpre
+        if p == 0:
+            first_out[0] = dpre
+        if p == planes - 1:
+            last_out[0] = dpre
 
 
 def _input_kernel(lo, mid, hi, wall, mask, out, *, planes, first, depth):
     chans, lanes = mid.shape[1], mid.shape[2]
     for n in range(out.shape[0]):
-        y = jnp.dot(wall[...], _stacked(lo, mid, hi, first + n, planes), preferred_element_type=jnp.float32)
+        y = jnp.dot(wall[...], _stacked_parts(lo, mid, hi, first + n, planes), preferred_element_type=jnp.float32)
         out[n] = _shifted_sum(y, mask, chans, lanes, depth, -1).astype(out.dtype)
 
 
-def _weight_kernel(lo, mid, hi, dpre, mask, gw_out, gb_out, *, planes, depth):
+def _weight_kernel(haloed, dpre, mask, gw_out, gb_out, *, planes, depth):
     chans, lanes = dpre.shape[1], dpre.shape[2]
     gw = jnp.zeros(gw_out.shape, jnp.float32)
     gb = jnp.zeros(gb_out.shape, jnp.float32)
@@ -71,7 +81,7 @@
                 e = pltpu.roll(jnp.where(mask[k] > 0.5, d, 0.0), off % lanes, 1)
             parts.append(e.astype(jnp.bfloat16))
         gw = gw + lax.dot_general(
-            jnp.concatenate(parts, axis=0), _stacked(lo, mid, hi, p, planes),
+            jnp.concatenate(parts, axis=0), _stacked(haloed, p),
             (((1,), (1,)), ((), ())), preferred_element_type=jnp.float32,
         )
     gw_out[...] = gw
@@ -82,17 +92,18 @@
     return [pl.BlockSpec(memory_space=pltpu.VMEM)] * n
 
 
-def forward_call(lo, mid, hi, wall, bias, cot, mask, depth):
-    planes, chans, lanes = mid.shape
-    shape = jax.ShapeDtypeStruct(mid.shape, jnp.bfloat16)
+def forward_call(haloed, wall, bias, cot, mask, depth):
+    planes, chans, lanes = cot.shape
+    shape = jax.ShapeDtypeStruct(cot.shape, jnp.bfloat16)
+    edge = jax.ShapeDtypeStruct((1, chans, lanes), jnp.bfloat16)
     flops = 2 * planes * wall.shape[0] * wall.shape[1] * lanes
     return pl.pallas_call(
         functools.partial(_forward_kernel, planes=planes, depth=depth),
-        out_shape=(shape, shape),
-        in_specs=_vmem(7),
-        out_specs=tuple(_vmem(2)),
-        cost_estimate=pl.CostEstimate(flops=flops, transcendentals=planes * chans * lanes, bytes_accessed=5 * mid.size * 2),
-    )(lo, mid, hi, wall, bias, cot, mask)
+        out_shape=(shape, shape, edge, edge),
+        in_specs=_vmem(5),
+        out_specs=tuple(_vmem(4)),
+        cost_estimate=pl.CostEstimate(flops=flops, transcendentals=planes * chans * lanes, bytes_accessed=5 * cot.size * 2),
+    )(haloed, wall, bias, cot, mask)
 
 
 def input_call(lo, mid, hi, wall, mask, depth, first, count):
@@ -107,16 +118,16 @@
     )(lo, mid, hi, wall, mask)
 
 
-def weight_call(lo, mid, hi, dpre, mask, depth):
-    planes, chans, lanes = mid.shape
+def weight_call(haloed, dpre, mask, depth):
+    planes, chans, lanes = dpre.shape
     flops = 2 * planes * 9 * chans * 3 * chans * lanes
     return pl.pallas_call(
         functools.partial(_weight_kernel, planes=planes, depth=depth),
         out_shape=(jax.ShapeDtypeStruct((9 * chans, 3 * chans), jnp.float32), jax.ShapeDtypeStruct((chans, 1), jnp.float32)),
-        in_specs=_vmem(5),
+        in_specs=_vmem(3),
         out_specs=tuple(_vmem(2)),
-        cost_estimate=pl.CostEstimate(flops=flops, transcendentals=0, bytes_accessed=3 * mid.size * 2),
-    )(lo, mid, hi, dpre, mask)
+        cost_estimate=pl.CostEstimate(flops=flops, transcendentals=0, bytes_accessed=3 * dpre.size * 2),
+    )(haloed, dpre, mask)
 
 
 def neighbours(first, last, axis):
@@ -187,7 +198,7 @@
     w5 = whole_weight.reshape(out_chan, 3, 3, 3, chans)
     forward_w = w5.transpose(2, 3, 0, 1, 4).reshape(9 * out_chan, 3 * chans)
     backward_w = w5[:, ::-1].transpose(2, 3, 4, 1, 0).reshape(9 * chans, 3 * out_chan)
-    mask = plane_masks(rows, depth)
+    mask = jnp.asarray(plane_masks(rows, depth))
 
     def flat(value):
         return value.transpose(1, 0, 2, 3).reshape(planes, value.shape[0], lanes)
@@ -195,13 +206,14 @@
     def unflat(value):
         return value.reshape(planes, value.shape[1], rows, depth).transpose(1, 0, 2, 3)
 
-    mid = flat(field)
-    lo, hi = neighbours(mid[:1], mid[planes - 1 :], "strike")
-    act, dpre = forward_call(
-        lo, mid, hi, forward_w, whole_bias.astype(jnp.float32)[:, None], flat(cotangent[0]), mask, depth
+    below, above = neighbours(field[:, :1], field[:, planes - 1 :], "strike")
+    haloed = jnp.concatenate([below, field, above], axis=1)
+    haloed = haloed.transpose(1, 0, 2, 3).reshape(planes + 2, chans, lanes)
+    act, dpre, first, last = forward_call(
+        haloed, forward_w, whole_bias.astype(jnp.float32)[:, None], flat(cotangent[0]), mask, depth
     )
-    dlo, dhi = neighbours(dpre[:1], dpre[planes - 1 :], "strike")
-    g, gb = weight_call(lo, mid, hi, dpre, mask, depth)
+    dlo, dhi = neighbours(first, last, "strike")
+    g, gb = weight_call(haloed, dpre, mask, depth)
     local_weight = g.reshape(3, 3, out_chan, 3, chans).transpose(2, 3, 0, 1, 4).reshape(out_chan, 27 * chans)
     local_grads = jnp.concatenate([local_weight, gb], axis=1)
     work = [

time: 59.8 us -> 57.7 us (0.965)
  local copies, waits for them, and re-layouts: 15.2 us -> 12.2 us
  waiting for transfers between devices: 3.51 us -> 4.47 us
  other arithmetic: 2.04 us -> 1.11 us
  starting transfers between devices: 23 us -> 23.7 us
    reshape x0 -> x2, local copies, waits for them, and re-layouts: none -> 1.86 us  [local(): haloed = haloed.transpose(1, 0, 2, 3).reshape(planes + 2, chans, lanes)]
    unnamed x34 -> x24, local copies, waits for them, and re-layouts: 3.59 us -> 2 us
    slice x4 -> x1, local copies, waits for them, and re-layouts: 2.36 us -> 1.13 us  [local(): below, above = neighbours(field[:, :1], field[:, planes - 1:], 'strike')]
    reshape x4 -> x2, local copies, waits for them, and re-layouts: 2.41 us -> 1.21 us  [flat(): return value.transpose(1, 0, 2, 3).reshape(planes, value.shape[0], lanes)]
    ppermute x4, waiting for transfers between devices: 0.01 us -> 1.19 us  [neighbours(): return (lax.ppermute(last, axis, up), lax.ppermute(first, axis, down))]
    broadcast_in_dim x1 -> x0, local copies, waits for them, and re-layouts: 0.86 us -> none  [local(): unflat(act)[None]]
    convert_element_type x1 -> x0, other arithmetic: 0.8 us -> none  [plane_masks(): jnp.stack(masks).reshape(len(OFFSETS), 1, rows * depth).astype(jnp.float32)]
    ppermute x4, starting transfers between devices: 9.93 us -> 10.6 us  [neighbours(): return (lax.ppermute(last, axis, up), lax.ppermute(first, axis, down))]
  transfers between devices with their start and end apart: 12 -> 12, of which waited for: 2 -> 5; matrix products, arithmetic and copies ran while one was open for 20% -> 15% of each run, Pallas kernels for 17% -> 17%
where the time goes in v6:
time: 57.7 us; the launch traced here: 57.2 us
  starting transfers between devices  23.7 us (41%)
  Pallas kernels  14.8 us (26%)
  local copies, waits for them, and re-layouts  12.2 us (21%)
  waiting for transfers between devices  4.47 us (8%)
  other arithmetic  1.11 us (2%)
  between operations  0.9 us (2%)
    ppermute x8, starting transfers between devices, swap(): return lax.ppermute(value, axis, [(i, i ^ bit) for i in range(peers)])  13.2 us
    ppermute x4, starting transfers between devices, neighbours(): return (lax.ppermute(last, axis, up), lax.ppermute(first, axis, down))  10.6 us
    pallas_call x2, Pallas kernels, input_call(): pl.pallas_call(functools.partial(_input_kernel, planes=planes, first=firs...  6.09 us
    pallas_call x1, Pallas kernels, forward_call(): pl.pallas_call(functools.partial(_forward_kernel, planes=planes, depth=de...  5.04 us
    pallas_call x1, Pallas kernels, weight_call(): pl.pallas_call(functools.partial(_weight_kernel, planes=planes, depth=dep...  3.69 us
    ppermute x8, waiting for transfers between devices, swap(): return lax.ppermute(value, axis, [(i, i ^ bit) for i in range(peers)])  3.28 us
    unnamed x24, local copies, waits for them, and re-layouts  2 us
    reshape x2, local copies, waits for them, and re-layouts, local(): haloed = haloed.transpose(1, 0, 2, 3).reshape(planes + 2, chans, lanes)  1.86 us
  transfers between devices with their start and end apart: 12, of which 5 were waited for; matrix products, arithmetic and copies ran while one was open for 15% of the time, Pallas kernels for 17%

profile of v6, /device:TPU:0, one launch (start us, length us, event | category | flops | bytes accessed | tf_op | source)
XLA Modules:
  0.0 57.2 jit_solution(10782373879287049482)
XLA Ops:
  0.6 0.0 copy-start.10
  0.6 0.6 %copy-done.10 = bf16[8]{0:T(256)(128)(2,1)S(1)} copy-done((bf16[8]{0:T(256)(128)(2,1)S(1)}, bf16[8]{0:T(256)(128)(2,1)}, u32[]{:S(2)}) %copy-start.10) | copy-done | bytes 40
  1.3 0.1 copy.26
  1.4 0.7 %copy-done.9 = bf16[8,864]{1,0:T(8,128)(2,1)S(1)} copy-done((bf16[8,864]{1,0:T(8,128)(2,1)S(1)}, bf16[8,864]{1,0:T(8,128)(2,1)}, u32[]{:S(2)}) %copy-start.9) | copy-done | bytes 13848
  2.1 0.1 bitcast_dynamic-update-slice_fusion.3
  2.2 3.0 %collective-permute-start.3 = (bf16[8,865]{1,0:T(8,128)(2,1)S(1)}, bf16[8,865]{1,0:T(8,128)(2,1)S(1)}, u32[]{:S(2)}, u32[]{:S(2)}) collective-permute-start(bf16[8,865]{1,0:T(8,128)(2,1)S(1)} %get-tuple-element.49), channel_id=1, source_target_pairs={{0,16},{8,24},{16,0},{24,8},{1,17},{9,25},{17,1},{25,9},{2,18},{10... | collective-permute-start | bytes 41528 | tf_op jit(solution)/shard_map/ppermute | solution.py:142
  5.1 1.5 %collective-permute-start.2 = (bf16[8,865]{1,0:T(8,128)(2,1)S(1)}, bf16[8,865]{1,0:T(8,128)(2,1)S(1)}, u32[]{:S(2)}, u32[]{:S(2)}) collective-permute-start(bf16[8,865]{1,0:T(8,128)(2,1)S(1)} %get-tuple-element.49), channel_id=1, source_target_pairs={{0,8},{8,0},{16,24},{24,16},{1,9},{9,1},{17,25},{25,17},{2,10},{10... | collective-permute-start | bytes 41528 | tf_op jit(solution)/shard_map/ppermute | solution.py:142
  6.6 0.0 collective-permute-start.4
  6.7 1.1 %fusion.3 = (bf16[32,1,32,128]{3,2,1,0:T(8,128)(2,1)S(1)}, bf16[32,1,32,128]{3,2,1,0:T(8,128)(2,1)S(1)}) fusion(bf16[32,2,32,128]{3,2,1,0:T(8,128)(2,1)} %bitcast.57), kind=kLoop, calls=%fused_computation.22 | loop fusion | bytes 1048576 | tf_op jit(solution)/shard_map/slice | solution.py:209
  7.8 1.3 %collective-permute-start = (bf16[32,1,32,128]{3,2,1,0:T(8,128)(2,1)S(1)}, bf16[32,1,32,128]{3,2,1,0:T(8,128)(2,1)S(1)}, u32[]{:S(2)}, u32[]{:S(2)}) collective-permute-start(bf16[32,1,32,128]{3,2,1,0:T(8,128)(2,1)S(1)} %get-tuple-element.50), channel_id=1, source_target_pairs={{0,1},{1,2},{2,3},{3,4},{4,5},{5,6},{6,7},{8,9},{9,10},{10,11},{11... | collective-permute-start | bytes 786440 | tf_op jit(solution)/shard_map/ppermute | solution.py:137
  9.1 1.3 %collective-permute-start.1 = (bf16[32,1,32,128]{3,2,1,0:T(8,128)(2,1)S(1)}, bf16[32,1,32,128]{3,2,1,0:T(8,128)(2,1)S(1)}, u32[]{:S(2)}, u32[]{:S(2)}) collective-permute-start(bf16[32,1,32,128]{3,2,1,0:T(8,128)(2,1)S(1)} %get-tuple-element.51), channel_id=1, source_target_pairs={{1,0},{2,1},{3,2},{4,3},{5,4},{6,5},{7,6},{9,8},{10,9},{11,10},{12... | collective-permute-start | bytes 786440 | tf_op jit(solution)/shard_map/ppermute | solution.py:137
  10.5 0.0 copy-done.5
  10.5 0.1 reshape.49
  10.6 1.1 %copy.34.cot = bf16[2,32,4096]{2,1,0:T(8,128)(2,1)} copy(bf16[2,32,4096]{2,0,1:T(2,128)(2,1)S(1)} %reshape.49) | data formatting | bytes 1048576 | tf_op jit(solution)/shard_map/reshape | solution.py:204
  11.7 0.0 collective-permute-done.2
  11.7 0.0 collective-permute-done.3
  11.7 0.0 collective-permute-done.4
  11.8 0.2 reshape.40
  12.0 0.0 copy-start
  12.0 0.1 copy.27
  12.1 0.8 %reshape.41.wall = bf16[288,96]{1,0:T(8,128)(2,1)} reshape(bf16[3,3,32,3,32]{4,3,2,1,0:T(4,128)(2,1)S(1)} %copy.27) | data formatting | bytes 110592 | tf_op jit(solution)/shard_map/reshape | solution.py:199
  12.9 0.7 %slice_convert_fusion.bias = f32[32,1]{1,0:T(8,128)} fusion(bf16[32,865]{1,0:T(8,128)(2,1)S(1)} %bitcast.64), kind=kLoop, calls=%fused_computation.19 | loop fusion | flops 32 | bytes 192 | tf_op jit(solution)/shard_map/convert_element_type | solution.py:213
  13.6 0.0 collective-permute-done
  13.6 1.2 %collective-permute-done.1 = bf16[32,1,32,128]{3,2,1,0:T(8,128)(2,1)S(1)} collective-permute-done((bf16[32,1,32,128]{3,2,1,0:T(8,128)(2,1)S(1)}, bf16[32,1,32,128]{3,2,1,0:T(8,128)(2,1)S(1)}, u32[]{:S(2)}, u32[]{:S(2)}) %collective-permute-start.1) | collective-permute-done | bytes 262176 | tf_op jit(solution)/shard_map/ppermute | solution.py:137
  14.8 0.0 copy-done
  14.8 0.1 maximum_bitcast_fusion
  14.9 0.3 reshape.48
  15.2 1.6 %copy.33.haloed = bf16[4,32,4096]{2,1,0:T(8,128)(2,1)} copy(bf16[4,32,4096]{2,0,1:T(4,128)(2,1)S(1)} %reshape.48) | data formatting | bytes 2097152 | tf_op jit(solution)/shard_map/reshape | solution.py:211
  16.8 5.0 %shard_map.84 = (bf16[2,32,4096]{2,1,0:T(8,128)(2,1)}, bf16[2,32,4096]{2,1,0:T(8,128)(2,1)}, bf16[1,32,4096]{2,1,0:T(8,128)(2,1)}, bf16[1,32,4096]{2,1,0:T(8,128)(2,1)}) custom-call(bf16[4,32,4096]{2,1,0:T(8,128)(2,1)} %copy.33.haloed, bf16[288,96]{1,0:T(8,128)(2,1)} %reshape.41.wall, f32[32,1]{1,0:T(8,128)} %slice_convert_fusion.bias, ...), custom_call_target="tpu_custom_call" | custom-call | flops 452984832 | bytes 2621440 | tf_op jit(solution)/shard_map/pallas_call | solution.py:100
  21.8 6.7 %collective-permute-start.5 = (bf16[1,32,4096]{2,1,0:T(8,128)(2,1)}, bf16[1,32,4096]{2,1,0:T(8,128)(2,1)S(1)}, u32[]{:S(2)}, u32[]{:S(2)}) collective-permute-start(bf16[1,32,4096]{2,1,0:T(8,128)(2,1)} %get-tuple-element.30), channel_id=1, source_target_pairs={{0,1},{1,2},{2,3},{3,4},{4,5},{5,6},{6,7},{8,9},{9,10},{10,11},{11... | collective-permute-start | bytes 786440 | tf_op jit(solution)/shard_map/ppermute | solution.py:137
  28.5 1.3 %collective-permute-start.6 = (bf16[1,32,4096]{2,1,0:T(8,128)(2,1)}, bf16[1,32,4096]{2,1,0:T(8,128)(2,1)S(1)}, u32[]{:S(2)}, u32[]{:S(2)}) collective-permute-start(bf16[1,32,4096]{2,1,0:T(8,128)(2,1)} %get-tuple-element.31), channel_id=1, source_target_pairs={{1,0},{2,1},{3,2},{4,3},{5,4},{6,5},{7,6},{9,8},{10,9},{11,10},{12... | collective-permute-start | bytes 786440 | tf_op jit(solution)/shard_map/ppermute | solution.py:137
  29.8 0.1 reverse_bitcast_fusion
  29.9 0.3 copy.31
  30.2 0.8 %reshape.46.wall = bf16[288,96]{1,0:T(8,128)(2,1)} reshape(bf16[3,3,32,3,32]{4,3,2,1,0:T(4,128)(2,1)S(1)} %copy.31) | data formatting | bytes 110592 | tf_op jit(solution)/shard_map/reshape | solution.py:200
  31.0 3.7 %shard_map.85 = (f32[288,96]{1,0:T(8,128)}, f32[32,1]{1,0:T(8,128)}) custom-call(bf16[4,32,4096]{2,1,0:T(8,128)(2,1)} %copy.33.haloed, bf16[2,32,4096]{2,1,0:T(8,128)(2,1)} %get-tuple-element.42.dpre.mid, f32[9,1,4096]{2,1,0:T(1,128)} %constant.68.clone.mask), custom_call_target="tpu_custom_call" | custom-call | flops 452984832 | bytes 1572864 | tf_op jit(solution)/shard_map/pallas_call | solution.py:124
  34.7 1.1 %reshape.44 = f32[3,3,32,3,32]{4,3,2,1,0:T(4,128)S(1)} reshape(f32[288,96]{1,0:T(8,128)} %get-tuple-element.28) | data formatting | bytes 221184 | tf_op jit(solution)/shard_map/reshape | solution.py:217
  35.9 0.3 copy.30
  36.2 0.0 copy-start.7
  36.2 0.3 reshape.45
  36.5 0.4 copy-done.7
  36.9 0.1 fusion.2
  37.0 0.0 collective-permute-done.5.lo
  37.0 0.0 collective-permute-done.6.hi
  37.0 0.0 copy-start.2
  37.0 1.6 %collective-permute-start.7 = (f32[16,865]{1,0:T(8,128)S(1)}, f32[16,865]{1,0:T(8,128)S(1)}, u32[]{:S(2)}, u32[]{:S(2)}) collective-permute-start(f32[16,865]{1,0:T(8,128)S(1)} %fusion.2), channel_id=1, source_target_pairs={{0,16},{8,24},{16,0},{24,8},{1,17},{9,25},{17,1},{25,9},{2,18},{10... | collective-permute-start | bytes 166088 | tf_op jit(solution)/shard_map/ppermute | solution.py:142
  38.6 0.0 copy-done.1
  38.6 3.0 %shard_map.86 = bf16[1,32,4096]{2,1,0:T(8,128)(2,1)} custom-call(bf16[1,32,4096]{2,1,0:T(8,128)(2,1)} %copy-done.1, bf16[2,32,4096]{2,1,0:T(8,128)(2,1)} %get-tuple-element.42.dpre.mid, bf16[1,32,4096]{2,1,0:T(8,128)(2,1)} %copy-done.2, bf16[288,96]{1,0:T(8,128)(2,1)} %reshape.46.wall, f32[9,1,4096]{2,1,0:T(1,128)} %constant.68.clone.mask), custom_call_target="tpu_custom_call" | custom-call | flops 226492416 | bytes 1572864 | tf_op jit(solution)/shard_map/pallas_call | solution.py:112
  41.6 0.1 collective-permute-done.7
  41.7 0.1 fusion.1
  41.8 1.5 %collective-permute-start.8 = (f32[8,865]{1,0:T(8,128)S(1)}, f32[8,865]{1,0:T(8,128)S(1)}, u32[]{:S(2)}, u32[]{:S(2)}) collective-permute-start(f32[8,865]{1,0:T(8,128)S(1)} %constant_dynamic-slice_fusion), channel_id=1, source_target_pairs={{0,8},{8,0},{16,24},{24,16},{1,9},{9,1},{17,25},{25,17},{2,10},{10... | collective-permute-start | bytes 83048 | tf_op jit(solution)/shard_map/ppermute | solution.py:142
  43.3 3.1 %shard_map.87 = bf16[1,32,4096]{2,1,0:T(8,128)(2,1)} custom-call(bf16[1,32,4096]{2,1,0:T(8,128)(2,1)} %copy-done.1, bf16[2,32,4096]{2,1,0:T(8,128)(2,1)} %get-tuple-element.42.dpre.mid, bf16[1,32,4096]{2,1,0:T(8,128)(2,1)} %copy-done.2, bf16[288,96]{1,0:T(8,128)(2,1)} %reshape.46.wall, f32[9,1,4096]{2,1,0:T(1,128)} %constant.68.clone.mask), custom_call_target="tpu_custom_call" | custom-call | flops 226492416 | bytes 1572864 | tf_op jit(solution)/shard_map/pallas_call | solution.py:112
  46.4 0.0 collective-permute-done.8
  46.4 0.5 collective-permute-start.9
  46.9 0.0 copy-done.6
  46.9 0.1 copy.35
  47.0 0.8 %collective-permute-done.9 = f32[8,865]{1,0:T(8,128)S(1)} collective-permute-done((f32[8,865]{1,0:T(8,128)S(1)}, f32[8,865]{1,0:T(8,128)S(1)}, u32[]{:S(2)}, u32[]{:S(2)}) %collective-permute-start.9) | collective-permute-done | bytes 27712 | tf_op jit(solution)/shard_map/ppermute | solution.py:142
  47.8 2.0 %collective-permute-start.10 = (f32[8,865]{1,0:T(8,128)S(1)}, f32[8,865]{1,0:T(8,128)S(1)}, u32[]{:S(2)}, u32[]{:S(2)}) collective-permute-start(f32[8,865]{1,0:T(8,128)S(1)} %add.61), channel_id=1, source_target_pairs={{0,2},{1,3},{2,0},{3,1},{4,6},{5,7},{6,4},{7,5},{8,10},{9,11},{10,... | collective-permute-start | bytes 83048 | tf_op jit(solution)/shard_map/ppermute | solution.py:142
  49.8 0.1 pad_maximum_fusion
  49.9 0.1 copy.36
  50.0 1.7 %collective-permute-done.10 = f32[8,865]{1,0:T(8,128)S(1)} collective-permute-done((f32[8,865]{1,0:T(8,128)S(1)}, f32[8,865]{1,0:T(8,128)S(1)}, u32[]{:S(2)}, u32[]{:S(2)}) %collective-permute-start.10) | collective-permute-done | bytes 27712 | tf_op jit(solution)/shard_map/ppermute | solution.py:142
  51.7 3.0 %collective-permute-start.11 = (f32[8,865]{1,0:T(8,128)S(1)}, f32[8,865]{1,0:T(8,128)S(1)}, u32[]{:S(2)}, u32[]{:S(2)}) collective-permute-start(f32[8,865]{1,0:T(8,128)S(1)} %add.62), channel_id=1, source_target_pairs={{0,4},{1,5},{2,6},{3,7},{4,0},{5,1},{6,2},{7,3},{8,12},{9,13},{10,... | collective-permute-start | bytes 83048 | tf_op jit(solution)/shard_map/ppermute | solution.py:142
  54.7 1.1 %copy_bitcast_fusion = (bf16[1,32,2,32,128]{4,3,2,1,0:T(8,128)(2,1)}, bf16[1,32,2,32,128]{4,3,2,1,0:T(8,128)(2,1)}) fusion(bf16[2,32,32,128]{3,2,1,0:T(8,128)(2,1)S(1)} %bitcast.59, bf16[2,32,32,128]{3,2,1,0:T(8,128)(2,1)S(1)} %bitcast.60), kind=kLoop, calls=%fused_computation.2 | loop fusion | bytes 2097152 | tf_op jit(solution)/shard_map/broadcast_in_dim | solution.py:228
  55.8 0.7 %collective-permute-done.11 = f32[8,865]{1,0:T(8,128)S(1)} collective-permute-done((f32[8,865]{1,0:T(8,128)S(1)}, f32[8,865]{1,0:T(8,128)S(1)}, u32[]{:S(2)}, u32[]{:S(2)}) %collective-permute-start.11) | collective-permute-done | bytes 27712 | tf_op jit(solution)/shard_map/ppermute | solution.py:142
  56.6 0.7 %slice_reduce_fusion = f32[8]{0:T(128)} fusion(f32[8,865]{1,0:T(8,128)S(1)} %add_multiply_fusion), kind=kLoop, calls=%fused_computation.20 | loop fusion | bytes 64 | tf_op jit(solution)/shard_map/slice | solution.py:228
  (20 shorter events, 0.1 us)
Async XLA Ops:
  0.6 0.7 %copy-start.10 = (bf16[8]{0:T(256)(128)(2,1)S(1)}, bf16[8]{0:T(256)(128)(2,1)}, u32[]{:S(2)}) copy-start(bf16[8]{0:T(256)(128)(2,1)} %param.8) | copy-start | bytes 52
  1.4 0.7 %copy-start.9 = (bf16[8,864]{1,0:T(8,128)(2,1)S(1)}, bf16[8,864]{1,0:T(8,128)(2,1)}, u32[]{:S(2)}) copy-start(bf16[8,864]{1,0:T(8,128)(2,1)} %param.7) | copy-start | bytes 41476
  2.2 9.5 %collective-permute-start.3 = (bf16[8,865]{1,0:T(8,128)(2,1)S(1)}, bf16[8,865]{1,0:T(8,128)(2,1)S(1)}, u32[]{:S(2)}, u32[]{:S(2)}) collective-permute-start(bf16[8,865]{1,0:T(8,128)(2,1)S(1)} %get-tuple-element.49), channel_id=1, source_target_pairs={{0,16},{8,24},{16,0},{24,8},{1,17},{9,25},{17,1},{25,9},{2,18},{10... | collective-permute-start | bytes 41528 | tf_op jit(solution)/shard_map/ppermute | solution.py:142
  5.1 6.6 %collective-permute-start.2 = (bf16[8,865]{1,0:T(8,128)(2,1)S(1)}, bf16[8,865]{1,0:T(8,128)(2,1)S(1)}, u32[]{:S(2)}, u32[]{:S(2)}) collective-permute-start(bf16[8,865]{1,0:T(8,128)(2,1)S(1)} %get-tuple-element.49), channel_id=1, source_target_pairs={{0,8},{8,0},{16,24},{24,16},{1,9},{9,1},{17,25},{25,17},{2,10},{10... | collective-permute-start | bytes 41528 | tf_op jit(solution)/shard_map/ppermute | solution.py:142
  6.6 5.1 %collective-permute-start.4 = (bf16[8,865]{1,0:T(8,128)(2,1)S(1)}, bf16[8,865]{1,0:T(8,128)(2,1)S(1)}, u32[]{:S(2)}, u32[]{:S(2)}) collective-permute-start(bf16[8,865]{1,0:T(8,128)(2,1)S(1)} %get-tuple-element.49), channel_id=1, source_target_pairs={{0,24},{8,16},{16,8},{24,0},{1,25},{9,17},{17,9},{25,1},{2,26},{10... | collective-permute-start | bytes 41528 | tf_op jit(solution)/shard_map/ppermute | solution.py:142
  6.7 3.8 %copy-start.5 = (bf16[1,32,2,32,128]{4,3,2,1,0:T(8,128)(2,1)S(1)}, bf16[1,32,2,32,128]{4,3,2,1,0:T(8,128)(2,1)}, u32[]{:S(2)}) copy-start(bf16[1,32,2,32,128]{4,3,2,1,0:T(8,128)(2,1)} %param.6) | copy-start | bytes 1572868
  7.8 5.8 %collective-permute-start = (bf16[32,1,32,128]{3,2,1,0:T(8,128)(2,1)S(1)}, bf16[32,1,32,128]{3,2,1,0:T(8,128)(2,1)S(1)}, u32[]{:S(2)}, u32[]{:S(2)}) collective-permute-start(bf16[32,1,32,128]{3,2,1,0:T(8,128)(2,1)S(1)} %get-tuple-element.50), channel_id=1, source_target_pairs={{0,1},{1,2},{2,3},{3,4},{4,5},{5,6},{6,7},{8,9},{9,10},{10,11},{11... | collective-permute-start | bytes 786440 | tf_op jit(solution)/shard_map/ppermute | solution.py:137
  9.1 5.7 %collective-permute-start.1 = (bf16[32,1,32,128]{3,2,1,0:T(8,128)(2,1)S(1)}, bf16[32,1,32,128]{3,2,1,0:T(8,128)(2,1)S(1)}, u32[]{:S(2)}, u32[]{:S(2)}) collective-permute-start(bf16[32,1,32,128]{3,2,1,0:T(8,128)(2,1)S(1)} %get-tuple-element.51), channel_id=1, source_target_pairs={{1,0},{2,1},{3,2},{4,3},{5,4},{6,5},{7,6},{9,8},{10,9},{11,10},{12... | collective-permute-start | bytes 786440 | tf_op jit(solution)/shard_map/ppermute | solution.py:137
  12.0 2.8 %copy-start = (bf16[1,32,2,32,128]{4,3,2,1,0:T(8,128)(2,1)S(1)}, bf16[1,32,2,32,128]{4,3,2,1,0:T(8,128)(2,1)}, u32[]{:S(2)}) copy-start(bf16[1,32,2,32,128]{4,3,2,1,0:T(8,128)(2,1)} %param.5) | copy-start | bytes 1572868
  21.8 15.2 %collective-permute-start.5 = (bf16[1,32,4096]{2,1,0:T(8,128)(2,1)}, bf16[1,32,4096]{2,1,0:T(8,128)(2,1)S(1)}, u32[]{:S(2)}, u32[]{:S(2)}) collective-permute-start(bf16[1,32,4096]{2,1,0:T(8,128)(2,1)} %get-tuple-element.30), channel_id=1, source_target_pairs={{0,1},{1,2},{2,3},{3,4},{4,5},{5,6},{6,7},{8,9},{9,10},{10,11},{11... | collective-permute-start | bytes 786440 | tf_op jit(solution)/shard_map/ppermute | solution.py:137
  28.5 8.5 %collective-permute-start.6 = (bf16[1,32,4096]{2,1,0:T(8,128)(2,1)}, bf16[1,32,4096]{2,1,0:T(8,128)(2,1)S(1)}, u32[]{:S(2)}, u32[]{:S(2)}) collective-permute-start(bf16[1,32,4096]{2,1,0:T(8,128)(2,1)} %get-tuple-element.31), channel_id=1, source_target_pairs={{1,0},{2,1},{3,2},{4,3},{5,4},{6,5},{7,6},{9,8},{10,9},{11,10},{12... | collective-permute-start | bytes 786440 | tf_op jit(solution)/shard_map/ppermute | solution.py:137
  36.2 0.7 %copy-start.7 = (f32[32,1]{1,0:T(8,128)S(1)}, f32[32,1]{1,0:T(8,128)}, u32[]{:S(2)}) copy-start(f32[32,1]{1,0:T(8,128)} %get-tuple-element.29) | copy-start | bytes 388
  37.0 1.6 %copy-start.1 = (bf16[1,32,4096]{2,1,0:T(8,128)(2,1)}, bf16[1,32,4096]{2,1,0:T(8,128)(2,1)S(1)}, u32[]{:S(2)}) copy-start(bf16[1,32,4096]{2,1,0:T(8,128)(2,1)S(1)} %collective-permute-done.5.lo) | copy-start | bytes 786436
  37.0 1.6 %copy-start.2 = (bf16[1,32,4096]{2,1,0:T(8,128)(2,1)}, bf16[1,32,4096]{2,1,0:T(8,128)(2,1)S(1)}, u32[]{:S(2)}) copy-start(bf16[1,32,4096]{2,1,0:T(8,128)(2,1)S(1)} %collective-permute-done.6.hi) | copy-start | bytes 786436
  37.0 4.7 %collective-permute-start.7 = (f32[16,865]{1,0:T(8,128)S(1)}, f32[16,865]{1,0:T(8,128)S(1)}, u32[]{:S(2)}, u32[]{:S(2)}) collective-permute-start(f32[16,865]{1,0:T(8,128)S(1)} %fusion.2), channel_id=1, source_target_pairs={{0,16},{8,24},{16,0},{24,8},{1,17},{9,25},{17,1},{25,9},{2,18},{10... | collective-permute-start | bytes 166088 | tf_op jit(solution)/shard_map/ppermute | solution.py:142
  41.8 4.6 %collective-permute-start.8 = (f32[8,865]{1,0:T(8,128)S(1)}, f32[8,865]{1,0:T(8,128)S(1)}, u32[]{:S(2)}, u32[]{:S(2)}) collective-permute-start(f32[8,865]{1,0:T(8,128)S(1)} %constant_dynamic-slice_fusion), channel_id=1, source_target_pairs={{0,8},{8,0},{16,24},{24,16},{1,9},{9,1},{17,25},{25,17},{2,10},{10... | collective-permute-start | bytes 83048 | tf_op jit(solution)/shard_map/ppermute | solution.py:142
  43.3 3.6 %copy-start.6 = (bf16[2,32,4096]{2,1,0:T(8,128)(2,1)S(1)}, bf16[2,32,4096]{2,1,0:T(8,128)(2,1)}, u32[]{:S(2)}) copy-start(bf16[2,32,4096]{2,1,0:T(8,128)(2,1)} %get-tuple-element.26) | copy-start | bytes 1572868
  46.4 1.4 %collective-permute-start.9 = (f32[8,865]{1,0:T(8,128)S(1)}, f32[8,865]{1,0:T(8,128)S(1)}, u32[]{:S(2)}, u32[]{:S(2)}) collective-permute-start(f32[8,865]{1,0:T(8,128)S(1)} %dynamic-slice_add_fusion), channel_id=1, source_target_pairs={{0,1},{1,0},{2,3},{3,2},{4,5},{5,4},{6,7},{7,6},{8,9},{9,8},{10,11... | collective-permute-start | bytes 83048 | tf_op jit(solution)/shard_map/ppermute | solution.py:142
  46.9 2.9 %copy-start.3 = (bf16[1,32,4096]{2,1,0:T(8,128)(2,1)S(1)}, bf16[1,32,4096]{2,1,0:T(8,128)(2,1)}, u32[]{:S(2)}) copy-start(bf16[1,32,4096]{2,1,0:T(8,128)(2,1)} %shard_map.86) | copy-start | bytes 786436
  46.9 2.9 %copy-start.4 = (bf16[1,32,4096]{2,1,0:T(8,128)(2,1)S(1)}, bf16[1,32,4096]{2,1,0:T(8,128)(2,1)}, u32[]{:S(2)}) copy-start(bf16[1,32,4096]{2,1,0:T(8,128)(2,1)} %shard_map.87) | copy-start | bytes 786436
  47.8 3.9 %collective-permute-start.10 = (f32[8,865]{1,0:T(8,128)S(1)}, f32[8,865]{1,0:T(8,128)S(1)}, u32[]{:S(2)}, u32[]{:S(2)}) collective-permute-start(f32[8,865]{1,0:T(8,128)S(1)} %add.61), channel_id=1, source_target_pairs={{0,2},{1,3},{2,0},{3,1},{4,6},{5,7},{6,4},{7,5},{8,10},{9,11},{10,... | collective-permute-start | bytes 83048 | tf_op jit(solution)/shard_map/ppermute | solution.py:142
  51.7 4.9 %collective-permute-start.11 = (f32[8,865]{1,0:T(8,128)S(1)}, f32[8,865]{1,0:T(8,128)S(1)}, u32[]{:S(2)}, u32[]{:S(2)}) collective-permute-start(f32[8,865]{1,0:T(8,128)S(1)} %add.62), channel_id=1, source_target_pairs={{0,4},{1,5},{2,6},{3,7},{4,0},{5,1},{6,2},{7,3},{8,12},{9,13},{10,... | collective-permute-start | bytes 83048 | tf_op jit(solution)/shard_map/ppermute | solution.py:142
  56.5 0.7 %copy-start.8 = (f32[8,865]{1,0:T(8,128)}, f32[8,865]{1,0:T(8,128)S(1)}, u32[]{:S(2)}) copy-start(f32[8,865]{1,0:T(8,128)S(1)} %add_multiply_fusion) | copy-start | bytes 83044

commit v7 on v6

--- a/solution.py
+++ b/solution.py
@@ -66,10 +66,10 @@
         out[n] = _shifted_sum(y, mask, chans, lanes, depth, -1).astype(out.dtype)
 
 
-def _weight_kernel(haloed, dpre, mask, gw_out, gb_out, *, planes, depth):
+def _weight_kernel(haloed, dpre, mask, gw_out, *, planes, depth):
     chans, lanes = dpre.shape[1], dpre.shape[2]
-    gw = jnp.zeros(gw_out.shape, jnp.float32)
-    gb = jnp.zeros(gb_out.shape, jnp.float32)
+    gw = jnp.zeros((9 * chans, 3 * chans), jnp.float32)
+    gb = jnp.zeros((chans, 1), jnp.float32)
     for p in range(planes):
         d = dpre[p].astype(jnp.float32)
         gb = gb + jnp.sum(d, axis=1, keepdims=True)
@@ -84,8 +84,12 @@
             jnp.concatenate(parts, axis=0), _stacked(haloed, p),
             (((1,), (1,)), ((), ())), preferred_element_type=jnp.float32,
         )
-    gw_out[...] = gw
-    gb_out[...] = gb
+    chans_in = gw.shape[1] // 3
+    for k in range(len(OFFSETS)):
+        for a in range(3):
+            t = 9 * a + k
+            gw_out[:, t * chans_in : (t + 1) * chans_in] = gw[k * chans : (k + 1) * chans, a * chans_in : (a + 1) * chans_in]
+    gw_out[:, 27 * chans_in :] = gb
 
 
 def _vmem(n):
@@ -123,9 +127,9 @@
     flops = 2 * planes * 9 * chans * 3 * chans * lanes
     return pl.pallas_call(
         functools.partial(_weight_kernel, planes=planes, depth=depth),
-        out_shape=(jax.ShapeDtypeStruct((9 * chans, 3 * chans), jnp.float32), jax.ShapeDtypeStruct((chans, 1), jnp.float32)),
+        out_shape=jax.ShapeDtypeStruct((chans, 27 * chans + 1), jnp.float32),
         in_specs=_vmem(3),
-        out_specs=tuple(_vmem(2)),
+        out_specs=_vmem(1)[0],
         cost_estimate=pl.CostEstimate(flops=flops, transcendentals=0, bytes_accessed=3 * dpre.size * 2),
     )(haloed, dpre, mask)
 
@@ -213,9 +217,7 @@
         haloed, forward_w, whole_bias.astype(jnp.float32)[:, None], flat(cotangent[0]), mask, depth
     )
     dlo, dhi = neighbours(first, last, "strike")
-    g, gb = weight_call(haloed, dpre, mask, depth)
-    local_weight = g.reshape(3, 3, out_chan, 3, chans).transpose(2, 3, 0, 1, 4).reshape(out_chan, 27 * chans)
-    local_grads = jnp.concatenate([local_weight, gb], axis=1)
+    local_grads = weight_call(haloed, dpre, mask, depth)
     work = [
         (functools.partial(input_call, depth=depth, first=p, count=1), (dlo, dpre, dhi, backward_w, mask))
         for p in range(planes)

time: 57.7 us -> 56.3 us (0.976)
  local copies, waits for them, and re-layouts: 12.2 us -> 10.8 us
    reshape x2 -> x0, local copies, waits for them, and re-layouts: 1.42 us -> none  [local(): g.reshape(3, 3, out_chan, 3, chans).transpose(2, 3, 0, 1, 4)]
    dynamic_slice x1 -> x2, local copies, waits for them, and re-layouts: 0.01 us -> 0.84 us  [reduce_beside(): send = lax.dynamic_slice_in_dim(value, (1 - upper) * half, half, 0)]
  transfers between devices with their start and end apart: 12 -> 12, of which waited for: 5 -> 4; matrix products, arithmetic and copies ran while one was open for 15% -> 13% of each run, Pallas kernels for 17% -> 18%
where the time goes in v7:
time: 56.3 us; the launch traced here: 55.9 us
  starting transfers between devices  23.9 us (42%)
  Pallas kernels  14.9 us (26%)
  local copies, waits for them, and re-layouts  10.8 us (19%)
  waiting for transfers between devices  4.43 us (8%)
  other arithmetic  0.96 us (2%)
  between operations  0.89 us (2%)
    ppermute x8, starting transfers between devices, swap(): return lax.ppermute(value, axis, [(i, i ^ bit) for i in range(peers)])  13.3 us
    ppermute x4, starting transfers between devices, neighbours(): return (lax.ppermute(last, axis, up), lax.ppermute(first, axis, down))  10.6 us
    pallas_call x2, Pallas kernels, input_call(): pl.pallas_call(functools.partial(_input_kernel, planes=planes, first=firs...  6.14 us
    pallas_call x1, Pallas kernels, forward_call(): pl.pallas_call(functools.partial(_forward_kernel, planes=planes, depth=de...  5.05 us
    pallas_call x1, Pallas kernels, weight_call(): pl.pallas_call(functools.partial(_weight_kernel, planes=planes, depth=dep...  3.75 us
    ppermute x8, waiting for transfers between devices, swap(): return lax.ppermute(value, axis, [(i, i ^ bit) for i in range(peers)])  3.23 us
    reshape x2, local copies, waits for them, and re-layouts, local(): haloed = haloed.transpose(1, 0, 2, 3).reshape(planes + 2, chans, lanes)  1.85 us
    unnamed x24, local copies, waits for them, and re-layouts  1.56 us
  transfers between devices with their start and end apart: 12, of which 4 were waited for; matrix products, arithmetic and copies ran while one was open for 13% of the time, Pallas kernels for 18%

profile of v7, /device:TPU:0, one launch (start us, length us, event | category | flops | bytes accessed | tf_op | source)
XLA Modules:
  0.0 55.9 jit_solution(10715070237109321713)
XLA Ops:
  0.6 0.0 copy-start.10
  0.6 0.6 %copy-done.10 = bf16[8]{0:T(256)(128)(2,1)S(1)} copy-done((bf16[8]{0:T(256)(128)(2,1)S(1)}, bf16[8]{0:T(256)(128)(2,1)}, u32[]{:S(2)}) %copy-start.10) | copy-done | bytes 40
  1.3 0.1 copy.17
  1.4 0.0 copy-start.9
  1.4 0.7 %copy-done.9 = bf16[8,864]{1,0:T(8,128)(2,1)S(1)} copy-done((bf16[8,864]{1,0:T(8,128)(2,1)S(1)}, bf16[8,864]{1,0:T(8,128)(2,1)}, u32[]{:S(2)}) %copy-start.9) | copy-done | bytes 13848
  2.1 0.1 bitcast_dynamic-update-slice_fusion.3
  2.2 3.0 %collective-permute-start.3 = (bf16[8,865]{1,0:T(8,128)(2,1)S(1)}, bf16[8,865]{1,0:T(8,128)(2,1)S(1)}, u32[]{:S(2)}, u32[]{:S(2)}) collective-permute-start(bf16[8,865]{1,0:T(8,128)(2,1)S(1)} %get-tuple-element.45), channel_id=1, source_target_pairs={{0,16},{8,24},{16,0},{24,8},{1,17},{9,25},{17,1},{25,9},{2,18},{10... | collective-permute-start | bytes 41528 | tf_op jit(solution)/shard_map/ppermute | solution.py:146
  5.1 1.5 %collective-permute-start.2 = (bf16[8,865]{1,0:T(8,128)(2,1)S(1)}, bf16[8,865]{1,0:T(8,128)(2,1)S(1)}, u32[]{:S(2)}, u32[]{:S(2)}) collective-permute-start(bf16[8,865]{1,0:T(8,128)(2,1)S(1)} %get-tuple-element.45), channel_id=1, source_target_pairs={{0,8},{8,0},{16,24},{24,16},{1,9},{9,1},{17,25},{25,17},{2,10},{10... | collective-permute-start | bytes 41528 | tf_op jit(solution)/shard_map/ppermute | solution.py:146
  6.6 0.0 collective-permute-start.4
  6.7 1.1 %fusion = (bf16[32,1,32,128]{3,2,1,0:T(8,128)(2,1)S(1)}, bf16[32,1,32,128]{3,2,1,0:T(8,128)(2,1)S(1)}) fusion(bf16[32,2,32,128]{3,2,1,0:T(8,128)(2,1)} %bitcast.55), kind=kLoop, calls=%fused_computation.17 | loop fusion | bytes 1048576 | tf_op jit(solution)/shard_map/slice | solution.py:213
  7.8 1.3 %collective-permute-start = (bf16[32,1,32,128]{3,2,1,0:T(8,128)(2,1)S(1)}, bf16[32,1,32,128]{3,2,1,0:T(8,128)(2,1)S(1)}, u32[]{:S(2)}, u32[]{:S(2)}) collective-permute-start(bf16[32,1,32,128]{3,2,1,0:T(8,128)(2,1)S(1)} %get-tuple-element.46), channel_id=1, source_target_pairs={{0,1},{1,2},{2,3},{3,4},{4,5},{5,6},{6,7},{8,9},{9,10},{10,11},{11... | collective-permute-start | bytes 786440 | tf_op jit(solution)/shard_map/ppermute | solution.py:141
  9.1 1.3 %collective-permute-start.1 = (bf16[32,1,32,128]{3,2,1,0:T(8,128)(2,1)S(1)}, bf16[32,1,32,128]{3,2,1,0:T(8,128)(2,1)S(1)}, u32[]{:S(2)}, u32[]{:S(2)}) collective-permute-start(bf16[32,1,32,128]{3,2,1,0:T(8,128)(2,1)S(1)} %get-tuple-element.47), channel_id=1, source_target_pairs={{1,0},{2,1},{3,2},{4,3},{5,4},{6,5},{7,6},{9,8},{10,9},{11,10},{12... | collective-permute-start | bytes 786440 | tf_op jit(solution)/shard_map/ppermute | solution.py:141
  10.5 0.0 copy-done.5
  10.5 0.1 reshape.41
  10.6 1.1 %copy.24.cot = bf16[2,32,4096]{2,1,0:T(8,128)(2,1)} copy(bf16[2,32,4096]{2,0,1:T(2,128)(2,1)S(1)} %reshape.41) | data formatting | bytes 1048576 | tf_op jit(solution)/shard_map/reshape | solution.py:208
  11.7 0.0 collective-permute-done.2
  11.7 0.0 collective-permute-done.3
  11.7 0.0 collective-permute-done.4
  11.8 0.2 reshape.34
  12.0 0.0 copy-start
  12.0 0.1 copy.18
  12.1 0.8 %reshape.35.wall = bf16[288,96]{1,0:T(8,128)(2,1)} reshape(bf16[3,3,32,3,32]{4,3,2,1,0:T(4,128)(2,1)S(1)} %copy.18) | data formatting | bytes 110592 | tf_op jit(solution)/shard_map/reshape | solution.py:203
  12.9 0.7 %slice_convert_fusion.bias = f32[32,1]{1,0:T(8,128)} fusion(bf16[32,865]{1,0:T(8,128)(2,1)S(1)} %bitcast.62), kind=kLoop, calls=%fused_computation.13 | loop fusion | flops 32 | bytes 192 | tf_op jit(solution)/shard_map/convert_element_type | solution.py:217
  13.6 0.0 collective-permute-done
  13.6 1.2 %collective-permute-done.1 = bf16[32,1,32,128]{3,2,1,0:T(8,128)(2,1)S(1)} collective-permute-done((bf16[32,1,32,128]{3,2,1,0:T(8,128)(2,1)S(1)}, bf16[32,1,32,128]{3,2,1,0:T(8,128)(2,1)S(1)}, u32[]{:S(2)}, u32[]{:S(2)}) %collective-permute-start.1) | collective-permute-done | bytes 262176 | tf_op jit(solution)/shard_map/ppermute | solution.py:141
  14.8 0.0 copy-done
  14.8 0.1 maximum_bitcast_fusion
  14.9 0.3 reshape.40
  15.2 1.6 %copy.23.haloed = bf16[4,32,4096]{2,1,0:T(8,128)(2,1)} copy(bf16[4,32,4096]{2,0,1:T(4,128)(2,1)S(1)} %reshape.40) | data formatting | bytes 2097152 | tf_op jit(solution)/shard_map/reshape | solution.py:215
  16.8 5.0 %shard_map.84 = (bf16[2,32,4096]{2,1,0:T(8,128)(2,1)}, bf16[2,32,4096]{2,1,0:T(8,128)(2,1)}, bf16[1,32,4096]{2,1,0:T(8,128)(2,1)}, bf16[1,32,4096]{2,1,0:T(8,128)(2,1)}) custom-call(bf16[4,32,4096]{2,1,0:T(8,128)(2,1)} %copy.23.haloed, bf16[288,96]{1,0:T(8,128)(2,1)} %reshape.35.wall, f32[32,1]{1,0:T(8,128)} %slice_convert_fusion.bias, ...), custom_call_target="tpu_custom_call" | custom-call | flops 452984832 | bytes 2621440 | tf_op jit(solution)/shard_map/pallas_call | solution.py:104
  21.8 6.7 %collective-permute-start.5 = (bf16[1,32,4096]{2,1,0:T(8,128)(2,1)}, bf16[1,32,4096]{2,1,0:T(8,128)(2,1)S(1)}, u32[]{:S(2)}, u32[]{:S(2)}) collective-permute-start(bf16[1,32,4096]{2,1,0:T(8,128)(2,1)} %get-tuple-element.26), channel_id=1, source_target_pairs={{0,1},{1,2},{2,3},{3,4},{4,5},{5,6},{6,7},{8,9},{9,10},{10,11},{11... | collective-permute-start | bytes 786440 | tf_op jit(solution)/shard_map/ppermute | solution.py:141
  28.5 1.3 %collective-permute-start.6 = (bf16[1,32,4096]{2,1,0:T(8,128)(2,1)}, bf16[1,32,4096]{2,1,0:T(8,128)(2,1)S(1)}, u32[]{:S(2)}, u32[]{:S(2)}) collective-permute-start(bf16[1,32,4096]{2,1,0:T(8,128)(2,1)} %get-tuple-element.27), channel_id=1, source_target_pairs={{1,0},{2,1},{3,2},{4,3},{5,4},{6,5},{7,6},{9,8},{10,9},{11,10},{12... | collective-permute-start | bytes 786440 | tf_op jit(solution)/shard_map/ppermute | solution.py:141
  29.8 0.1 reverse_bitcast_fusion
  29.9 0.3 copy.21
  30.2 0.8 %reshape.38.wall = bf16[288,96]{1,0:T(8,128)(2,1)} reshape(bf16[3,3,32,3,32]{4,3,2,1,0:T(4,128)(2,1)S(1)} %copy.21) | data formatting | bytes 110592 | tf_op jit(solution)/shard_map/reshape | solution.py:204
  31.0 3.8 %shard_map.85 = f32[32,865]{1,0:T(8,128)} custom-call(bf16[4,32,4096]{2,1,0:T(8,128)(2,1)} %copy.23.haloed, bf16[2,32,4096]{2,1,0:T(8,128)(2,1)} %get-tuple-element.38.dpre.mid, f32[9,1,4096]{2,1,0:T(1,128)} %constant.68.clone.mask), custom_call_target="tpu_custom_call" | custom-call | flops 452984832 | bytes 1572864 | tf_op jit(solution)/shard_map/pallas_call | solution.py:128
  34.7 0.8 %constant_dynamic-slice_fusion.1 = f32[16,865]{1,0:T(8,128)S(1)} fusion(f32[32,865]{1,0:T(8,128)} %shard_map.85, s32[]{:T(128)S(6)} %select_n.47), kind=kLoop, calls=%fused_computation.16 | loop fusion | bytes 110724 | tf_op jit(solution)/shard_map/dynamic_slice | solution.py:176
  35.5 0.0 collective-permute-done.5.lo
  35.6 0.0 collective-permute-done.6.hi
  35.6 0.0 copy-start.2
  35.6 1.6 %collective-permute-start.7 = (f32[16,865]{1,0:T(8,128)S(1)}, f32[16,865]{1,0:T(8,128)S(1)}, u32[]{:S(2)}, u32[]{:S(2)}) collective-permute-start(f32[16,865]{1,0:T(8,128)S(1)} %constant_dynamic-slice_fusion.1), channel_id=1, source_target_pairs={{0,16},{8,24},{16,0},{24,8},{1,17},{9,25},{17,1},{25,9},{2,18},{10... | collective-permute-start | bytes 166088 | tf_op jit(solution)/shard_map/ppermute | solution.py:146
  37.2 0.0 copy-done.1
  37.2 0.0 copy-done.2
  37.2 3.1 %shard_map.86 = bf16[1,32,4096]{2,1,0:T(8,128)(2,1)} custom-call(bf16[1,32,4096]{2,1,0:T(8,128)(2,1)} %copy-done.1, bf16[2,32,4096]{2,1,0:T(8,128)(2,1)} %get-tuple-element.38.dpre.mid, bf16[1,32,4096]{2,1,0:T(8,128)(2,1)} %copy-done.2, bf16[288,96]{1,0:T(8,128)(2,1)} %reshape.38.wall, f32[9,1,4096]{2,1,0:T(1,128)} %constant.68.clone.mask), custom_call_target="tpu_custom_call" | custom-call | flops 226492416 | bytes 1572864 | tf_op jit(solution)/shard_map/pallas_call | solution.py:116
  40.2 0.0 collective-permute-done.7
  40.3 0.0 copy-done.7
  40.3 1.6 %collective-permute-start.8 = (f32[8,865]{1,0:T(8,128)S(1)}, f32[8,865]{1,0:T(8,128)S(1)}, u32[]{:S(2)}, u32[]{:S(2)}) collective-permute-start(f32[8,865]{1,0:T(8,128)S(1)} %constant_dynamic-slice_fusion), channel_id=1, source_target_pairs={{0,8},{8,0},{16,24},{24,16},{1,9},{9,1},{17,25},{25,17},{2,10},{10... | collective-permute-start | bytes 83048 | tf_op jit(solution)/shard_map/ppermute | solution.py:146
  41.9 3.1 %shard_map.87 = bf16[1,32,4096]{2,1,0:T(8,128)(2,1)} custom-call(bf16[1,32,4096]{2,1,0:T(8,128)(2,1)} %copy-done.1, bf16[2,32,4096]{2,1,0:T(8,128)(2,1)} %get-tuple-element.38.dpre.mid, bf16[1,32,4096]{2,1,0:T(8,128)(2,1)} %copy-done.2, bf16[288,96]{1,0:T(8,128)(2,1)} %reshape.38.wall, f32[9,1,4096]{2,1,0:T(1,128)} %constant.68.clone.mask), custom_call_target="tpu_custom_call" | custom-call | flops 226492416 | bytes 1572864 | tf_op jit(solution)/shard_map/pallas_call | solution.py:116
  45.0 0.0 collective-permute-done.8
  45.0 0.6 %collective-permute-start.9 = (f32[8,865]{1,0:T(8,128)S(1)}, f32[8,865]{1,0:T(8,128)S(1)}, u32[]{:S(2)}, u32[]{:S(2)}) collective-permute-start(f32[8,865]{1,0:T(8,128)S(1)} %dynamic-slice_add_fusion.1), channel_id=1, source_target_pairs={{0,1},{1,0},{2,3},{3,2},{4,5},{5,4},{6,7},{7,6},{8,9},{9,8},{10,11... | collective-permute-start | bytes 83048 | tf_op jit(solution)/shard_map/ppermute | solution.py:146
  45.6 0.0 copy-done.6
  45.6 0.1 copy.25
  45.7 0.8 %collective-permute-done.9 = f32[8,865]{1,0:T(8,128)S(1)} collective-permute-done((f32[8,865]{1,0:T(8,128)S(1)}, f32[8,865]{1,0:T(8,128)S(1)}, u32[]{:S(2)}, u32[]{:S(2)}) %collective-permute-start.9) | collective-permute-done | bytes 27712 | tf_op jit(solution)/shard_map/ppermute | solution.py:146
  46.4 2.0 %collective-permute-start.10 = (f32[8,865]{1,0:T(8,128)S(1)}, f32[8,865]{1,0:T(8,128)S(1)}, u32[]{:S(2)}, u32[]{:S(2)}) collective-permute-start(f32[8,865]{1,0:T(8,128)S(1)} %add.61), channel_id=1, source_target_pairs={{0,2},{1,3},{2,0},{3,1},{4,6},{5,7},{6,4},{7,5},{8,10},{9,11},{10,... | collective-permute-start | bytes 83048 | tf_op jit(solution)/shard_map/ppermute | solution.py:146
  48.4 0.0 copy-done.3
  48.5 0.0 copy-done.4
  48.5 0.1 pad_maximum_fusion
  48.5 0.1 copy.26
  48.6 1.7 %collective-permute-done.10 = f32[8,865]{1,0:T(8,128)S(1)} collective-permute-done((f32[8,865]{1,0:T(8,128)S(1)}, f32[8,865]{1,0:T(8,128)S(1)}, u32[]{:S(2)}, u32[]{:S(2)}) %collective-permute-start.10) | collective-permute-done | bytes 27712 | tf_op jit(solution)/shard_map/ppermute | solution.py:146
  50.3 3.0 %collective-permute-start.11 = (f32[8,865]{1,0:T(8,128)S(1)}, f32[8,865]{1,0:T(8,128)S(1)}, u32[]{:S(2)}, u32[]{:S(2)}) collective-permute-start(f32[8,865]{1,0:T(8,128)S(1)} %add.62), channel_id=1, source_target_pairs={{0,4},{1,5},{2,6},{3,7},{4,0},{5,1},{6,2},{7,3},{8,12},{9,13},{10,... | collective-permute-start | bytes 83048 | tf_op jit(solution)/shard_map/ppermute | solution.py:146
  53.3 1.1 %copy_bitcast_fusion = (bf16[1,32,2,32,128]{4,3,2,1,0:T(8,128)(2,1)}, bf16[1,32,2,32,128]{4,3,2,1,0:T(8,128)(2,1)}) fusion(bf16[2,32,32,128]{3,2,1,0:T(8,128)(2,1)S(1)} %bitcast.57, bf16[2,32,32,128]{3,2,1,0:T(8,128)(2,1)S(1)} %bitcast.58), kind=kLoop, calls=%fused_computation.2 | loop fusion | bytes 2097152 | tf_op jit(solution)/shard_map/broadcast_in_dim | solution.py:230
  54.5 0.7 %collective-permute-done.11 = f32[8,865]{1,0:T(8,128)S(1)} collective-permute-done((f32[8,865]{1,0:T(8,128)S(1)}, f32[8,865]{1,0:T(8,128)S(1)}, u32[]{:S(2)}, u32[]{:S(2)}) %collective-permute-start.11) | collective-permute-done | bytes 27712 | tf_op jit(solution)/shard_map/ppermute | solution.py:146
  55.2 0.7 %slice_reduce_fusion = f32[8]{0:T(128)} fusion(f32[8,865]{1,0:T(8,128)S(1)} %add_multiply_fusion), kind=kLoop, calls=%fused_computation.14 | loop fusion | bytes 64 | tf_op jit(solution)/shard_map/slice | solution.py:230
  55.9 0.0 copy-done.8
  (17 shorter events, 0.1 us)
Async XLA Ops:
  0.6 0.7 %copy-start.10 = (bf16[8]{0:T(256)(128)(2,1)S(1)}, bf16[8]{0:T(256)(128)(2,1)}, u32[]{:S(2)}) copy-start(bf16[8]{0:T(256)(128)(2,1)} %param.8) | copy-start | bytes 52
  1.4 0.7 %copy-start.9 = (bf16[8,864]{1,0:T(8,128)(2,1)S(1)}, bf16[8,864]{1,0:T(8,128)(2,1)}, u32[]{:S(2)}) copy-start(bf16[8,864]{1,0:T(8,128)(2,1)} %param.7) | copy-start | bytes 41476
  2.2 9.5 %collective-permute-start.3 = (bf16[8,865]{1,0:T(8,128)(2,1)S(1)}, bf16[8,865]{1,0:T(8,128)(2,1)S(1)}, u32[]{:S(2)}, u32[]{:S(2)}) collective-permute-start(bf16[8,865]{1,0:T(8,128)(2,1)S(1)} %get-tuple-element.45), channel_id=1, source_target_pairs={{0,16},{8,24},{16,0},{24,8},{1,17},{9,25},{17,1},{25,9},{2,18},{10... | collective-permute-start | bytes 41528 | tf_op jit(solution)/shard_map/ppermute | solution.py:146
  5.1 6.6 %collective-permute-start.2 = (bf16[8,865]{1,0:T(8,128)(2,1)S(1)}, bf16[8,865]{1,0:T(8,128)(2,1)S(1)}, u32[]{:S(2)}, u32[]{:S(2)}) collective-permute-start(bf16[8,865]{1,0:T(8,128)(2,1)S(1)} %get-tuple-element.45), channel_id=1, source_target_pairs={{0,8},{8,0},{16,24},{24,16},{1,9},{9,1},{17,25},{25,17},{2,10},{10... | collective-permute-start | bytes 41528 | tf_op jit(solution)/shard_map/ppermute | solution.py:146
  6.6 5.1 %collective-permute-start.4 = (bf16[8,865]{1,0:T(8,128)(2,1)S(1)}, bf16[8,865]{1,0:T(8,128)(2,1)S(1)}, u32[]{:S(2)}, u32[]{:S(2)}) collective-permute-start(bf16[8,865]{1,0:T(8,128)(2,1)S(1)} %get-tuple-element.45), channel_id=1, source_target_pairs={{0,24},{8,16},{16,8},{24,0},{1,25},{9,17},{17,9},{25,1},{2,26},{10... | collective-permute-start | bytes 41528 | tf_op jit(solution)/shard_map/ppermute | solution.py:146
  6.7 3.8 %copy-start.5 = (bf16[1,32,2,32,128]{4,3,2,1,0:T(8,128)(2,1)S(1)}, bf16[1,32,2,32,128]{4,3,2,1,0:T(8,128)(2,1)}, u32[]{:S(2)}) copy-start(bf16[1,32,2,32,128]{4,3,2,1,0:T(8,128)(2,1)} %param.6) | copy-start | bytes 1572868
  7.8 5.8 %collective-permute-start = (bf16[32,1,32,128]{3,2,1,0:T(8,128)(2,1)S(1)}, bf16[32,1,32,128]{3,2,1,0:T(8,128)(2,1)S(1)}, u32[]{:S(2)}, u32[]{:S(2)}) collective-permute-start(bf16[32,1,32,128]{3,2,1,0:T(8,128)(2,1)S(1)} %get-tuple-element.46), channel_id=1, source_target_pairs={{0,1},{1,2},{2,3},{3,4},{4,5},{5,6},{6,7},{8,9},{9,10},{10,11},{11... | collective-permute-start | bytes 786440 | tf_op jit(solution)/shard_map/ppermute | solution.py:141
  9.1 5.7 %collective-permute-start.1 = (bf16[32,1,32,128]{3,2,1,0:T(8,128)(2,1)S(1)}, bf16[32,1,32,128]{3,2,1,0:T(8,128)(2,1)S(1)}, u32[]{:S(2)}, u32[]{:S(2)}) collective-permute-start(bf16[32,1,32,128]{3,2,1,0:T(8,128)(2,1)S(1)} %get-tuple-element.47), channel_id=1, source_target_pairs={{1,0},{2,1},{3,2},{4,3},{5,4},{6,5},{7,6},{9,8},{10,9},{11,10},{12... | collective-permute-start | bytes 786440 | tf_op jit(solution)/shard_map/ppermute | solution.py:141
  12.0 2.8 %copy-start = (bf16[1,32,2,32,128]{4,3,2,1,0:T(8,128)(2,1)S(1)}, bf16[1,32,2,32,128]{4,3,2,1,0:T(8,128)(2,1)}, u32[]{:S(2)}) copy-start(bf16[1,32,2,32,128]{4,3,2,1,0:T(8,128)(2,1)} %param.5) | copy-start | bytes 1572868
  21.8 13.7 %collective-permute-start.5 = (bf16[1,32,4096]{2,1,0:T(8,128)(2,1)}, bf16[1,32,4096]{2,1,0:T(8,128)(2,1)S(1)}, u32[]{:S(2)}, u32[]{:S(2)}) collective-permute-start(bf16[1,32,4096]{2,1,0:T(8,128)(2,1)} %get-tuple-element.26), channel_id=1, source_target_pairs={{0,1},{1,2},{2,3},{3,4},{4,5},{5,6},{6,7},{8,9},{9,10},{10,11},{11... | collective-permute-start | bytes 786440 | tf_op jit(solution)/shard_map/ppermute | solution.py:141
  28.5 7.1 %collective-permute-start.6 = (bf16[1,32,4096]{2,1,0:T(8,128)(2,1)}, bf16[1,32,4096]{2,1,0:T(8,128)(2,1)S(1)}, u32[]{:S(2)}, u32[]{:S(2)}) collective-permute-start(bf16[1,32,4096]{2,1,0:T(8,128)(2,1)} %get-tuple-element.27), channel_id=1, source_target_pairs={{1,0},{2,1},{3,2},{4,3},{5,4},{6,5},{7,6},{9,8},{10,9},{11,10},{12... | collective-permute-start | bytes 786440 | tf_op jit(solution)/shard_map/ppermute | solution.py:141
  35.5 1.6 %copy-start.1 = (bf16[1,32,4096]{2,1,0:T(8,128)(2,1)}, bf16[1,32,4096]{2,1,0:T(8,128)(2,1)S(1)}, u32[]{:S(2)}) copy-start(bf16[1,32,4096]{2,1,0:T(8,128)(2,1)S(1)} %collective-permute-done.5.lo) | copy-start | bytes 786436
  35.6 1.6 %copy-start.2 = (bf16[1,32,4096]{2,1,0:T(8,128)(2,1)}, bf16[1,32,4096]{2,1,0:T(8,128)(2,1)S(1)}, u32[]{:S(2)}) copy-start(bf16[1,32,4096]{2,1,0:T(8,128)(2,1)S(1)} %collective-permute-done.6.hi) | copy-start | bytes 786436
  35.6 4.7 %collective-permute-start.7 = (f32[16,865]{1,0:T(8,128)S(1)}, f32[16,865]{1,0:T(8,128)S(1)}, u32[]{:S(2)}, u32[]{:S(2)}) collective-permute-start(f32[16,865]{1,0:T(8,128)S(1)} %constant_dynamic-slice_fusion.1), channel_id=1, source_target_pairs={{0,16},{8,24},{16,0},{24,8},{1,17},{9,25},{17,1},{25,9},{2,18},{10... | collective-permute-start | bytes 166088 | tf_op jit(solution)/shard_map/ppermute | solution.py:146
  37.2 3.1 %copy-start.7 = (f32[32,865]{1,0:T(8,128)S(1)}, f32[32,865]{1,0:T(8,128)}, u32[]{:S(2)}) copy-start(f32[32,865]{1,0:T(8,128)} %shard_map.85) | copy-start | bytes 332164
  40.3 4.6 %collective-permute-start.8 = (f32[8,865]{1,0:T(8,128)S(1)}, f32[8,865]{1,0:T(8,128)S(1)}, u32[]{:S(2)}, u32[]{:S(2)}) collective-permute-start(f32[8,865]{1,0:T(8,128)S(1)} %constant_dynamic-slice_fusion), channel_id=1, source_target_pairs={{0,8},{8,0},{16,24},{24,16},{1,9},{9,1},{17,25},{25,17},{2,10},{10... | collective-permute-start | bytes 83048 | tf_op jit(solution)/shard_map/ppermute | solution.py:146
  41.9 3.7 %copy-start.6 = (bf16[2,32,4096]{2,1,0:T(8,128)(2,1)S(1)}, bf16[2,32,4096]{2,1,0:T(8,128)(2,1)}, u32[]{:S(2)}) copy-start(bf16[2,32,4096]{2,1,0:T(8,128)(2,1)} %get-tuple-element.24) | copy-start | bytes 1572868
  45.0 1.4 %collective-permute-start.9 = (f32[8,865]{1,0:T(8,128)S(1)}, f32[8,865]{1,0:T(8,128)S(1)}, u32[]{:S(2)}, u32[]{:S(2)}) collective-permute-start(f32[8,865]{1,0:T(8,128)S(1)} %dynamic-slice_add_fusion.1), channel_id=1, source_target_pairs={{0,1},{1,0},{2,3},{3,2},{4,5},{5,4},{6,7},{7,6},{8,9},{9,8},{10,11... | collective-permute-start | bytes 83048 | tf_op jit(solution)/shard_map/ppermute | solution.py:146
  45.6 2.9 %copy-start.3 = (bf16[1,32,4096]{2,1,0:T(8,128)(2,1)S(1)}, bf16[1,32,4096]{2,1,0:T(8,128)(2,1)}, u32[]{:S(2)}) copy-start(bf16[1,32,4096]{2,1,0:T(8,128)(2,1)} %shard_map.86) | copy-start | bytes 786436
  45.6 2.9 %copy-start.4 = (bf16[1,32,4096]{2,1,0:T(8,128)(2,1)S(1)}, bf16[1,32,4096]{2,1,0:T(8,128)(2,1)}, u32[]{:S(2)}) copy-start(bf16[1,32,4096]{2,1,0:T(8,128)(2,1)} %shard_map.87) | copy-start | bytes 786436
  46.4 3.9 %collective-permute-start.10 = (f32[8,865]{1,0:T(8,128)S(1)}, f32[8,865]{1,0:T(8,128)S(1)}, u32[]{:S(2)}, u32[]{:S(2)}) collective-permute-start(f32[8,865]{1,0:T(8,128)S(1)} %add.61), channel_id=1, source_target_pairs={{0,2},{1,3},{2,0},{3,1},{4,6},{5,7},{6,4},{7,5},{8,10},{9,11},{10,... | collective-permute-start | bytes 83048 | tf_op jit(solution)/shard_map/ppermute | solution.py:146
  50.3 4.9 %collective-permute-start.11 = (f32[8,865]{1,0:T(8,128)S(1)}, f32[8,865]{1,0:T(8,128)S(1)}, u32[]{:S(2)}, u32[]{:S(2)}) collective-permute-start(f32[8,865]{1,0:T(8,128)S(1)} %add.62), channel_id=1, source_target_pairs={{0,4},{1,5},{2,6},{3,7},{4,0},{5,1},{6,2},{7,3},{8,12},{9,13},{10,... | collective-permute-start | bytes 83048 | tf_op jit(solution)/shard_map/ppermute | solution.py:146
  55.2 0.7 %copy-start.8 = (f32[8,865]{1,0:T(8,128)}, f32[8,865]{1,0:T(8,128)S(1)}, u32[]{:S(2)}) copy-start(f32[8,865]{1,0:T(8,128)S(1)} %add_multiply_fusion) | copy-start | bytes 83044

commit v8 on v7

--- a/solution.py
+++ b/solution.py
@@ -134,11 +134,16 @@
     )(haloed, dpre, mask)
 
 
-def neighbours(first, last, axis):
+def neighbours(first, last, axis, ordered=False):
     peers = lax.axis_size(axis)
-    up = [(i, i + 1) for i in range(peers - 1)]
-    down = [(j, i) for i, j in up]
-    return lax.ppermute(last, axis, up), lax.ppermute(first, axis, down)
+    odd = lax.axis_index(axis) % 2 == 1
+    pairs = [(i, i + 1) for i in range(1, peers - 1, 2)]
+    within_send = jnp.where(odd, first, last)
+    across = lax.ppermute(jnp.where(odd, last, first), axis, pairs + [(j, i) for i, j in pairs])
+    if ordered:
+        within_send, across = lax.optimization_barrier((within_send, across))
+    within = swap(within_send, axis, 1)
+    return jnp.where(odd, within, across), jnp.where(odd, across, within)
 
 
 def swap(value, axis, bit):
@@ -210,7 +215,7 @@
     def unflat(value):
         return value.reshape(planes, value.shape[1], rows, depth).transpose(1, 0, 2, 3)
 
-    below, above = neighbours(field[:, :1], field[:, planes - 1 :], "strike")
+    below, above = neighbours(field[:, :1], field[:, planes - 1 :], "strike", ordered=True)
     haloed = jnp.concatenate([below, field, above], axis=1)
     haloed = haloed.transpose(1, 0, 2, 3).reshape(planes + 2, chans, lanes)
     act, dpre, first, last = forward_call(

time: 56.3 us -> 57.7 us (1.025)
  other arithmetic: 0.96 us -> 4.02 us
  starting transfers between devices: 23.9 us -> 22.3 us
    ppermute x4 -> x2, starting transfers between devices: 10.6 us -> 1.35 us  [neighbours(): lax.ppermute(jnp.where(odd, last, first), axis, pairs + [(j, i) for i, j...]
    ppermute x8 -> x10, starting transfers between devices: 13.3 us -> 20.9 us  [swap(): return lax.ppermute(value, axis, [(i, i ^ bit) for i in range(peers)])]
    select_n x0 -> x4, other arithmetic: none -> 3.07 us  [the longest x2 2.2 us: neighbours(): jnp.where(odd, last, first)]
    ppermute x4 -> x2, waiting for transfers between devices: 1.21 us -> 0.01 us  [neighbours(): lax.ppermute(jnp.where(odd, last, first), axis, pairs + [(j, i) for i, j...]
    ppermute x8 -> x10, waiting for transfers between devices: 3.23 us -> 4.38 us  [swap(): return lax.ppermute(value, axis, [(i, i ^ bit) for i in range(peers)])]
    slice x1 -> x0, local copies, waits for them, and re-layouts: 1.13 us -> none  [local(): below, above = neighbours(field[:, :1], field[:, planes - 1:], 'strike')]
    unnamed x24 -> x20, local copies, waits for them, and re-layouts: 1.56 us -> 2.55 us
  transfers between devices with their start and end apart: 12 -> 12, of which waited for: 4 -> 3; matrix products, arithmetic and copies ran while one was open for 13% -> 13% of each run, Pallas kernels for 18% -> 17%
where the time goes in v8:
time: 57.7 us; the launch traced here: 57.2 us
  starting transfers between devices  22.3 us (39%)
  Pallas kernels  14.9 us (26%)
  local copies, waits for them, and re-layouts  10.7 us (19%)
  waiting for transfers between devices  4.39 us (8%)
  other arithmetic  4.02 us (7%)
  between operations  0.88 us (2%)
    ppermute x10, starting transfers between devices, swap(): return lax.ppermute(value, axis, [(i, i ^ bit) for i in range(peers)])  20.9 us
    pallas_call x2, Pallas kernels, input_call(): pl.pallas_call(functools.partial(_input_kernel, planes=planes, first=firs...  6.13 us
    pallas_call x1, Pallas kernels, forward_call(): pl.pallas_call(functools.partial(_forward_kernel, planes=planes, depth=de...  5.04 us
    ppermute x10, waiting for transfers between devices, swap(): return lax.ppermute(value, axis, [(i, i ^ bit) for i in range(peers)])  4.38 us
    pallas_call x1, Pallas kernels, weight_call(): pl.pallas_call(functools.partial(_weight_kernel, planes=planes, depth=dep...  3.74 us
    unnamed x20, local copies, waits for them, and re-layouts  2.55 us
    select_n x2, other arithmetic, neighbours(): jnp.where(odd, last, first)  2.2 us
    reshape x2, local copies, waits for them, and re-layouts, local(): haloed = haloed.transpose(1, 0, 2, 3).reshape(planes + 2, chans, lanes)  1.86 us
  transfers between devices with their start and end apart: 12, of which 3 were waited for; matrix products, arithmetic and copies ran while one was open for 13% of the time, Pallas kernels for 17%

profile of v8, /device:TPU:0, one launch (start us, length us, event | category | flops | bytes accessed | tf_op | source)
XLA Modules:
  0.0 57.2 jit_solution(7842121005678877727)
XLA Ops:
  0.6 0.0 copy-start.8
  0.6 0.6 %copy-done.8 = bf16[8]{0:T(256)(128)(2,1)S(1)} copy-done((bf16[8]{0:T(256)(128)(2,1)S(1)}, bf16[8]{0:T(256)(128)(2,1)}, u32[]{:S(2)}) %copy-start.8) | copy-done | bytes 40
  1.3 0.1 copy.17
  1.4 0.0 copy-start.7
  1.4 0.7 %copy-done.7 = bf16[8,864]{1,0:T(8,128)(2,1)S(1)} copy-done((bf16[8,864]{1,0:T(8,128)(2,1)S(1)}, bf16[8,864]{1,0:T(8,128)(2,1)}, u32[]{:S(2)}) %copy-start.7) | copy-done | bytes 13848
  2.1 0.1 bitcast_dynamic-update-slice_fusion.3
  2.2 3.0 %collective-permute-start.3 = (bf16[8,865]{1,0:T(8,128)(2,1)S(1)}, bf16[8,865]{1,0:T(8,128)(2,1)S(1)}, u32[]{:S(2)}, u32[]{:S(2)}) collective-permute-start(bf16[8,865]{1,0:T(8,128)(2,1)S(1)} %get-tuple-element.49), channel_id=1, source_target_pairs={{0,16},{8,24},{16,0},{24,8},{1,17},{9,25},{17,1},{25,9},{2,18},{10... | collective-permute-start | bytes 41528 | tf_op jit(solution)/shard_map/ppermute | solution.py:151
  5.2 1.5 %collective-permute-start.2 = (bf16[8,865]{1,0:T(8,128)(2,1)S(1)}, bf16[8,865]{1,0:T(8,128)(2,1)S(1)}, u32[]{:S(2)}, u32[]{:S(2)}) collective-permute-start(bf16[8,865]{1,0:T(8,128)(2,1)S(1)} %get-tuple-element.49), channel_id=1, source_target_pairs={{0,8},{8,0},{16,24},{24,16},{1,9},{9,1},{17,25},{25,17},{2,10},{10... | collective-permute-start | bytes 41528 | tf_op jit(solution)/shard_map/ppermute | solution.py:151
  6.6 0.0 collective-permute-start.4
  6.7 1.1 %broadcast_select_fusion.6 = (bf16[32,1,32,128]{3,2,1,0:T(8,128)(2,1)S(1)}, bf16[32,1,32,128]{3,2,1,0:T(8,128)(2,1)S(1)}) fusion(pred[]{:T(512)S(6)} %eq.9, bf16[32,2,32,128]{3,2,1,0:T(8,128)(2,1)} %bitcast.57), kind=kLoop, calls=%fused_computation.11 | loop fusion | flops 262144 | bytes 1048577 | tf_op jit(solution)/shard_map/jit(_where)/select_n | solution.py:142
  7.8 0.7 %collective-permute-start = (bf16[32,1,32,128]{3,2,1,0:T(8,128)(2,1)S(1)}, bf16[32,1,32,128]{3,2,1,0:T(8,128)(2,1)S(1)}, u32[]{:S(2)}, u32[]{:S(2)}) collective-permute-start(bf16[32,1,32,128]{3,2,1,0:T(8,128)(2,1)S(1)} %get-tuple-element.56), channel_id=1, source_target_pairs={{1,2},{3,4},{5,6},{2,1},{4,3},{6,5},{9,10},{11,12},{13,14},{10,9},... | collective-permute-start | bytes 786440 | tf_op jit(solution)/shard_map/ppermute | solution.py:142
  8.6 0.0 copy-done.3
  8.6 0.1 reshape.41
  8.7 1.1 %copy.24.cot = bf16[2,32,4096]{2,1,0:T(8,128)(2,1)} copy(bf16[2,32,4096]{2,0,1:T(2,128)(2,1)S(1)} %reshape.41) | data formatting | bytes 1048576 | tf_op jit(solution)/shard_map/reshape | solution.py:213
  9.8 0.0 collective-permute-done.2
  9.8 0.0 collective-permute-done.3
  9.8 0.0 collective-permute-done
  9.8 6.1 %collective-permute-start.1 = (bf16[32,1,32,128]{3,2,1,0:T(8,128)(2,1)S(1)}, bf16[32,1,32,128]{3,2,1,0:T(8,128)(2,1)S(1)}, u32[]{:S(2)}, u32[]{:S(2)}) collective-permute-start(bf16[32,1,32,128]{3,2,1,0:T(8,128)(2,1)S(1)} %get-tuple-element.26), channel_id=1, source_target_pairs={{0,1},{1,0},{2,3},{3,2},{4,5},{5,4},{6,7},{7,6},{8,9},{9,8},{10,11... | collective-permute-start | bytes 786440 | tf_op jit(solution)/shard_map/ppermute | solution.py:151
  15.9 0.0 collective-permute-done.4
  15.9 0.2 reshape.34
  16.1 0.1 copy.18
  16.3 0.8 %reshape.35.wall = bf16[288,96]{1,0:T(8,128)(2,1)} reshape(bf16[3,3,32,3,32]{4,3,2,1,0:T(4,128)(2,1)S(1)} %copy.18) | data formatting | bytes 110592 | tf_op jit(solution)/shard_map/reshape | solution.py:208
  17.1 0.7 %slice_convert_fusion.bias = f32[32,1]{1,0:T(8,128)} fusion(bf16[32,865]{1,0:T(8,128)(2,1)S(1)} %bitcast.62), kind=kLoop, calls=%fused_computation.21 | loop fusion | flops 32 | bytes 192 | tf_op jit(solution)/shard_map/convert_element_type | solution.py:222
  17.8 0.0 collective-permute-done.1
  17.8 1.0 %copy-done = bf16[1,32,2,32,128]{4,3,2,1,0:T(8,128)(2,1)S(1)} copy-done((bf16[1,32,2,32,128]{4,3,2,1,0:T(8,128)(2,1)S(1)}, bf16[1,32,2,32,128]{4,3,2,1,0:T(8,128)(2,1)}, u32[]{:S(2)}) %copy-start) | copy-done | bytes 524312
  18.8 0.1 maximum_bitcast_fusion
  18.9 0.3 reshape.40
  19.2 1.6 %copy.23.haloed = bf16[4,32,4096]{2,1,0:T(8,128)(2,1)} copy(bf16[4,32,4096]{2,0,1:T(4,128)(2,1)S(1)} %reshape.40) | data formatting | bytes 2097152 | tf_op jit(solution)/shard_map/reshape | solution.py:220
  20.8 5.0 %shard_map.84 = (bf16[2,32,4096]{2,1,0:T(8,128)(2,1)}, bf16[2,32,4096]{2,1,0:T(8,128)(2,1)}, bf16[1,32,4096]{2,1,0:T(8,128)(2,1)}, bf16[1,32,4096]{2,1,0:T(8,128)(2,1)}) custom-call(bf16[4,32,4096]{2,1,0:T(8,128)(2,1)} %copy.23.haloed, bf16[288,96]{1,0:T(8,128)(2,1)} %reshape.35.wall, f32[32,1]{1,0:T(8,128)} %slice_convert_fusion.bias, ...), custom_call_target="tpu_custom_call" | custom-call | flops 452984832 | bytes 2621440 | tf_op jit(solution)/shard_map/pallas_call | solution.py:104
  25.8 1.1 %broadcast_select_fusion.2 = (bf16[1,32,4096]{2,1,0:T(8,128)(2,1)S(1)}, bf16[1,32,4096]{2,1,0:T(8,128)(2,1)S(1)}) fusion(bf16[1,32,4096]{2,1,0:T(8,128)(2,1)} %get-tuple-element.31, bf16[1,32,4096]{2,1,0:T(8,128)(2,1)} %get-tuple-element.30, pred[]{:T(512)S(6)} %eq.9), kind=kLoop, calls=%fused_computation.7 | loop fusion | flops 262144 | bytes 1048577 | tf_op jit(solution)/shard_map/jit(_where)/select_n | solution.py:142
  26.9 0.7 %collective-permute-start.6 = (bf16[1,32,4096]{2,1,0:T(8,128)(2,1)S(1)}, bf16[1,32,4096]{2,1,0:T(8,128)(2,1)S(1)}, u32[]{:S(2)}, u32[]{:S(2)}) collective-permute-start(bf16[1,32,4096]{2,1,0:T(8,128)(2,1)S(1)} %get-tuple-element.52), channel_id=1, source_target_pairs={{1,2},{3,4},{5,6},{2,1},{4,3},{6,5},{9,10},{11,12},{13,14},{10,9},... | collective-permute-start | bytes 786440 | tf_op jit(solution)/shard_map/ppermute | solution.py:142
  27.6 3.1 %collective-permute-start.5 = (bf16[1,32,4096]{2,1,0:T(8,128)(2,1)S(1)}, bf16[1,32,4096]{2,1,0:T(8,128)(2,1)S(1)}, u32[]{:S(2)}, u32[]{:S(2)}) collective-permute-start(bf16[1,32,4096]{2,1,0:T(8,128)(2,1)S(1)} %get-tuple-element.53), channel_id=1, source_target_pairs={{0,1},{1,0},{2,3},{3,2},{4,5},{5,4},{6,7},{7,6},{8,9},{9,8},{10,11... | collective-permute-start | bytes 786440 | tf_op jit(solution)/shard_map/ppermute | solution.py:151
  30.7 0.1 reverse_bitcast_fusion
  30.8 0.3 copy.21
  31.1 0.8 %reshape.38.wall = bf16[288,96]{1,0:T(8,128)(2,1)} reshape(bf16[3,3,32,3,32]{4,3,2,1,0:T(4,128)(2,1)S(1)} %copy.21) | data formatting | bytes 110592 | tf_op jit(solution)/shard_map/reshape | solution.py:209
  31.9 3.7 %shard_map.85 = f32[32,865]{1,0:T(8,128)} custom-call(bf16[4,32,4096]{2,1,0:T(8,128)(2,1)} %copy.23.haloed, bf16[2,32,4096]{2,1,0:T(8,128)(2,1)} %get-tuple-element.42.dpre.mid, f32[9,1,4096]{2,1,0:T(1,128)} %constant.77.clone.mask), custom_call_target="tpu_custom_call" | custom-call | flops 452984832 | bytes 1572864 | tf_op jit(solution)/shard_map/pallas_call | solution.py:128
  35.7 0.8 %constant_dynamic-slice_fusion.1 = f32[16,865]{1,0:T(8,128)S(1)} fusion(f32[32,865]{1,0:T(8,128)} %shard_map.85, s32[]{:T(128)S(6)} %select_n.99), kind=kLoop, calls=%fused_computation.24 | loop fusion | bytes 110724 | tf_op jit(solution)/shard_map/dynamic_slice | solution.py:181
  36.5 0.0 collective-permute-done.6
  36.5 0.0 collective-permute-done.5
  36.5 0.8 %broadcast_select_fusion = (bf16[1,32,4096]{2,1,0:T(8,128)(2,1)}, bf16[1,32,4096]{2,1,0:T(8,128)(2,1)}) fusion(bf16[1,32,4096]{2,1,0:T(8,128)(2,1)S(1)} %collective-permute-done.6, bf16[1,32,4096]{2,1,0:T(8,128)(2,1)S(1)} %collective-permute-done.5, pred[]{:T(512)S(6)} %eq.9), kind=kLoop, calls=%fused_computation.5 | loop fusion | flops 262144 | bytes 1048577 | tf_op jit(solution)/shard_map/jit(_where)/select_n | solution.py:146
  37.3 1.5 %collective-permute-start.7 = (f32[16,865]{1,0:T(8,128)S(1)}, f32[16,865]{1,0:T(8,128)S(1)}, u32[]{:S(2)}, u32[]{:S(2)}) collective-permute-start(f32[16,865]{1,0:T(8,128)S(1)} %constant_dynamic-slice_fusion.1), channel_id=1, source_target_pairs={{0,16},{8,24},{16,0},{24,8},{1,17},{9,25},{17,1},{25,9},{2,18},{10... | collective-permute-start | bytes 166088 | tf_op jit(solution)/shard_map/ppermute | solution.py:151
  38.8 3.1 %shard_map.86 = bf16[1,32,4096]{2,1,0:T(8,128)(2,1)} custom-call(bf16[1,32,4096]{2,1,0:T(8,128)(2,1)} %get-tuple-element.41.lo, bf16[2,32,4096]{2,1,0:T(8,128)(2,1)} %get-tuple-element.42.dpre.mid, bf16[1,32,4096]{2,1,0:T(8,128)(2,1)} %get-tuple-element.43.hi, bf16[288,96]{1,0:T(8,128)(2,1)} %reshape.38.wall, f32[9,1,4096]{2,1,0:T(1,128)} %constant.77.clone.mask), custom_call_target="tpu_custom_call" | custom-call | flops 226492416 | bytes 1572864 | tf_op jit(solution)/shard_map/pallas_call | solution.py:116
  41.9 0.0 collective-permute-done.7
  41.9 0.0 copy-done.5
  41.9 1.6 %collective-permute-start.8 = (f32[8,865]{1,0:T(8,128)S(1)}, f32[8,865]{1,0:T(8,128)S(1)}, u32[]{:S(2)}, u32[]{:S(2)}) collective-permute-start(f32[8,865]{1,0:T(8,128)S(1)} %constant_dynamic-slice_fusion), channel_id=1, source_target_pairs={{0,8},{8,0},{16,24},{24,16},{1,9},{9,1},{17,25},{25,17},{2,10},{10... | collective-permute-start | bytes 83048 | tf_op jit(solution)/shard_map/ppermute | solution.py:151
  43.5 3.1 %shard_map.87 = bf16[1,32,4096]{2,1,0:T(8,128)(2,1)} custom-call(bf16[1,32,4096]{2,1,0:T(8,128)(2,1)} %get-tuple-element.41.lo, bf16[2,32,4096]{2,1,0:T(8,128)(2,1)} %get-tuple-element.42.dpre.mid, bf16[1,32,4096]{2,1,0:T(8,128)(2,1)} %get-tuple-element.43.hi, bf16[288,96]{1,0:T(8,128)(2,1)} %reshape.38.wall, f32[9,1,4096]{2,1,0:T(1,128)} %constant.77.clone.mask), custom_call_target="tpu_custom_call" | custom-call | flops 226492416 | bytes 1572864 | tf_op jit(solution)/shard_map/pallas_call | solution.py:116
  46.6 0.0 collective-permute-done.8
  46.6 0.1 collective-permute-start.9
  46.7 0.0 copy-done.4
  46.7 0.0 copy-start.1
  46.7 0.0 copy-start.2
  46.7 0.1 copy.25
  46.8 1.1 %collective-permute-done.9 = f32[8,865]{1,0:T(8,128)S(1)} collective-permute-done((f32[8,865]{1,0:T(8,128)S(1)}, f32[8,865]{1,0:T(8,128)S(1)}, u32[]{:S(2)}, u32[]{:S(2)}) %collective-permute-start.9) | collective-permute-done | bytes 27712 | tf_op jit(solution)/shard_map/ppermute | solution.py:151
  47.9 1.6 %collective-permute-start.10 = (f32[8,865]{1,0:T(8,128)S(1)}, f32[8,865]{1,0:T(8,128)S(1)}, u32[]{:S(2)}, u32[]{:S(2)}) collective-permute-start(f32[8,865]{1,0:T(8,128)S(1)} %add.66), channel_id=1, source_target_pairs={{0,2},{1,3},{2,0},{3,1},{4,6},{5,7},{6,4},{7,5},{8,10},{9,11},{10,... | collective-permute-start | bytes 83048 | tf_op jit(solution)/shard_map/ppermute | solution.py:151
  49.4 0.0 copy-done.1
  49.4 0.0 copy-done.2
  49.4 0.1 pad_maximum_fusion
  49.5 0.1 copy.26
  49.6 2.1 %collective-permute-done.10 = f32[8,865]{1,0:T(8,128)S(1)} collective-permute-done((f32[8,865]{1,0:T(8,128)S(1)}, f32[8,865]{1,0:T(8,128)S(1)}, u32[]{:S(2)}, u32[]{:S(2)}) %collective-permute-start.10) | collective-permute-done | bytes 27712 | tf_op jit(solution)/shard_map/ppermute | solution.py:151
  51.7 2.5 %collective-permute-start.11 = (f32[8,865]{1,0:T(8,128)S(1)}, f32[8,865]{1,0:T(8,128)S(1)}, u32[]{:S(2)}, u32[]{:S(2)}) collective-permute-start(f32[8,865]{1,0:T(8,128)S(1)} %add.67), channel_id=1, source_target_pairs={{0,4},{1,5},{2,6},{3,7},{4,0},{5,1},{6,2},{7,3},{8,12},{9,13},{10,... | collective-permute-start | bytes 83048 | tf_op jit(solution)/shard_map/ppermute | solution.py:151
  54.2 1.1 %copy_bitcast_fusion = (bf16[1,32,2,32,128]{4,3,2,1,0:T(8,128)(2,1)}, bf16[1,32,2,32,128]{4,3,2,1,0:T(8,128)(2,1)}) fusion(bf16[2,32,32,128]{3,2,1,0:T(8,128)(2,1)S(1)} %bitcast.55, bf16[2,32,32,128]{3,2,1,0:T(8,128)(2,1)S(1)} %bitcast.56), kind=kLoop, calls=%fused_computation.2 | loop fusion | bytes 2097152 | tf_op jit(solution)/shard_map/broadcast_in_dim | solution.py:235
  55.3 1.2 %collective-permute-done.11 = f32[8,865]{1,0:T(8,128)S(1)} collective-permute-done((f32[8,865]{1,0:T(8,128)S(1)}, f32[8,865]{1,0:T(8,128)S(1)}, u32[]{:S(2)}, u32[]{:S(2)}) %collective-permute-start.11) | collective-permute-done | bytes 27712 | tf_op jit(solution)/shard_map/ppermute | solution.py:151
  56.5 0.7 %slice_reduce_fusion = f32[8]{0:T(128)} fusion(f32[8,865]{1,0:T(8,128)S(1)} %add_multiply_fusion), kind=kLoop, calls=%fused_computation.22 | loop fusion | bytes 64 | tf_op jit(solution)/shard_map/slice | solution.py:235
  57.2 0.0 copy-done.6
  (16 shorter events, 0.1 us)
Async XLA Ops:
  0.6 0.7 %copy-start.8 = (bf16[8]{0:T(256)(128)(2,1)S(1)}, bf16[8]{0:T(256)(128)(2,1)}, u32[]{:S(2)}) copy-start(bf16[8]{0:T(256)(128)(2,1)} %param.8) | copy-start | bytes 52
  1.4 0.7 %copy-start.7 = (bf16[8,864]{1,0:T(8,128)(2,1)S(1)}, bf16[8,864]{1,0:T(8,128)(2,1)}, u32[]{:S(2)}) copy-start(bf16[8,864]{1,0:T(8,128)(2,1)} %param.7) | copy-start | bytes 41476
  2.2 7.6 %collective-permute-start.3 = (bf16[8,865]{1,0:T(8,128)(2,1)S(1)}, bf16[8,865]{1,0:T(8,128)(2,1)S(1)}, u32[]{:S(2)}, u32[]{:S(2)}) collective-permute-start(bf16[8,865]{1,0:T(8,128)(2,1)S(1)} %get-tuple-element.49), channel_id=1, source_target_pairs={{0,16},{8,24},{16,0},{24,8},{1,17},{9,25},{17,1},{25,9},{2,18},{10... | collective-permute-start | bytes 41528 | tf_op jit(solution)/shard_map/ppermute | solution.py:151
  5.2 4.6 %collective-permute-start.2 = (bf16[8,865]{1,0:T(8,128)(2,1)S(1)}, bf16[8,865]{1,0:T(8,128)(2,1)S(1)}, u32[]{:S(2)}, u32[]{:S(2)}) collective-permute-start(bf16[8,865]{1,0:T(8,128)(2,1)S(1)} %get-tuple-element.49), channel_id=1, source_target_pairs={{0,8},{8,0},{16,24},{24,16},{1,9},{9,1},{17,25},{25,17},{2,10},{10... | collective-permute-start | bytes 41528 | tf_op jit(solution)/shard_map/ppermute | solution.py:151
  6.6 9.3 %collective-permute-start.4 = (bf16[8,865]{1,0:T(8,128)(2,1)S(1)}, bf16[8,865]{1,0:T(8,128)(2,1)S(1)}, u32[]{:S(2)}, u32[]{:S(2)}) collective-permute-start(bf16[8,865]{1,0:T(8,128)(2,1)S(1)} %get-tuple-element.49), channel_id=1, source_target_pairs={{0,24},{8,16},{16,8},{24,0},{1,25},{9,17},{17,9},{25,1},{2,26},{10... | collective-permute-start | bytes 41528 | tf_op jit(solution)/shard_map/ppermute | solution.py:151
  6.7 1.9 %copy-start.3 = (bf16[1,32,2,32,128]{4,3,2,1,0:T(8,128)(2,1)S(1)}, bf16[1,32,2,32,128]{4,3,2,1,0:T(8,128)(2,1)}, u32[]{:S(2)}) copy-start(bf16[1,32,2,32,128]{4,3,2,1,0:T(8,128)(2,1)} %param.6) | copy-start | bytes 1572868
  7.8 2.0 %collective-permute-start = (bf16[32,1,32,128]{3,2,1,0:T(8,128)(2,1)S(1)}, bf16[32,1,32,128]{3,2,1,0:T(8,128)(2,1)S(1)}, u32[]{:S(2)}, u32[]{:S(2)}) collective-permute-start(bf16[32,1,32,128]{3,2,1,0:T(8,128)(2,1)S(1)} %get-tuple-element.56), channel_id=1, source_target_pairs={{1,2},{3,4},{5,6},{2,1},{4,3},{6,5},{9,10},{11,12},{13,14},{10,9},... | collective-permute-start | bytes 786440 | tf_op jit(solution)/shard_map/ppermute | solution.py:142
  9.8 7.9 %collective-permute-start.1 = (bf16[32,1,32,128]{3,2,1,0:T(8,128)(2,1)S(1)}, bf16[32,1,32,128]{3,2,1,0:T(8,128)(2,1)S(1)}, u32[]{:S(2)}, u32[]{:S(2)}) collective-permute-start(bf16[32,1,32,128]{3,2,1,0:T(8,128)(2,1)S(1)} %get-tuple-element.26), channel_id=1, source_target_pairs={{0,1},{1,0},{2,3},{3,2},{4,5},{5,4},{6,7},{7,6},{8,9},{9,8},{10,11... | collective-permute-start | bytes 786440 | tf_op jit(solution)/shard_map/ppermute | solution.py:151
  17.8 1.0 %copy-start = (bf16[1,32,2,32,128]{4,3,2,1,0:T(8,128)(2,1)S(1)}, bf16[1,32,2,32,128]{4,3,2,1,0:T(8,128)(2,1)}, u32[]{:S(2)}) copy-start(bf16[1,32,2,32,128]{4,3,2,1,0:T(8,128)(2,1)} %param.5) | copy-start | bytes 1572868
  26.9 9.6 %collective-permute-start.6 = (bf16[1,32,4096]{2,1,0:T(8,128)(2,1)S(1)}, bf16[1,32,4096]{2,1,0:T(8,128)(2,1)S(1)}, u32[]{:S(2)}, u32[]{:S(2)}) collective-permute-start(bf16[1,32,4096]{2,1,0:T(8,128)(2,1)S(1)} %get-tuple-element.52), channel_id=1, source_target_pairs={{1,2},{3,4},{5,6},{2,1},{4,3},{6,5},{9,10},{11,12},{13,14},{10,9},... | collective-permute-start | bytes 786440 | tf_op jit(solution)/shard_map/ppermute | solution.py:142
  27.6 8.9 %collective-permute-start.5 = (bf16[1,32,4096]{2,1,0:T(8,128)(2,1)S(1)}, bf16[1,32,4096]{2,1,0:T(8,128)(2,1)S(1)}, u32[]{:S(2)}, u32[]{:S(2)}) collective-permute-start(bf16[1,32,4096]{2,1,0:T(8,128)(2,1)S(1)} %get-tuple-element.53), channel_id=1, source_target_pairs={{0,1},{1,0},{2,3},{3,2},{4,5},{5,4},{6,7},{7,6},{8,9},{9,8},{10,11... | collective-permute-start | bytes 786440 | tf_op jit(solution)/shard_map/ppermute | solution.py:151
  37.3 4.6 %collective-permute-start.7 = (f32[16,865]{1,0:T(8,128)S(1)}, f32[16,865]{1,0:T(8,128)S(1)}, u32[]{:S(2)}, u32[]{:S(2)}) collective-permute-start(f32[16,865]{1,0:T(8,128)S(1)} %constant_dynamic-slice_fusion.1), channel_id=1, source_target_pairs={{0,16},{8,24},{16,0},{24,8},{1,17},{9,25},{17,1},{25,9},{2,18},{10... | collective-permute-start | bytes 166088 | tf_op jit(solution)/shard_map/ppermute | solution.py:151
  38.8 3.1 %copy-start.5 = (f32[32,865]{1,0:T(8,128)S(1)}, f32[32,865]{1,0:T(8,128)}, u32[]{:S(2)}) copy-start(f32[32,865]{1,0:T(8,128)} %shard_map.85) | copy-start | bytes 332164
  41.9 4.6 %collective-permute-start.8 = (f32[8,865]{1,0:T(8,128)S(1)}, f32[8,865]{1,0:T(8,128)S(1)}, u32[]{:S(2)}, u32[]{:S(2)}) collective-permute-start(f32[8,865]{1,0:T(8,128)S(1)} %constant_dynamic-slice_fusion), channel_id=1, source_target_pairs={{0,8},{8,0},{16,24},{24,16},{1,9},{9,1},{17,25},{25,17},{2,10},{10... | collective-permute-start | bytes 83048 | tf_op jit(solution)/shard_map/ppermute | solution.py:151
  43.5 3.2 %copy-start.4 = (bf16[2,32,4096]{2,1,0:T(8,128)(2,1)S(1)}, bf16[2,32,4096]{2,1,0:T(8,128)(2,1)}, u32[]{:S(2)}) copy-start(bf16[2,32,4096]{2,1,0:T(8,128)(2,1)} %get-tuple-element.28) | copy-start | bytes 1572868
  46.6 1.3 %collective-permute-start.9 = (f32[8,865]{1,0:T(8,128)S(1)}, f32[8,865]{1,0:T(8,128)S(1)}, u32[]{:S(2)}, u32[]{:S(2)}) collective-permute-start(f32[8,865]{1,0:T(8,128)S(1)} %dynamic-slice_add_fusion.1), channel_id=1, source_target_pairs={{0,1},{1,0},{2,3},{3,2},{4,5},{5,4},{6,7},{7,6},{8,9},{9,8},{10,11... | collective-permute-start | bytes 83048 | tf_op jit(solution)/shard_map/ppermute | solution.py:151
  46.7 2.8 %copy-start.1 = (bf16[1,32,4096]{2,1,0:T(8,128)(2,1)S(1)}, bf16[1,32,4096]{2,1,0:T(8,128)(2,1)}, u32[]{:S(2)}) copy-start(bf16[1,32,4096]{2,1,0:T(8,128)(2,1)} %shard_map.86) | copy-start | bytes 786436
  46.7 2.8 %copy-start.2 = (bf16[1,32,4096]{2,1,0:T(8,128)(2,1)S(1)}, bf16[1,32,4096]{2,1,0:T(8,128)(2,1)}, u32[]{:S(2)}) copy-start(bf16[1,32,4096]{2,1,0:T(8,128)(2,1)} %shard_map.87) | copy-start | bytes 786436
  47.9 3.9 %collective-permute-start.10 = (f32[8,865]{1,0:T(8,128)S(1)}, f32[8,865]{1,0:T(8,128)S(1)}, u32[]{:S(2)}, u32[]{:S(2)}) collective-permute-start(f32[8,865]{1,0:T(8,128)S(1)} %add.66), channel_id=1, source_target_pairs={{0,2},{1,3},{2,0},{3,1},{4,6},{5,7},{6,4},{7,5},{8,10},{9,11},{10,... | collective-permute-start | bytes 83048 | tf_op jit(solution)/shard_map/ppermute | solution.py:151
  51.7 4.8 %collective-permute-start.11 = (f32[8,865]{1,0:T(8,128)S(1)}, f32[8,865]{1,0:T(8,128)S(1)}, u32[]{:S(2)}, u32[]{:S(2)}) collective-permute-start(f32[8,865]{1,0:T(8,128)S(1)} %add.67), channel_id=1, source_target_pairs={{0,4},{1,5},{2,6},{3,7},{4,0},{5,1},{6,2},{7,3},{8,12},{9,13},{10,... | collective-permute-start | bytes 83048 | tf_op jit(solution)/shard_map/ppermute | solution.py:151
  56.5 0.7 %copy-start.6 = (f32[8,865]{1,0:T(8,128)}, f32[8,865]{1,0:T(8,128)S(1)}, u32[]{:S(2)}) copy-start(f32[8,865]{1,0:T(8,128)S(1)} %add_multiply_fusion) | copy-start | bytes 83044

commit v9 on v7

--- a/solution.py
+++ b/solution.py
@@ -44,11 +44,12 @@
     return total
 
 
-def _forward_kernel(haloed, wall, bias, cot, mask, act_out, dpre_out, first_out, last_out, *, planes, depth):
+def _forward_kernel(haloed, wall, packed, cot, mask, act_out, dpre_out, first_out, last_out, *, planes, depth):
     chans, lanes = haloed.shape[1], haloed.shape[2]
+    bias = packed[:, packed.shape[1] - 1 :].astype(jnp.float32)
     for p in range(planes):
         y = jnp.dot(wall[...], _stacked(haloed, p), preferred_element_type=jnp.float32)
-        pre = _shifted_sum(y, mask, chans, lanes, depth, 1) + bias[...]
+        pre = _shifted_sum(y, mask, chans, lanes, depth, 1) + bias
         sig = 1.0 / (1.0 + jnp.exp(-pre))
         act_out[p] = (pre * sig).astype(act_out.dtype)
         dpre = (cot[p].astype(jnp.float32) * sig * (1.0 + pre * (1.0 - sig))).astype(dpre_out.dtype)
@@ -96,7 +97,7 @@
     return [pl.BlockSpec(memory_space=pltpu.VMEM)] * n
 
 
-def forward_call(haloed, wall, bias, cot, mask, depth):
+def forward_call(haloed, wall, packed, cot, mask, depth):
     planes, chans, lanes = cot.shape
     shape = jax.ShapeDtypeStruct(cot.shape, jnp.bfloat16)
     edge = jax.ShapeDtypeStruct((1, chans, lanes), jnp.bfloat16)
@@ -107,7 +108,7 @@
         in_specs=_vmem(5),
         out_specs=tuple(_vmem(4)),
         cost_estimate=pl.CostEstimate(flops=flops, transcendentals=planes * chans * lanes, bytes_accessed=5 * cot.size * 2),
-    )(haloed, wall, bias, cot, mask)
+    )(haloed, wall, packed, cot, mask)
 
 
 def input_call(lo, mid, hi, wall, mask, depth, first, count):
@@ -156,7 +157,7 @@
     return blocks.reshape((peers * value.shape[0],) + value.shape[1:])
 
 
-def reduce_beside(local_grads, work):
+def reduce_beside(value, carry, jobs):
     rounds = []
     bit = lax.axis_size("real") // 2
     while bit >= 1:
@@ -166,8 +167,6 @@
     while bit < lax.axis_size("strike"):
         rounds.append(("strike", bit))
         bit *= 2
-    results = []
-    value = local_grads
     for k, (axis, bit) in enumerate(rounds):
         if axis == "real":
             half = value.shape[0] // 2
@@ -176,18 +175,17 @@
             send = lax.dynamic_slice_in_dim(value, (1 - upper) * half, half, 0)
         else:
             keep, send = value, value
-        if k < len(work):
-            send, inputs = lax.optimization_barrier((send, work[k][1]))
+        if k < len(jobs):
+            send, carry = lax.optimization_barrier((send, carry))
             received = swap(send, axis, bit)
-            result = work[k][0](*inputs)
-            received, result = lax.optimization_barrier((received, result))
-            results.append(result)
+            carry = jobs[k](carry)
+            received, carry = lax.optimization_barrier((received, carry))
         else:
             received = swap(send, axis, bit)
         value = keep + received
-    for job, inputs in work[len(rounds) :]:
-        results.append(job(*inputs))
-    return value, results
+    for job in jobs[len(rounds) :]:
+        carry = job(carry)
+    return value, carry
 
 
 def local(grades, cotangent, weight, bias):
@@ -197,11 +195,10 @@
     taps_in = weight.shape[1]
     packed = jnp.concatenate([weight, bias[:, None]], axis=1)
     whole = gather_rows(packed, "real")
-    whole_weight, whole_bias = whole[:, :taps_in], whole[:, taps_in]
+    whole_weight = whole[:, :taps_in]
     out_chan = whole_weight.shape[0]
     w5 = whole_weight.reshape(out_chan, 3, 3, 3, chans)
     forward_w = w5.transpose(2, 3, 0, 1, 4).reshape(9 * out_chan, 3 * chans)
-    backward_w = w5[:, ::-1].transpose(2, 3, 4, 1, 0).reshape(9 * chans, 3 * out_chan)
     mask = jnp.asarray(plane_masks(rows, depth))
 
     def flat(value):
@@ -214,16 +211,24 @@
     haloed = jnp.concatenate([below, field, above], axis=1)
     haloed = haloed.transpose(1, 0, 2, 3).reshape(planes + 2, chans, lanes)
     act, dpre, first, last = forward_call(
-        haloed, forward_w, whole_bias.astype(jnp.float32)[:, None], flat(cotangent[0]), mask, depth
+        haloed, forward_w, whole, flat(cotangent[0]), mask, depth
     )
     dlo, dhi = neighbours(first, last, "strike")
     local_grads = weight_call(haloed, dpre, mask, depth)
-    work = [
-        (functools.partial(input_call, depth=depth, first=p, count=1), (dlo, dpre, dhi, backward_w, mask))
-        for p in range(planes)
-    ]
-    owned, pieces = reduce_beside(local_grads, work)
-    grad_input = unflat(jnp.concatenate(pieces, axis=0))
+
+    def plane_job(p, first_job):
+        def job(carry):
+            lo_d, mid_d, hi_d, weights = carry[:4]
+            if first_job:
+                weights = weights.reshape(out_chan, 3, 3, 3, chans)[:, ::-1]
+                weights = weights.transpose(2, 3, 4, 1, 0).reshape(9 * chans, 3 * out_chan)
+            piece = input_call(lo_d, mid_d, hi_d, weights, mask, depth=depth, first=p, count=1)
+            return (lo_d, mid_d, hi_d, weights) + carry[4:] + (piece,)
+        return job
+
+    jobs = [plane_job(p, p == 0) for p in range(planes)]
+    owned, carry = reduce_beside(local_grads, (dlo, dpre, dhi, whole_weight), jobs)
+    grad_input = unflat(jnp.concatenate(carry[4:], axis=0))
     cells = lax.axis_size("real") * lax.axis_size("strike") * planes * rows * depth
     factor = 1.0 / cells**0.5
     owned = owned * factor

time: 56.3 us -> 57.4 us (1.020)
  waiting for transfers between devices: 4.43 us -> 5.5 us
  local copies, waits for them, and re-layouts: 10.8 us -> 11.5 us
  other arithmetic: 0.96 us -> 0.28 us
    ppermute x8, waiting for transfers between devices: 3.23 us -> 3.96 us  [swap(): return lax.ppermute(value, axis, [(i, i ^ bit) for i in range(peers)])]
    convert_element_type x1 -> x0, other arithmetic: 0.68 us -> none  [local(): whole_bias.astype(jnp.float32)[:, None]]
    unnamed x24 -> x28, local copies, waits for them, and re-layouts: 1.56 us -> 1.97 us
  transfers between devices with their start and end apart: 12 -> 12, of which waited for: 4 -> 4; matrix products, arithmetic and copies ran while one was open for 13% -> 12% of each run, Pallas kernels for 18% -> 17%
where the time goes in v9:
time: 57.4 us; the launch traced here: 57 us
  starting transfers between devices  23.8 us (41%)
  Pallas kernels  15 us (26%)
  local copies, waits for them, and re-layouts  11.5 us (20%)
  waiting for transfers between devices  5.5 us (10%)
  between operations  0.93 us (2%)
    ppermute x8, starting transfers between devices, swap(): return lax.ppermute(value, axis, [(i, i ^ bit) for i in range(peers)])  13.2 us
    ppermute x4, starting transfers between devices, neighbours(): return (lax.ppermute(last, axis, up), lax.ppermute(first, axis, down))  10.6 us
    pallas_call x2, Pallas kernels, input_call(): pl.pallas_call(functools.partial(_input_kernel, planes=planes, first=firs...  6.11 us
    pallas_call x1, Pallas kernels, forward_call(): pl.pallas_call(functools.partial(_forward_kernel, planes=planes, depth=de...  5.12 us
    ppermute x8, waiting for transfers between devices, swap(): return lax.ppermute(value, axis, [(i, i ^ bit) for i in range(peers)])  3.96 us
    pallas_call x1, Pallas kernels, weight_call(): pl.pallas_call(functools.partial(_weight_kernel, planes=planes, depth=dep...  3.76 us
    unnamed x28, local copies, waits for them, and re-layouts  1.97 us
    reshape x2, local copies, waits for them, and re-layouts, local(): haloed = haloed.transpose(1, 0, 2, 3).reshape(planes + 2, chans, lanes)  1.87 us
  transfers between devices with their start and end apart: 12, of which 4 were waited for; matrix products, arithmetic and copies ran while one was open for 12% of the time, Pallas kernels for 17%

profile of v9, /device:TPU:0, one launch (start us, length us, event | category | flops | bytes accessed | tf_op | source)
XLA Modules:
  0.0 57.0 jit_solution(7836415623228258865)
XLA Ops:
  0.6 0.0 copy-start.12
  0.6 0.6 %copy-done.12 = bf16[8]{0:T(256)(128)(2,1)S(1)} copy-done((bf16[8]{0:T(256)(128)(2,1)S(1)}, bf16[8]{0:T(256)(128)(2,1)}, u32[]{:S(2)}) %copy-start.12) | copy-done | bytes 40
  1.3 0.1 copy.17
  1.4 0.7 %copy-done.11 = bf16[8,864]{1,0:T(8,128)(2,1)S(1)} copy-done((bf16[8,864]{1,0:T(8,128)(2,1)S(1)}, bf16[8,864]{1,0:T(8,128)(2,1)}, u32[]{:S(2)}) %copy-start.11) | copy-done | bytes 13848
  2.1 0.1 bitcast_dynamic-update-slice_fusion.3
  2.2 2.9 %collective-permute-start.2 = (bf16[8,865]{1,0:T(8,128)(2,1)S(1)}, bf16[8,865]{1,0:T(8,128)(2,1)S(1)}, u32[]{:S(2)}, u32[]{:S(2)}) collective-permute-start(bf16[8,865]{1,0:T(8,128)(2,1)S(1)} %get-tuple-element.53), channel_id=1, source_target_pairs={{0,8},{8,0},{16,24},{24,16},{1,9},{9,1},{17,25},{25,17},{2,10},{10... | collective-permute-start | bytes 41528 | tf_op jit(solution)/shard_map/ppermute | solution.py:147
  5.1 1.5 %collective-permute-start.3 = (bf16[8,865]{1,0:T(8,128)(2,1)S(1)}, bf16[8,865]{1,0:T(8,128)(2,1)S(1)}, u32[]{:S(2)}, u32[]{:S(2)}) collective-permute-start(bf16[8,865]{1,0:T(8,128)(2,1)S(1)} %get-tuple-element.53), channel_id=1, source_target_pairs={{0,16},{8,24},{16,0},{24,8},{1,17},{9,25},{17,1},{25,9},{2,18},{10... | collective-permute-start | bytes 41528 | tf_op jit(solution)/shard_map/ppermute | solution.py:147
  6.6 0.0 collective-permute-start.4
  6.7 1.1 %fusion = (bf16[32,1,32,128]{3,2,1,0:T(8,128)(2,1)S(1)}, bf16[32,1,32,128]{3,2,1,0:T(8,128)(2,1)S(1)}) fusion(bf16[32,2,32,128]{3,2,1,0:T(8,128)(2,1)} %bitcast.54), kind=kLoop, calls=%fused_computation.16 | loop fusion | bytes 1048576 | tf_op jit(solution)/shard_map/slice | solution.py:210
  7.8 1.3 %collective-permute-start = (bf16[32,1,32,128]{3,2,1,0:T(8,128)(2,1)S(1)}, bf16[32,1,32,128]{3,2,1,0:T(8,128)(2,1)S(1)}, u32[]{:S(2)}, u32[]{:S(2)}) collective-permute-start(bf16[32,1,32,128]{3,2,1,0:T(8,128)(2,1)S(1)} %get-tuple-element.54), channel_id=1, source_target_pairs={{0,1},{1,2},{2,3},{3,4},{4,5},{5,6},{6,7},{8,9},{9,10},{10,11},{11... | collective-permute-start | bytes 786440 | tf_op jit(solution)/shard_map/ppermute | solution.py:142
  9.1 1.3 %collective-permute-start.1 = (bf16[32,1,32,128]{3,2,1,0:T(8,128)(2,1)S(1)}, bf16[32,1,32,128]{3,2,1,0:T(8,128)(2,1)S(1)}, u32[]{:S(2)}, u32[]{:S(2)}) collective-permute-start(bf16[32,1,32,128]{3,2,1,0:T(8,128)(2,1)S(1)} %get-tuple-element.55), channel_id=1, source_target_pairs={{1,0},{2,1},{3,2},{4,3},{5,4},{6,5},{7,6},{9,8},{10,9},{11,10},{12... | collective-permute-start | bytes 786440 | tf_op jit(solution)/shard_map/ppermute | solution.py:142
  10.4 0.0 copy-done.7
  10.4 0.1 reshape.45
  10.6 1.1 %copy.24.cot = bf16[2,32,4096]{2,1,0:T(8,128)(2,1)} copy(bf16[2,32,4096]{2,0,1:T(2,128)(2,1)S(1)} %reshape.45) | data formatting | bytes 1048576 | tf_op jit(solution)/shard_map/reshape | solution.py:205
  11.6 0.0 collective-permute-done.2
  11.7 0.0 collective-permute-done.3
  11.7 0.0 collective-permute-done.4
  11.7 0.0 copy-start.5
  11.7 0.2 reshape.37
  11.9 0.4 copy-done.5
  12.3 0.1 copy.18
  12.4 0.8 %reshape.38.wall = bf16[288,96]{1,0:T(8,128)(2,1)} reshape(bf16[3,3,32,3,32]{4,3,2,1,0:T(4,128)(2,1)S(1)} %copy.18) | data formatting | bytes 110592 | tf_op jit(solution)/shard_map/reshape | solution.py:201
  13.2 0.0 collective-permute-done
  13.3 1.5 %collective-permute-done.1 = bf16[32,1,32,128]{3,2,1,0:T(8,128)(2,1)S(1)} collective-permute-done((bf16[32,1,32,128]{3,2,1,0:T(8,128)(2,1)S(1)}, bf16[32,1,32,128]{3,2,1,0:T(8,128)(2,1)S(1)}, u32[]{:S(2)}, u32[]{:S(2)}) %collective-permute-start.1) | collective-permute-done | bytes 262176 | tf_op jit(solution)/shard_map/ppermute | solution.py:142
  14.8 0.0 copy-done
  14.8 0.1 maximum_bitcast_fusion
  14.9 0.3 reshape.44
  15.2 1.6 %copy.23.haloed = bf16[4,32,4096]{2,1,0:T(8,128)(2,1)} copy(bf16[4,32,4096]{2,0,1:T(4,128)(2,1)S(1)} %reshape.44) | data formatting | bytes 2097152 | tf_op jit(solution)/shard_map/reshape | solution.py:212
  16.8 5.1 %shard_map.84 = (bf16[2,32,4096]{2,1,0:T(8,128)(2,1)}, bf16[2,32,4096]{2,1,0:T(8,128)(2,1)}, bf16[1,32,4096]{2,1,0:T(8,128)(2,1)}, bf16[1,32,4096]{2,1,0:T(8,128)(2,1)}) custom-call(bf16[4,32,4096]{2,1,0:T(8,128)(2,1)} %copy.23.haloed, bf16[288,96]{1,0:T(8,128)(2,1)} %reshape.38.wall, bf16[32,865]{1,0:T(8,128)(2,1)} %bitcast.60, ...), custom_call_target="tpu_custom_call" | custom-call | flops 452984832 | bytes 2621440 | tf_op jit(solution)/shard_map/pallas_call | solution.py:105
  21.9 6.7 %collective-permute-start.5 = (bf16[1,32,4096]{2,1,0:T(8,128)(2,1)}, bf16[1,32,4096]{2,1,0:T(8,128)(2,1)S(1)}, u32[]{:S(2)}, u32[]{:S(2)}) collective-permute-start(bf16[1,32,4096]{2,1,0:T(8,128)(2,1)} %get-tuple-element.30), channel_id=1, source_target_pairs={{0,1},{1,2},{2,3},{3,4},{4,5},{5,6},{6,7},{8,9},{9,10},{10,11},{11... | collective-permute-start | bytes 786440 | tf_op jit(solution)/shard_map/ppermute | solution.py:142
  28.6 1.3 %collective-permute-start.6 = (bf16[1,32,4096]{2,1,0:T(8,128)(2,1)}, bf16[1,32,4096]{2,1,0:T(8,128)(2,1)S(1)}, u32[]{:S(2)}, u32[]{:S(2)}) collective-permute-start(bf16[1,32,4096]{2,1,0:T(8,128)(2,1)} %get-tuple-element.31), channel_id=1, source_target_pairs={{1,0},{2,1},{3,2},{4,3},{5,4},{6,5},{7,6},{9,8},{10,9},{11,10},{12... | collective-permute-start | bytes 786440 | tf_op jit(solution)/shard_map/ppermute | solution.py:142
  29.9 3.8 %shard_map.85 = f32[32,865]{1,0:T(8,128)} custom-call(bf16[4,32,4096]{2,1,0:T(8,128)(2,1)} %copy.23.haloed, bf16[2,32,4096]{2,1,0:T(8,128)(2,1)} %get-tuple-element.45.dpre.mid, f32[9,1,4096]{2,1,0:T(1,128)} %constant.68.clone.mask), custom_call_target="tpu_custom_call" | custom-call | flops 452984832 | bytes 1572864 | tf_op jit(solution)/shard_map/pallas_call | solution.py:129
  33.7 0.8 %constant_dynamic-slice_fusion.1 = f32[16,865]{1,0:T(8,128)S(1)} fusion(f32[32,865]{1,0:T(8,128)} %shard_map.85, s32[]{:T(128)S(6)} %select_n.48), kind=kLoop, calls=%fused_computation.15 | loop fusion | bytes 110724 | tf_op jit(solution)/shard_map/dynamic_slice | solution.py:175
  34.5 0.0 collective-permute-done.5.lo
  34.6 0.0 collective-permute-done.6.hi
  34.6 0.0 copy-done.6
  34.6 0.0 copy-start.2
  34.6 0.2 reshape.41
  34.8 1.6 %collective-permute-start.7 = (f32[16,865]{1,0:T(8,128)S(1)}, f32[16,865]{1,0:T(8,128)S(1)}, u32[]{:S(2)}, u32[]{:S(2)}) collective-permute-start(f32[16,865]{1,0:T(8,128)S(1)} %constant_dynamic-slice_fusion.1), channel_id=1, source_target_pairs={{0,16},{8,24},{16,0},{24,8},{1,17},{9,25},{17,1},{25,9},{2,18},{10... | collective-permute-start | bytes 166088 | tf_op jit(solution)/shard_map/ppermute | solution.py:147
  36.4 0.1 reverse_bitcast_fusion
  36.5 0.0 copy-done.1
  36.5 0.0 copy-done.2
  36.5 0.3 copy.21
  36.8 0.8 %reshape.42.wall = bf16[288,96]{1,0:T(8,128)(2,1)} reshape(bf16[3,3,32,3,32]{4,3,2,1,0:T(4,128)(2,1)S(1)} %copy.21) | data formatting | bytes 110592 | tf_op jit(solution)/shard_map/reshape | solution.py:224
  37.6 3.0 %shard_map.86 = bf16[1,32,4096]{2,1,0:T(8,128)(2,1)} custom-call(bf16[1,32,4096]{2,1,0:T(8,128)(2,1)} %copy-done.1, bf16[2,32,4096]{2,1,0:T(8,128)(2,1)} %get-tuple-element.45.dpre.mid, bf16[1,32,4096]{2,1,0:T(8,128)(2,1)} %copy-done.2, bf16[288,96]{1,0:T(8,128)(2,1)} %reshape.42.wall, f32[9,1,4096]{2,1,0:T(1,128)} %constant.68.clone.mask), custom_call_target="tpu_custom_call" | custom-call | flops 226492416 | bytes 1572864 | tf_op jit(solution)/shard_map/pallas_call | solution.py:117
  40.6 0.0 collective-permute-done.7
  40.6 0.0 copy-done.9
  40.7 1.6 %collective-permute-start.8 = (f32[8,865]{1,0:T(8,128)S(1)}, f32[8,865]{1,0:T(8,128)S(1)}, u32[]{:S(2)}, u32[]{:S(2)}) collective-permute-start(f32[8,865]{1,0:T(8,128)S(1)} %constant_dynamic-slice_fusion), channel_id=1, source_target_pairs={{0,8},{8,0},{16,24},{24,16},{1,9},{9,1},{17,25},{25,17},{2,10},{10... | collective-permute-start | bytes 83048 | tf_op jit(solution)/shard_map/ppermute | solution.py:147
  42.2 3.1 %shard_map.87 = bf16[1,32,4096]{2,1,0:T(8,128)(2,1)} custom-call(bf16[1,32,4096]{2,1,0:T(8,128)(2,1)} %copy-done.1, bf16[2,32,4096]{2,1,0:T(8,128)(2,1)} %get-tuple-element.45.dpre.mid, bf16[1,32,4096]{2,1,0:T(8,128)(2,1)} %copy-done.2, bf16[288,96]{1,0:T(8,128)(2,1)} %reshape.42.wall, f32[9,1,4096]{2,1,0:T(1,128)} %constant.68.clone.mask), custom_call_target="tpu_custom_call" | custom-call | flops 226492416 | bytes 1572864 | tf_op jit(solution)/shard_map/pallas_call | solution.py:117
  45.3 0.0 collective-permute-done.8
  45.3 1.4 %collective-permute-start.9 = (f32[8,865]{1,0:T(8,128)S(1)}, f32[8,865]{1,0:T(8,128)S(1)}, u32[]{:S(2)}, u32[]{:S(2)}) collective-permute-start(f32[8,865]{1,0:T(8,128)S(1)} %dynamic-slice_add_fusion.1), channel_id=1, source_target_pairs={{0,1},{1,0},{2,3},{3,2},{4,5},{5,4},{6,7},{7,6},{8,9},{9,8},{10,11... | collective-permute-start | bytes 83048 | tf_op jit(solution)/shard_map/ppermute | solution.py:147
  46.7 0.0 copy-done.8
  46.7 0.1 copy.25
  46.8 0.8 %collective-permute-done.9 = f32[8,865]{1,0:T(8,128)S(1)} collective-permute-done((f32[8,865]{1,0:T(8,128)S(1)}, f32[8,865]{1,0:T(8,128)S(1)}, u32[]{:S(2)}, u32[]{:S(2)}) %collective-permute-start.9) | collective-permute-done | bytes 27712 | tf_op jit(solution)/shard_map/ppermute | solution.py:147
  47.6 1.6 %collective-permute-start.10 = (f32[8,865]{1,0:T(8,128)S(1)}, f32[8,865]{1,0:T(8,128)S(1)}, u32[]{:S(2)}, u32[]{:S(2)}) collective-permute-start(f32[8,865]{1,0:T(8,128)S(1)} %add.61), channel_id=1, source_target_pairs={{0,2},{1,3},{2,0},{3,1},{4,6},{5,7},{6,4},{7,5},{8,10},{9,11},{10,... | collective-permute-start | bytes 83048 | tf_op jit(solution)/shard_map/ppermute | solution.py:147
  49.2 0.0 copy-done.3
  49.2 0.0 copy-done.4
  49.2 0.1 pad_maximum_fusion
  49.2 0.1 copy.26
  49.3 2.1 %collective-permute-done.10 = f32[8,865]{1,0:T(8,128)S(1)} collective-permute-done((f32[8,865]{1,0:T(8,128)S(1)}, f32[8,865]{1,0:T(8,128)S(1)}, u32[]{:S(2)}, u32[]{:S(2)}) %collective-permute-start.10) | collective-permute-done | bytes 27712 | tf_op jit(solution)/shard_map/ppermute | solution.py:147
  51.5 2.6 %collective-permute-start.11 = (f32[8,865]{1,0:T(8,128)S(1)}, f32[8,865]{1,0:T(8,128)S(1)}, u32[]{:S(2)}, u32[]{:S(2)}) collective-permute-start(f32[8,865]{1,0:T(8,128)S(1)} %add.62), channel_id=1, source_target_pairs={{0,4},{1,5},{2,6},{3,7},{4,0},{5,1},{6,2},{7,3},{8,12},{9,13},{10,... | collective-permute-start | bytes 83048 | tf_op jit(solution)/shard_map/ppermute | solution.py:147
  54.1 1.1 %copy_bitcast_fusion = (bf16[1,32,2,32,128]{4,3,2,1,0:T(8,128)(2,1)}, bf16[1,32,2,32,128]{4,3,2,1,0:T(8,128)(2,1)}) fusion(bf16[2,32,32,128]{3,2,1,0:T(8,128)(2,1)S(1)} %bitcast.56, bf16[2,32,32,128]{3,2,1,0:T(8,128)(2,1)S(1)} %bitcast.57), kind=kLoop, calls=%fused_computation.2 | loop fusion | bytes 2097152 | tf_op jit(solution)/shard_map/broadcast_in_dim | solution.py:235
  55.2 1.1 %collective-permute-done.11 = f32[8,865]{1,0:T(8,128)S(1)} collective-permute-done((f32[8,865]{1,0:T(8,128)S(1)}, f32[8,865]{1,0:T(8,128)S(1)}, u32[]{:S(2)}, u32[]{:S(2)}) %collective-permute-start.11) | collective-permute-done | bytes 27712 | tf_op jit(solution)/shard_map/ppermute | solution.py:147
  56.3 0.7 %slice_reduce_fusion = f32[8]{0:T(128)} fusion(f32[8,865]{1,0:T(8,128)S(1)} %add_multiply_fusion), kind=kLoop, calls=%fused_computation.13 | loop fusion | bytes 64 | tf_op jit(solution)/shard_map/slice | solution.py:235
  (21 shorter events, 0.1 us)
Async XLA Ops:
  0.6 0.7 %copy-start.12 = (bf16[8]{0:T(256)(128)(2,1)S(1)}, bf16[8]{0:T(256)(128)(2,1)}, u32[]{:S(2)}) copy-start(bf16[8]{0:T(256)(128)(2,1)} %param.8) | copy-start | bytes 52
  1.4 0.7 %copy-start.11 = (bf16[8,864]{1,0:T(8,128)(2,1)S(1)}, bf16[8,864]{1,0:T(8,128)(2,1)}, u32[]{:S(2)}) copy-start(bf16[8,864]{1,0:T(8,128)(2,1)} %param.7) | copy-start | bytes 41476
  2.2 9.5 %collective-permute-start.2 = (bf16[8,865]{1,0:T(8,128)(2,1)S(1)}, bf16[8,865]{1,0:T(8,128)(2,1)S(1)}, u32[]{:S(2)}, u32[]{:S(2)}) collective-permute-start(bf16[8,865]{1,0:T(8,128)(2,1)S(1)} %get-tuple-element.53), channel_id=1, source_target_pairs={{0,8},{8,0},{16,24},{24,16},{1,9},{9,1},{17,25},{25,17},{2,10},{10... | collective-permute-start | bytes 41528 | tf_op jit(solution)/shard_map/ppermute | solution.py:147
  5.1 6.5 %collective-permute-start.3 = (bf16[8,865]{1,0:T(8,128)(2,1)S(1)}, bf16[8,865]{1,0:T(8,128)(2,1)S(1)}, u32[]{:S(2)}, u32[]{:S(2)}) collective-permute-start(bf16[8,865]{1,0:T(8,128)(2,1)S(1)} %get-tuple-element.53), channel_id=1, source_target_pairs={{0,16},{8,24},{16,0},{24,8},{1,17},{9,25},{17,1},{25,9},{2,18},{10... | collective-permute-start | bytes 41528 | tf_op jit(solution)/shard_map/ppermute | solution.py:147
  6.6 5.0 %collective-permute-start.4 = (bf16[8,865]{1,0:T(8,128)(2,1)S(1)}, bf16[8,865]{1,0:T(8,128)(2,1)S(1)}, u32[]{:S(2)}, u32[]{:S(2)}) collective-permute-start(bf16[8,865]{1,0:T(8,128)(2,1)S(1)} %get-tuple-element.53), channel_id=1, source_target_pairs={{0,24},{8,16},{16,8},{24,0},{1,25},{9,17},{17,9},{25,1},{2,26},{10... | collective-permute-start | bytes 41528 | tf_op jit(solution)/shard_map/ppermute | solution.py:147
  6.7 3.8 %copy-start.7 = (bf16[1,32,2,32,128]{4,3,2,1,0:T(8,128)(2,1)S(1)}, bf16[1,32,2,32,128]{4,3,2,1,0:T(8,128)(2,1)}, u32[]{:S(2)}) copy-start(bf16[1,32,2,32,128]{4,3,2,1,0:T(8,128)(2,1)} %param.6) | copy-start | bytes 1572868
  7.8 5.5 %collective-permute-start = (bf16[32,1,32,128]{3,2,1,0:T(8,128)(2,1)S(1)}, bf16[32,1,32,128]{3,2,1,0:T(8,128)(2,1)S(1)}, u32[]{:S(2)}, u32[]{:S(2)}) collective-permute-start(bf16[32,1,32,128]{3,2,1,0:T(8,128)(2,1)S(1)} %get-tuple-element.54), channel_id=1, source_target_pairs={{0,1},{1,2},{2,3},{3,4},{4,5},{5,6},{6,7},{8,9},{9,10},{10,11},{11... | collective-permute-start | bytes 786440 | tf_op jit(solution)/shard_map/ppermute | solution.py:142
  9.1 5.7 %collective-permute-start.1 = (bf16[32,1,32,128]{3,2,1,0:T(8,128)(2,1)S(1)}, bf16[32,1,32,128]{3,2,1,0:T(8,128)(2,1)S(1)}, u32[]{:S(2)}, u32[]{:S(2)}) collective-permute-start(bf16[32,1,32,128]{3,2,1,0:T(8,128)(2,1)S(1)} %get-tuple-element.55), channel_id=1, source_target_pairs={{1,0},{2,1},{3,2},{4,3},{5,4},{6,5},{7,6},{9,8},{10,9},{11,10},{12... | collective-permute-start | bytes 786440 | tf_op jit(solution)/shard_map/ppermute | solution.py:142
  11.7 0.6 %copy-start.5 = (bf16[4,8,865]{2,1,0:T(8,128)(2,1)}, bf16[4,8,865]{2,1,0:T(8,128)(2,1)S(1)}, u32[]{:S(2)}) copy-start(bf16[4,8,865]{2,1,0:T(8,128)(2,1)S(1)} %bitcast_dynamic-update-slice_fusion) | copy-start | bytes 166084
  12.3 2.5 %copy-start = (bf16[1,32,2,32,128]{4,3,2,1,0:T(8,128)(2,1)S(1)}, bf16[1,32,2,32,128]{4,3,2,1,0:T(8,128)(2,1)}, u32[]{:S(2)}) copy-start(bf16[1,32,2,32,128]{4,3,2,1,0:T(8,128)(2,1)} %param.5) | copy-start | bytes 1572868
  21.9 12.6 %collective-permute-start.5 = (bf16[1,32,4096]{2,1,0:T(8,128)(2,1)}, bf16[1,32,4096]{2,1,0:T(8,128)(2,1)S(1)}, u32[]{:S(2)}, u32[]{:S(2)}) collective-permute-start(bf16[1,32,4096]{2,1,0:T(8,128)(2,1)} %get-tuple-element.30), channel_id=1, source_target_pairs={{0,1},{1,2},{2,3},{3,4},{4,5},{5,6},{6,7},{8,9},{9,10},{10,11},{11... | collective-permute-start | bytes 786440 | tf_op jit(solution)/shard_map/ppermute | solution.py:142
  28.6 6.0 %collective-permute-start.6 = (bf16[1,32,4096]{2,1,0:T(8,128)(2,1)}, bf16[1,32,4096]{2,1,0:T(8,128)(2,1)S(1)}, u32[]{:S(2)}, u32[]{:S(2)}) collective-permute-start(bf16[1,32,4096]{2,1,0:T(8,128)(2,1)} %get-tuple-element.31), channel_id=1, source_target_pairs={{1,0},{2,1},{3,2},{4,3},{5,4},{6,5},{7,6},{9,8},{10,9},{11,10},{12... | collective-permute-start | bytes 786440 | tf_op jit(solution)/shard_map/ppermute | solution.py:142
  33.7 0.9 %copy-start.6 = (bf16[4,8,865]{2,1,0:T(8,128)(2,1)S(1)}, bf16[4,8,865]{2,1,0:T(8,128)(2,1)}, u32[]{:S(2)}) copy-start(bf16[4,8,865]{2,1,0:T(8,128)(2,1)} %copy-done.5) | copy-start | bytes 166084
  34.5 1.9 %copy-start.1 = (bf16[1,32,4096]{2,1,0:T(8,128)(2,1)}, bf16[1,32,4096]{2,1,0:T(8,128)(2,1)S(1)}, u32[]{:S(2)}) copy-start(bf16[1,32,4096]{2,1,0:T(8,128)(2,1)S(1)} %collective-permute-done.5.lo) | copy-start | bytes 786436
  34.6 1.9 %copy-start.2 = (bf16[1,32,4096]{2,1,0:T(8,128)(2,1)}, bf16[1,32,4096]{2,1,0:T(8,128)(2,1)S(1)}, u32[]{:S(2)}) copy-start(bf16[1,32,4096]{2,1,0:T(8,128)(2,1)S(1)} %collective-permute-done.6.hi) | copy-start | bytes 786436
  34.8 5.8 %collective-permute-start.7 = (f32[16,865]{1,0:T(8,128)S(1)}, f32[16,865]{1,0:T(8,128)S(1)}, u32[]{:S(2)}, u32[]{:S(2)}) collective-permute-start(f32[16,865]{1,0:T(8,128)S(1)} %constant_dynamic-slice_fusion.1), channel_id=1, source_target_pairs={{0,16},{8,24},{16,0},{24,8},{1,17},{9,25},{17,1},{25,9},{2,18},{10... | collective-permute-start | bytes 166088 | tf_op jit(solution)/shard_map/ppermute | solution.py:147
  37.6 3.0 %copy-start.9 = (f32[32,865]{1,0:T(8,128)S(1)}, f32[32,865]{1,0:T(8,128)}, u32[]{:S(2)}) copy-start(f32[32,865]{1,0:T(8,128)} %shard_map.85) | copy-start | bytes 332164
  40.7 4.6 %collective-permute-start.8 = (f32[8,865]{1,0:T(8,128)S(1)}, f32[8,865]{1,0:T(8,128)S(1)}, u32[]{:S(2)}, u32[]{:S(2)}) collective-permute-start(f32[8,865]{1,0:T(8,128)S(1)} %constant_dynamic-slice_fusion), channel_id=1, source_target_pairs={{0,8},{8,0},{16,24},{24,16},{1,9},{9,1},{17,25},{25,17},{2,10},{10... | collective-permute-start | bytes 83048 | tf_op jit(solution)/shard_map/ppermute | solution.py:147
  42.2 4.5 %copy-start.8 = (bf16[2,32,4096]{2,1,0:T(8,128)(2,1)S(1)}, bf16[2,32,4096]{2,1,0:T(8,128)(2,1)}, u32[]{:S(2)}) copy-start(bf16[2,32,4096]{2,1,0:T(8,128)(2,1)} %get-tuple-element.28) | copy-start | bytes 1572868
  45.3 2.3 %collective-permute-start.9 = (f32[8,865]{1,0:T(8,128)S(1)}, f32[8,865]{1,0:T(8,128)S(1)}, u32[]{:S(2)}, u32[]{:S(2)}) collective-permute-start(f32[8,865]{1,0:T(8,128)S(1)} %dynamic-slice_add_fusion.1), channel_id=1, source_target_pairs={{0,1},{1,0},{2,3},{3,2},{4,5},{5,4},{6,7},{7,6},{8,9},{9,8},{10,11... | collective-permute-start | bytes 83048 | tf_op jit(solution)/shard_map/ppermute | solution.py:147
  46.7 2.4 %copy-start.3 = (bf16[1,32,4096]{2,1,0:T(8,128)(2,1)S(1)}, bf16[1,32,4096]{2,1,0:T(8,128)(2,1)}, u32[]{:S(2)}) copy-start(bf16[1,32,4096]{2,1,0:T(8,128)(2,1)} %shard_map.86) | copy-start | bytes 786436
  46.7 2.4 %copy-start.4 = (bf16[1,32,4096]{2,1,0:T(8,128)(2,1)S(1)}, bf16[1,32,4096]{2,1,0:T(8,128)(2,1)}, u32[]{:S(2)}) copy-start(bf16[1,32,4096]{2,1,0:T(8,128)(2,1)} %shard_map.87) | copy-start | bytes 786436
  47.6 3.9 %collective-permute-start.10 = (f32[8,865]{1,0:T(8,128)S(1)}, f32[8,865]{1,0:T(8,128)S(1)}, u32[]{:S(2)}, u32[]{:S(2)}) collective-permute-start(f32[8,865]{1,0:T(8,128)S(1)} %add.61), channel_id=1, source_target_pairs={{0,2},{1,3},{2,0},{3,1},{4,6},{5,7},{6,4},{7,5},{8,10},{9,11},{10,... | collective-permute-start | bytes 83048 | tf_op jit(solution)/shard_map/ppermute | solution.py:147
  51.5 4.8 %collective-permute-start.11 = (f32[8,865]{1,0:T(8,128)S(1)}, f32[8,865]{1,0:T(8,128)S(1)}, u32[]{:S(2)}, u32[]{:S(2)}) collective-permute-start(f32[8,865]{1,0:T(8,128)S(1)} %add.62), channel_id=1, source_target_pairs={{0,4},{1,5},{2,6},{3,7},{4,0},{5,1},{6,2},{7,3},{8,12},{9,13},{10,... | collective-permute-start | bytes 83048 | tf_op jit(solution)/shard_map/ppermute | solution.py:147
  56.3 0.7 %copy-start.10 = (f32[8,865]{1,0:T(8,128)}, f32[8,865]{1,0:T(8,128)S(1)}, u32[]{:S(2)}) copy-start(f32[8,865]{1,0:T(8,128)S(1)} %add_multiply_fusion) | copy-start | bytes 83044

commit v10 on v7

--- a/solution.py
+++ b/solution.py
@@ -66,7 +66,7 @@
         out[n] = _shifted_sum(y, mask, chans, lanes, depth, -1).astype(out.dtype)
 
 
-def _weight_kernel(haloed, dpre, mask, gw_out, *, planes, depth):
+def _weight_kernel(upper, haloed, dpre, mask, keep_out, send_out, full, *, planes, depth):
     chans, lanes = dpre.shape[1], dpre.shape[2]
     gw = jnp.zeros((9 * chans, 3 * chans), jnp.float32)
     gb = jnp.zeros((chans, 1), jnp.float32)
@@ -88,8 +88,12 @@
     for k in range(len(OFFSETS)):
         for a in range(3):
             t = 9 * a + k
-            gw_out[:, t * chans_in : (t + 1) * chans_in] = gw[k * chans : (k + 1) * chans, a * chans_in : (a + 1) * chans_in]
-    gw_out[:, 27 * chans_in :] = gb
+            full[:, t * chans_in : (t + 1) * chans_in] = gw[k * chans : (k + 1) * chans, a * chans_in : (a + 1) * chans_in]
+    full[:, 27 * chans_in :] = gb
+    half = keep_out.shape[0]
+    kept = upper[0]
+    keep_out[...] = full[pl.ds(pl.multiple_of(kept * half, 8), half), :]
+    send_out[...] = full[pl.ds(pl.multiple_of((1 - kept) * half, 8), half), :]
 
 
 def _vmem(n):
@@ -122,16 +126,18 @@
     )(lo, mid, hi, wall, mask)
 
 
-def weight_call(haloed, dpre, mask, depth):
+def weight_call(upper, haloed, dpre, mask, depth):
     planes, chans, lanes = dpre.shape
     flops = 2 * planes * 9 * chans * 3 * chans * lanes
+    half = jax.ShapeDtypeStruct((chans // 2, 27 * chans + 1), jnp.float32)
     return pl.pallas_call(
         functools.partial(_weight_kernel, planes=planes, depth=depth),
-        out_shape=jax.ShapeDtypeStruct((chans, 27 * chans + 1), jnp.float32),
-        in_specs=_vmem(3),
-        out_specs=_vmem(1)[0],
+        out_shape=(half, half),
+        in_specs=[pl.BlockSpec(memory_space=pltpu.SMEM)] + _vmem(3),
+        out_specs=tuple(_vmem(2)),
+        scratch_shapes=[pltpu.VMEM((chans, 27 * chans + 1), jnp.float32)],
         cost_estimate=pl.CostEstimate(flops=flops, transcendentals=0, bytes_accessed=3 * dpre.size * 2),
-    )(haloed, dpre, mask)
+    )(upper, haloed, dpre, mask)
 
 
 def neighbours(first, last, axis):
@@ -154,6 +160,10 @@
     for k in range(1, peers):
         blocks = lax.dynamic_update_index_in_dim(blocks, swap(value, axis, k), me ^ k, 0)
     return blocks.reshape((peers * value.shape[0],) + value.shape[1:])
+
+
+def first_upper():
+    return (lax.axis_index("real") // (lax.axis_size("real") // 2)) % 2
 
 
 def reduce_beside(local_grads, work):
@@ -167,9 +177,11 @@
         rounds.append(("strike", bit))
         bit *= 2
     results = []
-    value = local_grads
+    value = None
     for k, (axis, bit) in enumerate(rounds):
-        if axis == "real":
+        if k == 0:
+            keep, send = local_grads
+        elif axis == "real":
             half = value.shape[0] // 2
             upper = (lax.axis_index(axis) // bit) % 2
             keep = lax.dynamic_slice_in_dim(value, upper * half, half, 0)
@@ -217,7 +229,7 @@
         haloed, forward_w, whole_bias.astype(jnp.float32)[:, None], flat(cotangent[0]), mask, depth
     )
     dlo, dhi = neighbours(first, last, "strike")
-    local_grads = weight_call(haloed, dpre, mask, depth)
+    local_grads = weight_call(first_upper().astype(jnp.int32)[None], haloed, dpre, mask, depth)
     work = [
         (functools.partial(input_call, depth=depth, first=p, count=1), (dlo, dpre, dhi, backward_w, mask))
         for p in range(planes)

time: 56.3 us -> 55.8 us (level)
  local copies, waits for them, and re-layouts: 10.8 us -> 10 us
    dynamic_slice x2 -> x1, local copies, waits for them, and re-layouts: 0.84 us -> 0.01 us  [reduce_beside(): send = lax.dynamic_slice_in_dim(value, (1 - upper) * half, half, 0)]
  transfers between devices with their start and end apart: 12 -> 12, of which waited for: 4 -> 4; matrix products, arithmetic and copies ran while one was open for 13% -> 12% of each run, Pallas kernels for 18% -> 18%
where the time goes in v10:
time: 55.8 us; the launch traced here: 55.4 us
  starting transfers between devices  24.2 us (43%)
  Pallas kernels  14.9 us (27%)
  local copies, waits for them, and re-layouts  10 us (18%)
  waiting for transfers between devices  4.47 us (8%)
  other arithmetic  0.96 us (2%)
  between operations  0.88 us (2%)
    ppermute x8, starting transfers between devices, swap(): return lax.ppermute(value, axis, [(i, i ^ bit) for i in range(peers)])  13.6 us
    ppermute x4, starting transfers between devices, neighbours(): return (lax.ppermute(last, axis, up), lax.ppermute(first, axis, down))  10.6 us
    pallas_call x2, Pallas kernels, input_call(): pl.pallas_call(functools.partial(_input_kernel, planes=planes, first=firs...  6.09 us
    pallas_call x1, Pallas kernels, forward_call(): pl.pallas_call(functools.partial(_forward_kernel, planes=planes, depth=de...  5.04 us
    pallas_call x1, Pallas kernels, weight_call(): pl.pallas_call(functools.partial(_weight_kernel, planes=planes, depth=dep...  3.74 us
    ppermute x8, waiting for transfers between devices, swap(): return lax.ppermute(value, axis, [(i, i ^ bit) for i in range(peers)])  3.25 us
    reshape x2, local copies, waits for them, and re-layouts, local(): haloed = haloed.transpose(1, 0, 2, 3).reshape(planes + 2, chans, lanes)  1.86 us
    unnamed x24, local copies, waits for them, and re-layouts  1.56 us
  transfers between devices with their start and end apart: 12, of which 4 were waited for; matrix products, arithmetic and copies ran while one was open for 12% of the time, Pallas kernels for 18%

profile of v10, /device:TPU:0, one launch (start us, length us, event | category | flops | bytes accessed | tf_op | source)
XLA Modules:
  0.0 55.4 jit_solution(12822300073459441456)
XLA Ops:
  0.6 0.0 copy-start.10
  0.6 0.6 %copy-done.10 = bf16[8]{0:T(256)(128)(2,1)S(1)} copy-done((bf16[8]{0:T(256)(128)(2,1)S(1)}, bf16[8]{0:T(256)(128)(2,1)}, u32[]{:S(2)}) %copy-start.10) | copy-done | bytes 40
  1.3 0.1 copy.17
  1.4 0.0 copy-start.9
  1.4 0.7 %copy-done.9 = bf16[8,864]{1,0:T(8,128)(2,1)S(1)} copy-done((bf16[8,864]{1,0:T(8,128)(2,1)S(1)}, bf16[8,864]{1,0:T(8,128)(2,1)}, u32[]{:S(2)}) %copy-start.9) | copy-done | bytes 13848
  2.1 0.1 bitcast_dynamic-update-slice_fusion.3
  2.2 3.0 %collective-permute-start.3 = (bf16[8,865]{1,0:T(8,128)(2,1)S(1)}, bf16[8,865]{1,0:T(8,128)(2,1)S(1)}, u32[]{:S(2)}, u32[]{:S(2)}) collective-permute-start(bf16[8,865]{1,0:T(8,128)(2,1)S(1)} %get-tuple-element.49), channel_id=1, source_target_pairs={{0,16},{8,24},{16,0},{24,8},{1,17},{9,25},{17,1},{25,9},{2,18},{10... | collective-permute-start | bytes 41528 | tf_op jit(solution)/shard_map/ppermute | solution.py:152
  5.1 1.5 %collective-permute-start.2 = (bf16[8,865]{1,0:T(8,128)(2,1)S(1)}, bf16[8,865]{1,0:T(8,128)(2,1)S(1)}, u32[]{:S(2)}, u32[]{:S(2)}) collective-permute-start(bf16[8,865]{1,0:T(8,128)(2,1)S(1)} %get-tuple-element.49), channel_id=1, source_target_pairs={{0,8},{8,0},{16,24},{24,16},{1,9},{9,1},{17,25},{25,17},{2,10},{10... | collective-permute-start | bytes 41528 | tf_op jit(solution)/shard_map/ppermute | solution.py:152
  6.6 0.0 collective-permute-start.4
  6.7 0.0 copy-start.5
  6.7 1.1 %fusion = (bf16[32,1,32,128]{3,2,1,0:T(8,128)(2,1)S(1)}, bf16[32,1,32,128]{3,2,1,0:T(8,128)(2,1)S(1)}) fusion(bf16[32,2,32,128]{3,2,1,0:T(8,128)(2,1)} %bitcast.56), kind=kLoop, calls=%fused_computation.15 | loop fusion | bytes 1048576 | tf_op jit(solution)/shard_map/slice | solution.py:225
  7.8 1.3 %collective-permute-start = (bf16[32,1,32,128]{3,2,1,0:T(8,128)(2,1)S(1)}, bf16[32,1,32,128]{3,2,1,0:T(8,128)(2,1)S(1)}, u32[]{:S(2)}, u32[]{:S(2)}) collective-permute-start(bf16[32,1,32,128]{3,2,1,0:T(8,128)(2,1)S(1)} %get-tuple-element.50), channel_id=1, source_target_pairs={{0,1},{1,2},{2,3},{3,4},{4,5},{5,6},{6,7},{8,9},{9,10},{10,11},{11... | collective-permute-start | bytes 786440 | tf_op jit(solution)/shard_map/ppermute | solution.py:147
  9.1 1.3 %collective-permute-start.1 = (bf16[32,1,32,128]{3,2,1,0:T(8,128)(2,1)S(1)}, bf16[32,1,32,128]{3,2,1,0:T(8,128)(2,1)S(1)}, u32[]{:S(2)}, u32[]{:S(2)}) collective-permute-start(bf16[32,1,32,128]{3,2,1,0:T(8,128)(2,1)S(1)} %get-tuple-element.51), channel_id=1, source_target_pairs={{1,0},{2,1},{3,2},{4,3},{5,4},{6,5},{7,6},{9,8},{10,9},{11,10},{12... | collective-permute-start | bytes 786440 | tf_op jit(solution)/shard_map/ppermute | solution.py:147
  10.4 0.0 copy-done.5
  10.5 0.1 reshape.41
  10.6 1.1 %copy.24.cot = bf16[2,32,4096]{2,1,0:T(8,128)(2,1)} copy(bf16[2,32,4096]{2,0,1:T(2,128)(2,1)S(1)} %reshape.41) | data formatting | bytes 1048576 | tf_op jit(solution)/shard_map/reshape | solution.py:220
  11.7 0.0 collective-permute-done.2
  11.7 0.0 collective-permute-done.3
  11.7 0.0 collective-permute-done.4
  11.7 0.2 reshape.34
  11.9 0.0 copy-start
  11.9 0.1 copy.18
  12.1 0.8 %reshape.35.wall = bf16[288,96]{1,0:T(8,128)(2,1)} reshape(bf16[3,3,32,3,32]{4,3,2,1,0:T(4,128)(2,1)S(1)} %copy.18) | data formatting | bytes 110592 | tf_op jit(solution)/shard_map/reshape | solution.py:215
  12.9 0.7 %slice_convert_fusion.bias = f32[32,1]{1,0:T(8,128)} fusion(bf16[32,865]{1,0:T(8,128)(2,1)S(1)} %bitcast.63), kind=kLoop, calls=%fused_computation.12 | loop fusion | flops 32 | bytes 192 | tf_op jit(solution)/shard_map/convert_element_type | solution.py:229
  13.6 0.0 collective-permute-done
  13.6 1.2 %collective-permute-done.1 = bf16[32,1,32,128]{3,2,1,0:T(8,128)(2,1)S(1)} collective-permute-done((bf16[32,1,32,128]{3,2,1,0:T(8,128)(2,1)S(1)}, bf16[32,1,32,128]{3,2,1,0:T(8,128)(2,1)S(1)}, u32[]{:S(2)}, u32[]{:S(2)}) %collective-permute-start.1) | collective-permute-done | bytes 262176 | tf_op jit(solution)/shard_map/ppermute | solution.py:147
  14.8 0.0 copy-done
  14.8 0.1 maximum_bitcast_fusion
  14.9 0.3 reshape.40
  15.2 1.6 %copy.23.haloed = bf16[4,32,4096]{2,1,0:T(8,128)(2,1)} copy(bf16[4,32,4096]{2,0,1:T(4,128)(2,1)S(1)} %reshape.40) | data formatting | bytes 2097152 | tf_op jit(solution)/shard_map/reshape | solution.py:227
  16.8 5.0 %shard_map.84 = (bf16[2,32,4096]{2,1,0:T(8,128)(2,1)}, bf16[2,32,4096]{2,1,0:T(8,128)(2,1)}, bf16[1,32,4096]{2,1,0:T(8,128)(2,1)}, bf16[1,32,4096]{2,1,0:T(8,128)(2,1)}) custom-call(bf16[4,32,4096]{2,1,0:T(8,128)(2,1)} %copy.23.haloed, bf16[288,96]{1,0:T(8,128)(2,1)} %reshape.35.wall, f32[32,1]{1,0:T(8,128)} %slice_convert_fusion.bias, ...), custom_call_target="tpu_custom_call" | custom-call | flops 452984832 | bytes 2621440 | tf_op jit(solution)/shard_map/pallas_call | solution.py:108
  21.8 6.7 %collective-permute-start.5 = (bf16[1,32,4096]{2,1,0:T(8,128)(2,1)}, bf16[1,32,4096]{2,1,0:T(8,128)(2,1)S(1)}, u32[]{:S(2)}, u32[]{:S(2)}) collective-permute-start(bf16[1,32,4096]{2,1,0:T(8,128)(2,1)} %get-tuple-element.29), channel_id=1, source_target_pairs={{0,1},{1,2},{2,3},{3,4},{4,5},{5,6},{6,7},{8,9},{9,10},{10,11},{11... | collective-permute-start | bytes 786440 | tf_op jit(solution)/shard_map/ppermute | solution.py:147
  28.5 1.3 %collective-permute-start.6 = (bf16[1,32,4096]{2,1,0:T(8,128)(2,1)}, bf16[1,32,4096]{2,1,0:T(8,128)(2,1)S(1)}, u32[]{:S(2)}, u32[]{:S(2)}) collective-permute-start(bf16[1,32,4096]{2,1,0:T(8,128)(2,1)} %get-tuple-element.30), channel_id=1, source_target_pairs={{1,0},{2,1},{3,2},{4,3},{5,4},{6,5},{7,6},{9,8},{10,9},{11,10},{12... | collective-permute-start | bytes 786440 | tf_op jit(solution)/shard_map/ppermute | solution.py:147
  29.8 0.1 reverse_bitcast_fusion
  29.9 0.3 copy.21
  30.2 0.8 %reshape.38.wall = bf16[288,96]{1,0:T(8,128)(2,1)} reshape(bf16[3,3,32,3,32]{4,3,2,1,0:T(4,128)(2,1)S(1)} %copy.21) | data formatting | bytes 110592 | tf_op jit(solution)/shard_map/reshape | solution.py:216
  31.0 3.7 %shard_map.85 = (f32[16,865]{1,0:T(8,128)}, f32[16,865]{1,0:T(8,128)}) custom-call(s32[1]{0:T(128)} %bitcast.13.upper, bf16[4,32,4096]{2,1,0:T(8,128)(2,1)} %copy.23.haloed, bf16[2,32,4096]{2,1,0:T(8,128)(2,1)} %get-tuple-element.42.dpre.mid, f32[9,1,4096]{2,1,0:T(1,128)} %constant.66.clone.mask), custom_call_target="tpu_custom_call" | custom-call | flops 452984832 | bytes 1572864 | tf_op jit(solution)/shard_map/pallas_call | solution.py:133
  34.8 0.0 collective-permute-done.5.lo
  34.8 0.0 collective-permute-done.6.hi
  34.8 0.0 copy-start.2
  34.8 1.6 %collective-permute-start.7 = (f32[16,865]{1,0:T(8,128)}, f32[16,865]{1,0:T(8,128)S(1)}, u32[]{:S(2)}, u32[]{:S(2)}) collective-permute-start(f32[16,865]{1,0:T(8,128)} %get-tuple-element.31), channel_id=1, source_target_pairs={{0,16},{8,24},{16,0},{24,8},{1,17},{9,25},{17,1},{25,9},{2,18},{10... | collective-permute-start | bytes 166088 | tf_op jit(solution)/shard_map/ppermute | solution.py:152
  36.4 0.0 copy-done.1
  36.4 0.0 copy-done.2
  36.4 3.0 %shard_map.86 = bf16[1,32,4096]{2,1,0:T(8,128)(2,1)} custom-call(bf16[1,32,4096]{2,1,0:T(8,128)(2,1)} %copy-done.1, bf16[2,32,4096]{2,1,0:T(8,128)(2,1)} %get-tuple-element.42.dpre.mid, bf16[1,32,4096]{2,1,0:T(8,128)(2,1)} %copy-done.2, bf16[288,96]{1,0:T(8,128)(2,1)} %reshape.38.wall, f32[9,1,4096]{2,1,0:T(1,128)} %constant.66.clone.mask), custom_call_target="tpu_custom_call" | custom-call | flops 226492416 | bytes 1572864 | tf_op jit(solution)/shard_map/pallas_call | solution.py:120
  39.4 0.0 collective-permute-done.7
  39.4 0.0 copy-done.7
  39.5 1.6 %collective-permute-start.8 = (f32[8,865]{1,0:T(8,128)S(1)}, f32[8,865]{1,0:T(8,128)S(1)}, u32[]{:S(2)}, u32[]{:S(2)}) collective-permute-start(f32[8,865]{1,0:T(8,128)S(1)} %constant_dynamic-slice_fusion), channel_id=1, source_target_pairs={{0,8},{8,0},{16,24},{24,16},{1,9},{9,1},{17,25},{25,17},{2,10},{10... | collective-permute-start | bytes 83048 | tf_op jit(solution)/shard_map/ppermute | solution.py:152
  41.0 3.1 %shard_map.87 = bf16[1,32,4096]{2,1,0:T(8,128)(2,1)} custom-call(bf16[1,32,4096]{2,1,0:T(8,128)(2,1)} %copy-done.1, bf16[2,32,4096]{2,1,0:T(8,128)(2,1)} %get-tuple-element.42.dpre.mid, bf16[1,32,4096]{2,1,0:T(8,128)(2,1)} %copy-done.2, bf16[288,96]{1,0:T(8,128)(2,1)} %reshape.38.wall, f32[9,1,4096]{2,1,0:T(1,128)} %constant.66.clone.mask), custom_call_target="tpu_custom_call" | custom-call | flops 226492416 | bytes 1572864 | tf_op jit(solution)/shard_map/pallas_call | solution.py:120
  44.1 0.0 collective-permute-done.8
  44.1 1.0 %collective-permute-start.9 = (f32[8,865]{1,0:T(8,128)S(1)}, f32[8,865]{1,0:T(8,128)S(1)}, u32[]{:S(2)}, u32[]{:S(2)}) collective-permute-start(f32[8,865]{1,0:T(8,128)S(1)} %dynamic-slice_add_fusion), channel_id=1, source_target_pairs={{0,1},{1,0},{2,3},{3,2},{4,5},{5,4},{6,7},{7,6},{8,9},{9,8},{10,11... | collective-permute-start | bytes 83048 | tf_op jit(solution)/shard_map/ppermute | solution.py:152
  45.1 0.0 copy-done.6
  45.1 0.1 copy.25
  45.2 0.8 %collective-permute-done.9 = f32[8,865]{1,0:T(8,128)S(1)} collective-permute-done((f32[8,865]{1,0:T(8,128)S(1)}, f32[8,865]{1,0:T(8,128)S(1)}, u32[]{:S(2)}, u32[]{:S(2)}) %collective-permute-start.9) | collective-permute-done | bytes 27712 | tf_op jit(solution)/shard_map/ppermute | solution.py:152
  46.0 2.0 %collective-permute-start.10 = (f32[8,865]{1,0:T(8,128)S(1)}, f32[8,865]{1,0:T(8,128)S(1)}, u32[]{:S(2)}, u32[]{:S(2)}) collective-permute-start(f32[8,865]{1,0:T(8,128)S(1)} %add.53), channel_id=1, source_target_pairs={{0,2},{1,3},{2,0},{3,1},{4,6},{5,7},{6,4},{7,5},{8,10},{9,11},{10,... | collective-permute-start | bytes 83048 | tf_op jit(solution)/shard_map/ppermute | solution.py:152
  48.0 0.0 copy-done.3
  48.0 0.0 copy-done.4
  48.0 0.1 pad_maximum_fusion
  48.0 0.1 copy.26
  48.1 1.8 %collective-permute-done.10 = f32[8,865]{1,0:T(8,128)S(1)} collective-permute-done((f32[8,865]{1,0:T(8,128)S(1)}, f32[8,865]{1,0:T(8,128)S(1)}, u32[]{:S(2)}, u32[]{:S(2)}) %collective-permute-start.10) | collective-permute-done | bytes 27712 | tf_op jit(solution)/shard_map/ppermute | solution.py:152
  49.9 3.0 %collective-permute-start.11 = (f32[8,865]{1,0:T(8,128)S(1)}, f32[8,865]{1,0:T(8,128)S(1)}, u32[]{:S(2)}, u32[]{:S(2)}) collective-permute-start(f32[8,865]{1,0:T(8,128)S(1)} %add.54), channel_id=1, source_target_pairs={{0,4},{1,5},{2,6},{3,7},{4,0},{5,1},{6,2},{7,3},{8,12},{9,13},{10,... | collective-permute-start | bytes 83048 | tf_op jit(solution)/shard_map/ppermute | solution.py:152
  52.8 1.1 %copy_bitcast_fusion = (bf16[1,32,2,32,128]{4,3,2,1,0:T(8,128)(2,1)}, bf16[1,32,2,32,128]{4,3,2,1,0:T(8,128)(2,1)}) fusion(bf16[2,32,32,128]{3,2,1,0:T(8,128)(2,1)S(1)} %bitcast.58, bf16[2,32,32,128]{3,2,1,0:T(8,128)(2,1)S(1)} %bitcast.59), kind=kLoop, calls=%fused_computation.2 | loop fusion | bytes 2097152 | tf_op jit(solution)/shard_map/broadcast_in_dim | solution.py:242
  54.0 0.7 %collective-permute-done.11 = f32[8,865]{1,0:T(8,128)S(1)} collective-permute-done((f32[8,865]{1,0:T(8,128)S(1)}, f32[8,865]{1,0:T(8,128)S(1)}, u32[]{:S(2)}, u32[]{:S(2)}) %collective-permute-start.11) | collective-permute-done | bytes 27712 | tf_op jit(solution)/shard_map/ppermute | solution.py:152
  54.7 0.7 %slice_reduce_fusion = f32[8]{0:T(128)} fusion(f32[8,865]{1,0:T(8,128)S(1)} %add_multiply_fusion), kind=kLoop, calls=%fused_computation.13 | loop fusion | bytes 64 | tf_op jit(solution)/shard_map/slice | solution.py:242
  55.4 0.0 copy-done.8
  (16 shorter events, 0.1 us)
Async XLA Ops:
  0.6 0.7 %copy-start.10 = (bf16[8]{0:T(256)(128)(2,1)S(1)}, bf16[8]{0:T(256)(128)(2,1)}, u32[]{:S(2)}) copy-start(bf16[8]{0:T(256)(128)(2,1)} %param.8) | copy-start | bytes 52
  1.4 0.7 %copy-start.9 = (bf16[8,864]{1,0:T(8,128)(2,1)S(1)}, bf16[8,864]{1,0:T(8,128)(2,1)}, u32[]{:S(2)}) copy-start(bf16[8,864]{1,0:T(8,128)(2,1)} %param.7) | copy-start | bytes 41476
  2.2 9.5 %collective-permute-start.3 = (bf16[8,865]{1,0:T(8,128)(2,1)S(1)}, bf16[8,865]{1,0:T(8,128)(2,1)S(1)}, u32[]{:S(2)}, u32[]{:S(2)}) collective-permute-start(bf16[8,865]{1,0:T(8,128)(2,1)S(1)} %get-tuple-element.49), channel_id=1, source_target_pairs={{0,16},{8,24},{16,0},{24,8},{1,17},{9,25},{17,1},{25,9},{2,18},{10... | collective-permute-start | bytes 41528 | tf_op jit(solution)/shard_map/ppermute | solution.py:152
  5.1 6.5 %collective-permute-start.2 = (bf16[8,865]{1,0:T(8,128)(2,1)S(1)}, bf16[8,865]{1,0:T(8,128)(2,1)S(1)}, u32[]{:S(2)}, u32[]{:S(2)}) collective-permute-start(bf16[8,865]{1,0:T(8,128)(2,1)S(1)} %get-tuple-element.49), channel_id=1, source_target_pairs={{0,8},{8,0},{16,24},{24,16},{1,9},{9,1},{17,25},{25,17},{2,10},{10... | collective-permute-start | bytes 41528 | tf_op jit(solution)/shard_map/ppermute | solution.py:152
  6.6 5.1 %collective-permute-start.4 = (bf16[8,865]{1,0:T(8,128)(2,1)S(1)}, bf16[8,865]{1,0:T(8,128)(2,1)S(1)}, u32[]{:S(2)}, u32[]{:S(2)}) collective-permute-start(bf16[8,865]{1,0:T(8,128)(2,1)S(1)} %get-tuple-element.49), channel_id=1, source_target_pairs={{0,24},{8,16},{16,8},{24,0},{1,25},{9,17},{17,9},{25,1},{2,26},{10... | collective-permute-start | bytes 41528 | tf_op jit(solution)/shard_map/ppermute | solution.py:152
  6.7 3.8 %copy-start.5 = (bf16[1,32,2,32,128]{4,3,2,1,0:T(8,128)(2,1)S(1)}, bf16[1,32,2,32,128]{4,3,2,1,0:T(8,128)(2,1)}, u32[]{:S(2)}) copy-start(bf16[1,32,2,32,128]{4,3,2,1,0:T(8,128)(2,1)} %param.6) | copy-start | bytes 1572868
  7.8 5.8 %collective-permute-start = (bf16[32,1,32,128]{3,2,1,0:T(8,128)(2,1)S(1)}, bf16[32,1,32,128]{3,2,1,0:T(8,128)(2,1)S(1)}, u32[]{:S(2)}, u32[]{:S(2)}) collective-permute-start(bf16[32,1,32,128]{3,2,1,0:T(8,128)(2,1)S(1)} %get-tuple-element.50), channel_id=1, source_target_pairs={{0,1},{1,2},{2,3},{3,4},{4,5},{5,6},{6,7},{8,9},{9,10},{10,11},{11... | collective-permute-start | bytes 786440 | tf_op jit(solution)/shard_map/ppermute | solution.py:147
  9.1 5.7 %collective-permute-start.1 = (bf16[32,1,32,128]{3,2,1,0:T(8,128)(2,1)S(1)}, bf16[32,1,32,128]{3,2,1,0:T(8,128)(2,1)S(1)}, u32[]{:S(2)}, u32[]{:S(2)}) collective-permute-start(bf16[32,1,32,128]{3,2,1,0:T(8,128)(2,1)S(1)} %get-tuple-element.51), channel_id=1, source_target_pairs={{1,0},{2,1},{3,2},{4,3},{5,4},{6,5},{7,6},{9,8},{10,9},{11,10},{12... | collective-permute-start | bytes 786440 | tf_op jit(solution)/shard_map/ppermute | solution.py:147
  11.9 2.9 %copy-start = (bf16[1,32,2,32,128]{4,3,2,1,0:T(8,128)(2,1)S(1)}, bf16[1,32,2,32,128]{4,3,2,1,0:T(8,128)(2,1)}, u32[]{:S(2)}) copy-start(bf16[1,32,2,32,128]{4,3,2,1,0:T(8,128)(2,1)} %param.5) | copy-start | bytes 1572868
  21.8 13.0 %collective-permute-start.5 = (bf16[1,32,4096]{2,1,0:T(8,128)(2,1)}, bf16[1,32,4096]{2,1,0:T(8,128)(2,1)S(1)}, u32[]{:S(2)}, u32[]{:S(2)}) collective-permute-start(bf16[1,32,4096]{2,1,0:T(8,128)(2,1)} %get-tuple-element.29), channel_id=1, source_target_pairs={{0,1},{1,2},{2,3},{3,4},{4,5},{5,6},{6,7},{8,9},{9,10},{10,11},{11... | collective-permute-start | bytes 786440 | tf_op jit(solution)/shard_map/ppermute | solution.py:147
  28.5 6.3 %collective-permute-start.6 = (bf16[1,32,4096]{2,1,0:T(8,128)(2,1)}, bf16[1,32,4096]{2,1,0:T(8,128)(2,1)S(1)}, u32[]{:S(2)}, u32[]{:S(2)}) collective-permute-start(bf16[1,32,4096]{2,1,0:T(8,128)(2,1)} %get-tuple-element.30), channel_id=1, source_target_pairs={{1,0},{2,1},{3,2},{4,3},{5,4},{6,5},{7,6},{9,8},{10,9},{11,10},{12... | collective-permute-start | bytes 786440 | tf_op jit(solution)/shard_map/ppermute | solution.py:147
  34.8 1.6 %copy-start.1 = (bf16[1,32,4096]{2,1,0:T(8,128)(2,1)}, bf16[1,32,4096]{2,1,0:T(8,128)(2,1)S(1)}, u32[]{:S(2)}) copy-start(bf16[1,32,4096]{2,1,0:T(8,128)(2,1)S(1)} %collective-permute-done.5.lo) | copy-start | bytes 786436
  34.8 1.6 %copy-start.2 = (bf16[1,32,4096]{2,1,0:T(8,128)(2,1)}, bf16[1,32,4096]{2,1,0:T(8,128)(2,1)S(1)}, u32[]{:S(2)}) copy-start(bf16[1,32,4096]{2,1,0:T(8,128)(2,1)S(1)} %collective-permute-done.6.hi) | copy-start | bytes 786436
  34.8 4.6 %collective-permute-start.7 = (f32[16,865]{1,0:T(8,128)}, f32[16,865]{1,0:T(8,128)S(1)}, u32[]{:S(2)}, u32[]{:S(2)}) collective-permute-start(f32[16,865]{1,0:T(8,128)} %get-tuple-element.31), channel_id=1, source_target_pairs={{0,16},{8,24},{16,0},{24,8},{1,17},{9,25},{17,1},{25,9},{2,18},{10... | collective-permute-start | bytes 166088 | tf_op jit(solution)/shard_map/ppermute | solution.py:152
  36.4 3.0 %copy-start.7 = (f32[16,865]{1,0:T(8,128)S(1)}, f32[16,865]{1,0:T(8,128)}, u32[]{:S(2)}) copy-start(f32[16,865]{1,0:T(8,128)} %get-tuple-element.38) | copy-start | bytes 166084
  39.5 4.6 %collective-permute-start.8 = (f32[8,865]{1,0:T(8,128)S(1)}, f32[8,865]{1,0:T(8,128)S(1)}, u32[]{:S(2)}, u32[]{:S(2)}) collective-permute-start(f32[8,865]{1,0:T(8,128)S(1)} %constant_dynamic-slice_fusion), channel_id=1, source_target_pairs={{0,8},{8,0},{16,24},{24,16},{1,9},{9,1},{17,25},{25,17},{2,10},{10... | collective-permute-start | bytes 83048 | tf_op jit(solution)/shard_map/ppermute | solution.py:152
  41.0 4.1 %copy-start.6 = (bf16[2,32,4096]{2,1,0:T(8,128)(2,1)S(1)}, bf16[2,32,4096]{2,1,0:T(8,128)(2,1)}, u32[]{:S(2)}) copy-start(bf16[2,32,4096]{2,1,0:T(8,128)(2,1)} %get-tuple-element.26) | copy-start | bytes 1572868
  44.1 1.9 %collective-permute-start.9 = (f32[8,865]{1,0:T(8,128)S(1)}, f32[8,865]{1,0:T(8,128)S(1)}, u32[]{:S(2)}, u32[]{:S(2)}) collective-permute-start(f32[8,865]{1,0:T(8,128)S(1)} %dynamic-slice_add_fusion), channel_id=1, source_target_pairs={{0,1},{1,0},{2,3},{3,2},{4,5},{5,4},{6,7},{7,6},{8,9},{9,8},{10,11... | collective-permute-start | bytes 83048 | tf_op jit(solution)/shard_map/ppermute | solution.py:152
  45.1 2.8 %copy-start.3 = (bf16[1,32,4096]{2,1,0:T(8,128)(2,1)S(1)}, bf16[1,32,4096]{2,1,0:T(8,128)(2,1)}, u32[]{:S(2)}) copy-start(bf16[1,32,4096]{2,1,0:T(8,128)(2,1)} %shard_map.86) | copy-start | bytes 786436
  45.1 2.8 %copy-start.4 = (bf16[1,32,4096]{2,1,0:T(8,128)(2,1)S(1)}, bf16[1,32,4096]{2,1,0:T(8,128)(2,1)}, u32[]{:S(2)}) copy-start(bf16[1,32,4096]{2,1,0:T(8,128)(2,1)} %shard_map.87) | copy-start | bytes 786436
  46.0 3.9 %collective-permute-start.10 = (f32[8,865]{1,0:T(8,128)S(1)}, f32[8,865]{1,0:T(8,128)S(1)}, u32[]{:S(2)}, u32[]{:S(2)}) collective-permute-start(f32[8,865]{1,0:T(8,128)S(1)} %add.53), channel_id=1, source_target_pairs={{0,2},{1,3},{2,0},{3,1},{4,6},{5,7},{6,4},{7,5},{8,10},{9,11},{10,... | collective-permute-start | bytes 83048 | tf_op jit(solution)/shard_map/ppermute | solution.py:152
  49.9 4.8 %collective-permute-start.11 = (f32[8,865]{1,0:T(8,128)S(1)}, f32[8,865]{1,0:T(8,128)S(1)}, u32[]{:S(2)}, u32[]{:S(2)}) collective-permute-start(f32[8,865]{1,0:T(8,128)S(1)} %add.54), channel_id=1, source_target_pairs={{0,4},{1,5},{2,6},{3,7},{4,0},{5,1},{6,2},{7,3},{8,12},{9,13},{10,... | collective-permute-start | bytes 83048 | tf_op jit(solution)/shard_map/ppermute | solution.py:152
  54.7 0.7 %copy-start.8 = (f32[8,865]{1,0:T(8,128)}, f32[8,865]{1,0:T(8,128)S(1)}, u32[]{:S(2)}) copy-start(f32[8,865]{1,0:T(8,128)S(1)} %add_multiply_fusion) | copy-start | bytes 83044

commit v11 on v10

--- a/solution.py
+++ b/solution.py
@@ -225,6 +225,7 @@
     below, above = neighbours(field[:, :1], field[:, planes - 1 :], "strike")
     haloed = jnp.concatenate([below, field, above], axis=1)
     haloed = haloed.transpose(1, 0, 2, 3).reshape(planes + 2, chans, lanes)
+    haloed, backward_w = lax.optimization_barrier((haloed, backward_w))
     act, dpre, first, last = forward_call(
         haloed, forward_w, whole_bias.astype(jnp.float32)[:, None], flat(cotangent[0]), mask, depth
     )

time: 55.8 us -> 56 us (level)
  starting transfers between devices: 24.2 us -> 24.9 us
    ppermute x4, waiting for transfers between devices: 1.22 us -> 0.08 us  [neighbours(): return (lax.ppermute(last, axis, up), lax.ppermute(first, axis, down))]
    ppermute x8, waiting for transfers between devices: 3.25 us -> 3.96 us  [swap(): return lax.ppermute(value, axis, [(i, i ^ bit) for i in range(peers)])]
    ppermute x8, starting transfers between devices: 13.6 us -> 14.3 us  [swap(): return lax.ppermute(value, axis, [(i, i ^ bit) for i in range(peers)])]
where the time goes in v11:
time: 56 us; the launch traced here: 55.6 us
  starting transfers between devices  24.9 us (44%)
  Pallas kernels  14.9 us (27%)
  local copies, waits for them, and re-layouts  10 us (18%)
  waiting for transfers between devices  4.04 us (7%)
  other arithmetic  0.96 us (2%)
  between operations  0.87 us (2%)
    ppermute x8, starting transfers between devices, swap(): return lax.ppermute(value, axis, [(i, i ^ bit) for i in range(peers)])  14.3 us
    ppermute x4, starting transfers between devices, neighbours(): return (lax.ppermute(last, axis, up), lax.ppermute(first, axis, down))  10.6 us
    pallas_call x2, Pallas kernels, input_call(): pl.pallas_call(functools.partial(_input_kernel, planes=planes, first=firs...  6.09 us
    pallas_call x1, Pallas kernels, forward_call(): pl.pallas_call(functools.partial(_forward_kernel, planes=planes, depth=de...  5.04 us
    ppermute x8, waiting for transfers between devices, swap(): return lax.ppermute(value, axis, [(i, i ^ bit) for i in range(peers)])  3.96 us
    pallas_call x1, Pallas kernels, weight_call(): pl.pallas_call(functools.partial(_weight_kernel, planes=planes, depth=dep...  3.75 us
    reshape x2, local copies, waits for them, and re-layouts, local(): haloed = haloed.transpose(1, 0, 2, 3).reshape(planes + 2, chans, lanes)  1.86 us
    unnamed x24, local copies, waits for them, and re-layouts  1.56 us
  transfers between devices with their start and end apart: 12, of which 4 were waited for; matrix products, arithmetic and copies ran while one was open for 12% of the time, Pallas kernels for 18%

profile of v11, /device:TPU:0, one launch (start us, length us, event | category | flops | bytes accessed | tf_op | source)
XLA Modules:
  0.0 55.6 jit_solution(3885584009710413839)
XLA Ops:
  0.6 0.0 copy-start.10
  0.6 0.6 %copy-done.10 = bf16[8]{0:T(256)(128)(2,1)S(1)} copy-done((bf16[8]{0:T(256)(128)(2,1)S(1)}, bf16[8]{0:T(256)(128)(2,1)}, u32[]{:S(2)}) %copy-start.10) | copy-done | bytes 40
  1.3 0.1 copy.17
  1.4 0.0 copy-start.9
  1.4 0.7 %copy-done.9 = bf16[8,864]{1,0:T(8,128)(2,1)S(1)} copy-done((bf16[8,864]{1,0:T(8,128)(2,1)S(1)}, bf16[8,864]{1,0:T(8,128)(2,1)}, u32[]{:S(2)}) %copy-start.9) | copy-done | bytes 13848
  2.1 0.1 bitcast_dynamic-update-slice_fusion.3
  2.2 2.9 %collective-permute-start.2 = (bf16[8,865]{1,0:T(8,128)(2,1)S(1)}, bf16[8,865]{1,0:T(8,128)(2,1)S(1)}, u32[]{:S(2)}, u32[]{:S(2)}) collective-permute-start(bf16[8,865]{1,0:T(8,128)(2,1)S(1)} %get-tuple-element.53), channel_id=1, source_target_pairs={{0,8},{8,0},{16,24},{24,16},{1,9},{9,1},{17,25},{25,17},{2,10},{10... | collective-permute-start | bytes 41528 | tf_op jit(solution)/shard_map/ppermute | solution.py:152
  5.1 1.5 %collective-permute-start.3 = (bf16[8,865]{1,0:T(8,128)(2,1)S(1)}, bf16[8,865]{1,0:T(8,128)(2,1)S(1)}, u32[]{:S(2)}, u32[]{:S(2)}) collective-permute-start(bf16[8,865]{1,0:T(8,128)(2,1)S(1)} %get-tuple-element.53), channel_id=1, source_target_pairs={{0,16},{8,24},{16,0},{24,8},{1,17},{9,25},{17,1},{25,9},{2,18},{10... | collective-permute-start | bytes 41528 | tf_op jit(solution)/shard_map/ppermute | solution.py:152
  6.6 0.0 collective-permute-start.4
  6.7 0.0 copy-start.5
  6.7 1.1 %fusion = (bf16[32,1,32,128]{3,2,1,0:T(8,128)(2,1)S(1)}, bf16[32,1,32,128]{3,2,1,0:T(8,128)(2,1)S(1)}) fusion(bf16[32,2,32,128]{3,2,1,0:T(8,128)(2,1)} %bitcast.56), kind=kLoop, calls=%fused_computation.15 | loop fusion | bytes 1048576 | tf_op jit(solution)/shard_map/slice | solution.py:225
  7.8 1.3 %collective-permute-start = (bf16[32,1,32,128]{3,2,1,0:T(8,128)(2,1)S(1)}, bf16[32,1,32,128]{3,2,1,0:T(8,128)(2,1)S(1)}, u32[]{:S(2)}, u32[]{:S(2)}) collective-permute-start(bf16[32,1,32,128]{3,2,1,0:T(8,128)(2,1)S(1)} %get-tuple-element.54), channel_id=1, source_target_pairs={{0,1},{1,2},{2,3},{3,4},{4,5},{5,6},{6,7},{8,9},{9,10},{10,11},{11... | collective-permute-start | bytes 786440 | tf_op jit(solution)/shard_map/ppermute | solution.py:147
  9.1 1.3 %collective-permute-start.1 = (bf16[32,1,32,128]{3,2,1,0:T(8,128)(2,1)S(1)}, bf16[32,1,32,128]{3,2,1,0:T(8,128)(2,1)S(1)}, u32[]{:S(2)}, u32[]{:S(2)}) collective-permute-start(bf16[32,1,32,128]{3,2,1,0:T(8,128)(2,1)S(1)} %get-tuple-element.55), channel_id=1, source_target_pairs={{1,0},{2,1},{3,2},{4,3},{5,4},{6,5},{7,6},{9,8},{10,9},{11,10},{12... | collective-permute-start | bytes 786440 | tf_op jit(solution)/shard_map/ppermute | solution.py:147
  10.4 0.0 copy-done.5
  10.4 0.1 reshape.41
  10.6 1.1 %copy.24.cot = bf16[2,32,4096]{2,1,0:T(8,128)(2,1)} copy(bf16[2,32,4096]{2,0,1:T(2,128)(2,1)S(1)} %reshape.41) | data formatting | bytes 1048576 | tf_op jit(solution)/shard_map/reshape | solution.py:220
  11.6 0.0 collective-permute-done.2
  11.7 0.0 collective-permute-done.3
  11.7 0.0 collective-permute-done.4
  11.7 0.2 reshape.34
  11.9 0.1 reverse_bitcast_fusion
  12.0 0.3 copy.18
  12.3 0.8 %reshape.35.wall = bf16[288,96]{1,0:T(8,128)(2,1)} reshape(bf16[3,3,32,3,32]{4,3,2,1,0:T(4,128)(2,1)S(1)} %copy.18) | data formatting | bytes 110592 | tf_op jit(solution)/shard_map/reshape | solution.py:216
  13.1 0.0 copy-start
  13.1 0.1 copy.19
  13.2 0.8 %reshape.36.wall = bf16[288,96]{1,0:T(8,128)(2,1)} reshape(bf16[3,3,32,3,32]{4,3,2,1,0:T(4,128)(2,1)S(1)} %copy.19) | data formatting | bytes 110592 | tf_op jit(solution)/shard_map/reshape | solution.py:215
  14.0 0.7 %slice_convert_fusion.bias = f32[32,1]{1,0:T(8,128)} fusion(bf16[32,865]{1,0:T(8,128)(2,1)S(1)} %bitcast.63), kind=kLoop, calls=%fused_computation.12 | loop fusion | flops 32 | bytes 192 | tf_op jit(solution)/shard_map/convert_element_type | solution.py:230
  14.7 0.0 collective-permute-done
  14.7 0.1 collective-permute-done.1
  14.8 0.0 copy-done
  14.8 0.1 maximum_bitcast_fusion
  14.9 0.3 reshape.40
  15.2 1.6 %copy.23.haloed = bf16[4,32,4096]{2,1,0:T(8,128)(2,1)} copy(bf16[4,32,4096]{2,0,1:T(4,128)(2,1)S(1)} %reshape.40) | data formatting | bytes 2097152 | tf_op jit(solution)/shard_map/reshape | solution.py:227
  16.8 5.0 %shard_map.84 = (bf16[2,32,4096]{2,1,0:T(8,128)(2,1)}, bf16[2,32,4096]{2,1,0:T(8,128)(2,1)}, bf16[1,32,4096]{2,1,0:T(8,128)(2,1)}, bf16[1,32,4096]{2,1,0:T(8,128)(2,1)}) custom-call(bf16[4,32,4096]{2,1,0:T(8,128)(2,1)} %copy.23.haloed, bf16[288,96]{1,0:T(8,128)(2,1)} %reshape.36.wall, f32[32,1]{1,0:T(8,128)} %slice_convert_fusion.bias, ...), custom_call_target="tpu_custom_call" | custom-call | flops 452984832 | bytes 2621440 | tf_op jit(solution)/shard_map/pallas_call | solution.py:108
  21.8 6.7 %collective-permute-start.5 = (bf16[1,32,4096]{2,1,0:T(8,128)(2,1)}, bf16[1,32,4096]{2,1,0:T(8,128)(2,1)S(1)}, u32[]{:S(2)}, u32[]{:S(2)}) collective-permute-start(bf16[1,32,4096]{2,1,0:T(8,128)(2,1)} %get-tuple-element.32), channel_id=1, source_target_pairs={{0,1},{1,2},{2,3},{3,4},{4,5},{5,6},{6,7},{8,9},{9,10},{10,11},{11... | collective-permute-start | bytes 786440 | tf_op jit(solution)/shard_map/ppermute | solution.py:147
  28.5 1.3 %collective-permute-start.6 = (bf16[1,32,4096]{2,1,0:T(8,128)(2,1)}, bf16[1,32,4096]{2,1,0:T(8,128)(2,1)S(1)}, u32[]{:S(2)}, u32[]{:S(2)}) collective-permute-start(bf16[1,32,4096]{2,1,0:T(8,128)(2,1)} %get-tuple-element.33), channel_id=1, source_target_pairs={{1,0},{2,1},{3,2},{4,3},{5,4},{6,5},{7,6},{9,8},{10,9},{11,10},{12... | collective-permute-start | bytes 786440 | tf_op jit(solution)/shard_map/ppermute | solution.py:147
  29.8 3.7 %shard_map.85 = (f32[16,865]{1,0:T(8,128)}, f32[16,865]{1,0:T(8,128)}) custom-call(s32[1]{0:T(128)} %bitcast.14.upper, bf16[4,32,4096]{2,1,0:T(8,128)(2,1)} %copy.23.haloed, bf16[2,32,4096]{2,1,0:T(8,128)(2,1)} %get-tuple-element.46.dpre.mid, f32[9,1,4096]{2,1,0:T(1,128)} %constant.66.clone.mask), custom_call_target="tpu_custom_call" | custom-call | flops 452984832 | bytes 1572864 | tf_op jit(solution)/shard_map/pallas_call | solution.py:133
  33.6 0.0 collective-permute-done.5.lo
  33.6 0.0 collective-permute-done.6.hi
  33.6 0.0 copy-start.2
  33.6 1.6 %collective-permute-start.7 = (f32[16,865]{1,0:T(8,128)}, f32[16,865]{1,0:T(8,128)S(1)}, u32[]{:S(2)}, u32[]{:S(2)}) collective-permute-start(f32[16,865]{1,0:T(8,128)} %get-tuple-element.35), channel_id=1, source_target_pairs={{0,16},{8,24},{16,0},{24,8},{1,17},{9,25},{17,1},{25,9},{2,18},{10... | collective-permute-start | bytes 166088 | tf_op jit(solution)/shard_map/ppermute | solution.py:152
  35.2 0.0 copy-done.1
  35.2 0.0 copy-done.2
  35.2 3.0 %shard_map.86 = bf16[1,32,4096]{2,1,0:T(8,128)(2,1)} custom-call(bf16[1,32,4096]{2,1,0:T(8,128)(2,1)} %copy-done.1, bf16[2,32,4096]{2,1,0:T(8,128)(2,1)} %get-tuple-element.46.dpre.mid, bf16[1,32,4096]{2,1,0:T(8,128)(2,1)} %copy-done.2, bf16[288,96]{1,0:T(8,128)(2,1)} %reshape.35.wall, f32[9,1,4096]{2,1,0:T(1,128)} %constant.66.clone.mask), custom_call_target="tpu_custom_call" | custom-call | flops 226492416 | bytes 1572864 | tf_op jit(solution)/shard_map/pallas_call | solution.py:120
  38.2 0.0 collective-permute-done.7
  38.2 0.0 copy-done.7
  38.3 1.6 %collective-permute-start.8 = (f32[8,865]{1,0:T(8,128)S(1)}, f32[8,865]{1,0:T(8,128)S(1)}, u32[]{:S(2)}, u32[]{:S(2)}) collective-permute-start(f32[8,865]{1,0:T(8,128)S(1)} %constant_dynamic-slice_fusion), channel_id=1, source_target_pairs={{0,8},{8,0},{16,24},{24,16},{1,9},{9,1},{17,25},{25,17},{2,10},{10... | collective-permute-start | bytes 83048 | tf_op jit(solution)/shard_map/ppermute | solution.py:152
  39.8 3.1 %shard_map.87 = bf16[1,32,4096]{2,1,0:T(8,128)(2,1)} custom-call(bf16[1,32,4096]{2,1,0:T(8,128)(2,1)} %copy-done.1, bf16[2,32,4096]{2,1,0:T(8,128)(2,1)} %get-tuple-element.46.dpre.mid, bf16[1,32,4096]{2,1,0:T(8,128)(2,1)} %copy-done.2, bf16[288,96]{1,0:T(8,128)(2,1)} %reshape.35.wall, f32[9,1,4096]{2,1,0:T(1,128)} %constant.66.clone.mask), custom_call_target="tpu_custom_call" | custom-call | flops 226492416 | bytes 1572864 | tf_op jit(solution)/shard_map/pallas_call | solution.py:120
  42.9 0.0 collective-permute-done.8
  42.9 2.5 %collective-permute-start.9 = (f32[8,865]{1,0:T(8,128)S(1)}, f32[8,865]{1,0:T(8,128)S(1)}, u32[]{:S(2)}, u32[]{:S(2)}) collective-permute-start(f32[8,865]{1,0:T(8,128)S(1)} %dynamic-slice_add_fusion), channel_id=1, source_target_pairs={{0,1},{1,0},{2,3},{3,2},{4,5},{5,4},{6,7},{7,6},{8,9},{9,8},{10,11... | collective-permute-start | bytes 83048 | tf_op jit(solution)/shard_map/ppermute | solution.py:152
  45.4 0.0 copy-done.6
  45.4 0.1 copy.25
  45.5 0.8 %collective-permute-done.9 = f32[8,865]{1,0:T(8,128)S(1)} collective-permute-done((f32[8,865]{1,0:T(8,128)S(1)}, f32[8,865]{1,0:T(8,128)S(1)}, u32[]{:S(2)}, u32[]{:S(2)}) %collective-permute-start.9) | collective-permute-done | bytes 27712 | tf_op jit(solution)/shard_map/ppermute | solution.py:152
  46.3 1.6 %collective-permute-start.10 = (f32[8,865]{1,0:T(8,128)S(1)}, f32[8,865]{1,0:T(8,128)S(1)}, u32[]{:S(2)}, u32[]{:S(2)}) collective-permute-start(f32[8,865]{1,0:T(8,128)S(1)} %add.53), channel_id=1, source_target_pairs={{0,2},{1,3},{2,0},{3,1},{4,6},{5,7},{6,4},{7,5},{8,10},{9,11},{10,... | collective-permute-start | bytes 83048 | tf_op jit(solution)/shard_map/ppermute | solution.py:152
  47.9 0.0 copy-done.3
  47.9 0.0 copy-done.4
  47.9 0.1 pad_maximum_fusion
  47.9 0.1 copy.26
  48.0 2.1 %collective-permute-done.10 = f32[8,865]{1,0:T(8,128)S(1)} collective-permute-done((f32[8,865]{1,0:T(8,128)S(1)}, f32[8,865]{1,0:T(8,128)S(1)}, u32[]{:S(2)}, u32[]{:S(2)}) %collective-permute-start.10) | collective-permute-done | bytes 27712 | tf_op jit(solution)/shard_map/ppermute | solution.py:152
  50.2 2.6 %collective-permute-start.11 = (f32[8,865]{1,0:T(8,128)S(1)}, f32[8,865]{1,0:T(8,128)S(1)}, u32[]{:S(2)}, u32[]{:S(2)}) collective-permute-start(f32[8,865]{1,0:T(8,128)S(1)} %add.54), channel_id=1, source_target_pairs={{0,4},{1,5},{2,6},{3,7},{4,0},{5,1},{6,2},{7,3},{8,12},{9,13},{10,... | collective-permute-start | bytes 83048 | tf_op jit(solution)/shard_map/ppermute | solution.py:152
  52.8 1.1 %copy_bitcast_fusion = (bf16[1,32,2,32,128]{4,3,2,1,0:T(8,128)(2,1)}, bf16[1,32,2,32,128]{4,3,2,1,0:T(8,128)(2,1)}) fusion(bf16[2,32,32,128]{3,2,1,0:T(8,128)(2,1)S(1)} %bitcast.58, bf16[2,32,32,128]{3,2,1,0:T(8,128)(2,1)S(1)} %bitcast.59), kind=kLoop, calls=%fused_computation.2 | loop fusion | bytes 2097152 | tf_op jit(solution)/shard_map/broadcast_in_dim | solution.py:243
  53.9 1.1 %collective-permute-done.11 = f32[8,865]{1,0:T(8,128)S(1)} collective-permute-done((f32[8,865]{1,0:T(8,128)S(1)}, f32[8,865]{1,0:T(8,128)S(1)}, u32[]{:S(2)}, u32[]{:S(2)}) %collective-permute-start.11) | collective-permute-done | bytes 27712 | tf_op jit(solution)/shard_map/ppermute | solution.py:152
  54.9 0.7 %slice_reduce_fusion = f32[8]{0:T(128)} fusion(f32[8,865]{1,0:T(8,128)S(1)} %add_multiply_fusion), kind=kLoop, calls=%fused_computation.13 | loop fusion | bytes 64 | tf_op jit(solution)/shard_map/slice | solution.py:243
  55.6 0.0 copy-done.8
  (16 shorter events, 0.1 us)
Async XLA Ops:
  0.6 0.7 %copy-start.10 = (bf16[8]{0:T(256)(128)(2,1)S(1)}, bf16[8]{0:T(256)(128)(2,1)}, u32[]{:S(2)}) copy-start(bf16[8]{0:T(256)(128)(2,1)} %param.8) | copy-start | bytes 52
  1.4 0.7 %copy-start.9 = (bf16[8,864]{1,0:T(8,128)(2,1)S(1)}, bf16[8,864]{1,0:T(8,128)(2,1)}, u32[]{:S(2)}) copy-start(bf16[8,864]{1,0:T(8,128)(2,1)} %param.7) | copy-start | bytes 41476
  2.2 9.5 %collective-permute-start.2 = (bf16[8,865]{1,0:T(8,128)(2,1)S(1)}, bf16[8,865]{1,0:T(8,128)(2,1)S(1)}, u32[]{:S(2)}, u32[]{:S(2)}) collective-permute-start(bf16[8,865]{1,0:T(8,128)(2,1)S(1)} %get-tuple-element.53), channel_id=1, source_target_pairs={{0,8},{8,0},{16,24},{24,16},{1,9},{9,1},{17,25},{25,17},{2,10},{10... | collective-permute-start | bytes 41528 | tf_op jit(solution)/shard_map/ppermute | solution.py:152
  5.1 6.5 %collective-permute-start.3 = (bf16[8,865]{1,0:T(8,128)(2,1)S(1)}, bf16[8,865]{1,0:T(8,128)(2,1)S(1)}, u32[]{:S(2)}, u32[]{:S(2)}) collective-permute-start(bf16[8,865]{1,0:T(8,128)(2,1)S(1)} %get-tuple-element.53), channel_id=1, source_target_pairs={{0,16},{8,24},{16,0},{24,8},{1,17},{9,25},{17,1},{25,9},{2,18},{10... | collective-permute-start | bytes 41528 | tf_op jit(solution)/shard_map/ppermute | solution.py:152
  6.6 5.0 %collective-permute-start.4 = (bf16[8,865]{1,0:T(8,128)(2,1)S(1)}, bf16[8,865]{1,0:T(8,128)(2,1)S(1)}, u32[]{:S(2)}, u32[]{:S(2)}) collective-permute-start(bf16[8,865]{1,0:T(8,128)(2,1)S(1)} %get-tuple-element.53), channel_id=1, source_target_pairs={{0,24},{8,16},{16,8},{24,0},{1,25},{9,17},{17,9},{25,1},{2,26},{10... | collective-permute-start | bytes 41528 | tf_op jit(solution)/shard_map/ppermute | solution.py:152
  6.7 3.8 %copy-start.5 = (bf16[1,32,2,32,128]{4,3,2,1,0:T(8,128)(2,1)S(1)}, bf16[1,32,2,32,128]{4,3,2,1,0:T(8,128)(2,1)}, u32[]{:S(2)}) copy-start(bf16[1,32,2,32,128]{4,3,2,1,0:T(8,128)(2,1)} %param.6) | copy-start | bytes 1572868
  7.8 6.9 %collective-permute-start = (bf16[32,1,32,128]{3,2,1,0:T(8,128)(2,1)S(1)}, bf16[32,1,32,128]{3,2,1,0:T(8,128)(2,1)S(1)}, u32[]{:S(2)}, u32[]{:S(2)}) collective-permute-start(bf16[32,1,32,128]{3,2,1,0:T(8,128)(2,1)S(1)} %get-tuple-element.54), channel_id=1, source_target_pairs={{0,1},{1,2},{2,3},{3,4},{4,5},{5,6},{6,7},{8,9},{9,10},{10,11},{11... | collective-permute-start | bytes 786440 | tf_op jit(solution)/shard_map/ppermute | solution.py:147
  9.1 5.7 %collective-permute-start.1 = (bf16[32,1,32,128]{3,2,1,0:T(8,128)(2,1)S(1)}, bf16[32,1,32,128]{3,2,1,0:T(8,128)(2,1)S(1)}, u32[]{:S(2)}, u32[]{:S(2)}) collective-permute-start(bf16[32,1,32,128]{3,2,1,0:T(8,128)(2,1)S(1)} %get-tuple-element.55), channel_id=1, source_target_pairs={{1,0},{2,1},{3,2},{4,3},{5,4},{6,5},{7,6},{9,8},{10,9},{11,10},{12... | collective-permute-start | bytes 786440 | tf_op jit(solution)/shard_map/ppermute | solution.py:147
  13.1 1.7 %copy-start = (bf16[1,32,2,32,128]{4,3,2,1,0:T(8,128)(2,1)S(1)}, bf16[1,32,2,32,128]{4,3,2,1,0:T(8,128)(2,1)}, u32[]{:S(2)}) copy-start(bf16[1,32,2,32,128]{4,3,2,1,0:T(8,128)(2,1)} %param.5) | copy-start | bytes 1572868
  21.8 11.8 %collective-permute-start.5 = (bf16[1,32,4096]{2,1,0:T(8,128)(2,1)}, bf16[1,32,4096]{2,1,0:T(8,128)(2,1)S(1)}, u32[]{:S(2)}, u32[]{:S(2)}) collective-permute-start(bf16[1,32,4096]{2,1,0:T(8,128)(2,1)} %get-tuple-element.32), channel_id=1, source_target_pairs={{0,1},{1,2},{2,3},{3,4},{4,5},{5,6},{6,7},{8,9},{9,10},{10,11},{11... | collective-permute-start | bytes 786440 | tf_op jit(solution)/shard_map/ppermute | solution.py:147
  28.5 5.1 %collective-permute-start.6 = (bf16[1,32,4096]{2,1,0:T(8,128)(2,1)}, bf16[1,32,4096]{2,1,0:T(8,128)(2,1)S(1)}, u32[]{:S(2)}, u32[]{:S(2)}) collective-permute-start(bf16[1,32,4096]{2,1,0:T(8,128)(2,1)} %get-tuple-element.33), channel_id=1, source_target_pairs={{1,0},{2,1},{3,2},{4,3},{5,4},{6,5},{7,6},{9,8},{10,9},{11,10},{12... | collective-permute-start | bytes 786440 | tf_op jit(solution)/shard_map/ppermute | solution.py:147
  33.6 1.6 %copy-start.1 = (bf16[1,32,4096]{2,1,0:T(8,128)(2,1)}, bf16[1,32,4096]{2,1,0:T(8,128)(2,1)S(1)}, u32[]{:S(2)}) copy-start(bf16[1,32,4096]{2,1,0:T(8,128)(2,1)S(1)} %collective-permute-done.5.lo) | copy-start | bytes 786436
  33.6 1.6 %copy-start.2 = (bf16[1,32,4096]{2,1,0:T(8,128)(2,1)}, bf16[1,32,4096]{2,1,0:T(8,128)(2,1)S(1)}, u32[]{:S(2)}) copy-start(bf16[1,32,4096]{2,1,0:T(8,128)(2,1)S(1)} %collective-permute-done.6.hi) | copy-start | bytes 786436
  33.6 4.6 %collective-permute-start.7 = (f32[16,865]{1,0:T(8,128)}, f32[16,865]{1,0:T(8,128)S(1)}, u32[]{:S(2)}, u32[]{:S(2)}) collective-permute-start(f32[16,865]{1,0:T(8,128)} %get-tuple-element.35), channel_id=1, source_target_pairs={{0,16},{8,24},{16,0},{24,8},{1,17},{9,25},{17,1},{25,9},{2,18},{10... | collective-permute-start | bytes 166088 | tf_op jit(solution)/shard_map/ppermute | solution.py:152
  35.2 3.0 %copy-start.7 = (f32[16,865]{1,0:T(8,128)S(1)}, f32[16,865]{1,0:T(8,128)}, u32[]{:S(2)}) copy-start(f32[16,865]{1,0:T(8,128)} %get-tuple-element.42) | copy-start | bytes 166084
  38.3 4.6 %collective-permute-start.8 = (f32[8,865]{1,0:T(8,128)S(1)}, f32[8,865]{1,0:T(8,128)S(1)}, u32[]{:S(2)}, u32[]{:S(2)}) collective-permute-start(f32[8,865]{1,0:T(8,128)S(1)} %constant_dynamic-slice_fusion), channel_id=1, source_target_pairs={{0,8},{8,0},{16,24},{24,16},{1,9},{9,1},{17,25},{25,17},{2,10},{10... | collective-permute-start | bytes 83048 | tf_op jit(solution)/shard_map/ppermute | solution.py:152
  39.8 5.6 %copy-start.6 = (bf16[2,32,4096]{2,1,0:T(8,128)(2,1)S(1)}, bf16[2,32,4096]{2,1,0:T(8,128)(2,1)}, u32[]{:S(2)}) copy-start(bf16[2,32,4096]{2,1,0:T(8,128)(2,1)} %get-tuple-element.29) | copy-start | bytes 1572868
  42.9 3.4 %collective-permute-start.9 = (f32[8,865]{1,0:T(8,128)S(1)}, f32[8,865]{1,0:T(8,128)S(1)}, u32[]{:S(2)}, u32[]{:S(2)}) collective-permute-start(f32[8,865]{1,0:T(8,128)S(1)} %dynamic-slice_add_fusion), channel_id=1, source_target_pairs={{0,1},{1,0},{2,3},{3,2},{4,5},{5,4},{6,7},{7,6},{8,9},{9,8},{10,11... | collective-permute-start | bytes 83048 | tf_op jit(solution)/shard_map/ppermute | solution.py:152
  45.4 2.4 %copy-start.3 = (bf16[1,32,4096]{2,1,0:T(8,128)(2,1)S(1)}, bf16[1,32,4096]{2,1,0:T(8,128)(2,1)}, u32[]{:S(2)}) copy-start(bf16[1,32,4096]{2,1,0:T(8,128)(2,1)} %shard_map.86) | copy-start | bytes 786436
  45.4 2.4 %copy-start.4 = (bf16[1,32,4096]{2,1,0:T(8,128)(2,1)S(1)}, bf16[1,32,4096]{2,1,0:T(8,128)(2,1)}, u32[]{:S(2)}) copy-start(bf16[1,32,4096]{2,1,0:T(8,128)(2,1)} %shard_map.87) | copy-start | bytes 786436
  46.3 3.9 %collective-permute-start.10 = (f32[8,865]{1,0:T(8,128)S(1)}, f32[8,865]{1,0:T(8,128)S(1)}, u32[]{:S(2)}, u32[]{:S(2)}) collective-permute-start(f32[8,865]{1,0:T(8,128)S(1)} %add.53), channel_id=1, source_target_pairs={{0,2},{1,3},{2,0},{3,1},{4,6},{5,7},{6,4},{7,5},{8,10},{9,11},{10,... | collective-permute-start | bytes 83048 | tf_op jit(solution)/shard_map/ppermute | solution.py:152
  50.2 4.8 %collective-permute-start.11 = (f32[8,865]{1,0:T(8,128)S(1)}, f32[8,865]{1,0:T(8,128)S(1)}, u32[]{:S(2)}, u32[]{:S(2)}) collective-permute-start(f32[8,865]{1,0:T(8,128)S(1)} %add.54), channel_id=1, source_target_pairs={{0,4},{1,5},{2,6},{3,7},{4,0},{5,1},{6,2},{7,3},{8,12},{9,13},{10,... | collective-permute-start | bytes 83048 | tf_op jit(solution)/shard_map/ppermute | solution.py:152
  54.9 0.7 %copy-start.8 = (f32[8,865]{1,0:T(8,128)}, f32[8,865]{1,0:T(8,128)S(1)}, u32[]{:S(2)}) copy-start(f32[8,865]{1,0:T(8,128)S(1)} %add_multiply_fusion) | copy-start | bytes 83044

commit v12 on v11

--- a/solution.py
+++ b/solution.py
@@ -208,6 +208,9 @@
     lanes = rows * depth
     taps_in = weight.shape[1]
     packed = jnp.concatenate([weight, bias[:, None]], axis=1)
+    edges = (field[:, :1], field[:, planes - 1 :])
+    below, above = neighbours(*edges, "strike")
+    packed, below = lax.optimization_barrier((packed, below))
     whole = gather_rows(packed, "real")
     whole_weight, whole_bias = whole[:, :taps_in], whole[:, taps_in]
     out_chan = whole_weight.shape[0]
@@ -222,7 +225,6 @@
     def unflat(value):
         return value.reshape(planes, value.shape[1], rows, depth).transpose(1, 0, 2, 3)
 
-    below, above = neighbours(field[:, :1], field[:, planes - 1 :], "strike")
     haloed = jnp.concatenate([below, field, above], axis=1)
     haloed = haloed.transpose(1, 0, 2, 3).reshape(planes + 2, chans, lanes)
     haloed, backward_w = lax.optimization_barrier((haloed, backward_w))

time: 56 us -> 55.9 us (level)
  waiting for transfers between devices: 4.04 us -> 9.15 us
  starting transfers between devices: 24.9 us -> 20.8 us
  local copies, waits for them, and re-layouts: 10 us -> 8.86 us
    ppermute x8, waiting for transfers between devices: 3.96 us -> 7.42 us  [swap(): return lax.ppermute(value, axis, [(i, i ^ bit) for i in range(peers)])]
    ppermute x4, starting transfers between devices: 10.6 us -> 8.08 us  [neighbours(): return (lax.ppermute(last, axis, up), lax.ppermute(first, axis, down))]
    ppermute x4, waiting for transfers between devices: 0.08 us -> 1.73 us  [neighbours(): return (lax.ppermute(last, axis, up), lax.ppermute(first, axis, down))]
    ppermute x8, starting transfers between devices: 14.3 us -> 12.8 us  [swap(): return lax.ppermute(value, axis, [(i, i ^ bit) for i in range(peers)])]
    unnamed x24, local copies, waits for them, and re-layouts: 1.56 us -> 0.42 us
  transfers between devices with their start and end apart: 12 -> 12, of which waited for: 4 -> 8; matrix products, arithmetic and copies ran while one was open for 12% -> 8% of each run, Pallas kernels for 18% -> 18%
where the time goes in v12:
time: 55.9 us; the launch traced here: 55.6 us
  starting transfers between devices  20.8 us (37%)
  Pallas kernels  14.9 us (27%)
  waiting for transfers between devices  9.15 us (16%)
  local copies, waits for them, and re-layouts  8.86 us (16%)
  other arithmetic  0.96 us (2%)
  between operations  0.87 us (2%)
    ppermute x8, starting transfers between devices, swap(): return lax.ppermute(value, axis, [(i, i ^ bit) for i in range(peers)])  12.8 us
    ppermute x4, starting transfers between devices, neighbours(): return (lax.ppermute(last, axis, up), lax.ppermute(first, axis, down))  8.08 us
    ppermute x8, waiting for transfers between devices, swap(): return lax.ppermute(value, axis, [(i, i ^ bit) for i in range(peers)])  7.42 us
    pallas_call x2, Pallas kernels, input_call(): pl.pallas_call(functools.partial(_input_kernel, planes=planes, first=firs...  6.11 us
    pallas_call x1, Pallas kernels, forward_call(): pl.pallas_call(functools.partial(_forward_kernel, planes=planes, depth=de...  5.05 us
    pallas_call x1, Pallas kernels, weight_call(): pl.pallas_call(functools.partial(_weight_kernel, planes=planes, depth=dep...  3.75 us
    reshape x2, local copies, waits for them, and re-layouts, local(): haloed = haloed.transpose(1, 0, 2, 3).reshape(planes + 2, chans, lanes)  1.85 us
    ppermute x4, waiting for transfers between devices, neighbours(): return (lax.ppermute(last, axis, up), lax.ppermute(first, axis, down))  1.73 us
  transfers between devices with their start and end apart: 12, of which 8 were waited for; matrix products, arithmetic and copies ran while one was open for 8% of the time, Pallas kernels for 18%

profile of v12, /device:TPU:0, one launch (start us, length us, event | category | flops | bytes accessed | tf_op | source)
XLA Modules:
  0.0 55.6 jit_solution(1177337324788797875)
XLA Ops:
  0.6 0.0 copy-start.9
  0.6 0.0 copy-start.5
  0.7 1.1 %fusion = (bf16[32,1,32,128]{3,2,1,0:T(8,128)(2,1)S(1)}, bf16[32,1,32,128]{3,2,1,0:T(8,128)(2,1)S(1)}) fusion(bf16[32,2,32,128]{3,2,1,0:T(8,128)(2,1)} %bitcast.56), kind=kLoop, calls=%fused_computation.15 | loop fusion | bytes 1048576 | tf_op jit(solution)/shard_map/slice | solution.py:211
  1.8 2.4 %collective-permute-start = (bf16[32,1,32,128]{3,2,1,0:T(8,128)(2,1)S(1)}, bf16[32,1,32,128]{3,2,1,0:T(8,128)(2,1)S(1)}, u32[]{:S(2)}, u32[]{:S(2)}) collective-permute-start(bf16[32,1,32,128]{3,2,1,0:T(8,128)(2,1)S(1)} %get-tuple-element.56), channel_id=1, source_target_pairs={{0,1},{1,2},{2,3},{3,4},{4,5},{5,6},{6,7},{8,9},{9,10},{10,11},{11... | collective-permute-start | bytes 786440 | tf_op jit(solution)/shard_map/ppermute | solution.py:147
  4.2 0.0 copy-start.10
  4.2 1.3 %collective-permute-start.1 = (bf16[32,1,32,128]{3,2,1,0:T(8,128)(2,1)S(1)}, bf16[32,1,32,128]{3,2,1,0:T(8,128)(2,1)S(1)}, u32[]{:S(2)}, u32[]{:S(2)}) collective-permute-start(bf16[32,1,32,128]{3,2,1,0:T(8,128)(2,1)S(1)} %get-tuple-element.57), channel_id=1, source_target_pairs={{1,0},{2,1},{3,2},{4,3},{5,4},{6,5},{7,6},{9,8},{10,9},{11,10},{12... | collective-permute-start | bytes 786440 | tf_op jit(solution)/shard_map/ppermute | solution.py:147
  5.5 0.0 copy-done.10
  5.5 0.1 copy.16
  5.6 0.0 copy-done.9
  5.6 0.1 pad_maximum_fusion.1
  5.7 0.0 copy-done.5
  5.7 0.1 reshape.41
  5.8 0.0 copy-start
  5.8 1.1 %copy.24.cot = bf16[2,32,4096]{2,1,0:T(8,128)(2,1)} copy(bf16[2,32,4096]{2,0,1:T(2,128)(2,1)S(1)} %reshape.41) | data formatting | bytes 1048576 | tf_op jit(solution)/shard_map/reshape | solution.py:223
  6.9 0.0 collective-permute-done
  6.9 2.3 %collective-permute-start.2 = (bf16[8,865]{1,0:T(8,128)(2,1)S(1)}, bf16[8,865]{1,0:T(8,128)(2,1)S(1)}, u32[]{:S(2)}, u32[]{:S(2)}) collective-permute-start(bf16[8,865]{1,0:T(8,128)(2,1)S(1)} %pad_maximum_fusion.1), channel_id=1, source_target_pairs={{0,8},{8,0},{16,24},{24,16},{1,9},{9,1},{17,25},{25,17},{2,10},{10... | collective-permute-start | bytes 41528 | tf_op jit(solution)/shard_map/ppermute | solution.py:152
  9.2 1.5 %collective-permute-start.3 = (bf16[8,865]{1,0:T(8,128)(2,1)S(1)}, bf16[8,865]{1,0:T(8,128)(2,1)S(1)}, u32[]{:S(2)}, u32[]{:S(2)}) collective-permute-start(bf16[8,865]{1,0:T(8,128)(2,1)S(1)} %pad_maximum_fusion.1), channel_id=1, source_target_pairs={{0,16},{8,24},{16,0},{24,8},{1,17},{9,25},{17,1},{25,9},{2,18},{10... | collective-permute-start | bytes 41528 | tf_op jit(solution)/shard_map/ppermute | solution.py:152
  10.7 0.0 collective-permute-start.4
  10.8 0.0 collective-permute-done.1
  10.8 0.0 copy-done
  10.8 0.1 maximum_bitcast_fusion
  10.9 0.3 reshape.40
  11.2 1.6 %copy.23.haloed = bf16[4,32,4096]{2,1,0:T(8,128)(2,1)} copy(bf16[4,32,4096]{2,0,1:T(4,128)(2,1)S(1)} %reshape.40) | data formatting | bytes 2097152 | tf_op jit(solution)/shard_map/reshape | solution.py:229
  12.8 0.0 collective-permute-done.2
  12.8 0.2 collective-permute-done.3
  12.9 2.4 %collective-permute-done.4 = bf16[8,865]{1,0:T(8,128)(2,1)S(1)} collective-permute-done((bf16[8,865]{1,0:T(8,128)(2,1)S(1)}, bf16[8,865]{1,0:T(8,128)(2,1)S(1)}, u32[]{:S(2)}, u32[]{:S(2)}) %collective-permute-start.4) | collective-permute-done | bytes 13872 | tf_op jit(solution)/shard_map/ppermute | solution.py:152
  15.4 0.7 %slice_convert_fusion.bias = f32[32,1]{1,0:T(8,128)} fusion(bf16[32,865]{1,0:T(8,128)(2,1)S(1)} %bitcast.62), kind=kLoop, calls=%fused_computation.12 | loop fusion | flops 32 | bytes 192 | tf_op jit(solution)/shard_map/convert_element_type | solution.py:232
  16.0 0.2 reshape.34
  16.2 0.1 reverse_bitcast_fusion
  16.4 0.3 copy.18
  16.6 0.8 %reshape.35.wall = bf16[288,96]{1,0:T(8,128)(2,1)} reshape(bf16[3,3,32,3,32]{4,3,2,1,0:T(4,128)(2,1)S(1)} %copy.18) | data formatting | bytes 110592 | tf_op jit(solution)/shard_map/reshape | solution.py:219
  17.4 0.1 copy.19
  17.6 0.8 %reshape.36.wall = bf16[288,96]{1,0:T(8,128)(2,1)} reshape(bf16[3,3,32,3,32]{4,3,2,1,0:T(4,128)(2,1)S(1)} %copy.19) | data formatting | bytes 110592 | tf_op jit(solution)/shard_map/reshape | solution.py:218
  18.4 5.0 %shard_map.84 = (bf16[2,32,4096]{2,1,0:T(8,128)(2,1)}, bf16[2,32,4096]{2,1,0:T(8,128)(2,1)}, bf16[1,32,4096]{2,1,0:T(8,128)(2,1)}, bf16[1,32,4096]{2,1,0:T(8,128)(2,1)}) custom-call(bf16[4,32,4096]{2,1,0:T(8,128)(2,1)} %copy.23.haloed, bf16[288,96]{1,0:T(8,128)(2,1)} %reshape.36.wall, f32[32,1]{1,0:T(8,128)} %slice_convert_fusion.bias, ...), custom_call_target="tpu_custom_call" | custom-call | flops 452984832 | bytes 2621440 | tf_op jit(solution)/shard_map/pallas_call | solution.py:108
  23.4 3.1 %collective-permute-start.5 = (bf16[1,32,4096]{2,1,0:T(8,128)(2,1)}, bf16[1,32,4096]{2,1,0:T(8,128)(2,1)S(1)}, u32[]{:S(2)}, u32[]{:S(2)}) collective-permute-start(bf16[1,32,4096]{2,1,0:T(8,128)(2,1)} %get-tuple-element.36), channel_id=1, source_target_pairs={{0,1},{1,2},{2,3},{3,4},{4,5},{5,6},{6,7},{8,9},{9,10},{10,11},{11... | collective-permute-start | bytes 786440 | tf_op jit(solution)/shard_map/ppermute | solution.py:147
  26.5 1.3 %collective-permute-start.6 = (bf16[1,32,4096]{2,1,0:T(8,128)(2,1)}, bf16[1,32,4096]{2,1,0:T(8,128)(2,1)S(1)}, u32[]{:S(2)}, u32[]{:S(2)}) collective-permute-start(bf16[1,32,4096]{2,1,0:T(8,128)(2,1)} %get-tuple-element.37), channel_id=1, source_target_pairs={{1,0},{2,1},{3,2},{4,3},{5,4},{6,5},{7,6},{9,8},{10,9},{11,10},{12... | collective-permute-start | bytes 786440 | tf_op jit(solution)/shard_map/ppermute | solution.py:147
  27.9 3.7 %shard_map.85 = (f32[16,865]{1,0:T(8,128)}, f32[16,865]{1,0:T(8,128)}) custom-call(s32[1]{0:T(128)} %bitcast.14.upper, bf16[4,32,4096]{2,1,0:T(8,128)(2,1)} %copy.23.haloed, bf16[2,32,4096]{2,1,0:T(8,128)(2,1)} %get-tuple-element.50.dpre.mid, f32[9,1,4096]{2,1,0:T(1,128)} %constant.66.clone.mask), custom_call_target="tpu_custom_call" | custom-call | flops 452984832 | bytes 1572864 | tf_op jit(solution)/shard_map/pallas_call | solution.py:133
  31.6 0.0 collective-permute-done.5.lo
  31.6 0.0 copy-start.1
  31.6 1.7 %collective-permute-done.6.hi = bf16[1,32,4096]{2,1,0:T(8,128)(2,1)S(1)} collective-permute-done((bf16[1,32,4096]{2,1,0:T(8,128)(2,1)}, bf16[1,32,4096]{2,1,0:T(8,128)(2,1)S(1)}, u32[]{:S(2)}, u32[]{:S(2)}) %collective-permute-start.6) | collective-permute-done | bytes 262176 | tf_op jit(solution)/shard_map/ppermute | solution.py:147
  33.4 0.5 collective-permute-start.7
  33.9 0.0 copy-done.1
  33.9 0.2 copy-done.2
  34.1 3.0 %shard_map.86 = bf16[1,32,4096]{2,1,0:T(8,128)(2,1)} custom-call(bf16[1,32,4096]{2,1,0:T(8,128)(2,1)} %copy-done.1, bf16[2,32,4096]{2,1,0:T(8,128)(2,1)} %get-tuple-element.50.dpre.mid, bf16[1,32,4096]{2,1,0:T(8,128)(2,1)} %copy-done.2, bf16[288,96]{1,0:T(8,128)(2,1)} %reshape.35.wall, f32[9,1,4096]{2,1,0:T(1,128)} %constant.66.clone.mask), custom_call_target="tpu_custom_call" | custom-call | flops 226492416 | bytes 1572864 | tf_op jit(solution)/shard_map/pallas_call | solution.py:120
  37.1 0.6 %collective-permute-done.7 = f32[16,865]{1,0:T(8,128)S(1)} collective-permute-done((f32[16,865]{1,0:T(8,128)}, f32[16,865]{1,0:T(8,128)S(1)}, u32[]{:S(2)}, u32[]{:S(2)}) %collective-permute-start.7) | collective-permute-done | bytes 55392 | tf_op jit(solution)/shard_map/ppermute | solution.py:152
  37.7 0.0 copy-done.7
  37.8 0.6 %collective-permute-start.8 = (f32[8,865]{1,0:T(8,128)S(1)}, f32[8,865]{1,0:T(8,128)S(1)}, u32[]{:S(2)}, u32[]{:S(2)}) collective-permute-start(f32[8,865]{1,0:T(8,128)S(1)} %constant_dynamic-slice_fusion), channel_id=1, source_target_pairs={{0,8},{8,0},{16,24},{24,16},{1,9},{9,1},{17,25},{25,17},{2,10},{10... | collective-permute-start | bytes 83048 | tf_op jit(solution)/shard_map/ppermute | solution.py:152
  38.4 3.1 %shard_map.87 = bf16[1,32,4096]{2,1,0:T(8,128)(2,1)} custom-call(bf16[1,32,4096]{2,1,0:T(8,128)(2,1)} %copy-done.1, bf16[2,32,4096]{2,1,0:T(8,128)(2,1)} %get-tuple-element.50.dpre.mid, bf16[1,32,4096]{2,1,0:T(8,128)(2,1)} %copy-done.2, bf16[288,96]{1,0:T(8,128)(2,1)} %reshape.35.wall, f32[9,1,4096]{2,1,0:T(1,128)} %constant.66.clone.mask), custom_call_target="tpu_custom_call" | custom-call | flops 226492416 | bytes 1572864 | tf_op jit(solution)/shard_map/pallas_call | solution.py:120
  41.4 0.3 collective-permute-done.8
  41.7 3.6 %collective-permute-start.9 = (f32[8,865]{1,0:T(8,128)S(1)}, f32[8,865]{1,0:T(8,128)S(1)}, u32[]{:S(2)}, u32[]{:S(2)}) collective-permute-start(f32[8,865]{1,0:T(8,128)S(1)} %dynamic-slice_add_fusion), channel_id=1, source_target_pairs={{0,1},{1,0},{2,3},{3,2},{4,5},{5,4},{6,7},{7,6},{8,9},{9,8},{10,11... | collective-permute-start | bytes 83048 | tf_op jit(solution)/shard_map/ppermute | solution.py:152
  45.4 0.0 copy-done.6
  45.4 0.1 copy.25
  45.5 0.8 %collective-permute-done.9 = f32[8,865]{1,0:T(8,128)S(1)} collective-permute-done((f32[8,865]{1,0:T(8,128)S(1)}, f32[8,865]{1,0:T(8,128)S(1)}, u32[]{:S(2)}, u32[]{:S(2)}) %collective-permute-start.9) | collective-permute-done | bytes 27712 | tf_op jit(solution)/shard_map/ppermute | solution.py:152
  46.2 1.6 %collective-permute-start.10 = (f32[8,865]{1,0:T(8,128)S(1)}, f32[8,865]{1,0:T(8,128)S(1)}, u32[]{:S(2)}, u32[]{:S(2)}) collective-permute-start(f32[8,865]{1,0:T(8,128)S(1)} %add.53), channel_id=1, source_target_pairs={{0,2},{1,3},{2,0},{3,1},{4,6},{5,7},{6,4},{7,5},{8,10},{9,11},{10,... | collective-permute-start | bytes 83048 | tf_op jit(solution)/shard_map/ppermute | solution.py:152
  47.8 0.0 copy-done.3
  47.8 0.0 copy-done.4
  47.8 0.1 pad_maximum_fusion
  47.9 0.1 copy.26
  48.0 2.1 %collective-permute-done.10 = f32[8,865]{1,0:T(8,128)S(1)} collective-permute-done((f32[8,865]{1,0:T(8,128)S(1)}, f32[8,865]{1,0:T(8,128)S(1)}, u32[]{:S(2)}, u32[]{:S(2)}) %collective-permute-start.10) | collective-permute-done | bytes 27712 | tf_op jit(solution)/shard_map/ppermute | solution.py:152
  50.1 2.6 %collective-permute-start.11 = (f32[8,865]{1,0:T(8,128)S(1)}, f32[8,865]{1,0:T(8,128)S(1)}, u32[]{:S(2)}, u32[]{:S(2)}) collective-permute-start(f32[8,865]{1,0:T(8,128)S(1)} %add.54), channel_id=1, source_target_pairs={{0,4},{1,5},{2,6},{3,7},{4,0},{5,1},{6,2},{7,3},{8,12},{9,13},{10,... | collective-permute-start | bytes 83048 | tf_op jit(solution)/shard_map/ppermute | solution.py:152
  52.7 1.1 %copy_bitcast_fusion = (bf16[1,32,2,32,128]{4,3,2,1,0:T(8,128)(2,1)}, bf16[1,32,2,32,128]{4,3,2,1,0:T(8,128)(2,1)}) fusion(bf16[2,32,32,128]{3,2,1,0:T(8,128)(2,1)S(1)} %bitcast.58, bf16[2,32,32,128]{3,2,1,0:T(8,128)(2,1)S(1)} %bitcast.59), kind=kLoop, calls=%fused_computation.2 | loop fusion | bytes 2097152 | tf_op jit(solution)/shard_map/broadcast_in_dim | solution.py:245
  53.8 1.1 %collective-permute-done.11 = f32[8,865]{1,0:T(8,128)S(1)} collective-permute-done((f32[8,865]{1,0:T(8,128)S(1)}, f32[8,865]{1,0:T(8,128)S(1)}, u32[]{:S(2)}, u32[]{:S(2)}) %collective-permute-start.11) | collective-permute-done | bytes 27712 | tf_op jit(solution)/shard_map/ppermute | solution.py:152
  54.9 0.7 %slice_reduce_fusion = f32[8]{0:T(128)} fusion(f32[8,865]{1,0:T(8,128)S(1)} %add_multiply_fusion), kind=kLoop, calls=%fused_computation.13 | loop fusion | bytes 64 | tf_op jit(solution)/shard_map/slice | solution.py:245
  55.6 0.0 copy-done.8
  (17 shorter events, 0.1 us)
Async XLA Ops:
  0.6 5.0 %copy-start.9 = (bf16[8,864]{1,0:T(8,128)(2,1)S(1)}, bf16[8,864]{1,0:T(8,128)(2,1)}, u32[]{:S(2)}) copy-start(bf16[8,864]{1,0:T(8,128)(2,1)} %param.7) | copy-start | bytes 41476
  0.6 5.0 %copy-start.5 = (bf16[1,32,2,32,128]{4,3,2,1,0:T(8,128)(2,1)S(1)}, bf16[1,32,2,32,128]{4,3,2,1,0:T(8,128)(2,1)}, u32[]{:S(2)}) copy-start(bf16[1,32,2,32,128]{4,3,2,1,0:T(8,128)(2,1)} %param.6) | copy-start | bytes 1572868
  1.8 5.1 %collective-permute-start = (bf16[32,1,32,128]{3,2,1,0:T(8,128)(2,1)S(1)}, bf16[32,1,32,128]{3,2,1,0:T(8,128)(2,1)S(1)}, u32[]{:S(2)}, u32[]{:S(2)}) collective-permute-start(bf16[32,1,32,128]{3,2,1,0:T(8,128)(2,1)S(1)} %get-tuple-element.56), channel_id=1, source_target_pairs={{0,1},{1,2},{2,3},{3,4},{4,5},{5,6},{6,7},{8,9},{9,10},{10,11},{11... | collective-permute-start | bytes 786440 | tf_op jit(solution)/shard_map/ppermute | solution.py:147
  4.2 1.3 %copy-start.10 = (bf16[8]{0:T(256)(128)(2,1)S(1)}, bf16[8]{0:T(256)(128)(2,1)}, u32[]{:S(2)}) copy-start(bf16[8]{0:T(256)(128)(2,1)} %param.8) | copy-start | bytes 52
  4.2 6.6 %collective-permute-start.1 = (bf16[32,1,32,128]{3,2,1,0:T(8,128)(2,1)S(1)}, bf16[32,1,32,128]{3,2,1,0:T(8,128)(2,1)S(1)}, u32[]{:S(2)}, u32[]{:S(2)}) collective-permute-start(bf16[32,1,32,128]{3,2,1,0:T(8,128)(2,1)S(1)} %get-tuple-element.57), channel_id=1, source_target_pairs={{1,0},{2,1},{3,2},{4,3},{5,4},{6,5},{7,6},{9,8},{10,9},{11,10},{12... | collective-permute-start | bytes 786440 | tf_op jit(solution)/shard_map/ppermute | solution.py:147
  5.8 5.0 %copy-start = (bf16[1,32,2,32,128]{4,3,2,1,0:T(8,128)(2,1)S(1)}, bf16[1,32,2,32,128]{4,3,2,1,0:T(8,128)(2,1)}, u32[]{:S(2)}) copy-start(bf16[1,32,2,32,128]{4,3,2,1,0:T(8,128)(2,1)} %param.5) | copy-start | bytes 1572868
  6.9 5.9 %collective-permute-start.2 = (bf16[8,865]{1,0:T(8,128)(2,1)S(1)}, bf16[8,865]{1,0:T(8,128)(2,1)S(1)}, u32[]{:S(2)}, u32[]{:S(2)}) collective-permute-start(bf16[8,865]{1,0:T(8,128)(2,1)S(1)} %pad_maximum_fusion.1), channel_id=1, source_target_pairs={{0,8},{8,0},{16,24},{24,16},{1,9},{9,1},{17,25},{25,17},{2,10},{10... | collective-permute-start | bytes 41528 | tf_op jit(solution)/shard_map/ppermute | solution.py:152
  9.2 3.7 %collective-permute-start.3 = (bf16[8,865]{1,0:T(8,128)(2,1)S(1)}, bf16[8,865]{1,0:T(8,128)(2,1)S(1)}, u32[]{:S(2)}, u32[]{:S(2)}) collective-permute-start(bf16[8,865]{1,0:T(8,128)(2,1)S(1)} %pad_maximum_fusion.1), channel_id=1, source_target_pairs={{0,16},{8,24},{16,0},{24,8},{1,17},{9,25},{17,1},{25,9},{2,18},{10... | collective-permute-start | bytes 41528 | tf_op jit(solution)/shard_map/ppermute | solution.py:152
  10.7 4.6 %collective-permute-start.4 = (bf16[8,865]{1,0:T(8,128)(2,1)S(1)}, bf16[8,865]{1,0:T(8,128)(2,1)S(1)}, u32[]{:S(2)}, u32[]{:S(2)}) collective-permute-start(bf16[8,865]{1,0:T(8,128)(2,1)S(1)} %pad_maximum_fusion.1), channel_id=1, source_target_pairs={{0,24},{8,16},{16,8},{24,0},{1,25},{9,17},{17,9},{25,1},{2,26},{10... | collective-permute-start | bytes 41528 | tf_op jit(solution)/shard_map/ppermute | solution.py:152
  23.4 8.2 %collective-permute-start.5 = (bf16[1,32,4096]{2,1,0:T(8,128)(2,1)}, bf16[1,32,4096]{2,1,0:T(8,128)(2,1)S(1)}, u32[]{:S(2)}, u32[]{:S(2)}) collective-permute-start(bf16[1,32,4096]{2,1,0:T(8,128)(2,1)} %get-tuple-element.36), channel_id=1, source_target_pairs={{0,1},{1,2},{2,3},{3,4},{4,5},{5,6},{6,7},{8,9},{9,10},{10,11},{11... | collective-permute-start | bytes 786440 | tf_op jit(solution)/shard_map/ppermute | solution.py:147
  26.5 6.8 %collective-permute-start.6 = (bf16[1,32,4096]{2,1,0:T(8,128)(2,1)}, bf16[1,32,4096]{2,1,0:T(8,128)(2,1)S(1)}, u32[]{:S(2)}, u32[]{:S(2)}) collective-permute-start(bf16[1,32,4096]{2,1,0:T(8,128)(2,1)} %get-tuple-element.37), channel_id=1, source_target_pairs={{1,0},{2,1},{3,2},{4,3},{5,4},{6,5},{7,6},{9,8},{10,9},{11,10},{12... | collective-permute-start | bytes 786440 | tf_op jit(solution)/shard_map/ppermute | solution.py:147
  31.6 2.2 %copy-start.1 = (bf16[1,32,4096]{2,1,0:T(8,128)(2,1)}, bf16[1,32,4096]{2,1,0:T(8,128)(2,1)S(1)}, u32[]{:S(2)}) copy-start(bf16[1,32,4096]{2,1,0:T(8,128)(2,1)S(1)} %collective-permute-done.5.lo) | copy-start | bytes 786436
  33.3 0.7 %copy-start.2 = (bf16[1,32,4096]{2,1,0:T(8,128)(2,1)}, bf16[1,32,4096]{2,1,0:T(8,128)(2,1)S(1)}, u32[]{:S(2)}) copy-start(bf16[1,32,4096]{2,1,0:T(8,128)(2,1)S(1)} %collective-permute-done.6.hi) | copy-start | bytes 786436
  33.4 4.4 %collective-permute-start.7 = (f32[16,865]{1,0:T(8,128)}, f32[16,865]{1,0:T(8,128)S(1)}, u32[]{:S(2)}, u32[]{:S(2)}) collective-permute-start(f32[16,865]{1,0:T(8,128)} %get-tuple-element.39), channel_id=1, source_target_pairs={{0,16},{8,24},{16,0},{24,8},{1,17},{9,25},{17,1},{25,9},{2,18},{10... | collective-permute-start | bytes 166088 | tf_op jit(solution)/shard_map/ppermute | solution.py:152
  34.1 3.7 %copy-start.7 = (f32[16,865]{1,0:T(8,128)S(1)}, f32[16,865]{1,0:T(8,128)}, u32[]{:S(2)}) copy-start(f32[16,865]{1,0:T(8,128)} %get-tuple-element.46) | copy-start | bytes 166084
  37.8 3.9 %collective-permute-start.8 = (f32[8,865]{1,0:T(8,128)S(1)}, f32[8,865]{1,0:T(8,128)S(1)}, u32[]{:S(2)}, u32[]{:S(2)}) collective-permute-start(f32[8,865]{1,0:T(8,128)S(1)} %constant_dynamic-slice_fusion), channel_id=1, source_target_pairs={{0,8},{8,0},{16,24},{24,16},{1,9},{9,1},{17,25},{25,17},{2,10},{10... | collective-permute-start | bytes 83048 | tf_op jit(solution)/shard_map/ppermute | solution.py:152
  38.4 7.0 %copy-start.6 = (bf16[2,32,4096]{2,1,0:T(8,128)(2,1)S(1)}, bf16[2,32,4096]{2,1,0:T(8,128)(2,1)}, u32[]{:S(2)}) copy-start(bf16[2,32,4096]{2,1,0:T(8,128)(2,1)} %get-tuple-element.33) | copy-start | bytes 1572868
  41.7 4.5 %collective-permute-start.9 = (f32[8,865]{1,0:T(8,128)S(1)}, f32[8,865]{1,0:T(8,128)S(1)}, u32[]{:S(2)}, u32[]{:S(2)}) collective-permute-start(f32[8,865]{1,0:T(8,128)S(1)} %dynamic-slice_add_fusion), channel_id=1, source_target_pairs={{0,1},{1,0},{2,3},{3,2},{4,5},{5,4},{6,7},{7,6},{8,9},{9,8},{10,11... | collective-permute-start | bytes 83048 | tf_op jit(solution)/shard_map/ppermute | solution.py:152
  45.4 2.4 %copy-start.3 = (bf16[1,32,4096]{2,1,0:T(8,128)(2,1)S(1)}, bf16[1,32,4096]{2,1,0:T(8,128)(2,1)}, u32[]{:S(2)}) copy-start(bf16[1,32,4096]{2,1,0:T(8,128)(2,1)} %shard_map.86) | copy-start | bytes 786436
  45.4 2.4 %copy-start.4 = (bf16[1,32,4096]{2,1,0:T(8,128)(2,1)S(1)}, bf16[1,32,4096]{2,1,0:T(8,128)(2,1)}, u32[]{:S(2)}) copy-start(bf16[1,32,4096]{2,1,0:T(8,128)(2,1)} %shard_map.87) | copy-start | bytes 786436
  46.2 3.9 %collective-permute-start.10 = (f32[8,865]{1,0:T(8,128)S(1)}, f32[8,865]{1,0:T(8,128)S(1)}, u32[]{:S(2)}, u32[]{:S(2)}) collective-permute-start(f32[8,865]{1,0:T(8,128)S(1)} %add.53), channel_id=1, source_target_pairs={{0,2},{1,3},{2,0},{3,1},{4,6},{5,7},{6,4},{7,5},{8,10},{9,11},{10,... | collective-permute-start | bytes 83048 | tf_op jit(solution)/shard_map/ppermute | solution.py:152
  50.1 4.8 %collective-permute-start.11 = (f32[8,865]{1,0:T(8,128)S(1)}, f32[8,865]{1,0:T(8,128)S(1)}, u32[]{:S(2)}, u32[]{:S(2)}) collective-permute-start(f32[8,865]{1,0:T(8,128)S(1)} %add.54), channel_id=1, source_target_pairs={{0,4},{1,5},{2,6},{3,7},{4,0},{5,1},{6,2},{7,3},{8,12},{9,13},{10,... | collective-permute-start | bytes 83048 | tf_op jit(solution)/shard_map/ppermute | solution.py:152
  54.9 0.7 %copy-start.8 = (f32[8,865]{1,0:T(8,128)}, f32[8,865]{1,0:T(8,128)S(1)}, u32[]{:S(2)}) copy-start(f32[8,865]{1,0:T(8,128)S(1)} %add_multiply_fusion) | copy-start | bytes 83044

commit v13 on v10

--- a/solution.py
+++ b/solution.py
@@ -152,14 +152,18 @@
     return lax.ppermute(value, axis, [(i, i ^ bit) for i in range(peers)])
 
 
-def gather_rows(value, axis):
+def gather_rows(value, axis, beside):
     peers = lax.axis_size(axis)
     me = lax.axis_index(axis)
-    blocks = jnp.zeros((peers,) + value.shape, value.dtype)
-    blocks = lax.dynamic_update_index_in_dim(blocks, value, me, 0)
-    for k in range(1, peers):
-        blocks = lax.dynamic_update_index_in_dim(blocks, swap(value, axis, k), me ^ k, 0)
-    return blocks.reshape((peers * value.shape[0],) + value.shape[1:])
+    held = value
+    bit = 1
+    while bit < peers:
+        got = swap(held, axis, bit)
+        if bit == 1:
+            got, beside = lax.optimization_barrier((got, beside))
+        held = jnp.where((me // bit) % 2 == 0, jnp.concatenate([held, got]), jnp.concatenate([got, held]))
+        bit *= 2
+    return held, beside
 
 
 def first_upper():
@@ -208,7 +212,7 @@
     lanes = rows * depth
     taps_in = weight.shape[1]
     packed = jnp.concatenate([weight, bias[:, None]], axis=1)
-    whole = gather_rows(packed, "real")
+    whole, edges = gather_rows(packed, "real", (field[:, :1], field[:, planes - 1 :]))
     whole_weight, whole_bias = whole[:, :taps_in], whole[:, taps_in]
     out_chan = whole_weight.shape[0]
     w5 = whole_weight.reshape(out_chan, 3, 3, 3, chans)
@@ -222,7 +226,7 @@
     def unflat(value):
         return value.reshape(planes, value.shape[1], rows, depth).transpose(1, 0, 2, 3)
 
-    below, above = neighbours(field[:, :1], field[:, planes - 1 :], "strike")
+    below, above = neighbours(*edges, "strike")
     haloed = jnp.concatenate([below, field, above], axis=1)
     haloed = haloed.transpose(1, 0, 2, 3).reshape(planes + 2, chans, lanes)
     act, dpre, first, last = forward_call(

time: 55.8 us -> 57.7 us (1.034)
  waiting for transfers between devices: 4.47 us -> 6.44 us
  other arithmetic: 0.96 us -> 1.76 us
    ppermute x8 -> x7, waiting for transfers between devices: 3.25 us -> 4.37 us  [swap(): return lax.ppermute(value, axis, [(i, i ^ bit) for i in range(peers)])]
    ppermute x4, waiting for transfers between devices: 1.22 us -> 2.07 us  [neighbours(): return (lax.ppermute(last, axis, up), lax.ppermute(first, axis, down))]
    concatenate x0 -> x1, other arithmetic: none -> 0.79 us  [local(): packed = jnp.concatenate([weight, bias[:, None]], axis=1)]
    ppermute x8 -> x7, starting transfers between devices: 13.6 us -> 13.2 us  [swap(): return lax.ppermute(value, axis, [(i, i ^ bit) for i in range(peers)])]
  transfers between devices with their start and end apart: 12 -> 11, of which waited for: 4 -> 6; matrix products, arithmetic and copies ran while one was open for 12% -> 12% of each run, Pallas kernels for 18% -> 17%
where the time goes in v13:
time: 57.7 us; the launch traced here: 57.3 us
  starting transfers between devices  23.8 us (41%)
  Pallas kernels  14.9 us (26%)
  local copies, waits for them, and re-layouts  9.6 us (17%)
  waiting for transfers between devices  6.44 us (11%)
  other arithmetic  1.76 us (3%)
  between operations  0.84 us (1%)
    ppermute x7, starting transfers between devices, swap(): return lax.ppermute(value, axis, [(i, i ^ bit) for i in range(peers)])  13.2 us
    ppermute x4, starting transfers between devices, neighbours(): return (lax.ppermute(last, axis, up), lax.ppermute(first, axis, down))  10.5 us
    pallas_call x2, Pallas kernels, input_call(): pl.pallas_call(functools.partial(_input_kernel, planes=planes, first=firs...  6.08 us
    pallas_call x1, Pallas kernels, forward_call(): pl.pallas_call(functools.partial(_forward_kernel, planes=planes, depth=de...  5.04 us
    ppermute x7, waiting for transfers between devices, swap(): return lax.ppermute(value, axis, [(i, i ^ bit) for i in range(peers)])  4.37 us
    pallas_call x1, Pallas kernels, weight_call(): pl.pallas_call(functools.partial(_weight_kernel, planes=planes, depth=dep...  3.74 us
    ppermute x4, waiting for transfers between devices, neighbours(): return (lax.ppermute(last, axis, up), lax.ppermute(first, axis, down))  2.07 us
    reshape x2, local copies, waits for them, and re-layouts, local(): haloed = haloed.transpose(1, 0, 2, 3).reshape(planes + 2, chans, lanes)  1.85 us
  transfers between devices with their start and end apart: 11, of which 6 were waited for; matrix products, arithmetic and copies ran while one was open for 12% of the time, Pallas kernels for 17%

profile of v13, /device:TPU:0, one launch (start us, length us, event | category | flops | bytes accessed | tf_op | source)
XLA Modules:
  0.0 57.3 jit_solution(14191923238975819891)
XLA Ops:
  0.6 0.0 copy-start.10
  0.6 0.6 %copy-done.10 = bf16[8]{0:T(256)(128)(2,1)S(1)} copy-done((bf16[8]{0:T(256)(128)(2,1)S(1)}, bf16[8]{0:T(256)(128)(2,1)}, u32[]{:S(2)}) %copy-start.10) | copy-done | bytes 40
  1.3 0.1 copy.16
  1.4 0.8 %pad_maximum_fusion.1 = bf16[8,865]{1,0:T(8,128)(2,1)S(1)} fusion(bf16[8,1]{1,0:T(8,128)(2,1)S(1)} %copy.16, bf16[8,864]{1,0:T(8,128)(2,1)} %param.7), kind=kLoop, calls=%fused_computation.9 | loop fusion | flops 27680 | bytes 27680 | tf_op jit(solution)/shard_map/concatenate | solution.py:214
  2.2 2.9 %collective-permute-start = (bf16[8,865]{1,0:T(8,128)(2,1)S(1)}, bf16[8,865]{1,0:T(8,128)(2,1)S(1)}, u32[]{:S(2)}, u32[]{:S(2)}) collective-permute-start(bf16[8,865]{1,0:T(8,128)(2,1)S(1)} %pad_maximum_fusion.1), channel_id=1, source_target_pairs={{0,8},{8,0},{16,24},{24,16},{1,9},{9,1},{17,25},{25,17},{2,10},{10... | collective-permute-start | bytes 41528 | tf_op jit(solution)/shard_map/ppermute | solution.py:152
  5.1 0.0 copy-start.5
  5.1 1.1 %fusion = (bf16[32,1,32,128]{3,2,1,0:T(8,128)(2,1)S(1)}, bf16[32,1,32,128]{3,2,1,0:T(8,128)(2,1)S(1)}) fusion(bf16[32,2,32,128]{3,2,1,0:T(8,128)(2,1)} %bitcast.47), kind=kLoop, calls=%fused_computation.13 | loop fusion | bytes 1048576 | tf_op jit(solution)/shard_map/slice | solution.py:215
  6.2 0.0 copy-start.7
  6.3 0.5 collective-permute-done
  6.8 0.2 copy-done.7
  7.0 0.1 maximum_select_fusion.1
  7.0 1.9 %collective-permute-start.3 = (bf16[16,865]{1,0:T(8,128)(2,1)S(1)}, bf16[16,865]{1,0:T(8,128)(2,1)S(1)}, u32[]{:S(2)}, u32[]{:S(2)}) collective-permute-start(bf16[16,865]{1,0:T(8,128)(2,1)S(1)} %maximum_select_fusion.1), channel_id=1, source_target_pairs={{0,16},{8,24},{16,0},{24,8},{1,17},{9,25},{17,1},{25,9},{2,18},{10... | collective-permute-start | bytes 83048 | tf_op jit(solution)/shard_map/ppermute | solution.py:152
  8.9 0.0 copy-done.5
  8.9 0.1 reshape.37
  9.1 1.1 %copy.24.cot = bf16[2,32,4096]{2,1,0:T(8,128)(2,1)} copy(bf16[2,32,4096]{2,0,1:T(2,128)(2,1)S(1)} %reshape.37) | data formatting | bytes 1048576 | tf_op jit(solution)/shard_map/reshape | solution.py:224
  10.2 1.3 %collective-permute-start.1 = (bf16[32,1,32,128]{3,2,1,0:T(8,128)(2,1)S(1)}, bf16[32,1,32,128]{3,2,1,0:T(8,128)(2,1)S(1)}, u32[]{:S(2)}, u32[]{:S(2)}) collective-permute-start(bf16[32,1,32,128]{3,2,1,0:T(8,128)(2,1)S(1)} %get-tuple-element.29), channel_id=1, source_target_pairs={{0,1},{1,2},{2,3},{3,4},{4,5},{5,6},{6,7},{8,9},{9,10},{10,11},{11... | collective-permute-start | bytes 786440 | tf_op jit(solution)/shard_map/ppermute | solution.py:147
  11.5 1.3 %collective-permute-start.2 = (bf16[32,1,32,128]{3,2,1,0:T(8,128)(2,1)S(1)}, bf16[32,1,32,128]{3,2,1,0:T(8,128)(2,1)S(1)}, u32[]{:S(2)}, u32[]{:S(2)}) collective-permute-start(bf16[32,1,32,128]{3,2,1,0:T(8,128)(2,1)S(1)} %get-tuple-element.30), channel_id=1, source_target_pairs={{1,0},{2,1},{3,2},{4,3},{5,4},{6,5},{7,6},{9,8},{10,9},{11,10},{12... | collective-permute-start | bytes 786440 | tf_op jit(solution)/shard_map/ppermute | solution.py:147
  12.8 0.0 collective-permute-done.3
  12.8 0.2 reshape.30
  13.0 0.0 copy-start
  13.0 0.1 copy.18
  13.1 0.8 %reshape.31.wall = bf16[288,96]{1,0:T(8,128)(2,1)} reshape(bf16[3,3,32,3,32]{4,3,2,1,0:T(4,128)(2,1)S(1)} %copy.18) | data formatting | bytes 110592 | tf_op jit(solution)/shard_map/reshape | solution.py:219
  13.9 0.7 %slice_convert_fusion.bias = f32[32,1]{1,0:T(8,128)} fusion(bf16[32,865]{1,0:T(8,128)(2,1)S(1)} %maximum_select_fusion), kind=kLoop, calls=%fused_computation.10 | loop fusion | flops 32 | bytes 192 | tf_op jit(solution)/shard_map/convert_element_type | solution.py:233
  14.6 0.0 collective-permute-done.1
  14.6 2.1 %collective-permute-done.2 = bf16[32,1,32,128]{3,2,1,0:T(8,128)(2,1)S(1)} collective-permute-done((bf16[32,1,32,128]{3,2,1,0:T(8,128)(2,1)S(1)}, bf16[32,1,32,128]{3,2,1,0:T(8,128)(2,1)S(1)}, u32[]{:S(2)}, u32[]{:S(2)}) %collective-permute-start.2) | collective-permute-done | bytes 262176 | tf_op jit(solution)/shard_map/ppermute | solution.py:147
  16.7 0.0 copy-done
  16.7 0.1 maximum_bitcast_fusion
  16.8 0.3 reshape.36
  17.1 1.6 %copy.23.haloed = bf16[4,32,4096]{2,1,0:T(8,128)(2,1)} copy(bf16[4,32,4096]{2,0,1:T(4,128)(2,1)S(1)} %reshape.36) | data formatting | bytes 2097152 | tf_op jit(solution)/shard_map/reshape | solution.py:231
  18.7 5.0 %shard_map.84 = (bf16[2,32,4096]{2,1,0:T(8,128)(2,1)}, bf16[2,32,4096]{2,1,0:T(8,128)(2,1)}, bf16[1,32,4096]{2,1,0:T(8,128)(2,1)}, bf16[1,32,4096]{2,1,0:T(8,128)(2,1)}) custom-call(bf16[4,32,4096]{2,1,0:T(8,128)(2,1)} %copy.23.haloed, bf16[288,96]{1,0:T(8,128)(2,1)} %reshape.31.wall, f32[32,1]{1,0:T(8,128)} %slice_convert_fusion.bias, ...), custom_call_target="tpu_custom_call" | custom-call | flops 452984832 | bytes 2621440 | tf_op jit(solution)/shard_map/pallas_call | solution.py:108
  23.7 6.7 %collective-permute-start.4 = (bf16[1,32,4096]{2,1,0:T(8,128)(2,1)}, bf16[1,32,4096]{2,1,0:T(8,128)(2,1)S(1)}, u32[]{:S(2)}, u32[]{:S(2)}) collective-permute-start(bf16[1,32,4096]{2,1,0:T(8,128)(2,1)} %get-tuple-element.35), channel_id=1, source_target_pairs={{0,1},{1,2},{2,3},{3,4},{4,5},{5,6},{6,7},{8,9},{9,10},{10,11},{11... | collective-permute-start | bytes 786440 | tf_op jit(solution)/shard_map/ppermute | solution.py:147
  30.4 1.3 %collective-permute-start.5 = (bf16[1,32,4096]{2,1,0:T(8,128)(2,1)}, bf16[1,32,4096]{2,1,0:T(8,128)(2,1)S(1)}, u32[]{:S(2)}, u32[]{:S(2)}) collective-permute-start(bf16[1,32,4096]{2,1,0:T(8,128)(2,1)} %get-tuple-element.36), channel_id=1, source_target_pairs={{1,0},{2,1},{3,2},{4,3},{5,4},{6,5},{7,6},{9,8},{10,9},{11,10},{12... | collective-permute-start | bytes 786440 | tf_op jit(solution)/shard_map/ppermute | solution.py:147
  31.7 0.1 reverse_bitcast_fusion
  31.8 0.3 copy.21
  32.1 0.8 %reshape.34.wall = bf16[288,96]{1,0:T(8,128)(2,1)} reshape(bf16[3,3,32,3,32]{4,3,2,1,0:T(4,128)(2,1)S(1)} %copy.21) | data formatting | bytes 110592 | tf_op jit(solution)/shard_map/reshape | solution.py:220
  32.9 3.7 %shard_map.85 = (f32[16,865]{1,0:T(8,128)}, f32[16,865]{1,0:T(8,128)}) custom-call(s32[1]{0:T(128)} %bitcast.8.upper, bf16[4,32,4096]{2,1,0:T(8,128)(2,1)} %copy.23.haloed, bf16[2,32,4096]{2,1,0:T(8,128)(2,1)} %get-tuple-element.48.dpre.mid, f32[9,1,4096]{2,1,0:T(1,128)} %constant.59.clone.mask), custom_call_target="tpu_custom_call" | custom-call | flops 452984832 | bytes 1572864 | tf_op jit(solution)/shard_map/pallas_call | solution.py:133
  36.6 0.0 collective-permute-done.4.lo
  36.6 0.0 copy-start.1
  36.6 0.0 collective-permute-done.5.hi
  36.6 0.0 copy-start.2
  36.6 0.6 %collective-permute-start.6 = (f32[16,865]{1,0:T(8,128)}, f32[16,865]{1,0:T(8,128)S(1)}, u32[]{:S(2)}, u32[]{:S(2)}) collective-permute-start(f32[16,865]{1,0:T(8,128)} %get-tuple-element.37), channel_id=1, source_target_pairs={{0,16},{8,24},{16,0},{24,8},{1,17},{9,25},{17,1},{25,9},{2,18},{10... | collective-permute-start | bytes 166088 | tf_op jit(solution)/shard_map/ppermute | solution.py:152
  37.2 0.1 copy-done.1
  37.3 0.1 copy-done.2
  37.4 3.0 %shard_map.86 = bf16[1,32,4096]{2,1,0:T(8,128)(2,1)} custom-call(bf16[1,32,4096]{2,1,0:T(8,128)(2,1)} %copy-done.1, bf16[2,32,4096]{2,1,0:T(8,128)(2,1)} %get-tuple-element.48.dpre.mid, bf16[1,32,4096]{2,1,0:T(8,128)(2,1)} %copy-done.2, bf16[288,96]{1,0:T(8,128)(2,1)} %reshape.34.wall, f32[9,1,4096]{2,1,0:T(1,128)} %constant.59.clone.mask), custom_call_target="tpu_custom_call" | custom-call | flops 226492416 | bytes 1572864 | tf_op jit(solution)/shard_map/pallas_call | solution.py:120
  40.4 0.7 %collective-permute-done.6 = f32[16,865]{1,0:T(8,128)S(1)} collective-permute-done((f32[16,865]{1,0:T(8,128)}, f32[16,865]{1,0:T(8,128)S(1)}, u32[]{:S(2)}, u32[]{:S(2)}) %collective-permute-start.6) | collective-permute-done | bytes 55392 | tf_op jit(solution)/shard_map/ppermute | solution.py:152
  41.1 0.0 copy-done.8
  41.1 1.6 %collective-permute-start.7 = (f32[8,865]{1,0:T(8,128)S(1)}, f32[8,865]{1,0:T(8,128)S(1)}, u32[]{:S(2)}, u32[]{:S(2)}) collective-permute-start(f32[8,865]{1,0:T(8,128)S(1)} %constant_dynamic-slice_fusion), channel_id=1, source_target_pairs={{0,8},{8,0},{16,24},{24,16},{1,9},{9,1},{17,25},{25,17},{2,10},{10... | collective-permute-start | bytes 83048 | tf_op jit(solution)/shard_map/ppermute | solution.py:152
  42.7 3.1 %shard_map.87 = bf16[1,32,4096]{2,1,0:T(8,128)(2,1)} custom-call(bf16[1,32,4096]{2,1,0:T(8,128)(2,1)} %copy-done.1, bf16[2,32,4096]{2,1,0:T(8,128)(2,1)} %get-tuple-element.48.dpre.mid, bf16[1,32,4096]{2,1,0:T(8,128)(2,1)} %copy-done.2, bf16[288,96]{1,0:T(8,128)(2,1)} %reshape.34.wall, f32[9,1,4096]{2,1,0:T(1,128)} %constant.59.clone.mask), custom_call_target="tpu_custom_call" | custom-call | flops 226492416 | bytes 1572864 | tf_op jit(solution)/shard_map/pallas_call | solution.py:120
  45.7 0.0 collective-permute-done.7
  45.8 0.7 %collective-permute-start.8 = (f32[8,865]{1,0:T(8,128)S(1)}, f32[8,865]{1,0:T(8,128)S(1)}, u32[]{:S(2)}, u32[]{:S(2)}) collective-permute-start(f32[8,865]{1,0:T(8,128)S(1)} %dynamic-slice_add_fusion), channel_id=1, source_target_pairs={{0,1},{1,0},{2,3},{3,2},{4,5},{5,4},{6,7},{7,6},{8,9},{9,8},{10,11... | collective-permute-start | bytes 83048 | tf_op jit(solution)/shard_map/ppermute | solution.py:152
  46.5 0.0 copy-done.6
  46.5 0.1 copy.25
  46.6 0.8 %collective-permute-done.8 = f32[8,865]{1,0:T(8,128)S(1)} collective-permute-done((f32[8,865]{1,0:T(8,128)S(1)}, f32[8,865]{1,0:T(8,128)S(1)}, u32[]{:S(2)}, u32[]{:S(2)}) %collective-permute-start.8) | collective-permute-done | bytes 27712 | tf_op jit(solution)/shard_map/ppermute | solution.py:152
  47.3 2.5 %collective-permute-start.9 = (f32[8,865]{1,0:T(8,128)S(1)}, f32[8,865]{1,0:T(8,128)S(1)}, u32[]{:S(2)}, u32[]{:S(2)}) collective-permute-start(f32[8,865]{1,0:T(8,128)S(1)} %add.38), channel_id=1, source_target_pairs={{0,2},{1,3},{2,0},{3,1},{4,6},{5,7},{6,4},{7,5},{8,10},{9,11},{10,... | collective-permute-start | bytes 83048 | tf_op jit(solution)/shard_map/ppermute | solution.py:152
  49.8 0.0 copy-done.3
  49.8 0.0 copy-done.4
  49.8 0.1 pad_maximum_fusion
  49.9 0.1 copy.26
  50.0 1.7 %collective-permute-done.9 = f32[8,865]{1,0:T(8,128)S(1)} collective-permute-done((f32[8,865]{1,0:T(8,128)S(1)}, f32[8,865]{1,0:T(8,128)S(1)}, u32[]{:S(2)}, u32[]{:S(2)}) %collective-permute-start.9) | collective-permute-done | bytes 27712 | tf_op jit(solution)/shard_map/ppermute | solution.py:152
  51.7 3.0 %collective-permute-start.10 = (f32[8,865]{1,0:T(8,128)S(1)}, f32[8,865]{1,0:T(8,128)S(1)}, u32[]{:S(2)}, u32[]{:S(2)}) collective-permute-start(f32[8,865]{1,0:T(8,128)S(1)} %add.39), channel_id=1, source_target_pairs={{0,4},{1,5},{2,6},{3,7},{4,0},{5,1},{6,2},{7,3},{8,12},{9,13},{10,... | collective-permute-start | bytes 83048 | tf_op jit(solution)/shard_map/ppermute | solution.py:152
  54.7 1.1 %copy_bitcast_fusion = (bf16[1,32,2,32,128]{4,3,2,1,0:T(8,128)(2,1)}, bf16[1,32,2,32,128]{4,3,2,1,0:T(8,128)(2,1)}) fusion(bf16[2,32,32,128]{3,2,1,0:T(8,128)(2,1)S(1)} %bitcast.49, bf16[2,32,32,128]{3,2,1,0:T(8,128)(2,1)S(1)} %bitcast.50), kind=kLoop, calls=%fused_computation.2 | loop fusion | bytes 2097152 | tf_op jit(solution)/shard_map/broadcast_in_dim | solution.py:246
  55.8 0.7 %collective-permute-done.10 = f32[8,865]{1,0:T(8,128)S(1)} collective-permute-done((f32[8,865]{1,0:T(8,128)S(1)}, f32[8,865]{1,0:T(8,128)S(1)}, u32[]{:S(2)}, u32[]{:S(2)}) %collective-permute-start.10) | collective-permute-done | bytes 27712 | tf_op jit(solution)/shard_map/ppermute | solution.py:152
  56.6 0.7 %slice_reduce_fusion = f32[8]{0:T(128)} fusion(f32[8,865]{1,0:T(8,128)S(1)} %add_multiply_fusion), kind=kLoop, calls=%fused_computation.11 | loop fusion | bytes 64 | tf_op jit(solution)/shard_map/slice | solution.py:246
  57.3 0.0 copy-done.9
  (12 shorter events, 0.1 us)
Async XLA Ops:
  0.6 0.7 %copy-start.10 = (bf16[8]{0:T(256)(128)(2,1)S(1)}, bf16[8]{0:T(256)(128)(2,1)}, u32[]{:S(2)}) copy-start(bf16[8]{0:T(256)(128)(2,1)} %param.8) | copy-start | bytes 52
  2.2 4.6 %collective-permute-start = (bf16[8,865]{1,0:T(8,128)(2,1)S(1)}, bf16[8,865]{1,0:T(8,128)(2,1)S(1)}, u32[]{:S(2)}, u32[]{:S(2)}) collective-permute-start(bf16[8,865]{1,0:T(8,128)(2,1)S(1)} %pad_maximum_fusion.1), channel_id=1, source_target_pairs={{0,8},{8,0},{16,24},{24,16},{1,9},{9,1},{17,25},{25,17},{2,10},{10... | collective-permute-start | bytes 41528 | tf_op jit(solution)/shard_map/ppermute | solution.py:152
  5.1 3.8 %copy-start.5 = (bf16[1,32,2,32,128]{4,3,2,1,0:T(8,128)(2,1)S(1)}, bf16[1,32,2,32,128]{4,3,2,1,0:T(8,128)(2,1)}, u32[]{:S(2)}) copy-start(bf16[1,32,2,32,128]{4,3,2,1,0:T(8,128)(2,1)} %param.6) | copy-start | bytes 1572868
  6.2 0.7 %copy-start.7 = (bf16[8,864]{1,0:T(8,128)(2,1)S(1)}, bf16[8,864]{1,0:T(8,128)(2,1)}, u32[]{:S(2)}) copy-start(bf16[8,864]{1,0:T(8,128)(2,1)} %param.7) | copy-start | bytes 41476
  7.0 5.7 %collective-permute-start.3 = (bf16[16,865]{1,0:T(8,128)(2,1)S(1)}, bf16[16,865]{1,0:T(8,128)(2,1)S(1)}, u32[]{:S(2)}, u32[]{:S(2)}) collective-permute-start(bf16[16,865]{1,0:T(8,128)(2,1)S(1)} %maximum_select_fusion.1), channel_id=1, source_target_pairs={{0,16},{8,24},{16,0},{24,8},{1,17},{9,25},{17,1},{25,9},{2,18},{10... | collective-permute-start | bytes 83048 | tf_op jit(solution)/shard_map/ppermute | solution.py:152
  10.2 4.5 %collective-permute-start.1 = (bf16[32,1,32,128]{3,2,1,0:T(8,128)(2,1)S(1)}, bf16[32,1,32,128]{3,2,1,0:T(8,128)(2,1)S(1)}, u32[]{:S(2)}, u32[]{:S(2)}) collective-permute-start(bf16[32,1,32,128]{3,2,1,0:T(8,128)(2,1)S(1)} %get-tuple-element.29), channel_id=1, source_target_pairs={{0,1},{1,2},{2,3},{3,4},{4,5},{5,6},{6,7},{8,9},{9,10},{10,11},{11... | collective-permute-start | bytes 786440 | tf_op jit(solution)/shard_map/ppermute | solution.py:147
  11.5 5.2 %collective-permute-start.2 = (bf16[32,1,32,128]{3,2,1,0:T(8,128)(2,1)S(1)}, bf16[32,1,32,128]{3,2,1,0:T(8,128)(2,1)S(1)}, u32[]{:S(2)}, u32[]{:S(2)}) collective-permute-start(bf16[32,1,32,128]{3,2,1,0:T(8,128)(2,1)S(1)} %get-tuple-element.30), channel_id=1, source_target_pairs={{1,0},{2,1},{3,2},{4,3},{5,4},{6,5},{7,6},{9,8},{10,9},{11,10},{12... | collective-permute-start | bytes 786440 | tf_op jit(solution)/shard_map/ppermute | solution.py:147
  13.0 3.7 %copy-start = (bf16[1,32,2,32,128]{4,3,2,1,0:T(8,128)(2,1)S(1)}, bf16[1,32,2,32,128]{4,3,2,1,0:T(8,128)(2,1)}, u32[]{:S(2)}) copy-start(bf16[1,32,2,32,128]{4,3,2,1,0:T(8,128)(2,1)} %param.5) | copy-start | bytes 1572868
  23.7 12.9 %collective-permute-start.4 = (bf16[1,32,4096]{2,1,0:T(8,128)(2,1)}, bf16[1,32,4096]{2,1,0:T(8,128)(2,1)S(1)}, u32[]{:S(2)}, u32[]{:S(2)}) collective-permute-start(bf16[1,32,4096]{2,1,0:T(8,128)(2,1)} %get-tuple-element.35), channel_id=1, source_target_pairs={{0,1},{1,2},{2,3},{3,4},{4,5},{5,6},{6,7},{8,9},{9,10},{10,11},{11... | collective-permute-start | bytes 786440 | tf_op jit(solution)/shard_map/ppermute | solution.py:147
  30.4 6.2 %collective-permute-start.5 = (bf16[1,32,4096]{2,1,0:T(8,128)(2,1)}, bf16[1,32,4096]{2,1,0:T(8,128)(2,1)S(1)}, u32[]{:S(2)}, u32[]{:S(2)}) collective-permute-start(bf16[1,32,4096]{2,1,0:T(8,128)(2,1)} %get-tuple-element.36), channel_id=1, source_target_pairs={{1,0},{2,1},{3,2},{4,3},{5,4},{6,5},{7,6},{9,8},{10,9},{11,10},{12... | collective-permute-start | bytes 786440 | tf_op jit(solution)/shard_map/ppermute | solution.py:147
  36.6 0.7 %copy-start.1 = (bf16[1,32,4096]{2,1,0:T(8,128)(2,1)}, bf16[1,32,4096]{2,1,0:T(8,128)(2,1)S(1)}, u32[]{:S(2)}) copy-start(bf16[1,32,4096]{2,1,0:T(8,128)(2,1)S(1)} %collective-permute-done.4.lo) | copy-start | bytes 786436
  36.6 0.8 %copy-start.2 = (bf16[1,32,4096]{2,1,0:T(8,128)(2,1)}, bf16[1,32,4096]{2,1,0:T(8,128)(2,1)S(1)}, u32[]{:S(2)}) copy-start(bf16[1,32,4096]{2,1,0:T(8,128)(2,1)S(1)} %collective-permute-done.5.hi) | copy-start | bytes 786436
  36.6 4.5 %collective-permute-start.6 = (f32[16,865]{1,0:T(8,128)}, f32[16,865]{1,0:T(8,128)S(1)}, u32[]{:S(2)}, u32[]{:S(2)}) collective-permute-start(f32[16,865]{1,0:T(8,128)} %get-tuple-element.37), channel_id=1, source_target_pairs={{0,16},{8,24},{16,0},{24,8},{1,17},{9,25},{17,1},{25,9},{2,18},{10... | collective-permute-start | bytes 166088 | tf_op jit(solution)/shard_map/ppermute | solution.py:152
  37.4 3.7 %copy-start.8 = (f32[16,865]{1,0:T(8,128)S(1)}, f32[16,865]{1,0:T(8,128)}, u32[]{:S(2)}) copy-start(f32[16,865]{1,0:T(8,128)} %get-tuple-element.44) | copy-start | bytes 166084
  41.1 4.6 %collective-permute-start.7 = (f32[8,865]{1,0:T(8,128)S(1)}, f32[8,865]{1,0:T(8,128)S(1)}, u32[]{:S(2)}, u32[]{:S(2)}) collective-permute-start(f32[8,865]{1,0:T(8,128)S(1)} %constant_dynamic-slice_fusion), channel_id=1, source_target_pairs={{0,8},{8,0},{16,24},{24,16},{1,9},{9,1},{17,25},{25,17},{2,10},{10... | collective-permute-start | bytes 83048 | tf_op jit(solution)/shard_map/ppermute | solution.py:152
  42.7 3.8 %copy-start.6 = (bf16[2,32,4096]{2,1,0:T(8,128)(2,1)S(1)}, bf16[2,32,4096]{2,1,0:T(8,128)(2,1)}, u32[]{:S(2)}) copy-start(bf16[2,32,4096]{2,1,0:T(8,128)(2,1)} %get-tuple-element.32) | copy-start | bytes 1572868
  45.8 1.6 %collective-permute-start.8 = (f32[8,865]{1,0:T(8,128)S(1)}, f32[8,865]{1,0:T(8,128)S(1)}, u32[]{:S(2)}, u32[]{:S(2)}) collective-permute-start(f32[8,865]{1,0:T(8,128)S(1)} %dynamic-slice_add_fusion), channel_id=1, source_target_pairs={{0,1},{1,0},{2,3},{3,2},{4,5},{5,4},{6,7},{7,6},{8,9},{9,8},{10,11... | collective-permute-start | bytes 83048 | tf_op jit(solution)/shard_map/ppermute | solution.py:152
  46.5 3.4 %copy-start.3 = (bf16[1,32,4096]{2,1,0:T(8,128)(2,1)S(1)}, bf16[1,32,4096]{2,1,0:T(8,128)(2,1)}, u32[]{:S(2)}) copy-start(bf16[1,32,4096]{2,1,0:T(8,128)(2,1)} %shard_map.86) | copy-start | bytes 786436
  46.5 3.4 %copy-start.4 = (bf16[1,32,4096]{2,1,0:T(8,128)(2,1)S(1)}, bf16[1,32,4096]{2,1,0:T(8,128)(2,1)}, u32[]{:S(2)}) copy-start(bf16[1,32,4096]{2,1,0:T(8,128)(2,1)} %shard_map.87) | copy-start | bytes 786436
  47.3 4.4 %collective-permute-start.9 = (f32[8,865]{1,0:T(8,128)S(1)}, f32[8,865]{1,0:T(8,128)S(1)}, u32[]{:S(2)}, u32[]{:S(2)}) collective-permute-start(f32[8,865]{1,0:T(8,128)S(1)} %add.38), channel_id=1, source_target_pairs={{0,2},{1,3},{2,0},{3,1},{4,6},{5,7},{6,4},{7,5},{8,10},{9,11},{10,... | collective-permute-start | bytes 83048 | tf_op jit(solution)/shard_map/ppermute | solution.py:152
  51.7 4.9 %collective-permute-start.10 = (f32[8,865]{1,0:T(8,128)S(1)}, f32[8,865]{1,0:T(8,128)S(1)}, u32[]{:S(2)}, u32[]{:S(2)}) collective-permute-start(f32[8,865]{1,0:T(8,128)S(1)} %add.39), channel_id=1, source_target_pairs={{0,4},{1,5},{2,6},{3,7},{4,0},{5,1},{6,2},{7,3},{8,12},{9,13},{10,... | collective-permute-start | bytes 83048 | tf_op jit(solution)/shard_map/ppermute | solution.py:152
  56.6 0.7 %copy-start.9 = (f32[8,865]{1,0:T(8,128)}, f32[8,865]{1,0:T(8,128)S(1)}, u32[]{:S(2)}) copy-start(f32[8,865]{1,0:T(8,128)S(1)} %add_multiply_fusion) | copy-start | bytes 83044

commit v14 on v10

--- a/solution.py
+++ b/solution.py
@@ -16,10 +16,6 @@
     z = np.arange(depth)[None, :]
     masks = [((y + b >= 0) & (y + b < rows) & (z + c >= 0) & (z + c < depth)) for b, c in OFFSETS]
     return np.stack(masks).reshape(len(OFFSETS), 1, rows * depth).astype(np.float32)
-
-
-def _stacked(haloed, h):
-    return jnp.concatenate([haloed[h], haloed[h + 1], haloed[h + 2]], axis=0)
 
 
 def _stacked_parts(lo, mid, hi, h, planes):
@@ -44,10 +40,10 @@
     return total
 
 
-def _forward_kernel(haloed, wall, bias, cot, mask, act_out, dpre_out, first_out, last_out, *, planes, depth):
-    chans, lanes = haloed.shape[1], haloed.shape[2]
+def _forward_kernel(lo, mid, hi, wall, bias, cot, mask, act_out, dpre_out, first_out, last_out, *, planes, depth):
+    chans, lanes = mid.shape[1], mid.shape[2]
     for p in range(planes):
-        y = jnp.dot(wall[...], _stacked(haloed, p), preferred_element_type=jnp.float32)
+        y = jnp.dot(wall[...], _stacked_parts(lo, mid, hi, p, planes), preferred_element_type=jnp.float32)
         pre = _shifted_sum(y, mask, chans, lanes, depth, 1) + bias[...]
         sig = 1.0 / (1.0 + jnp.exp(-pre))
         act_out[p] = (pre * sig).astype(act_out.dtype)
@@ -66,7 +62,7 @@
         out[n] = _shifted_sum(y, mask, chans, lanes, depth, -1).astype(out.dtype)
 
 
-def _weight_kernel(upper, haloed, dpre, mask, keep_out, send_out, full, *, planes, depth):
+def _weight_kernel(upper, lo, mid, hi, dpre, mask, keep_out, send_out, full, *, planes, depth):
     chans, lanes = dpre.shape[1], dpre.shape[2]
     gw = jnp.zeros((9 * chans, 3 * chans), jnp.float32)
     gb = jnp.zeros((chans, 1), jnp.float32)
@@ -81,7 +77,7 @@
                 e = pltpu.roll(jnp.where(mask[k] > 0.5, d, 0.0), off % lanes, 1)
             parts.append(e.astype(jnp.bfloat16))
         gw = gw + lax.dot_general(
-            jnp.concatenate(parts, axis=0), _stacked(haloed, p),
+            jnp.concatenate(parts, axis=0), _stacked_parts(lo, mid, hi, p, planes),
             (((1,), (1,)), ((), ())), preferred_element_type=jnp.float32,
         )
     chans_in = gw.shape[1] // 3
@@ -100,7 +96,7 @@
     return [pl.BlockSpec(memory_space=pltpu.VMEM)] * n
 
 
-def forward_call(haloed, wall, bias, cot, mask, depth):
+def forward_call(lo, mid, hi, wall, bias, cot, mask, depth):
     planes, chans, lanes = cot.shape
     shape = jax.ShapeDtypeStruct(cot.shape, jnp.bfloat16)
     edge = jax.ShapeDtypeStruct((1, chans, lanes), jnp.bfloat16)
@@ -108,10 +104,10 @@
     return pl.pallas_call(
         functools.partial(_forward_kernel, planes=planes, depth=depth),
         out_shape=(shape, shape, edge, edge),
-        in_specs=_vmem(5),
+        in_specs=_vmem(7),
         out_specs=tuple(_vmem(4)),
         cost_estimate=pl.CostEstimate(flops=flops, transcendentals=planes * chans * lanes, bytes_accessed=5 * cot.size * 2),
-    )(haloed, wall, bias, cot, mask)
+    )(lo, mid, hi, wall, bias, cot, mask)
 
 
 def input_call(lo, mid, hi, wall, mask, depth, first, count):
@@ -126,18 +122,18 @@
     )(lo, mid, hi, wall, mask)
 
 
-def weight_call(upper, haloed, dpre, mask, depth):
+def weight_call(upper, lo, mid, hi, dpre, mask, depth):
     planes, chans, lanes = dpre.shape
     flops = 2 * planes * 9 * chans * 3 * chans * lanes
     half = jax.ShapeDtypeStruct((chans // 2, 27 * chans + 1), jnp.float32)
     return pl.pallas_call(
         functools.partial(_weight_kernel, planes=planes, depth=depth),
         out_shape=(half, half),
-        in_specs=[pl.BlockSpec(memory_space=pltpu.SMEM)] + _vmem(3),
+        in_specs=[pl.BlockSpec(memory_space=pltpu.SMEM)] + _vmem(5),
         out_specs=tuple(_vmem(2)),
         scratch_shapes=[pltpu.VMEM((chans, 27 * chans + 1), jnp.float32)],
         cost_estimate=pl.CostEstimate(flops=flops, transcendentals=0, bytes_accessed=3 * dpre.size * 2),
-    )(upper, haloed, dpre, mask)
+    )(upper, lo, mid, hi, dpre, mask)
 
 
 def neighbours(first, last, axis):
@@ -217,19 +213,19 @@
     mask = jnp.asarray(plane_masks(rows, depth))
 
     def flat(value):
-        return value.transpose(1, 0, 2, 3).reshape(planes, value.shape[0], lanes)
+        return value.transpose(1, 0, 2, 3).reshape(value.shape[1], value.shape[0], lanes)
 
     def unflat(value):
         return value.reshape(planes, value.shape[1], rows, depth).transpose(1, 0, 2, 3)
 
     below, above = neighbours(field[:, :1], field[:, planes - 1 :], "strike")
-    haloed = jnp.concatenate([below, field, above], axis=1)
-    haloed = haloed.transpose(1, 0, 2, 3).reshape(planes + 2, chans, lanes)
+    mid = flat(field)
+    lo, hi = flat(below), flat(above)
     act, dpre, first, last = forward_call(
-        haloed, forward_w, whole_bias.astype(jnp.float32)[:, None], flat(cotangent[0]), mask, depth
+        lo, mid, hi, forward_w, whole_bias.astype(jnp.float32)[:, None], flat(cotangent[0]), mask, depth
     )
     dlo, dhi = neighbours(first, last, "strike")
-    local_grads = weight_call(first_upper().astype(jnp.int32)[None], haloed, dpre, mask, depth)
+    local_grads = weight_call(first_upper().astype(jnp.int32)[None], lo, mid, hi, dpre, mask, depth)
     work = [
         (functools.partial(input_call, depth=depth, first=p, count=1), (dlo, dpre, dhi, backward_w, mask))
         for p in range(planes)

time: 55.8 us -> 54.6 us (0.978)
  waiting for transfers between devices: 4.47 us -> 3.26 us
  local copies, waits for them, and re-layouts: 10 us -> 11 us
  starting transfers between devices: 24.2 us -> 23.4 us
    another operation x0 -> x2, local copies, waits for them, and re-layouts: none -> 1.62 us  [flat(): value.transpose(1, 0, 2, 3).reshape(value.shape[1], value.shape[0], lanes)]
    ppermute x4, starting transfers between devices: 10.6 us -> 9.15 us  [neighbours(): return (lax.ppermute(last, axis, up), lax.ppermute(first, axis, down))]
    ppermute x4, waiting for transfers between devices: 1.22 us -> 0.01 us  [neighbours(): return (lax.ppermute(last, axis, up), lax.ppermute(first, axis, down))]
    reshape x4, local copies, waits for them, and re-layouts: 3.07 us -> 2.41 us  [flat(): value.transpose(1, 0, 2, 3).reshape(value.shape[1], value.shape[0], lanes)]
    ppermute x8, starting transfers between devices: 13.6 us -> 14.2 us  [swap(): return lax.ppermute(value, axis, [(i, i ^ bit) for i in range(peers)])]
  transfers between devices with their start and end apart: 12 -> 12, of which waited for: 4 -> 3; matrix products, arithmetic and copies ran while one was open for 12% -> 16% of each run, Pallas kernels for 18% -> 18%
where the time goes in v14:
time: 54.6 us; the launch traced here: 54.2 us
  starting transfers between devices  23.4 us (43%)
  Pallas kernels  14.9 us (27%)
  local copies, waits for them, and re-layouts  11 us (20%)
  waiting for transfers between devices  3.26 us (6%)
  between operations  0.88 us (2%)
  other arithmetic  0.84 us (2%)
    ppermute x8, starting transfers between devices, swap(): return lax.ppermute(value, axis, [(i, i ^ bit) for i in range(peers)])  14.2 us
    ppermute x4, starting transfers between devices, neighbours(): return (lax.ppermute(last, axis, up), lax.ppermute(first, axis, down))  9.15 us
    pallas_call x2, Pallas kernels, input_call(): pl.pallas_call(functools.partial(_input_kernel, planes=planes, first=firs...  6.08 us
    pallas_call x1, Pallas kernels, forward_call(): pl.pallas_call(functools.partial(_forward_kernel, planes=planes, depth=de...  5.07 us
    pallas_call x1, Pallas kernels, weight_call(): pl.pallas_call(functools.partial(_weight_kernel, planes=planes, depth=dep...  3.74 us
    ppermute x8, waiting for transfers between devices, swap(): return lax.ppermute(value, axis, [(i, i ^ bit) for i in range(peers)])  3.25 us
    reshape x4, local copies, waits for them, and re-layouts, flat(): value.transpose(1, 0, 2, 3).reshape(value.shape[1], value.shape[0], lanes)  2.41 us
    another operation x2, local copies, waits for them, and re-layouts, flat(): value.transpose(1, 0, 2, 3).reshape(value.shape[1], value.shape[0], lanes)  1.62 us
  transfers between devices with their start and end apart: 12, of which 3 were waited for; matrix products, arithmetic and copies ran while one was open for 16% of the time, Pallas kernels for 18%

profile of v14, /device:TPU:0, one launch (start us, length us, event | category | flops | bytes accessed | tf_op | source)
XLA Modules:
  0.0 54.2 jit_solution(10570362605852758732)
XLA Ops:
  0.6 0.0 copy-start.10
  0.6 0.6 %copy-done.10 = bf16[8]{0:T(256)(128)(2,1)S(1)} copy-done((bf16[8]{0:T(256)(128)(2,1)S(1)}, bf16[8]{0:T(256)(128)(2,1)}, u32[]{:S(2)}) %copy-start.10) | copy-done | bytes 40
  1.3 0.1 copy.17
  1.4 0.0 copy-start.9
  1.4 0.7 %copy-done.9 = bf16[8,864]{1,0:T(8,128)(2,1)S(1)} copy-done((bf16[8,864]{1,0:T(8,128)(2,1)S(1)}, bf16[8,864]{1,0:T(8,128)(2,1)}, u32[]{:S(2)}) %copy-start.9) | copy-done | bytes 13848
  2.1 0.1 bitcast_dynamic-update-slice_fusion.3
  2.2 3.0 %collective-permute-start.3 = (bf16[8,865]{1,0:T(8,128)(2,1)S(1)}, bf16[8,865]{1,0:T(8,128)(2,1)S(1)}, u32[]{:S(2)}, u32[]{:S(2)}) collective-permute-start(bf16[8,865]{1,0:T(8,128)(2,1)S(1)} %get-tuple-element.49), channel_id=1, source_target_pairs={{0,16},{8,24},{16,0},{24,8},{1,17},{9,25},{17,1},{25,9},{2,18},{10... | collective-permute-start | bytes 41528 | tf_op jit(solution)/shard_map/ppermute | solution.py:148
  5.1 1.5 %collective-permute-start.2 = (bf16[8,865]{1,0:T(8,128)(2,1)S(1)}, bf16[8,865]{1,0:T(8,128)(2,1)S(1)}, u32[]{:S(2)}, u32[]{:S(2)}) collective-permute-start(bf16[8,865]{1,0:T(8,128)(2,1)S(1)} %get-tuple-element.49), channel_id=1, source_target_pairs={{0,8},{8,0},{16,24},{24,16},{1,9},{9,1},{17,25},{25,17},{2,10},{10... | collective-permute-start | bytes 41528 | tf_op jit(solution)/shard_map/ppermute | solution.py:148
  6.6 0.0 collective-permute-start.4
  6.7 1.1 %fusion = (bf16[32,1,32,128]{3,2,1,0:T(8,128)(2,1)S(1)}, bf16[32,1,32,128]{3,2,1,0:T(8,128)(2,1)S(1)}) fusion(bf16[32,2,32,128]{3,2,1,0:T(8,128)(2,1)} %bitcast.59), kind=kLoop, calls=%fused_computation.14 | loop fusion | bytes 1048576 | tf_op jit(solution)/shard_map/slice | solution.py:221
  7.8 1.3 %collective-permute-start.1 = (bf16[32,1,32,128]{3,2,1,0:T(8,128)(2,1)S(1)}, bf16[32,1,32,128]{3,2,1,0:T(8,128)(2,1)S(1)}, u32[]{:S(2)}, u32[]{:S(2)}) collective-permute-start(bf16[32,1,32,128]{3,2,1,0:T(8,128)(2,1)S(1)} %get-tuple-element.50), channel_id=1, source_target_pairs={{1,0},{2,1},{3,2},{4,3},{5,4},{6,5},{7,6},{9,8},{10,9},{11,10},{12... | collective-permute-start | bytes 786440 | tf_op jit(solution)/shard_map/ppermute | solution.py:143
  9.1 3.0 %collective-permute-start = (bf16[32,1,32,128]{3,2,1,0:T(8,128)(2,1)S(1)}, bf16[32,1,32,128]{3,2,1,0:T(8,128)(2,1)S(1)}, u32[]{:S(2)}, u32[]{:S(2)}) collective-permute-start(bf16[32,1,32,128]{3,2,1,0:T(8,128)(2,1)S(1)} %get-tuple-element.51), channel_id=1, source_target_pairs={{0,1},{1,2},{2,3},{3,4},{4,5},{5,6},{6,7},{8,9},{9,10},{10,11},{11... | collective-permute-start | bytes 786440 | tf_op jit(solution)/shard_map/ppermute | solution.py:143
  12.2 0.0 copy-done.5
  12.2 0.1 reshape.41
  12.3 0.0 copy-start
  12.3 1.1 %copy.24.cot = bf16[2,32,4096]{2,1,0:T(8,128)(2,1)} copy(bf16[2,32,4096]{2,0,1:T(2,128)(2,1)S(1)} %reshape.41) | data formatting | bytes 1048576 | tf_op jit(solution)/shard_map/reshape | solution.py:216
  13.4 0.0 copy-done
  13.4 0.1 reshape.40
  13.6 1.1 %copy.23.mid = bf16[2,32,4096]{2,1,0:T(8,128)(2,1)} copy(bf16[2,32,4096]{2,0,1:T(2,128)(2,1)S(1)} %reshape.40) | data formatting | bytes 1048576 | tf_op jit(solution)/shard_map/reshape | solution.py:216
  14.6 0.0 collective-permute-done.2
  14.6 0.0 collective-permute-done.3
  14.7 0.0 collective-permute-done.4
  14.7 0.2 reshape.34
  14.9 0.1 copy.18
  15.0 0.8 %reshape.35.wall = bf16[288,96]{1,0:T(8,128)(2,1)} reshape(bf16[3,3,32,3,32]{4,3,2,1,0:T(4,128)(2,1)S(1)} %copy.18) | data formatting | bytes 110592 | tf_op jit(solution)/shard_map/reshape | solution.py:211
  15.8 0.7 %slice_convert_fusion.bias = f32[32,1]{1,0:T(8,128)} fusion(bf16[32,865]{1,0:T(8,128)(2,1)S(1)} %bitcast.67), kind=kLoop, calls=%fused_computation.11 | loop fusion | flops 32 | bytes 192 | tf_op jit(solution)/shard_map/convert_element_type | solution.py:225
  16.5 0.0 collective-permute-done.1
  16.5 0.8 %reshape_transpose.7.hi = bf16[1,32,4096]{2,1,0:T(8,128)(2,1)} reshape(bf16[32,1,32,128]{3,2,1,0:T(8,128)(2,1)S(1)} %collective-permute-done.1) | data formatting | bytes 524288 | tf_op jit(solution)/shard_map/reshape;transpose | solution.py:216
  17.3 0.0 collective-permute-done
  17.3 0.8 %reshape_transpose.6.lo = bf16[1,32,4096]{2,1,0:T(8,128)(2,1)} reshape(bf16[32,1,32,128]{3,2,1,0:T(8,128)(2,1)S(1)} %collective-permute-done) | data formatting | bytes 524288 | tf_op jit(solution)/shard_map/reshape;transpose | solution.py:216
  18.2 5.1 %shard_map.84 = (bf16[2,32,4096]{2,1,0:T(8,128)(2,1)}, bf16[2,32,4096]{2,1,0:T(8,128)(2,1)}, bf16[1,32,4096]{2,1,0:T(8,128)(2,1)}, bf16[1,32,4096]{2,1,0:T(8,128)(2,1)}) custom-call(bf16[1,32,4096]{2,1,0:T(8,128)(2,1)} %reshape_transpose.6.lo, bf16[2,32,4096]{2,1,0:T(8,128)(2,1)} %copy.23.mid, bf16[1,32,4096]{2,1,0:T(8,128)(2,1)} %reshape_transpose.7.hi, ...), custom_call_target="tpu_custom_call" | custom-call | flops 452984832 | bytes 2621440 | tf_op jit(solution)/shard_map/pallas_call | solution.py:104
  23.2 3.5 %collective-permute-start.5 = (bf16[1,32,4096]{2,1,0:T(8,128)(2,1)}, bf16[1,32,4096]{2,1,0:T(8,128)(2,1)S(1)}, u32[]{:S(2)}, u32[]{:S(2)}) collective-permute-start(bf16[1,32,4096]{2,1,0:T(8,128)(2,1)} %get-tuple-element.29), channel_id=1, source_target_pairs={{0,1},{1,2},{2,3},{3,4},{4,5},{5,6},{6,7},{8,9},{9,10},{10,11},{11... | collective-permute-start | bytes 786440 | tf_op jit(solution)/shard_map/ppermute | solution.py:143
  26.7 1.3 %collective-permute-start.6 = (bf16[1,32,4096]{2,1,0:T(8,128)(2,1)}, bf16[1,32,4096]{2,1,0:T(8,128)(2,1)S(1)}, u32[]{:S(2)}, u32[]{:S(2)}) collective-permute-start(bf16[1,32,4096]{2,1,0:T(8,128)(2,1)} %get-tuple-element.30), channel_id=1, source_target_pairs={{1,0},{2,1},{3,2},{4,3},{5,4},{6,5},{7,6},{9,8},{10,9},{11,10},{12... | collective-permute-start | bytes 786440 | tf_op jit(solution)/shard_map/ppermute | solution.py:143
  28.1 0.1 reverse_bitcast_fusion
  28.2 0.3 copy.21
  28.5 0.8 %reshape.38.wall = bf16[288,96]{1,0:T(8,128)(2,1)} reshape(bf16[3,3,32,3,32]{4,3,2,1,0:T(4,128)(2,1)S(1)} %copy.21) | data formatting | bytes 110592 | tf_op jit(solution)/shard_map/reshape | solution.py:212
  29.3 3.7 %shard_map.85 = (f32[16,865]{1,0:T(8,128)}, f32[16,865]{1,0:T(8,128)}) custom-call(s32[1]{0:T(128)} %bitcast.13.upper, bf16[1,32,4096]{2,1,0:T(8,128)(2,1)} %reshape_transpose.6.lo, bf16[2,32,4096]{2,1,0:T(8,128)(2,1)} %copy.23.mid, bf16[1,32,4096]{2,1,0:T(8,128)(2,1)} %reshape_transpose.7.hi, bf16[2,32,4096]{2,1,0:T(8,128)(2,1)} %get-tuple-element.42.dpre.mid, ...), custom_call_target="tpu_custom_call" | custom-call | flops 452984832 | bytes 1572864 | tf_op jit(solution)/shard_map/pallas_call | solution.py:129
  33.0 0.0 collective-permute-done.5.lo
  33.0 0.0 collective-permute-done.6.hi
  33.0 0.0 copy-start.2
  33.0 1.6 %collective-permute-start.7 = (f32[16,865]{1,0:T(8,128)}, f32[16,865]{1,0:T(8,128)S(1)}, u32[]{:S(2)}, u32[]{:S(2)}) collective-permute-start(f32[16,865]{1,0:T(8,128)} %get-tuple-element.31), channel_id=1, source_target_pairs={{0,16},{8,24},{16,0},{24,8},{1,17},{9,25},{17,1},{25,9},{2,18},{10... | collective-permute-start | bytes 166088 | tf_op jit(solution)/shard_map/ppermute | solution.py:148
  34.6 0.0 copy-done.1
  34.6 0.0 copy-done.2
  34.6 3.0 %shard_map.86 = bf16[1,32,4096]{2,1,0:T(8,128)(2,1)} custom-call(bf16[1,32,4096]{2,1,0:T(8,128)(2,1)} %copy-done.1, bf16[2,32,4096]{2,1,0:T(8,128)(2,1)} %get-tuple-element.42.dpre.mid, bf16[1,32,4096]{2,1,0:T(8,128)(2,1)} %copy-done.2, bf16[288,96]{1,0:T(8,128)(2,1)} %reshape.38.wall, f32[9,1,4096]{2,1,0:T(1,128)} %constant.66.clone.mask), custom_call_target="tpu_custom_call" | custom-call | flops 226492416 | bytes 1572864 | tf_op jit(solution)/shard_map/pallas_call | solution.py:116
  37.7 0.0 collective-permute-done.7
  37.7 0.0 copy-done.7
  37.7 1.6 %collective-permute-start.8 = (f32[8,865]{1,0:T(8,128)S(1)}, f32[8,865]{1,0:T(8,128)S(1)}, u32[]{:S(2)}, u32[]{:S(2)}) collective-permute-start(f32[8,865]{1,0:T(8,128)S(1)} %constant_dynamic-slice_fusion), channel_id=1, source_target_pairs={{0,8},{8,0},{16,24},{24,16},{1,9},{9,1},{17,25},{25,17},{2,10},{10... | collective-permute-start | bytes 83048 | tf_op jit(solution)/shard_map/ppermute | solution.py:148
  39.2 3.1 %shard_map.87 = bf16[1,32,4096]{2,1,0:T(8,128)(2,1)} custom-call(bf16[1,32,4096]{2,1,0:T(8,128)(2,1)} %copy-done.1, bf16[2,32,4096]{2,1,0:T(8,128)(2,1)} %get-tuple-element.42.dpre.mid, bf16[1,32,4096]{2,1,0:T(8,128)(2,1)} %copy-done.2, bf16[288,96]{1,0:T(8,128)(2,1)} %reshape.38.wall, f32[9,1,4096]{2,1,0:T(1,128)} %constant.66.clone.mask), custom_call_target="tpu_custom_call" | custom-call | flops 226492416 | bytes 1572864 | tf_op jit(solution)/shard_map/pallas_call | solution.py:116
  42.3 0.0 collective-permute-done.8
  42.3 1.6 %collective-permute-start.9 = (f32[8,865]{1,0:T(8,128)S(1)}, f32[8,865]{1,0:T(8,128)S(1)}, u32[]{:S(2)}, u32[]{:S(2)}) collective-permute-start(f32[8,865]{1,0:T(8,128)S(1)} %dynamic-slice_add_fusion), channel_id=1, source_target_pairs={{0,1},{1,0},{2,3},{3,2},{4,5},{5,4},{6,7},{7,6},{8,9},{9,8},{10,11... | collective-permute-start | bytes 83048 | tf_op jit(solution)/shard_map/ppermute | solution.py:148
  44.0 0.0 copy-done.6
  44.0 0.1 copy.25
  44.1 0.8 %collective-permute-done.9 = f32[8,865]{1,0:T(8,128)S(1)} collective-permute-done((f32[8,865]{1,0:T(8,128)S(1)}, f32[8,865]{1,0:T(8,128)S(1)}, u32[]{:S(2)}, u32[]{:S(2)}) %collective-permute-start.9) | collective-permute-done | bytes 27712 | tf_op jit(solution)/shard_map/ppermute | solution.py:148
  44.8 2.0 %collective-permute-start.10 = (f32[8,865]{1,0:T(8,128)S(1)}, f32[8,865]{1,0:T(8,128)S(1)}, u32[]{:S(2)}, u32[]{:S(2)}) collective-permute-start(f32[8,865]{1,0:T(8,128)S(1)} %add.53), channel_id=1, source_target_pairs={{0,2},{1,3},{2,0},{3,1},{4,6},{5,7},{6,4},{7,5},{8,10},{9,11},{10,... | collective-permute-start | bytes 83048 | tf_op jit(solution)/shard_map/ppermute | solution.py:148
  46.8 0.0 copy-done.3
  46.8 0.0 copy-done.4
  46.8 0.1 pad_maximum_fusion
  46.9 0.1 copy.26
  47.0 1.8 %collective-permute-done.10 = f32[8,865]{1,0:T(8,128)S(1)} collective-permute-done((f32[8,865]{1,0:T(8,128)S(1)}, f32[8,865]{1,0:T(8,128)S(1)}, u32[]{:S(2)}, u32[]{:S(2)}) %collective-permute-start.10) | collective-permute-done | bytes 27712 | tf_op jit(solution)/shard_map/ppermute | solution.py:148
  48.7 3.0 %collective-permute-start.11 = (f32[8,865]{1,0:T(8,128)S(1)}, f32[8,865]{1,0:T(8,128)S(1)}, u32[]{:S(2)}, u32[]{:S(2)}) collective-permute-start(f32[8,865]{1,0:T(8,128)S(1)} %add.54), channel_id=1, source_target_pairs={{0,4},{1,5},{2,6},{3,7},{4,0},{5,1},{6,2},{7,3},{8,12},{9,13},{10,... | collective-permute-start | bytes 83048 | tf_op jit(solution)/shard_map/ppermute | solution.py:148
  51.7 1.1 %copy_bitcast_fusion = (bf16[1,32,2,32,128]{4,3,2,1,0:T(8,128)(2,1)}, bf16[1,32,2,32,128]{4,3,2,1,0:T(8,128)(2,1)}) fusion(bf16[2,32,32,128]{3,2,1,0:T(8,128)(2,1)S(1)} %bitcast.62, bf16[2,32,32,128]{3,2,1,0:T(8,128)(2,1)S(1)} %bitcast.63), kind=kLoop, calls=%fused_computation.1 | loop fusion | bytes 2097152 | tf_op jit(solution)/shard_map/broadcast_in_dim | solution.py:238
  52.8 0.7 %collective-permute-done.11 = f32[8,865]{1,0:T(8,128)S(1)} collective-permute-done((f32[8,865]{1,0:T(8,128)S(1)}, f32[8,865]{1,0:T(8,128)S(1)}, u32[]{:S(2)}, u32[]{:S(2)}) %collective-permute-start.11) | collective-permute-done | bytes 27712 | tf_op jit(solution)/shard_map/ppermute | solution.py:148
  53.5 0.7 %slice_reduce_fusion = f32[8]{0:T(128)} fusion(f32[8,865]{1,0:T(8,128)S(1)} %add_multiply_fusion), kind=kLoop, calls=%fused_computation.12 | loop fusion | bytes 64 | tf_op jit(solution)/shard_map/slice | solution.py:238
  54.2 0.0 copy-done.8
  (17 shorter events, 0.1 us)
Async XLA Ops:
  0.6 0.7 %copy-start.10 = (bf16[8]{0:T(256)(128)(2,1)S(1)}, bf16[8]{0:T(256)(128)(2,1)}, u32[]{:S(2)}) copy-start(bf16[8]{0:T(256)(128)(2,1)} %param.8) | copy-start | bytes 52
  1.4 0.7 %copy-start.9 = (bf16[8,864]{1,0:T(8,128)(2,1)S(1)}, bf16[8,864]{1,0:T(8,128)(2,1)}, u32[]{:S(2)}) copy-start(bf16[8,864]{1,0:T(8,128)(2,1)} %param.7) | copy-start | bytes 41476
  2.2 12.5 %collective-permute-start.3 = (bf16[8,865]{1,0:T(8,128)(2,1)S(1)}, bf16[8,865]{1,0:T(8,128)(2,1)S(1)}, u32[]{:S(2)}, u32[]{:S(2)}) collective-permute-start(bf16[8,865]{1,0:T(8,128)(2,1)S(1)} %get-tuple-element.49), channel_id=1, source_target_pairs={{0,16},{8,24},{16,0},{24,8},{1,17},{9,25},{17,1},{25,9},{2,18},{10... | collective-permute-start | bytes 41528 | tf_op jit(solution)/shard_map/ppermute | solution.py:148
  5.1 9.5 %collective-permute-start.2 = (bf16[8,865]{1,0:T(8,128)(2,1)S(1)}, bf16[8,865]{1,0:T(8,128)(2,1)S(1)}, u32[]{:S(2)}, u32[]{:S(2)}) collective-permute-start(bf16[8,865]{1,0:T(8,128)(2,1)S(1)} %get-tuple-element.49), channel_id=1, source_target_pairs={{0,8},{8,0},{16,24},{24,16},{1,9},{9,1},{17,25},{25,17},{2,10},{10... | collective-permute-start | bytes 41528 | tf_op jit(solution)/shard_map/ppermute | solution.py:148
  6.6 8.0 %collective-permute-start.4 = (bf16[8,865]{1,0:T(8,128)(2,1)S(1)}, bf16[8,865]{1,0:T(8,128)(2,1)S(1)}, u32[]{:S(2)}, u32[]{:S(2)}) collective-permute-start(bf16[8,865]{1,0:T(8,128)(2,1)S(1)} %get-tuple-element.49), channel_id=1, source_target_pairs={{0,24},{8,16},{16,8},{24,0},{1,25},{9,17},{17,9},{25,1},{2,26},{10... | collective-permute-start | bytes 41528 | tf_op jit(solution)/shard_map/ppermute | solution.py:148
  6.7 5.5 %copy-start.5 = (bf16[1,32,2,32,128]{4,3,2,1,0:T(8,128)(2,1)S(1)}, bf16[1,32,2,32,128]{4,3,2,1,0:T(8,128)(2,1)}, u32[]{:S(2)}) copy-start(bf16[1,32,2,32,128]{4,3,2,1,0:T(8,128)(2,1)} %param.6) | copy-start | bytes 1572868
  7.8 8.7 %collective-permute-start.1 = (bf16[32,1,32,128]{3,2,1,0:T(8,128)(2,1)S(1)}, bf16[32,1,32,128]{3,2,1,0:T(8,128)(2,1)S(1)}, u32[]{:S(2)}, u32[]{:S(2)}) collective-permute-start(bf16[32,1,32,128]{3,2,1,0:T(8,128)(2,1)S(1)} %get-tuple-element.50), channel_id=1, source_target_pairs={{1,0},{2,1},{3,2},{4,3},{5,4},{6,5},{7,6},{9,8},{10,9},{11,10},{12... | collective-permute-start | bytes 786440 | tf_op jit(solution)/shard_map/ppermute | solution.py:143
  9.1 8.2 %collective-permute-start = (bf16[32,1,32,128]{3,2,1,0:T(8,128)(2,1)S(1)}, bf16[32,1,32,128]{3,2,1,0:T(8,128)(2,1)S(1)}, u32[]{:S(2)}, u32[]{:S(2)}) collective-permute-start(bf16[32,1,32,128]{3,2,1,0:T(8,128)(2,1)S(1)} %get-tuple-element.51), channel_id=1, source_target_pairs={{0,1},{1,2},{2,3},{3,4},{4,5},{5,6},{6,7},{8,9},{9,10},{10,11},{11... | collective-permute-start | bytes 786440 | tf_op jit(solution)/shard_map/ppermute | solution.py:143
  12.3 1.1 %copy-start = (bf16[1,32,2,32,128]{4,3,2,1,0:T(8,128)(2,1)S(1)}, bf16[1,32,2,32,128]{4,3,2,1,0:T(8,128)(2,1)}, u32[]{:S(2)}) copy-start(bf16[1,32,2,32,128]{4,3,2,1,0:T(8,128)(2,1)} %param.5) | copy-start | bytes 1572868
  23.2 9.8 %collective-permute-start.5 = (bf16[1,32,4096]{2,1,0:T(8,128)(2,1)}, bf16[1,32,4096]{2,1,0:T(8,128)(2,1)S(1)}, u32[]{:S(2)}, u32[]{:S(2)}) collective-permute-start(bf16[1,32,4096]{2,1,0:T(8,128)(2,1)} %get-tuple-element.29), channel_id=1, source_target_pairs={{0,1},{1,2},{2,3},{3,4},{4,5},{5,6},{6,7},{8,9},{9,10},{10,11},{11... | collective-permute-start | bytes 786440 | tf_op jit(solution)/shard_map/ppermute | solution.py:143
  26.7 6.3 %collective-permute-start.6 = (bf16[1,32,4096]{2,1,0:T(8,128)(2,1)}, bf16[1,32,4096]{2,1,0:T(8,128)(2,1)S(1)}, u32[]{:S(2)}, u32[]{:S(2)}) collective-permute-start(bf16[1,32,4096]{2,1,0:T(8,128)(2,1)} %get-tuple-element.30), channel_id=1, source_target_pairs={{1,0},{2,1},{3,2},{4,3},{5,4},{6,5},{7,6},{9,8},{10,9},{11,10},{12... | collective-permute-start | bytes 786440 | tf_op jit(solution)/shard_map/ppermute | solution.py:143
  33.0 1.6 %copy-start.1 = (bf16[1,32,4096]{2,1,0:T(8,128)(2,1)}, bf16[1,32,4096]{2,1,0:T(8,128)(2,1)S(1)}, u32[]{:S(2)}) copy-start(bf16[1,32,4096]{2,1,0:T(8,128)(2,1)S(1)} %collective-permute-done.5.lo) | copy-start | bytes 786436
  33.0 1.6 %copy-start.2 = (bf16[1,32,4096]{2,1,0:T(8,128)(2,1)}, bf16[1,32,4096]{2,1,0:T(8,128)(2,1)S(1)}, u32[]{:S(2)}) copy-start(bf16[1,32,4096]{2,1,0:T(8,128)(2,1)S(1)} %collective-permute-done.6.hi) | copy-start | bytes 786436
  33.0 4.6 %collective-permute-start.7 = (f32[16,865]{1,0:T(8,128)}, f32[16,865]{1,0:T(8,128)S(1)}, u32[]{:S(2)}, u32[]{:S(2)}) collective-permute-start(f32[16,865]{1,0:T(8,128)} %get-tuple-element.31), channel_id=1, source_target_pairs={{0,16},{8,24},{16,0},{24,8},{1,17},{9,25},{17,1},{25,9},{2,18},{10... | collective-permute-start | bytes 166088 | tf_op jit(solution)/shard_map/ppermute | solution.py:148
  34.6 3.0 %copy-start.7 = (f32[16,865]{1,0:T(8,128)S(1)}, f32[16,865]{1,0:T(8,128)}, u32[]{:S(2)}) copy-start(f32[16,865]{1,0:T(8,128)} %get-tuple-element.38) | copy-start | bytes 166084
  37.7 4.6 %collective-permute-start.8 = (f32[8,865]{1,0:T(8,128)S(1)}, f32[8,865]{1,0:T(8,128)S(1)}, u32[]{:S(2)}, u32[]{:S(2)}) collective-permute-start(f32[8,865]{1,0:T(8,128)S(1)} %constant_dynamic-slice_fusion), channel_id=1, source_target_pairs={{0,8},{8,0},{16,24},{24,16},{1,9},{9,1},{17,25},{25,17},{2,10},{10... | collective-permute-start | bytes 83048 | tf_op jit(solution)/shard_map/ppermute | solution.py:148
  39.2 4.7 %copy-start.6 = (bf16[2,32,4096]{2,1,0:T(8,128)(2,1)S(1)}, bf16[2,32,4096]{2,1,0:T(8,128)(2,1)}, u32[]{:S(2)}) copy-start(bf16[2,32,4096]{2,1,0:T(8,128)(2,1)} %get-tuple-element.26) | copy-start | bytes 1572868
  42.3 2.5 %collective-permute-start.9 = (f32[8,865]{1,0:T(8,128)S(1)}, f32[8,865]{1,0:T(8,128)S(1)}, u32[]{:S(2)}, u32[]{:S(2)}) collective-permute-start(f32[8,865]{1,0:T(8,128)S(1)} %dynamic-slice_add_fusion), channel_id=1, source_target_pairs={{0,1},{1,0},{2,3},{3,2},{4,5},{5,4},{6,7},{7,6},{8,9},{9,8},{10,11... | collective-permute-start | bytes 83048 | tf_op jit(solution)/shard_map/ppermute | solution.py:148
  44.0 2.8 %copy-start.3 = (bf16[1,32,4096]{2,1,0:T(8,128)(2,1)S(1)}, bf16[1,32,4096]{2,1,0:T(8,128)(2,1)}, u32[]{:S(2)}) copy-start(bf16[1,32,4096]{2,1,0:T(8,128)(2,1)} %shard_map.86) | copy-start | bytes 786436
  44.0 2.8 %copy-start.4 = (bf16[1,32,4096]{2,1,0:T(8,128)(2,1)S(1)}, bf16[1,32,4096]{2,1,0:T(8,128)(2,1)}, u32[]{:S(2)}) copy-start(bf16[1,32,4096]{2,1,0:T(8,128)(2,1)} %shard_map.87) | copy-start | bytes 786436
  44.8 3.9 %collective-permute-start.10 = (f32[8,865]{1,0:T(8,128)S(1)}, f32[8,865]{1,0:T(8,128)S(1)}, u32[]{:S(2)}, u32[]{:S(2)}) collective-permute-start(f32[8,865]{1,0:T(8,128)S(1)} %add.53), channel_id=1, source_target_pairs={{0,2},{1,3},{2,0},{3,1},{4,6},{5,7},{6,4},{7,5},{8,10},{9,11},{10,... | collective-permute-start | bytes 83048 | tf_op jit(solution)/shard_map/ppermute | solution.py:148
  48.7 4.8 %collective-permute-start.11 = (f32[8,865]{1,0:T(8,128)S(1)}, f32[8,865]{1,0:T(8,128)S(1)}, u32[]{:S(2)}, u32[]{:S(2)}) collective-permute-start(f32[8,865]{1,0:T(8,128)S(1)} %add.54), channel_id=1, source_target_pairs={{0,4},{1,5},{2,6},{3,7},{4,0},{5,1},{6,2},{7,3},{8,12},{9,13},{10,... | collective-permute-start | bytes 83048 | tf_op jit(solution)/shard_map/ppermute | solution.py:148
  53.5 0.7 %copy-start.8 = (f32[8,865]{1,0:T(8,128)}, f32[8,865]{1,0:T(8,128)S(1)}, u32[]{:S(2)}) copy-start(f32[8,865]{1,0:T(8,128)S(1)} %add_multiply_fusion) | copy-start | bytes 83044

commit v15 on v14

--- a/solution.py
+++ b/solution.py
@@ -26,6 +26,10 @@
             return hi[0]
         return mid[index - 1]
     return jnp.concatenate([plane(h), plane(h + 1), plane(h + 2)], axis=0)
+
+
+def _stacked_edges(edges, mid, h, planes):
+    return _stacked_parts(edges.at[0:1], mid, edges.at[1:2], h, planes)
 
 
 def _shifted_sum(y, mask, chans, lanes, depth, sign):
@@ -40,10 +44,10 @@
     return total
 
 
-def _forward_kernel(lo, mid, hi, wall, bias, cot, mask, act_out, dpre_out, first_out, last_out, *, planes, depth):
+def _forward_kernel(edges, mid, wall, bias, cot, mask, act_out, dpre_out, first_out, last_out, *, planes, depth):
     chans, lanes = mid.shape[1], mid.shape[2]
     for p in range(planes):
-        y = jnp.dot(wall[...], _stacked_parts(lo, mid, hi, p, planes), preferred_element_type=jnp.float32)
+        y = jnp.dot(wall[...], _stacked_edges(edges, mid, p, planes), preferred_element_type=jnp.float32)
         pre = _shifted_sum(y, mask, chans, lanes, depth, 1) + bias[...]
         sig = 1.0 / (1.0 + jnp.exp(-pre))
         act_out[p] = (pre * sig).astype(act_out.dtype)
@@ -62,7 +66,7 @@
         out[n] = _shifted_sum(y, mask, chans, lanes, depth, -1).astype(out.dtype)
 
 
-def _weight_kernel(upper, lo, mid, hi, dpre, mask, keep_out, send_out, full, *, planes, depth):
+def _weight_kernel(upper, edges, mid, dpre, mask, keep_out, send_out, full, *, planes, depth):
     chans, lanes = dpre.shape[1], dpre.shape[2]
     gw = jnp.zeros((9 * chans, 3 * chans), jnp.float32)
     gb = jnp.zeros((chans, 1), jnp.float32)
@@ -77,7 +81,7 @@
                 e = pltpu.roll(jnp.where(mask[k] > 0.5, d, 0.0), off % lanes, 1)
             parts.append(e.astype(jnp.bfloat16))
         gw = gw + lax.dot_general(
-            jnp.concatenate(parts, axis=0), _stacked_parts(lo, mid, hi, p, planes),
+            jnp.concatenate(parts, axis=0), _stacked_edges(edges, mid, p, planes),
             (((1,), (1,)), ((), ())), preferred_element_type=jnp.float32,
         )
     chans_in = gw.shape[1] // 3
@@ -96,7 +100,7 @@
     return [pl.BlockSpec(memory_space=pltpu.VMEM)] * n
 
 
-def forward_call(lo, mid, hi, wall, bias, cot, mask, depth):
+def forward_call(edges, mid, wall, bias, cot, mask, depth):
     planes, chans, lanes = cot.shape
     shape = jax.ShapeDtypeStruct(cot.shape, jnp.bfloat16)
     edge = jax.ShapeDtypeStruct((1, chans, lanes), jnp.bfloat16)
@@ -104,10 +108,10 @@
     return pl.pallas_call(
         functools.partial(_forward_kernel, planes=planes, depth=depth),
         out_shape=(shape, shape, edge, edge),
-        in_specs=_vmem(7),
+        in_specs=_vmem(6),
         out_specs=tuple(_vmem(4)),
         cost_estimate=pl.CostEstimate(flops=flops, transcendentals=planes * chans * lanes, bytes_accessed=5 * cot.size * 2),
-    )(lo, mid, hi, wall, bias, cot, mask)
+    )(edges, mid, wall, bias, cot, mask)
 
 
 def input_call(lo, mid, hi, wall, mask, depth, first, count):
@@ -122,18 +126,18 @@
     )(lo, mid, hi, wall, mask)
 
 
-def weight_call(upper, lo, mid, hi, dpre, mask, depth):
+def weight_call(upper, edges, mid, dpre, mask, depth):
     planes, chans, lanes = dpre.shape
     flops = 2 * planes * 9 * chans * 3 * chans * lanes
     half = jax.ShapeDtypeStruct((chans // 2, 27 * chans + 1), jnp.float32)
     return pl.pallas_call(
         functools.partial(_weight_kernel, planes=planes, depth=depth),
         out_shape=(half, half),
-        in_specs=[pl.BlockSpec(memory_space=pltpu.SMEM)] + _vmem(5),
+        in_specs=[pl.BlockSpec(memory_space=pltpu.SMEM)] + _vmem(4),
         out_specs=tuple(_vmem(2)),
         scratch_shapes=[pltpu.VMEM((chans, 27 * chans + 1), jnp.float32)],
         cost_estimate=pl.CostEstimate(flops=flops, transcendentals=0, bytes_accessed=3 * dpre.size * 2),
-    )(upper, lo, mid, hi, dpre, mask)
+    )(upper, edges, mid, dpre, mask)
 
 
 def neighbours(first, last, axis):
@@ -220,12 +224,12 @@
 
     below, above = neighbours(field[:, :1], field[:, planes - 1 :], "strike")
     mid = flat(field)
-    lo, hi = flat(below), flat(above)
+    edges = flat(jnp.concatenate([below, above], axis=1))
     act, dpre, first, last = forward_call(
-        lo, mid, hi, forward_w, whole_bias.astype(jnp.float32)[:, None], flat(cotangent[0]), mask, depth
+        edges, mid, forward_w, whole_bias.astype(jnp.float32)[:, None], flat(cotangent[0]), mask, depth
     )
     dlo, dhi = neighbours(first, last, "strike")
-    local_grads = weight_call(first_upper().astype(jnp.int32)[None], lo, mid, hi, dpre, mask, depth)
+    local_grads = weight_call(first_upper().astype(jnp.int32)[None], edges, mid, dpre, mask, depth)
     work = [
         (functools.partial(input_call, depth=depth, first=p, count=1), (dlo, dpre, dhi, backward_w, mask))
         for p in range(planes)

time: 54.6 us -> 55.4 us (1.015)
  starting transfers between devices: 23.4 us -> 24.5 us
    another operation x2 -> x0, local copies, waits for them, and re-layouts: 1.62 us -> none  [flat(): value.transpose(1, 0, 2, 3).reshape(value.shape[1], value.shape[0], lanes)]
    ppermute x4, starting transfers between devices: 9.15 us -> 10.5 us  [neighbours(): return (lax.ppermute(last, axis, up), lax.ppermute(first, axis, down))]
    reshape x4 -> x6, local copies, waits for them, and re-layouts: 2.41 us -> 3.63 us  [flat(): value.transpose(1, 0, 2, 3).reshape(value.shape[1], value.shape[0], lanes)]
  transfers between devices with their start and end apart: 12 -> 12, of which waited for: 3 -> 3; matrix products, arithmetic and copies ran while one was open for 16% -> 14% of each run, Pallas kernels for 18% -> 18%
where the time goes in v15:
time: 55.4 us; the launch traced here: 55 us
  starting transfers between devices  24.5 us (44%)
  Pallas kernels  14.9 us (27%)
  local copies, waits for them, and re-layouts  10.6 us (19%)
  waiting for transfers between devices  3.25 us (6%)
  other arithmetic  0.89 us (2%)
  between operations  0.89 us (2%)
    ppermute x8, starting transfers between devices, swap(): return lax.ppermute(value, axis, [(i, i ^ bit) for i in range(peers)])  14 us
    ppermute x4, starting transfers between devices, neighbours(): return (lax.ppermute(last, axis, up), lax.ppermute(first, axis, down))  10.5 us
    pallas_call x2, Pallas kernels, input_call(): pl.pallas_call(functools.partial(_input_kernel, planes=planes, first=firs...  6.08 us
    pallas_call x1, Pallas kernels, forward_call(): pl.pallas_call(functools.partial(_forward_kernel, planes=planes, depth=de...  5.07 us
    pallas_call x1, Pallas kernels, weight_call(): pl.pallas_call(functools.partial(_weight_kernel, planes=planes, depth=dep...  3.75 us
    reshape x6, local copies, waits for them, and re-layouts, flat(): value.transpose(1, 0, 2, 3).reshape(value.shape[1], value.shape[0], lanes)  3.63 us
    ppermute x8, waiting for transfers between devices, swap(): return lax.ppermute(value, axis, [(i, i ^ bit) for i in range(peers)])  3.24 us
    unnamed x24, local copies, waits for them, and re-layouts  1.57 us
  transfers between devices with their start and end apart: 12, of which 3 were waited for; matrix products, arithmetic and copies ran while one was open for 14% of the time, Pallas kernels for 18%

profile of v15, /device:TPU:0, one launch (start us, length us, event | category | flops | bytes accessed | tf_op | source)
XLA Modules:
  0.0 55.0 jit_solution(10528669079609773594)
XLA Ops:
  0.6 0.0 copy-start.10
  0.6 0.6 %copy-done.10 = bf16[8]{0:T(256)(128)(2,1)S(1)} copy-done((bf16[8]{0:T(256)(128)(2,1)S(1)}, bf16[8]{0:T(256)(128)(2,1)}, u32[]{:S(2)}) %copy-start.10) | copy-done | bytes 40
  1.3 0.1 copy.19
  1.4 0.0 copy-start.9
  1.4 0.7 %copy-done.9 = bf16[8,864]{1,0:T(8,128)(2,1)S(1)} copy-done((bf16[8,864]{1,0:T(8,128)(2,1)S(1)}, bf16[8,864]{1,0:T(8,128)(2,1)}, u32[]{:S(2)}) %copy-start.9) | copy-done | bytes 13848
  2.1 0.1 bitcast_dynamic-update-slice_fusion.3
  2.2 3.0 %collective-permute-start.3 = (bf16[8,865]{1,0:T(8,128)(2,1)S(1)}, bf16[8,865]{1,0:T(8,128)(2,1)S(1)}, u32[]{:S(2)}, u32[]{:S(2)}) collective-permute-start(bf16[8,865]{1,0:T(8,128)(2,1)S(1)} %get-tuple-element.49), channel_id=1, source_target_pairs={{0,16},{8,24},{16,0},{24,8},{1,17},{9,25},{17,1},{25,9},{2,18},{10... | collective-permute-start | bytes 41528 | tf_op jit(solution)/shard_map/ppermute | solution.py:152
  5.1 1.5 %collective-permute-start.2 = (bf16[8,865]{1,0:T(8,128)(2,1)S(1)}, bf16[8,865]{1,0:T(8,128)(2,1)S(1)}, u32[]{:S(2)}, u32[]{:S(2)}) collective-permute-start(bf16[8,865]{1,0:T(8,128)(2,1)S(1)} %get-tuple-element.49), channel_id=1, source_target_pairs={{0,8},{8,0},{16,24},{24,16},{1,9},{9,1},{17,25},{25,17},{2,10},{10... | collective-permute-start | bytes 41528 | tf_op jit(solution)/shard_map/ppermute | solution.py:152
  6.6 0.0 collective-permute-start.4
  6.7 1.1 %fusion = (bf16[32,1,32,128]{3,2,1,0:T(8,128)(2,1)S(1)}, bf16[32,1,32,128]{3,2,1,0:T(8,128)(2,1)S(1)}) fusion(bf16[32,2,32,128]{3,2,1,0:T(8,128)(2,1)} %bitcast.61), kind=kLoop, calls=%fused_computation.15 | loop fusion | bytes 1048576 | tf_op jit(solution)/shard_map/slice | solution.py:225
  7.8 1.3 %collective-permute-start = (bf16[32,1,32,128]{3,2,1,0:T(8,128)(2,1)S(1)}, bf16[32,1,32,128]{3,2,1,0:T(8,128)(2,1)S(1)}, u32[]{:S(2)}, u32[]{:S(2)}) collective-permute-start(bf16[32,1,32,128]{3,2,1,0:T(8,128)(2,1)S(1)} %get-tuple-element.50), channel_id=1, source_target_pairs={{0,1},{1,2},{2,3},{3,4},{4,5},{5,6},{6,7},{8,9},{9,10},{10,11},{11... | collective-permute-start | bytes 786440 | tf_op jit(solution)/shard_map/ppermute | solution.py:147
  9.1 1.3 %collective-permute-start.1 = (bf16[32,1,32,128]{3,2,1,0:T(8,128)(2,1)S(1)}, bf16[32,1,32,128]{3,2,1,0:T(8,128)(2,1)S(1)}, u32[]{:S(2)}, u32[]{:S(2)}) collective-permute-start(bf16[32,1,32,128]{3,2,1,0:T(8,128)(2,1)S(1)} %get-tuple-element.51), channel_id=1, source_target_pairs={{1,0},{2,1},{3,2},{4,3},{5,4},{6,5},{7,6},{9,8},{10,9},{11,10},{12... | collective-permute-start | bytes 786440 | tf_op jit(solution)/shard_map/ppermute | solution.py:147
  10.4 0.0 copy-done.5
  10.5 0.1 reshape.46
  10.6 0.0 copy-start
  10.6 1.1 %copy.27.cot = bf16[2,32,4096]{2,1,0:T(8,128)(2,1)} copy(bf16[2,32,4096]{2,0,1:T(2,128)(2,1)S(1)} %reshape.46) | data formatting | bytes 1048576 | tf_op jit(solution)/shard_map/reshape | solution.py:220
  11.7 0.0 copy-done
  11.7 0.1 reshape.45
  11.8 1.1 %copy.26.mid = bf16[2,32,4096]{2,1,0:T(8,128)(2,1)} copy(bf16[2,32,4096]{2,0,1:T(2,128)(2,1)S(1)} %reshape.45) | data formatting | bytes 1048576 | tf_op jit(solution)/shard_map/reshape | solution.py:220
  12.9 0.0 collective-permute-done.2
  12.9 0.0 collective-permute-done.3
  12.9 0.0 collective-permute-done.4
  13.0 0.2 reshape.38
  13.2 0.1 copy.20
  13.3 0.8 %reshape.39.wall = bf16[288,96]{1,0:T(8,128)(2,1)} reshape(bf16[3,3,32,3,32]{4,3,2,1,0:T(4,128)(2,1)S(1)} %copy.20) | data formatting | bytes 110592 | tf_op jit(solution)/shard_map/reshape | solution.py:215
  14.1 0.7 %slice_convert_fusion.bias = f32[32,1]{1,0:T(8,128)} fusion(bf16[32,865]{1,0:T(8,128)(2,1)S(1)} %bitcast.69), kind=kLoop, calls=%fused_computation.12 | loop fusion | flops 32 | bytes 192 | tf_op jit(solution)/shard_map/convert_element_type | solution.py:229
  14.8 0.0 collective-permute-done
  14.8 0.0 collective-permute-done.1
  14.9 0.1 reshape.44
  15.0 1.1 %copy.25.edges = bf16[2,32,4096]{2,1,0:T(8,128)(2,1)} copy(bf16[2,32,4096]{2,0,1:T(2,128)(2,1)S(1)} %reshape.44) | data formatting | bytes 1048576 | tf_op jit(solution)/shard_map/reshape | solution.py:220
  16.1 5.1 %shard_map.84 = (bf16[2,32,4096]{2,1,0:T(8,128)(2,1)}, bf16[2,32,4096]{2,1,0:T(8,128)(2,1)}, bf16[1,32,4096]{2,1,0:T(8,128)(2,1)}, bf16[1,32,4096]{2,1,0:T(8,128)(2,1)}) custom-call(bf16[2,32,4096]{2,1,0:T(8,128)(2,1)} %copy.25.edges, bf16[2,32,4096]{2,1,0:T(8,128)(2,1)} %copy.26.mid, bf16[288,96]{1,0:T(8,128)(2,1)} %reshape.39.wall, ...), custom_call_target="tpu_custom_call" | custom-call | flops 452984832 | bytes 2621440 | tf_op jit(solution)/shard_map/pallas_call | solution.py:108
  21.1 6.6 %collective-permute-start.5 = (bf16[1,32,4096]{2,1,0:T(8,128)(2,1)}, bf16[1,32,4096]{2,1,0:T(8,128)(2,1)S(1)}, u32[]{:S(2)}, u32[]{:S(2)}) collective-permute-start(bf16[1,32,4096]{2,1,0:T(8,128)(2,1)} %get-tuple-element.29), channel_id=1, source_target_pairs={{0,1},{1,2},{2,3},{3,4},{4,5},{5,6},{6,7},{8,9},{9,10},{10,11},{11... | collective-permute-start | bytes 786440 | tf_op jit(solution)/shard_map/ppermute | solution.py:147
  27.8 1.3 %collective-permute-start.6 = (bf16[1,32,4096]{2,1,0:T(8,128)(2,1)}, bf16[1,32,4096]{2,1,0:T(8,128)(2,1)S(1)}, u32[]{:S(2)}, u32[]{:S(2)}) collective-permute-start(bf16[1,32,4096]{2,1,0:T(8,128)(2,1)} %get-tuple-element.30), channel_id=1, source_target_pairs={{1,0},{2,1},{3,2},{4,3},{5,4},{6,5},{7,6},{9,8},{10,9},{11,10},{12... | collective-permute-start | bytes 786440 | tf_op jit(solution)/shard_map/ppermute | solution.py:147
  29.1 0.1 reverse_bitcast_fusion
  29.2 0.3 copy.23
  29.5 0.8 %reshape.42.wall = bf16[288,96]{1,0:T(8,128)(2,1)} reshape(bf16[3,3,32,3,32]{4,3,2,1,0:T(4,128)(2,1)S(1)} %copy.23) | data formatting | bytes 110592 | tf_op jit(solution)/shard_map/reshape | solution.py:216
  30.3 3.8 %shard_map.85 = (f32[16,865]{1,0:T(8,128)}, f32[16,865]{1,0:T(8,128)}) custom-call(s32[1]{0:T(128)} %bitcast.14.upper, bf16[2,32,4096]{2,1,0:T(8,128)(2,1)} %copy.25.edges, bf16[2,32,4096]{2,1,0:T(8,128)(2,1)} %copy.26.mid, bf16[2,32,4096]{2,1,0:T(8,128)(2,1)} %get-tuple-element.42.dpre.mid, f32[9,1,4096]{2,1,0:T(1,128)} %constant.66.clone.mask), custom_call_target="tpu_custom_call" | custom-call | flops 452984832 | bytes 1572864 | tf_op jit(solution)/shard_map/pallas_call | solution.py:133
  34.1 0.0 collective-permute-done.5.lo
  34.1 0.0 collective-permute-done.6.hi
  34.1 0.0 copy-start.2
  34.1 1.6 %collective-permute-start.7 = (f32[16,865]{1,0:T(8,128)}, f32[16,865]{1,0:T(8,128)S(1)}, u32[]{:S(2)}, u32[]{:S(2)}) collective-permute-start(f32[16,865]{1,0:T(8,128)} %get-tuple-element.31), channel_id=1, source_target_pairs={{0,16},{8,24},{16,0},{24,8},{1,17},{9,25},{17,1},{25,9},{2,18},{10... | collective-permute-start | bytes 166088 | tf_op jit(solution)/shard_map/ppermute | solution.py:152
  35.7 0.0 copy-done.1
  35.7 0.0 copy-done.2
  35.7 3.0 %shard_map.86 = bf16[1,32,4096]{2,1,0:T(8,128)(2,1)} custom-call(bf16[1,32,4096]{2,1,0:T(8,128)(2,1)} %copy-done.1, bf16[2,32,4096]{2,1,0:T(8,128)(2,1)} %get-tuple-element.42.dpre.mid, bf16[1,32,4096]{2,1,0:T(8,128)(2,1)} %copy-done.2, bf16[288,96]{1,0:T(8,128)(2,1)} %reshape.42.wall, f32[9,1,4096]{2,1,0:T(1,128)} %constant.66.clone.mask), custom_call_target="tpu_custom_call" | custom-call | flops 226492416 | bytes 1572864 | tf_op jit(solution)/shard_map/pallas_call | solution.py:120
  38.7 0.0 collective-permute-done.7
  38.7 0.0 copy-done.7
  38.8 1.6 %collective-permute-start.8 = (f32[8,865]{1,0:T(8,128)S(1)}, f32[8,865]{1,0:T(8,128)S(1)}, u32[]{:S(2)}, u32[]{:S(2)}) collective-permute-start(f32[8,865]{1,0:T(8,128)S(1)} %constant_dynamic-slice_fusion), channel_id=1, source_target_pairs={{0,8},{8,0},{16,24},{24,16},{1,9},{9,1},{17,25},{25,17},{2,10},{10... | collective-permute-start | bytes 83048 | tf_op jit(solution)/shard_map/ppermute | solution.py:152
  40.3 3.1 %shard_map.87 = bf16[1,32,4096]{2,1,0:T(8,128)(2,1)} custom-call(bf16[1,32,4096]{2,1,0:T(8,128)(2,1)} %copy-done.1, bf16[2,32,4096]{2,1,0:T(8,128)(2,1)} %get-tuple-element.42.dpre.mid, bf16[1,32,4096]{2,1,0:T(8,128)(2,1)} %copy-done.2, bf16[288,96]{1,0:T(8,128)(2,1)} %reshape.42.wall, f32[9,1,4096]{2,1,0:T(1,128)} %constant.66.clone.mask), custom_call_target="tpu_custom_call" | custom-call | flops 226492416 | bytes 1572864 | tf_op jit(solution)/shard_map/pallas_call | solution.py:120
  43.4 0.0 collective-permute-done.8
  43.4 1.4 %collective-permute-start.9 = (f32[8,865]{1,0:T(8,128)S(1)}, f32[8,865]{1,0:T(8,128)S(1)}, u32[]{:S(2)}, u32[]{:S(2)}) collective-permute-start(f32[8,865]{1,0:T(8,128)S(1)} %dynamic-slice_add_fusion), channel_id=1, source_target_pairs={{0,1},{1,0},{2,3},{3,2},{4,5},{5,4},{6,7},{7,6},{8,9},{9,8},{10,11... | collective-permute-start | bytes 83048 | tf_op jit(solution)/shard_map/ppermute | solution.py:152
  44.8 0.0 copy-done.6
  44.8 0.1 copy.28
  44.9 0.8 %collective-permute-done.9 = f32[8,865]{1,0:T(8,128)S(1)} collective-permute-done((f32[8,865]{1,0:T(8,128)S(1)}, f32[8,865]{1,0:T(8,128)S(1)}, u32[]{:S(2)}, u32[]{:S(2)}) %collective-permute-start.9) | collective-permute-done | bytes 27712 | tf_op jit(solution)/shard_map/ppermute | solution.py:152
  45.6 2.0 %collective-permute-start.10 = (f32[8,865]{1,0:T(8,128)S(1)}, f32[8,865]{1,0:T(8,128)S(1)}, u32[]{:S(2)}, u32[]{:S(2)}) collective-permute-start(f32[8,865]{1,0:T(8,128)S(1)} %add.53), channel_id=1, source_target_pairs={{0,2},{1,3},{2,0},{3,1},{4,6},{5,7},{6,4},{7,5},{8,10},{9,11},{10,... | collective-permute-start | bytes 83048 | tf_op jit(solution)/shard_map/ppermute | solution.py:152
  47.6 0.0 copy-done.3
  47.6 0.0 copy-done.4
  47.6 0.1 pad_maximum_fusion
  47.6 0.1 copy.29
  47.7 1.7 %collective-permute-done.10 = f32[8,865]{1,0:T(8,128)S(1)} collective-permute-done((f32[8,865]{1,0:T(8,128)S(1)}, f32[8,865]{1,0:T(8,128)S(1)}, u32[]{:S(2)}, u32[]{:S(2)}) %collective-permute-start.10) | collective-permute-done | bytes 27712 | tf_op jit(solution)/shard_map/ppermute | solution.py:152
  49.5 3.0 %collective-permute-start.11 = (f32[8,865]{1,0:T(8,128)S(1)}, f32[8,865]{1,0:T(8,128)S(1)}, u32[]{:S(2)}, u32[]{:S(2)}) collective-permute-start(f32[8,865]{1,0:T(8,128)S(1)} %add.54), channel_id=1, source_target_pairs={{0,4},{1,5},{2,6},{3,7},{4,0},{5,1},{6,2},{7,3},{8,12},{9,13},{10,... | collective-permute-start | bytes 83048 | tf_op jit(solution)/shard_map/ppermute | solution.py:152
  52.5 1.1 %copy_bitcast_fusion = (bf16[1,32,2,32,128]{4,3,2,1,0:T(8,128)(2,1)}, bf16[1,32,2,32,128]{4,3,2,1,0:T(8,128)(2,1)}) fusion(bf16[2,32,32,128]{3,2,1,0:T(8,128)(2,1)S(1)} %bitcast.64, bf16[2,32,32,128]{3,2,1,0:T(8,128)(2,1)S(1)} %bitcast.65), kind=kLoop, calls=%fused_computation.2 | loop fusion | bytes 2097152 | tf_op jit(solution)/shard_map/broadcast_in_dim | solution.py:242
  53.6 0.7 %collective-permute-done.11 = f32[8,865]{1,0:T(8,128)S(1)} collective-permute-done((f32[8,865]{1,0:T(8,128)S(1)}, f32[8,865]{1,0:T(8,128)S(1)}, u32[]{:S(2)}, u32[]{:S(2)}) %collective-permute-start.11) | collective-permute-done | bytes 27712 | tf_op jit(solution)/shard_map/ppermute | solution.py:152
  54.3 0.7 %slice_reduce_fusion = f32[8]{0:T(128)} fusion(f32[8,865]{1,0:T(8,128)S(1)} %add_multiply_fusion), kind=kLoop, calls=%fused_computation.13 | loop fusion | bytes 64 | tf_op jit(solution)/shard_map/slice | solution.py:242
  55.0 0.0 copy-done.8
  (18 shorter events, 0.1 us)
Async XLA Ops:
  0.6 0.7 %copy-start.10 = (bf16[8]{0:T(256)(128)(2,1)S(1)}, bf16[8]{0:T(256)(128)(2,1)}, u32[]{:S(2)}) copy-start(bf16[8]{0:T(256)(128)(2,1)} %param.8) | copy-start | bytes 52
  1.4 0.7 %copy-start.9 = (bf16[8,864]{1,0:T(8,128)(2,1)S(1)}, bf16[8,864]{1,0:T(8,128)(2,1)}, u32[]{:S(2)}) copy-start(bf16[8,864]{1,0:T(8,128)(2,1)} %param.7) | copy-start | bytes 41476
  2.2 10.7 %collective-permute-start.3 = (bf16[8,865]{1,0:T(8,128)(2,1)S(1)}, bf16[8,865]{1,0:T(8,128)(2,1)S(1)}, u32[]{:S(2)}, u32[]{:S(2)}) collective-permute-start(bf16[8,865]{1,0:T(8,128)(2,1)S(1)} %get-tuple-element.49), channel_id=1, source_target_pairs={{0,16},{8,24},{16,0},{24,8},{1,17},{9,25},{17,1},{25,9},{2,18},{10... | collective-permute-start | bytes 41528 | tf_op jit(solution)/shard_map/ppermute | solution.py:152
  5.1 7.8 %collective-permute-start.2 = (bf16[8,865]{1,0:T(8,128)(2,1)S(1)}, bf16[8,865]{1,0:T(8,128)(2,1)S(1)}, u32[]{:S(2)}, u32[]{:S(2)}) collective-permute-start(bf16[8,865]{1,0:T(8,128)(2,1)S(1)} %get-tuple-element.49), channel_id=1, source_target_pairs={{0,8},{8,0},{16,24},{24,16},{1,9},{9,1},{17,25},{25,17},{2,10},{10... | collective-permute-start | bytes 41528 | tf_op jit(solution)/shard_map/ppermute | solution.py:152
  6.6 6.3 %collective-permute-start.4 = (bf16[8,865]{1,0:T(8,128)(2,1)S(1)}, bf16[8,865]{1,0:T(8,128)(2,1)S(1)}, u32[]{:S(2)}, u32[]{:S(2)}) collective-permute-start(bf16[8,865]{1,0:T(8,128)(2,1)S(1)} %get-tuple-element.49), channel_id=1, source_target_pairs={{0,24},{8,16},{16,8},{24,0},{1,25},{9,17},{17,9},{25,1},{2,26},{10... | collective-permute-start | bytes 41528 | tf_op jit(solution)/shard_map/ppermute | solution.py:152
  6.7 3.8 %copy-start.5 = (bf16[1,32,2,32,128]{4,3,2,1,0:T(8,128)(2,1)S(1)}, bf16[1,32,2,32,128]{4,3,2,1,0:T(8,128)(2,1)}, u32[]{:S(2)}) copy-start(bf16[1,32,2,32,128]{4,3,2,1,0:T(8,128)(2,1)} %param.6) | copy-start | bytes 1572868
  7.8 7.0 %collective-permute-start = (bf16[32,1,32,128]{3,2,1,0:T(8,128)(2,1)S(1)}, bf16[32,1,32,128]{3,2,1,0:T(8,128)(2,1)S(1)}, u32[]{:S(2)}, u32[]{:S(2)}) collective-permute-start(bf16[32,1,32,128]{3,2,1,0:T(8,128)(2,1)S(1)} %get-tuple-element.50), channel_id=1, source_target_pairs={{0,1},{1,2},{2,3},{3,4},{4,5},{5,6},{6,7},{8,9},{9,10},{10,11},{11... | collective-permute-start | bytes 786440 | tf_op jit(solution)/shard_map/ppermute | solution.py:147
  9.1 5.7 %collective-permute-start.1 = (bf16[32,1,32,128]{3,2,1,0:T(8,128)(2,1)S(1)}, bf16[32,1,32,128]{3,2,1,0:T(8,128)(2,1)S(1)}, u32[]{:S(2)}, u32[]{:S(2)}) collective-permute-start(bf16[32,1,32,128]{3,2,1,0:T(8,128)(2,1)S(1)} %get-tuple-element.51), channel_id=1, source_target_pairs={{1,0},{2,1},{3,2},{4,3},{5,4},{6,5},{7,6},{9,8},{10,9},{11,10},{12... | collective-permute-start | bytes 786440 | tf_op jit(solution)/shard_map/ppermute | solution.py:147
  10.6 1.1 %copy-start = (bf16[1,32,2,32,128]{4,3,2,1,0:T(8,128)(2,1)S(1)}, bf16[1,32,2,32,128]{4,3,2,1,0:T(8,128)(2,1)}, u32[]{:S(2)}) copy-start(bf16[1,32,2,32,128]{4,3,2,1,0:T(8,128)(2,1)} %param.5) | copy-start | bytes 1572868
  21.1 12.9 %collective-permute-start.5 = (bf16[1,32,4096]{2,1,0:T(8,128)(2,1)}, bf16[1,32,4096]{2,1,0:T(8,128)(2,1)S(1)}, u32[]{:S(2)}, u32[]{:S(2)}) collective-permute-start(bf16[1,32,4096]{2,1,0:T(8,128)(2,1)} %get-tuple-element.29), channel_id=1, source_target_pairs={{0,1},{1,2},{2,3},{3,4},{4,5},{5,6},{6,7},{8,9},{9,10},{10,11},{11... | collective-permute-start | bytes 786440 | tf_op jit(solution)/shard_map/ppermute | solution.py:147
  27.8 6.3 %collective-permute-start.6 = (bf16[1,32,4096]{2,1,0:T(8,128)(2,1)}, bf16[1,32,4096]{2,1,0:T(8,128)(2,1)S(1)}, u32[]{:S(2)}, u32[]{:S(2)}) collective-permute-start(bf16[1,32,4096]{2,1,0:T(8,128)(2,1)} %get-tuple-element.30), channel_id=1, source_target_pairs={{1,0},{2,1},{3,2},{4,3},{5,4},{6,5},{7,6},{9,8},{10,9},{11,10},{12... | collective-permute-start | bytes 786440 | tf_op jit(solution)/shard_map/ppermute | solution.py:147
  34.1 1.6 %copy-start.1 = (bf16[1,32,4096]{2,1,0:T(8,128)(2,1)}, bf16[1,32,4096]{2,1,0:T(8,128)(2,1)S(1)}, u32[]{:S(2)}) copy-start(bf16[1,32,4096]{2,1,0:T(8,128)(2,1)S(1)} %collective-permute-done.5.lo) | copy-start | bytes 786436
  34.1 1.6 %copy-start.2 = (bf16[1,32,4096]{2,1,0:T(8,128)(2,1)}, bf16[1,32,4096]{2,1,0:T(8,128)(2,1)S(1)}, u32[]{:S(2)}) copy-start(bf16[1,32,4096]{2,1,0:T(8,128)(2,1)S(1)} %collective-permute-done.6.hi) | copy-start | bytes 786436
  34.1 4.6 %collective-permute-start.7 = (f32[16,865]{1,0:T(8,128)}, f32[16,865]{1,0:T(8,128)S(1)}, u32[]{:S(2)}, u32[]{:S(2)}) collective-permute-start(f32[16,865]{1,0:T(8,128)} %get-tuple-element.31), channel_id=1, source_target_pairs={{0,16},{8,24},{16,0},{24,8},{1,17},{9,25},{17,1},{25,9},{2,18},{10... | collective-permute-start | bytes 166088 | tf_op jit(solution)/shard_map/ppermute | solution.py:152
  35.7 3.0 %copy-start.7 = (f32[16,865]{1,0:T(8,128)S(1)}, f32[16,865]{1,0:T(8,128)}, u32[]{:S(2)}) copy-start(f32[16,865]{1,0:T(8,128)} %get-tuple-element.38) | copy-start | bytes 166084
  38.8 4.6 %collective-permute-start.8 = (f32[8,865]{1,0:T(8,128)S(1)}, f32[8,865]{1,0:T(8,128)S(1)}, u32[]{:S(2)}, u32[]{:S(2)}) collective-permute-start(f32[8,865]{1,0:T(8,128)S(1)} %constant_dynamic-slice_fusion), channel_id=1, source_target_pairs={{0,8},{8,0},{16,24},{24,16},{1,9},{9,1},{17,25},{25,17},{2,10},{10... | collective-permute-start | bytes 83048 | tf_op jit(solution)/shard_map/ppermute | solution.py:152
  40.3 4.4 %copy-start.6 = (bf16[2,32,4096]{2,1,0:T(8,128)(2,1)S(1)}, bf16[2,32,4096]{2,1,0:T(8,128)(2,1)}, u32[]{:S(2)}) copy-start(bf16[2,32,4096]{2,1,0:T(8,128)(2,1)} %get-tuple-element.26) | copy-start | bytes 1572868
  43.4 2.2 %collective-permute-start.9 = (f32[8,865]{1,0:T(8,128)S(1)}, f32[8,865]{1,0:T(8,128)S(1)}, u32[]{:S(2)}, u32[]{:S(2)}) collective-permute-start(f32[8,865]{1,0:T(8,128)S(1)} %dynamic-slice_add_fusion), channel_id=1, source_target_pairs={{0,1},{1,0},{2,3},{3,2},{4,5},{5,4},{6,7},{7,6},{8,9},{9,8},{10,11... | collective-permute-start | bytes 83048 | tf_op jit(solution)/shard_map/ppermute | solution.py:152
  44.8 2.8 %copy-start.3 = (bf16[1,32,4096]{2,1,0:T(8,128)(2,1)S(1)}, bf16[1,32,4096]{2,1,0:T(8,128)(2,1)}, u32[]{:S(2)}) copy-start(bf16[1,32,4096]{2,1,0:T(8,128)(2,1)} %shard_map.86) | copy-start | bytes 786436
  44.8 2.8 %copy-start.4 = (bf16[1,32,4096]{2,1,0:T(8,128)(2,1)S(1)}, bf16[1,32,4096]{2,1,0:T(8,128)(2,1)}, u32[]{:S(2)}) copy-start(bf16[1,32,4096]{2,1,0:T(8,128)(2,1)} %shard_map.87) | copy-start | bytes 786436
  45.6 3.9 %collective-permute-start.10 = (f32[8,865]{1,0:T(8,128)S(1)}, f32[8,865]{1,0:T(8,128)S(1)}, u32[]{:S(2)}, u32[]{:S(2)}) collective-permute-start(f32[8,865]{1,0:T(8,128)S(1)} %add.53), channel_id=1, source_target_pairs={{0,2},{1,3},{2,0},{3,1},{4,6},{5,7},{6,4},{7,5},{8,10},{9,11},{10,... | collective-permute-start | bytes 83048 | tf_op jit(solution)/shard_map/ppermute | solution.py:152
  49.5 4.8 %collective-permute-start.11 = (f32[8,865]{1,0:T(8,128)S(1)}, f32[8,865]{1,0:T(8,128)S(1)}, u32[]{:S(2)}, u32[]{:S(2)}) collective-permute-start(f32[8,865]{1,0:T(8,128)S(1)} %add.54), channel_id=1, source_target_pairs={{0,4},{1,5},{2,6},{3,7},{4,0},{5,1},{6,2},{7,3},{8,12},{9,13},{10,... | collective-permute-start | bytes 83048 | tf_op jit(solution)/shard_map/ppermute | solution.py:152
  54.3 0.7 %copy-start.8 = (f32[8,865]{1,0:T(8,128)}, f32[8,865]{1,0:T(8,128)S(1)}, u32[]{:S(2)}) copy-start(f32[8,865]{1,0:T(8,128)S(1)} %add_multiply_fusion) | copy-start | bytes 83044

commit v16 on v14

--- a/solution.py
+++ b/solution.py
@@ -40,11 +40,12 @@
     return total
 
 
-def _forward_kernel(lo, mid, hi, wall, bias, cot, mask, act_out, dpre_out, first_out, last_out, *, planes, depth):
+def _forward_kernel(lo, mid, hi, wall, packed, cot, mask, act_out, dpre_out, first_out, last_out, *, planes, depth):
     chans, lanes = mid.shape[1], mid.shape[2]
+    bias = packed[:, packed.shape[1] - 1 :].astype(jnp.float32)
     for p in range(planes):
         y = jnp.dot(wall[...], _stacked_parts(lo, mid, hi, p, planes), preferred_element_type=jnp.float32)
-        pre = _shifted_sum(y, mask, chans, lanes, depth, 1) + bias[...]
+        pre = _shifted_sum(y, mask, chans, lanes, depth, 1) + bias
         sig = 1.0 / (1.0 + jnp.exp(-pre))
         act_out[p] = (pre * sig).astype(act_out.dtype)
         dpre = (cot[p].astype(jnp.float32) * sig * (1.0 + pre * (1.0 - sig))).astype(dpre_out.dtype)
@@ -96,7 +97,7 @@
     return [pl.BlockSpec(memory_space=pltpu.VMEM)] * n
 
 
-def forward_call(lo, mid, hi, wall, bias, cot, mask, depth):
+def forward_call(lo, mid, hi, wall, packed, cot, mask, depth):
     planes, chans, lanes = cot.shape
     shape = jax.ShapeDtypeStruct(cot.shape, jnp.bfloat16)
     edge = jax.ShapeDtypeStruct((1, chans, lanes), jnp.bfloat16)
@@ -107,7 +108,7 @@
         in_specs=_vmem(7),
         out_specs=tuple(_vmem(4)),
         cost_estimate=pl.CostEstimate(flops=flops, transcendentals=planes * chans * lanes, bytes_accessed=5 * cot.size * 2),
-    )(lo, mid, hi, wall, bias, cot, mask)
+    )(lo, mid, hi, wall, packed, cot, mask)
 
 
 def input_call(lo, mid, hi, wall, mask, depth, first, count):
@@ -205,7 +206,7 @@
     taps_in = weight.shape[1]
     packed = jnp.concatenate([weight, bias[:, None]], axis=1)
     whole = gather_rows(packed, "real")
-    whole_weight, whole_bias = whole[:, :taps_in], whole[:, taps_in]
+    whole_weight = whole[:, :taps_in]
     out_chan = whole_weight.shape[0]
     w5 = whole_weight.reshape(out_chan, 3, 3, 3, chans)
     forward_w = w5.transpose(2, 3, 0, 1, 4).reshape(9 * out_chan, 3 * chans)
@@ -222,7 +223,7 @@
     mid = flat(field)
     lo, hi = flat(below), flat(above)
     act, dpre, first, last = forward_call(
-        lo, mid, hi, forward_w, whole_bias.astype(jnp.float32)[:, None], flat(cotangent[0]), mask, depth
+        lo, mid, hi, forward_w, whole, flat(cotangent[0]), mask, depth
     )
     dlo, dhi = neighbours(first, last, "strike")
     local_grads = weight_call(first_upper().astype(jnp.int32)[None], lo, mid, hi, dpre, mask, depth)

time: 54.6 us -> 54.8 us (level)
  other arithmetic: 0.84 us -> 0.16 us
    convert_element_type x1 -> x0, other arithmetic: 0.68 us -> none  [local(): whole_bias.astype(jnp.float32)[:, None]]
    unnamed x24 -> x26, local copies, waits for them, and re-layouts: 1.57 us -> 1.97 us
  transfers between devices with their start and end apart: 12 -> 12, of which waited for: 3 -> 3; matrix products, arithmetic and copies ran while one was open for 16% -> 15% of each run, Pallas kernels for 18% -> 18%
where the time goes in v16:
time: 54.8 us; the launch traced here: 54.4 us
  starting transfers between devices  23.6 us (43%)
  Pallas kernels  15 us (27%)
  local copies, waits for them, and re-layouts  11.4 us (21%)
  waiting for transfers between devices  3.27 us (6%)
  between operations  0.88 us (2%)
    ppermute x8, starting transfers between devices, swap(): return lax.ppermute(value, axis, [(i, i ^ bit) for i in range(peers)])  14.5 us
    ppermute x4, starting transfers between devices, neighbours(): return (lax.ppermute(last, axis, up), lax.ppermute(first, axis, down))  9.16 us
    pallas_call x2, Pallas kernels, input_call(): pl.pallas_call(functools.partial(_input_kernel, planes=planes, first=firs...  6.11 us
    pallas_call x1, Pallas kernels, forward_call(): pl.pallas_call(functools.partial(_forward_kernel, planes=planes, depth=de...  5.14 us
    pallas_call x1, Pallas kernels, weight_call(): pl.pallas_call(functools.partial(_weight_kernel, planes=planes, depth=dep...  3.73 us
    ppermute x8, waiting for transfers between devices, swap(): return lax.ppermute(value, axis, [(i, i ^ bit) for i in range(peers)])  3.26 us
    reshape x4, local copies, waits for them, and re-layouts, flat(): value.transpose(1, 0, 2, 3).reshape(value.shape[1], value.shape[0], lanes)  2.41 us
    unnamed x26, local copies, waits for them, and re-layouts  1.97 us
  transfers between devices with their start and end apart: 12, of which 3 were waited for; matrix products, arithmetic and copies ran while one was open for 15% of the time, Pallas kernels for 18%

profile of v16, /device:TPU:0, one launch (start us, length us, event | category | flops | bytes accessed | tf_op | source)
XLA Modules:
  0.0 54.4 jit_solution(16287267921817107846)
XLA Ops:
  0.6 0.0 copy-start.11
  0.6 0.6 %copy-done.11 = bf16[8]{0:T(256)(128)(2,1)S(1)} copy-done((bf16[8]{0:T(256)(128)(2,1)S(1)}, bf16[8]{0:T(256)(128)(2,1)}, u32[]{:S(2)}) %copy-start.11) | copy-done | bytes 40
  1.3 0.1 copy.17
  1.4 0.7 %copy-done.10 = bf16[8,864]{1,0:T(8,128)(2,1)S(1)} copy-done((bf16[8,864]{1,0:T(8,128)(2,1)S(1)}, bf16[8,864]{1,0:T(8,128)(2,1)}, u32[]{:S(2)}) %copy-start.10) | copy-done | bytes 13848
  2.1 0.1 bitcast_dynamic-update-slice_fusion.3
  2.2 3.0 %collective-permute-start.3 = (bf16[8,865]{1,0:T(8,128)(2,1)S(1)}, bf16[8,865]{1,0:T(8,128)(2,1)S(1)}, u32[]{:S(2)}, u32[]{:S(2)}) collective-permute-start(bf16[8,865]{1,0:T(8,128)(2,1)S(1)} %get-tuple-element.49), channel_id=1, source_target_pairs={{0,16},{8,24},{16,0},{24,8},{1,17},{9,25},{17,1},{25,9},{2,18},{10... | collective-permute-start | bytes 41528 | tf_op jit(solution)/shard_map/ppermute | solution.py:149
  5.1 1.5 %collective-permute-start.2 = (bf16[8,865]{1,0:T(8,128)(2,1)S(1)}, bf16[8,865]{1,0:T(8,128)(2,1)S(1)}, u32[]{:S(2)}, u32[]{:S(2)}) collective-permute-start(bf16[8,865]{1,0:T(8,128)(2,1)S(1)} %get-tuple-element.49), channel_id=1, source_target_pairs={{0,8},{8,0},{16,24},{24,16},{1,9},{9,1},{17,25},{25,17},{2,10},{10... | collective-permute-start | bytes 41528 | tf_op jit(solution)/shard_map/ppermute | solution.py:149
  6.6 0.0 collective-permute-start.4
  6.7 1.1 %fusion = (bf16[32,1,32,128]{3,2,1,0:T(8,128)(2,1)S(1)}, bf16[32,1,32,128]{3,2,1,0:T(8,128)(2,1)S(1)}) fusion(bf16[32,2,32,128]{3,2,1,0:T(8,128)(2,1)} %bitcast.59), kind=kLoop, calls=%fused_computation.13 | loop fusion | bytes 1048576 | tf_op jit(solution)/shard_map/slice | solution.py:222
  7.8 1.3 %collective-permute-start.1 = (bf16[32,1,32,128]{3,2,1,0:T(8,128)(2,1)S(1)}, bf16[32,1,32,128]{3,2,1,0:T(8,128)(2,1)S(1)}, u32[]{:S(2)}, u32[]{:S(2)}) collective-permute-start(bf16[32,1,32,128]{3,2,1,0:T(8,128)(2,1)S(1)} %get-tuple-element.50), channel_id=1, source_target_pairs={{1,0},{2,1},{3,2},{4,3},{5,4},{6,5},{7,6},{9,8},{10,9},{11,10},{12... | collective-permute-start | bytes 786440 | tf_op jit(solution)/shard_map/ppermute | solution.py:144
  9.1 3.0 %collective-permute-start = (bf16[32,1,32,128]{3,2,1,0:T(8,128)(2,1)S(1)}, bf16[32,1,32,128]{3,2,1,0:T(8,128)(2,1)S(1)}, u32[]{:S(2)}, u32[]{:S(2)}) collective-permute-start(bf16[32,1,32,128]{3,2,1,0:T(8,128)(2,1)S(1)} %get-tuple-element.51), channel_id=1, source_target_pairs={{0,1},{1,2},{2,3},{3,4},{4,5},{5,6},{6,7},{8,9},{9,10},{10,11},{11... | collective-permute-start | bytes 786440 | tf_op jit(solution)/shard_map/ppermute | solution.py:144
  12.2 0.0 copy-done.5
  12.2 0.1 reshape.41
  12.3 0.0 copy-start
  12.3 1.1 %copy.24.cot = bf16[2,32,4096]{2,1,0:T(8,128)(2,1)} copy(bf16[2,32,4096]{2,0,1:T(2,128)(2,1)S(1)} %reshape.41) | data formatting | bytes 1048576 | tf_op jit(solution)/shard_map/reshape | solution.py:217
  13.4 0.0 copy-done
  13.4 0.1 reshape.40
  13.6 1.1 %copy.23.mid = bf16[2,32,4096]{2,1,0:T(8,128)(2,1)} copy(bf16[2,32,4096]{2,0,1:T(2,128)(2,1)S(1)} %reshape.40) | data formatting | bytes 1048576 | tf_op jit(solution)/shard_map/reshape | solution.py:217
  14.6 0.0 collective-permute-done.2
  14.6 0.0 collective-permute-done.3
  14.7 0.0 collective-permute-done.4
  14.7 0.0 copy-start.7
  14.7 0.2 reshape.34
  14.9 0.4 copy-done.7
  15.3 0.1 copy.18
  15.4 0.8 %reshape.35.wall = bf16[288,96]{1,0:T(8,128)(2,1)} reshape(bf16[3,3,32,3,32]{4,3,2,1,0:T(4,128)(2,1)S(1)} %copy.18) | data formatting | bytes 110592 | tf_op jit(solution)/shard_map/reshape | solution.py:212
  16.2 0.0 collective-permute-done.1
  16.2 0.8 %reshape_transpose.7.hi = bf16[1,32,4096]{2,1,0:T(8,128)(2,1)} reshape(bf16[32,1,32,128]{3,2,1,0:T(8,128)(2,1)S(1)} %collective-permute-done.1) | data formatting | bytes 524288 | tf_op jit(solution)/shard_map/reshape;transpose | solution.py:217
  17.1 0.0 collective-permute-done
  17.1 0.8 %reshape_transpose.6.lo = bf16[1,32,4096]{2,1,0:T(8,128)(2,1)} reshape(bf16[32,1,32,128]{3,2,1,0:T(8,128)(2,1)S(1)} %collective-permute-done) | data formatting | bytes 524288 | tf_op jit(solution)/shard_map/reshape;transpose | solution.py:217
  17.9 5.1 %shard_map.84 = (bf16[2,32,4096]{2,1,0:T(8,128)(2,1)}, bf16[2,32,4096]{2,1,0:T(8,128)(2,1)}, bf16[1,32,4096]{2,1,0:T(8,128)(2,1)}, bf16[1,32,4096]{2,1,0:T(8,128)(2,1)}) custom-call(bf16[1,32,4096]{2,1,0:T(8,128)(2,1)} %reshape_transpose.6.lo, bf16[2,32,4096]{2,1,0:T(8,128)(2,1)} %copy.23.mid, bf16[1,32,4096]{2,1,0:T(8,128)(2,1)} %reshape_transpose.7.hi, ...), custom_call_target="tpu_custom_call" | custom-call | flops 452984832 | bytes 2621440 | tf_op jit(solution)/shard_map/pallas_call | solution.py:105
  23.0 3.5 %collective-permute-start.5 = (bf16[1,32,4096]{2,1,0:T(8,128)(2,1)}, bf16[1,32,4096]{2,1,0:T(8,128)(2,1)S(1)}, u32[]{:S(2)}, u32[]{:S(2)}) collective-permute-start(bf16[1,32,4096]{2,1,0:T(8,128)(2,1)} %get-tuple-element.29), channel_id=1, source_target_pairs={{0,1},{1,2},{2,3},{3,4},{4,5},{5,6},{6,7},{8,9},{9,10},{10,11},{11... | collective-permute-start | bytes 786440 | tf_op jit(solution)/shard_map/ppermute | solution.py:144
  26.6 1.3 %collective-permute-start.6 = (bf16[1,32,4096]{2,1,0:T(8,128)(2,1)}, bf16[1,32,4096]{2,1,0:T(8,128)(2,1)S(1)}, u32[]{:S(2)}, u32[]{:S(2)}) collective-permute-start(bf16[1,32,4096]{2,1,0:T(8,128)(2,1)} %get-tuple-element.30), channel_id=1, source_target_pairs={{1,0},{2,1},{3,2},{4,3},{5,4},{6,5},{7,6},{9,8},{10,9},{11,10},{12... | collective-permute-start | bytes 786440 | tf_op jit(solution)/shard_map/ppermute | solution.py:144
  27.9 0.1 reverse_bitcast_fusion
  28.0 0.3 copy.21
  28.3 0.8 %reshape.38.wall = bf16[288,96]{1,0:T(8,128)(2,1)} reshape(bf16[3,3,32,3,32]{4,3,2,1,0:T(4,128)(2,1)S(1)} %copy.21) | data formatting | bytes 110592 | tf_op jit(solution)/shard_map/reshape | solution.py:213
  29.1 3.7 %shard_map.85 = (f32[16,865]{1,0:T(8,128)}, f32[16,865]{1,0:T(8,128)}) custom-call(s32[1]{0:T(128)} %bitcast.13.upper, bf16[1,32,4096]{2,1,0:T(8,128)(2,1)} %reshape_transpose.6.lo, bf16[2,32,4096]{2,1,0:T(8,128)(2,1)} %copy.23.mid, bf16[1,32,4096]{2,1,0:T(8,128)(2,1)} %reshape_transpose.7.hi, bf16[2,32,4096]{2,1,0:T(8,128)(2,1)} %get-tuple-element.42.dpre.mid, ...), custom_call_target="tpu_custom_call" | custom-call | flops 452984832 | bytes 1572864 | tf_op jit(solution)/shard_map/pallas_call | solution.py:130
  32.8 0.0 collective-permute-done.5.lo
  32.8 0.0 collective-permute-done.6.hi
  32.8 0.0 copy-start.2
  32.9 1.6 %collective-permute-start.7 = (f32[16,865]{1,0:T(8,128)}, f32[16,865]{1,0:T(8,128)S(1)}, u32[]{:S(2)}, u32[]{:S(2)}) collective-permute-start(f32[16,865]{1,0:T(8,128)} %get-tuple-element.31), channel_id=1, source_target_pairs={{0,16},{8,24},{16,0},{24,8},{1,17},{9,25},{17,1},{25,9},{2,18},{10... | collective-permute-start | bytes 166088 | tf_op jit(solution)/shard_map/ppermute | solution.py:149
  34.4 0.0 copy-done.1
  34.4 0.0 copy-done.2
  34.5 3.0 %shard_map.86 = bf16[1,32,4096]{2,1,0:T(8,128)(2,1)} custom-call(bf16[1,32,4096]{2,1,0:T(8,128)(2,1)} %copy-done.1, bf16[2,32,4096]{2,1,0:T(8,128)(2,1)} %get-tuple-element.42.dpre.mid, bf16[1,32,4096]{2,1,0:T(8,128)(2,1)} %copy-done.2, bf16[288,96]{1,0:T(8,128)(2,1)} %reshape.38.wall, f32[9,1,4096]{2,1,0:T(1,128)} %constant.66.clone.mask), custom_call_target="tpu_custom_call" | custom-call | flops 226492416 | bytes 1572864 | tf_op jit(solution)/shard_map/pallas_call | solution.py:117
  37.5 0.0 collective-permute-done.7
  37.5 0.0 copy-done.8
  37.5 1.6 %collective-permute-start.8 = (f32[8,865]{1,0:T(8,128)S(1)}, f32[8,865]{1,0:T(8,128)S(1)}, u32[]{:S(2)}, u32[]{:S(2)}) collective-permute-start(f32[8,865]{1,0:T(8,128)S(1)} %constant_dynamic-slice_fusion), channel_id=1, source_target_pairs={{0,8},{8,0},{16,24},{24,16},{1,9},{9,1},{17,25},{25,17},{2,10},{10... | collective-permute-start | bytes 83048 | tf_op jit(solution)/shard_map/ppermute | solution.py:149
  39.1 3.1 %shard_map.87 = bf16[1,32,4096]{2,1,0:T(8,128)(2,1)} custom-call(bf16[1,32,4096]{2,1,0:T(8,128)(2,1)} %copy-done.1, bf16[2,32,4096]{2,1,0:T(8,128)(2,1)} %get-tuple-element.42.dpre.mid, bf16[1,32,4096]{2,1,0:T(8,128)(2,1)} %copy-done.2, bf16[288,96]{1,0:T(8,128)(2,1)} %reshape.38.wall, f32[9,1,4096]{2,1,0:T(1,128)} %constant.66.clone.mask), custom_call_target="tpu_custom_call" | custom-call | flops 226492416 | bytes 1572864 | tf_op jit(solution)/shard_map/pallas_call | solution.py:117
  42.2 0.0 collective-permute-done.8
  42.2 1.9 %collective-permute-start.9 = (f32[8,865]{1,0:T(8,128)S(1)}, f32[8,865]{1,0:T(8,128)S(1)}, u32[]{:S(2)}, u32[]{:S(2)}) collective-permute-start(f32[8,865]{1,0:T(8,128)S(1)} %dynamic-slice_add_fusion), channel_id=1, source_target_pairs={{0,1},{1,0},{2,3},{3,2},{4,5},{5,4},{6,7},{7,6},{8,9},{9,8},{10,11... | collective-permute-start | bytes 83048 | tf_op jit(solution)/shard_map/ppermute | solution.py:149
  44.1 0.0 copy-done.6
  44.1 0.1 copy.25
  44.2 0.8 %collective-permute-done.9 = f32[8,865]{1,0:T(8,128)S(1)} collective-permute-done((f32[8,865]{1,0:T(8,128)S(1)}, f32[8,865]{1,0:T(8,128)S(1)}, u32[]{:S(2)}, u32[]{:S(2)}) %collective-permute-start.9) | collective-permute-done | bytes 27712 | tf_op jit(solution)/shard_map/ppermute | solution.py:149
  45.0 1.9 %collective-permute-start.10 = (f32[8,865]{1,0:T(8,128)S(1)}, f32[8,865]{1,0:T(8,128)S(1)}, u32[]{:S(2)}, u32[]{:S(2)}) collective-permute-start(f32[8,865]{1,0:T(8,128)S(1)} %add.53), channel_id=1, source_target_pairs={{0,2},{1,3},{2,0},{3,1},{4,6},{5,7},{6,4},{7,5},{8,10},{9,11},{10,... | collective-permute-start | bytes 83048 | tf_op jit(solution)/shard_map/ppermute | solution.py:149
  46.9 0.0 copy-done.3
  46.9 0.0 copy-done.4
  46.9 0.1 pad_maximum_fusion
  47.0 0.1 copy.26
  47.1 1.8 %collective-permute-done.10 = f32[8,865]{1,0:T(8,128)S(1)} collective-permute-done((f32[8,865]{1,0:T(8,128)S(1)}, f32[8,865]{1,0:T(8,128)S(1)}, u32[]{:S(2)}, u32[]{:S(2)}) %collective-permute-start.10) | collective-permute-done | bytes 27712 | tf_op jit(solution)/shard_map/ppermute | solution.py:149
  48.8 3.0 %collective-permute-start.11 = (f32[8,865]{1,0:T(8,128)S(1)}, f32[8,865]{1,0:T(8,128)S(1)}, u32[]{:S(2)}, u32[]{:S(2)}) collective-permute-start(f32[8,865]{1,0:T(8,128)S(1)} %add.54), channel_id=1, source_target_pairs={{0,4},{1,5},{2,6},{3,7},{4,0},{5,1},{6,2},{7,3},{8,12},{9,13},{10,... | collective-permute-start | bytes 83048 | tf_op jit(solution)/shard_map/ppermute | solution.py:149
  51.8 1.1 %copy_bitcast_fusion = (bf16[1,32,2,32,128]{4,3,2,1,0:T(8,128)(2,1)}, bf16[1,32,2,32,128]{4,3,2,1,0:T(8,128)(2,1)}) fusion(bf16[2,32,32,128]{3,2,1,0:T(8,128)(2,1)S(1)} %bitcast.62, bf16[2,32,32,128]{3,2,1,0:T(8,128)(2,1)S(1)} %bitcast.63), kind=kLoop, calls=%fused_computation.1 | loop fusion | bytes 2097152 | tf_op jit(solution)/shard_map/broadcast_in_dim | solution.py:239
  52.9 0.7 %collective-permute-done.11 = f32[8,865]{1,0:T(8,128)S(1)} collective-permute-done((f32[8,865]{1,0:T(8,128)S(1)}, f32[8,865]{1,0:T(8,128)S(1)}, u32[]{:S(2)}, u32[]{:S(2)}) %collective-permute-start.11) | collective-permute-done | bytes 27712 | tf_op jit(solution)/shard_map/ppermute | solution.py:149
  53.7 0.7 %slice_reduce_fusion = f32[8]{0:T(128)} fusion(f32[8,865]{1,0:T(8,128)S(1)} %add_multiply_fusion), kind=kLoop, calls=%fused_computation.11 | loop fusion | bytes 64 | tf_op jit(solution)/shard_map/slice | solution.py:239
  54.4 0.0 copy-done.9
  (18 shorter events, 0.1 us)
Async XLA Ops:
  0.6 0.7 %copy-start.11 = (bf16[8]{0:T(256)(128)(2,1)S(1)}, bf16[8]{0:T(256)(128)(2,1)}, u32[]{:S(2)}) copy-start(bf16[8]{0:T(256)(128)(2,1)} %param.8) | copy-start | bytes 52
  1.4 0.7 %copy-start.10 = (bf16[8,864]{1,0:T(8,128)(2,1)S(1)}, bf16[8,864]{1,0:T(8,128)(2,1)}, u32[]{:S(2)}) copy-start(bf16[8,864]{1,0:T(8,128)(2,1)} %param.7) | copy-start | bytes 41476
  2.2 12.5 %collective-permute-start.3 = (bf16[8,865]{1,0:T(8,128)(2,1)S(1)}, bf16[8,865]{1,0:T(8,128)(2,1)S(1)}, u32[]{:S(2)}, u32[]{:S(2)}) collective-permute-start(bf16[8,865]{1,0:T(8,128)(2,1)S(1)} %get-tuple-element.49), channel_id=1, source_target_pairs={{0,16},{8,24},{16,0},{24,8},{1,17},{9,25},{17,1},{25,9},{2,18},{10... | collective-permute-start | bytes 41528 | tf_op jit(solution)/shard_map/ppermute | solution.py:149
  5.1 9.5 %collective-permute-start.2 = (bf16[8,865]{1,0:T(8,128)(2,1)S(1)}, bf16[8,865]{1,0:T(8,128)(2,1)S(1)}, u32[]{:S(2)}, u32[]{:S(2)}) collective-permute-start(bf16[8,865]{1,0:T(8,128)(2,1)S(1)} %get-tuple-element.49), channel_id=1, source_target_pairs={{0,8},{8,0},{16,24},{24,16},{1,9},{9,1},{17,25},{25,17},{2,10},{10... | collective-permute-start | bytes 41528 | tf_op jit(solution)/shard_map/ppermute | solution.py:149
  6.6 8.0 %collective-permute-start.4 = (bf16[8,865]{1,0:T(8,128)(2,1)S(1)}, bf16[8,865]{1,0:T(8,128)(2,1)S(1)}, u32[]{:S(2)}, u32[]{:S(2)}) collective-permute-start(bf16[8,865]{1,0:T(8,128)(2,1)S(1)} %get-tuple-element.49), channel_id=1, source_target_pairs={{0,24},{8,16},{16,8},{24,0},{1,25},{9,17},{17,9},{25,1},{2,26},{10... | collective-permute-start | bytes 41528 | tf_op jit(solution)/shard_map/ppermute | solution.py:149
  6.7 5.5 %copy-start.5 = (bf16[1,32,2,32,128]{4,3,2,1,0:T(8,128)(2,1)S(1)}, bf16[1,32,2,32,128]{4,3,2,1,0:T(8,128)(2,1)}, u32[]{:S(2)}) copy-start(bf16[1,32,2,32,128]{4,3,2,1,0:T(8,128)(2,1)} %param.6) | copy-start | bytes 1572868
  7.8 8.4 %collective-permute-start.1 = (bf16[32,1,32,128]{3,2,1,0:T(8,128)(2,1)S(1)}, bf16[32,1,32,128]{3,2,1,0:T(8,128)(2,1)S(1)}, u32[]{:S(2)}, u32[]{:S(2)}) collective-permute-start(bf16[32,1,32,128]{3,2,1,0:T(8,128)(2,1)S(1)} %get-tuple-element.50), channel_id=1, source_target_pairs={{1,0},{2,1},{3,2},{4,3},{5,4},{6,5},{7,6},{9,8},{10,9},{11,10},{12... | collective-permute-start | bytes 786440 | tf_op jit(solution)/shard_map/ppermute | solution.py:144
  9.1 8.0 %collective-permute-start = (bf16[32,1,32,128]{3,2,1,0:T(8,128)(2,1)S(1)}, bf16[32,1,32,128]{3,2,1,0:T(8,128)(2,1)S(1)}, u32[]{:S(2)}, u32[]{:S(2)}) collective-permute-start(bf16[32,1,32,128]{3,2,1,0:T(8,128)(2,1)S(1)} %get-tuple-element.51), channel_id=1, source_target_pairs={{0,1},{1,2},{2,3},{3,4},{4,5},{5,6},{6,7},{8,9},{9,10},{10,11},{11... | collective-permute-start | bytes 786440 | tf_op jit(solution)/shard_map/ppermute | solution.py:144
  12.3 1.1 %copy-start = (bf16[1,32,2,32,128]{4,3,2,1,0:T(8,128)(2,1)S(1)}, bf16[1,32,2,32,128]{4,3,2,1,0:T(8,128)(2,1)}, u32[]{:S(2)}) copy-start(bf16[1,32,2,32,128]{4,3,2,1,0:T(8,128)(2,1)} %param.5) | copy-start | bytes 1572868
  14.7 0.6 %copy-start.7 = (bf16[4,8,865]{2,1,0:T(8,128)(2,1)}, bf16[4,8,865]{2,1,0:T(8,128)(2,1)S(1)}, u32[]{:S(2)}) copy-start(bf16[4,8,865]{2,1,0:T(8,128)(2,1)S(1)} %bitcast_dynamic-update-slice_fusion) | copy-start | bytes 166084
  23.0 9.8 %collective-permute-start.5 = (bf16[1,32,4096]{2,1,0:T(8,128)(2,1)}, bf16[1,32,4096]{2,1,0:T(8,128)(2,1)S(1)}, u32[]{:S(2)}, u32[]{:S(2)}) collective-permute-start(bf16[1,32,4096]{2,1,0:T(8,128)(2,1)} %get-tuple-element.29), channel_id=1, source_target_pairs={{0,1},{1,2},{2,3},{3,4},{4,5},{5,6},{6,7},{8,9},{9,10},{10,11},{11... | collective-permute-start | bytes 786440 | tf_op jit(solution)/shard_map/ppermute | solution.py:144
  26.6 6.3 %collective-permute-start.6 = (bf16[1,32,4096]{2,1,0:T(8,128)(2,1)}, bf16[1,32,4096]{2,1,0:T(8,128)(2,1)S(1)}, u32[]{:S(2)}, u32[]{:S(2)}) collective-permute-start(bf16[1,32,4096]{2,1,0:T(8,128)(2,1)} %get-tuple-element.30), channel_id=1, source_target_pairs={{1,0},{2,1},{3,2},{4,3},{5,4},{6,5},{7,6},{9,8},{10,9},{11,10},{12... | collective-permute-start | bytes 786440 | tf_op jit(solution)/shard_map/ppermute | solution.py:144
  32.8 1.6 %copy-start.1 = (bf16[1,32,4096]{2,1,0:T(8,128)(2,1)}, bf16[1,32,4096]{2,1,0:T(8,128)(2,1)S(1)}, u32[]{:S(2)}) copy-start(bf16[1,32,4096]{2,1,0:T(8,128)(2,1)S(1)} %collective-permute-done.5.lo) | copy-start | bytes 786436
  32.8 1.6 %copy-start.2 = (bf16[1,32,4096]{2,1,0:T(8,128)(2,1)}, bf16[1,32,4096]{2,1,0:T(8,128)(2,1)S(1)}, u32[]{:S(2)}) copy-start(bf16[1,32,4096]{2,1,0:T(8,128)(2,1)S(1)} %collective-permute-done.6.hi) | copy-start | bytes 786436
  32.9 4.6 %collective-permute-start.7 = (f32[16,865]{1,0:T(8,128)}, f32[16,865]{1,0:T(8,128)S(1)}, u32[]{:S(2)}, u32[]{:S(2)}) collective-permute-start(f32[16,865]{1,0:T(8,128)} %get-tuple-element.31), channel_id=1, source_target_pairs={{0,16},{8,24},{16,0},{24,8},{1,17},{9,25},{17,1},{25,9},{2,18},{10... | collective-permute-start | bytes 166088 | tf_op jit(solution)/shard_map/ppermute | solution.py:149
  34.4 3.0 %copy-start.8 = (f32[16,865]{1,0:T(8,128)S(1)}, f32[16,865]{1,0:T(8,128)}, u32[]{:S(2)}) copy-start(f32[16,865]{1,0:T(8,128)} %get-tuple-element.38) | copy-start | bytes 166084
  37.5 4.6 %collective-permute-start.8 = (f32[8,865]{1,0:T(8,128)S(1)}, f32[8,865]{1,0:T(8,128)S(1)}, u32[]{:S(2)}, u32[]{:S(2)}) collective-permute-start(f32[8,865]{1,0:T(8,128)S(1)} %constant_dynamic-slice_fusion), channel_id=1, source_target_pairs={{0,8},{8,0},{16,24},{24,16},{1,9},{9,1},{17,25},{25,17},{2,10},{10... | collective-permute-start | bytes 83048 | tf_op jit(solution)/shard_map/ppermute | solution.py:149
  39.1 5.0 %copy-start.6 = (bf16[2,32,4096]{2,1,0:T(8,128)(2,1)S(1)}, bf16[2,32,4096]{2,1,0:T(8,128)(2,1)}, u32[]{:S(2)}) copy-start(bf16[2,32,4096]{2,1,0:T(8,128)(2,1)} %get-tuple-element.26) | copy-start | bytes 1572868
  42.2 2.8 %collective-permute-start.9 = (f32[8,865]{1,0:T(8,128)S(1)}, f32[8,865]{1,0:T(8,128)S(1)}, u32[]{:S(2)}, u32[]{:S(2)}) collective-permute-start(f32[8,865]{1,0:T(8,128)S(1)} %dynamic-slice_add_fusion), channel_id=1, source_target_pairs={{0,1},{1,0},{2,3},{3,2},{4,5},{5,4},{6,7},{7,6},{8,9},{9,8},{10,11... | collective-permute-start | bytes 83048 | tf_op jit(solution)/shard_map/ppermute | solution.py:149
  44.1 2.8 %copy-start.3 = (bf16[1,32,4096]{2,1,0:T(8,128)(2,1)S(1)}, bf16[1,32,4096]{2,1,0:T(8,128)(2,1)}, u32[]{:S(2)}) copy-start(bf16[1,32,4096]{2,1,0:T(8,128)(2,1)} %shard_map.86) | copy-start | bytes 786436
  44.1 2.8 %copy-start.4 = (bf16[1,32,4096]{2,1,0:T(8,128)(2,1)S(1)}, bf16[1,32,4096]{2,1,0:T(8,128)(2,1)}, u32[]{:S(2)}) copy-start(bf16[1,32,4096]{2,1,0:T(8,128)(2,1)} %shard_map.87) | copy-start | bytes 786436
  45.0 3.9 %collective-permute-start.10 = (f32[8,865]{1,0:T(8,128)S(1)}, f32[8,865]{1,0:T(8,128)S(1)}, u32[]{:S(2)}, u32[]{:S(2)}) collective-permute-start(f32[8,865]{1,0:T(8,128)S(1)} %add.53), channel_id=1, source_target_pairs={{0,2},{1,3},{2,0},{3,1},{4,6},{5,7},{6,4},{7,5},{8,10},{9,11},{10,... | collective-permute-start | bytes 83048 | tf_op jit(solution)/shard_map/ppermute | solution.py:149
  48.8 4.8 %collective-permute-start.11 = (f32[8,865]{1,0:T(8,128)S(1)}, f32[8,865]{1,0:T(8,128)S(1)}, u32[]{:S(2)}, u32[]{:S(2)}) collective-permute-start(f32[8,865]{1,0:T(8,128)S(1)} %add.54), channel_id=1, source_target_pairs={{0,4},{1,5},{2,6},{3,7},{4,0},{5,1},{6,2},{7,3},{8,12},{9,13},{10,... | collective-permute-start | bytes 83048 | tf_op jit(solution)/shard_map/ppermute | solution.py:149
  53.7 0.7 %copy-start.9 = (f32[8,865]{1,0:T(8,128)}, f32[8,865]{1,0:T(8,128)S(1)}, u32[]{:S(2)}) copy-start(f32[8,865]{1,0:T(8,128)S(1)} %add_multiply_fusion) | copy-start | bytes 83044

commit v17 on v14

--- a/solution.py
+++ b/solution.py
@@ -168,10 +168,10 @@
     while bit >= 1:
         rounds.append(("real", bit))
         bit //= 2
-    bit = 1
-    while bit < lax.axis_size("strike"):
+    bit = lax.axis_size("strike") // 2
+    while bit >= 1:
         rounds.append(("strike", bit))
-        bit *= 2
+        bit //= 2
     results = []
     value = None
     for k, (axis, bit) in enumerate(rounds):

time: 54.6 us -> 54.6 us (level)
  no operation moved by 1% of the time
where the time goes in v17:
time: 54.6 us; the launch traced here: 54.2 us
  starting transfers between devices  23 us (42%)
  Pallas kernels  14.9 us (27%)
  local copies, waits for them, and re-layouts  11 us (20%)
  waiting for transfers between devices  3.65 us (7%)
  between operations  0.88 us (2%)
  other arithmetic  0.84 us (2%)
    ppermute x8, starting transfers between devices, swap(): return lax.ppermute(value, axis, [(i, i ^ bit) for i in range(peers)])  13.8 us
    ppermute x4, starting transfers between devices, neighbours(): return (lax.ppermute(last, axis, up), lax.ppermute(first, axis, down))  9.15 us
    pallas_call x2, Pallas kernels, input_call(): pl.pallas_call(functools.partial(_input_kernel, planes=planes, first=firs...  6.08 us
    pallas_call x1, Pallas kernels, forward_call(): pl.pallas_call(functools.partial(_forward_kernel, planes=planes, depth=de...  5.07 us
    pallas_call x1, Pallas kernels, weight_call(): pl.pallas_call(functools.partial(_weight_kernel, planes=planes, depth=dep...  3.74 us
    ppermute x8, waiting for transfers between devices, swap(): return lax.ppermute(value, axis, [(i, i ^ bit) for i in range(peers)])  3.64 us
    reshape x4, local copies, waits for them, and re-layouts, flat(): value.transpose(1, 0, 2, 3).reshape(value.shape[1], value.shape[0], lanes)  2.41 us
    another operation x2, local copies, waits for them, and re-layouts, flat(): value.transpose(1, 0, 2, 3).reshape(value.shape[1], value.shape[0], lanes)  1.62 us
  transfers between devices with their start and end apart: 12, of which 3 were waited for; matrix products, arithmetic and copies ran while one was open for 16% of the time, Pallas kernels for 18%

profile of v17, /device:TPU:0, one launch (start us, length us, event | category | flops | bytes accessed | tf_op | source)
XLA Modules:
  0.0 54.2 jit_solution(13341045256674755852)
XLA Ops:
  0.6 0.0 copy-start.10
  0.6 0.6 %copy-done.10 = bf16[8]{0:T(256)(128)(2,1)S(1)} copy-done((bf16[8]{0:T(256)(128)(2,1)S(1)}, bf16[8]{0:T(256)(128)(2,1)}, u32[]{:S(2)}) %copy-start.10) | copy-done | bytes 40
  1.3 0.1 copy.17
  1.4 0.0 copy-start.9
  1.4 0.7 %copy-done.9 = bf16[8,864]{1,0:T(8,128)(2,1)S(1)} copy-done((bf16[8,864]{1,0:T(8,128)(2,1)S(1)}, bf16[8,864]{1,0:T(8,128)(2,1)}, u32[]{:S(2)}) %copy-start.9) | copy-done | bytes 13848
  2.1 0.1 bitcast_dynamic-update-slice_fusion.3
  2.2 3.0 %collective-permute-start.3 = (bf16[8,865]{1,0:T(8,128)(2,1)S(1)}, bf16[8,865]{1,0:T(8,128)(2,1)S(1)}, u32[]{:S(2)}, u32[]{:S(2)}) collective-permute-start(bf16[8,865]{1,0:T(8,128)(2,1)S(1)} %get-tuple-element.49), channel_id=1, source_target_pairs={{0,16},{8,24},{16,0},{24,8},{1,17},{9,25},{17,1},{25,9},{2,18},{10... | collective-permute-start | bytes 41528 | tf_op jit(solution)/shard_map/ppermute | solution.py:148
  5.1 1.5 %collective-permute-start.2 = (bf16[8,865]{1,0:T(8,128)(2,1)S(1)}, bf16[8,865]{1,0:T(8,128)(2,1)S(1)}, u32[]{:S(2)}, u32[]{:S(2)}) collective-permute-start(bf16[8,865]{1,0:T(8,128)(2,1)S(1)} %get-tuple-element.49), channel_id=1, source_target_pairs={{0,8},{8,0},{16,24},{24,16},{1,9},{9,1},{17,25},{25,17},{2,10},{10... | collective-permute-start | bytes 41528 | tf_op jit(solution)/shard_map/ppermute | solution.py:148
  6.6 0.0 collective-permute-start.4
  6.7 1.1 %fusion = (bf16[32,1,32,128]{3,2,1,0:T(8,128)(2,1)S(1)}, bf16[32,1,32,128]{3,2,1,0:T(8,128)(2,1)S(1)}) fusion(bf16[32,2,32,128]{3,2,1,0:T(8,128)(2,1)} %bitcast.59), kind=kLoop, calls=%fused_computation.14 | loop fusion | bytes 1048576 | tf_op jit(solution)/shard_map/slice | solution.py:221
  7.8 1.3 %collective-permute-start.1 = (bf16[32,1,32,128]{3,2,1,0:T(8,128)(2,1)S(1)}, bf16[32,1,32,128]{3,2,1,0:T(8,128)(2,1)S(1)}, u32[]{:S(2)}, u32[]{:S(2)}) collective-permute-start(bf16[32,1,32,128]{3,2,1,0:T(8,128)(2,1)S(1)} %get-tuple-element.50), channel_id=1, source_target_pairs={{1,0},{2,1},{3,2},{4,3},{5,4},{6,5},{7,6},{9,8},{10,9},{11,10},{12... | collective-permute-start | bytes 786440 | tf_op jit(solution)/shard_map/ppermute | solution.py:143
  9.1 3.0 %collective-permute-start = (bf16[32,1,32,128]{3,2,1,0:T(8,128)(2,1)S(1)}, bf16[32,1,32,128]{3,2,1,0:T(8,128)(2,1)S(1)}, u32[]{:S(2)}, u32[]{:S(2)}) collective-permute-start(bf16[32,1,32,128]{3,2,1,0:T(8,128)(2,1)S(1)} %get-tuple-element.51), channel_id=1, source_target_pairs={{0,1},{1,2},{2,3},{3,4},{4,5},{5,6},{6,7},{8,9},{9,10},{10,11},{11... | collective-permute-start | bytes 786440 | tf_op jit(solution)/shard_map/ppermute | solution.py:143
  12.2 0.0 copy-done.5
  12.2 0.1 reshape.41
  12.3 0.0 copy-start
  12.3 1.1 %copy.24.cot = bf16[2,32,4096]{2,1,0:T(8,128)(2,1)} copy(bf16[2,32,4096]{2,0,1:T(2,128)(2,1)S(1)} %reshape.41) | data formatting | bytes 1048576 | tf_op jit(solution)/shard_map/reshape | solution.py:216
  13.4 0.0 copy-done
  13.4 0.1 reshape.40
  13.6 1.1 %copy.23.mid = bf16[2,32,4096]{2,1,0:T(8,128)(2,1)} copy(bf16[2,32,4096]{2,0,1:T(2,128)(2,1)S(1)} %reshape.40) | data formatting | bytes 1048576 | tf_op jit(solution)/shard_map/reshape | solution.py:216
  14.6 0.0 collective-permute-done.2
  14.6 0.0 collective-permute-done.3
  14.7 0.0 collective-permute-done.4
  14.7 0.2 reshape.34
  14.9 0.1 copy.18
  15.0 0.8 %reshape.35.wall = bf16[288,96]{1,0:T(8,128)(2,1)} reshape(bf16[3,3,32,3,32]{4,3,2,1,0:T(4,128)(2,1)S(1)} %copy.18) | data formatting | bytes 110592 | tf_op jit(solution)/shard_map/reshape | solution.py:211
  15.8 0.7 %slice_convert_fusion.bias = f32[32,1]{1,0:T(8,128)} fusion(bf16[32,865]{1,0:T(8,128)(2,1)S(1)} %bitcast.67), kind=kLoop, calls=%fused_computation.11 | loop fusion | flops 32 | bytes 192 | tf_op jit(solution)/shard_map/convert_element_type | solution.py:225
  16.5 0.0 collective-permute-done.1
  16.5 0.8 %reshape_transpose.7.hi = bf16[1,32,4096]{2,1,0:T(8,128)(2,1)} reshape(bf16[32,1,32,128]{3,2,1,0:T(8,128)(2,1)S(1)} %collective-permute-done.1) | data formatting | bytes 524288 | tf_op jit(solution)/shard_map/reshape;transpose | solution.py:216
  17.3 0.0 collective-permute-done
  17.3 0.8 %reshape_transpose.6.lo = bf16[1,32,4096]{2,1,0:T(8,128)(2,1)} reshape(bf16[32,1,32,128]{3,2,1,0:T(8,128)(2,1)S(1)} %collective-permute-done) | data formatting | bytes 524288 | tf_op jit(solution)/shard_map/reshape;transpose | solution.py:216
  18.2 5.1 %shard_map.84 = (bf16[2,32,4096]{2,1,0:T(8,128)(2,1)}, bf16[2,32,4096]{2,1,0:T(8,128)(2,1)}, bf16[1,32,4096]{2,1,0:T(8,128)(2,1)}, bf16[1,32,4096]{2,1,0:T(8,128)(2,1)}) custom-call(bf16[1,32,4096]{2,1,0:T(8,128)(2,1)} %reshape_transpose.6.lo, bf16[2,32,4096]{2,1,0:T(8,128)(2,1)} %copy.23.mid, bf16[1,32,4096]{2,1,0:T(8,128)(2,1)} %reshape_transpose.7.hi, ...), custom_call_target="tpu_custom_call" | custom-call | flops 452984832 | bytes 2621440 | tf_op jit(solution)/shard_map/pallas_call | solution.py:104
  23.2 3.5 %collective-permute-start.5 = (bf16[1,32,4096]{2,1,0:T(8,128)(2,1)}, bf16[1,32,4096]{2,1,0:T(8,128)(2,1)S(1)}, u32[]{:S(2)}, u32[]{:S(2)}) collective-permute-start(bf16[1,32,4096]{2,1,0:T(8,128)(2,1)} %get-tuple-element.29), channel_id=1, source_target_pairs={{0,1},{1,2},{2,3},{3,4},{4,5},{5,6},{6,7},{8,9},{9,10},{10,11},{11... | collective-permute-start | bytes 786440 | tf_op jit(solution)/shard_map/ppermute | solution.py:143
  26.7 1.3 %collective-permute-start.6 = (bf16[1,32,4096]{2,1,0:T(8,128)(2,1)}, bf16[1,32,4096]{2,1,0:T(8,128)(2,1)S(1)}, u32[]{:S(2)}, u32[]{:S(2)}) collective-permute-start(bf16[1,32,4096]{2,1,0:T(8,128)(2,1)} %get-tuple-element.30), channel_id=1, source_target_pairs={{1,0},{2,1},{3,2},{4,3},{5,4},{6,5},{7,6},{9,8},{10,9},{11,10},{12... | collective-permute-start | bytes 786440 | tf_op jit(solution)/shard_map/ppermute | solution.py:143
  28.1 0.1 reverse_bitcast_fusion
  28.2 0.3 copy.21
  28.5 0.8 %reshape.38.wall = bf16[288,96]{1,0:T(8,128)(2,1)} reshape(bf16[3,3,32,3,32]{4,3,2,1,0:T(4,128)(2,1)S(1)} %copy.21) | data formatting | bytes 110592 | tf_op jit(solution)/shard_map/reshape | solution.py:212
  29.3 3.7 %shard_map.85 = (f32[16,865]{1,0:T(8,128)}, f32[16,865]{1,0:T(8,128)}) custom-call(s32[1]{0:T(128)} %bitcast.13.upper, bf16[1,32,4096]{2,1,0:T(8,128)(2,1)} %reshape_transpose.6.lo, bf16[2,32,4096]{2,1,0:T(8,128)(2,1)} %copy.23.mid, bf16[1,32,4096]{2,1,0:T(8,128)(2,1)} %reshape_transpose.7.hi, bf16[2,32,4096]{2,1,0:T(8,128)(2,1)} %get-tuple-element.42.dpre.mid, ...), custom_call_target="tpu_custom_call" | custom-call | flops 452984832 | bytes 1572864 | tf_op jit(solution)/shard_map/pallas_call | solution.py:129
  33.0 0.0 collective-permute-done.5.lo
  33.0 0.0 collective-permute-done.6.hi
  33.0 0.0 copy-start.2
  33.0 1.6 %collective-permute-start.7 = (f32[16,865]{1,0:T(8,128)}, f32[16,865]{1,0:T(8,128)S(1)}, u32[]{:S(2)}, u32[]{:S(2)}) collective-permute-start(f32[16,865]{1,0:T(8,128)} %get-tuple-element.31), channel_id=1, source_target_pairs={{0,16},{8,24},{16,0},{24,8},{1,17},{9,25},{17,1},{25,9},{2,18},{10... | collective-permute-start | bytes 166088 | tf_op jit(solution)/shard_map/ppermute | solution.py:148
  34.6 0.0 copy-done.1
  34.6 0.0 copy-done.2
  34.6 3.0 %shard_map.86 = bf16[1,32,4096]{2,1,0:T(8,128)(2,1)} custom-call(bf16[1,32,4096]{2,1,0:T(8,128)(2,1)} %copy-done.1, bf16[2,32,4096]{2,1,0:T(8,128)(2,1)} %get-tuple-element.42.dpre.mid, bf16[1,32,4096]{2,1,0:T(8,128)(2,1)} %copy-done.2, bf16[288,96]{1,0:T(8,128)(2,1)} %reshape.38.wall, f32[9,1,4096]{2,1,0:T(1,128)} %constant.66.clone.mask), custom_call_target="tpu_custom_call" | custom-call | flops 226492416 | bytes 1572864 | tf_op jit(solution)/shard_map/pallas_call | solution.py:116
  37.7 0.0 collective-permute-done.7
  37.7 0.0 copy-done.7
  37.7 1.6 %collective-permute-start.8 = (f32[8,865]{1,0:T(8,128)S(1)}, f32[8,865]{1,0:T(8,128)S(1)}, u32[]{:S(2)}, u32[]{:S(2)}) collective-permute-start(f32[8,865]{1,0:T(8,128)S(1)} %constant_dynamic-slice_fusion), channel_id=1, source_target_pairs={{0,8},{8,0},{16,24},{24,16},{1,9},{9,1},{17,25},{25,17},{2,10},{10... | collective-permute-start | bytes 83048 | tf_op jit(solution)/shard_map/ppermute | solution.py:148
  39.2 3.1 %shard_map.87 = bf16[1,32,4096]{2,1,0:T(8,128)(2,1)} custom-call(bf16[1,32,4096]{2,1,0:T(8,128)(2,1)} %copy-done.1, bf16[2,32,4096]{2,1,0:T(8,128)(2,1)} %get-tuple-element.42.dpre.mid, bf16[1,32,4096]{2,1,0:T(8,128)(2,1)} %copy-done.2, bf16[288,96]{1,0:T(8,128)(2,1)} %reshape.38.wall, f32[9,1,4096]{2,1,0:T(1,128)} %constant.66.clone.mask), custom_call_target="tpu_custom_call" | custom-call | flops 226492416 | bytes 1572864 | tf_op jit(solution)/shard_map/pallas_call | solution.py:116
  42.3 0.0 collective-permute-done.8
  42.3 4.3 %collective-permute-start.9 = (f32[8,865]{1,0:T(8,128)S(1)}, f32[8,865]{1,0:T(8,128)S(1)}, u32[]{:S(2)}, u32[]{:S(2)}) collective-permute-start(f32[8,865]{1,0:T(8,128)S(1)} %dynamic-slice_add_fusion), channel_id=1, source_target_pairs={{0,4},{1,5},{2,6},{3,7},{4,0},{5,1},{6,2},{7,3},{8,12},{9,13},{10,... | collective-permute-start | bytes 83048 | tf_op jit(solution)/shard_map/ppermute | solution.py:148
  46.6 0.0 copy-done.6
  46.6 0.1 copy.25
  46.7 1.7 %collective-permute-done.9 = f32[8,865]{1,0:T(8,128)S(1)} collective-permute-done((f32[8,865]{1,0:T(8,128)S(1)}, f32[8,865]{1,0:T(8,128)S(1)}, u32[]{:S(2)}, u32[]{:S(2)}) %collective-permute-start.9) | collective-permute-done | bytes 27712 | tf_op jit(solution)/shard_map/ppermute | solution.py:148
  48.5 1.9 %collective-permute-start.10 = (f32[8,865]{1,0:T(8,128)S(1)}, f32[8,865]{1,0:T(8,128)S(1)}, u32[]{:S(2)}, u32[]{:S(2)}) collective-permute-start(f32[8,865]{1,0:T(8,128)S(1)} %add.53), channel_id=1, source_target_pairs={{0,2},{1,3},{2,0},{3,1},{4,6},{5,7},{6,4},{7,5},{8,10},{9,11},{10,... | collective-permute-start | bytes 83048 | tf_op jit(solution)/shard_map/ppermute | solution.py:148
  50.4 0.0 copy-done.3
  50.4 0.0 copy-done.4
  50.4 0.1 pad_maximum_fusion
  50.4 0.1 copy.26
  50.5 1.8 %collective-permute-done.10 = f32[8,865]{1,0:T(8,128)S(1)} collective-permute-done((f32[8,865]{1,0:T(8,128)S(1)}, f32[8,865]{1,0:T(8,128)S(1)}, u32[]{:S(2)}, u32[]{:S(2)}) %collective-permute-start.10) | collective-permute-done | bytes 27712 | tf_op jit(solution)/shard_map/ppermute | solution.py:148
  52.3 0.0 collective-permute-start.11
  52.3 1.1 %copy_bitcast_fusion = (bf16[1,32,2,32,128]{4,3,2,1,0:T(8,128)(2,1)}, bf16[1,32,2,32,128]{4,3,2,1,0:T(8,128)(2,1)}) fusion(bf16[2,32,32,128]{3,2,1,0:T(8,128)(2,1)S(1)} %bitcast.62, bf16[2,32,32,128]{3,2,1,0:T(8,128)(2,1)S(1)} %bitcast.63), kind=kLoop, calls=%fused_computation.1 | loop fusion | bytes 2097152 | tf_op jit(solution)/shard_map/broadcast_in_dim | solution.py:238
  53.5 0.1 collective-permute-done.11
  53.6 0.7 %slice_reduce_fusion = f32[8]{0:T(128)} fusion(f32[8,865]{1,0:T(8,128)S(1)} %add_multiply_fusion), kind=kLoop, calls=%fused_computation.12 | loop fusion | bytes 64 | tf_op jit(solution)/shard_map/slice | solution.py:238
  54.2 0.0 copy-done.8
  (17 shorter events, 0.1 us)
Async XLA Ops:
  0.6 0.7 %copy-start.10 = (bf16[8]{0:T(256)(128)(2,1)S(1)}, bf16[8]{0:T(256)(128)(2,1)}, u32[]{:S(2)}) copy-start(bf16[8]{0:T(256)(128)(2,1)} %param.8) | copy-start | bytes 52
  1.4 0.7 %copy-start.9 = (bf16[8,864]{1,0:T(8,128)(2,1)S(1)}, bf16[8,864]{1,0:T(8,128)(2,1)}, u32[]{:S(2)}) copy-start(bf16[8,864]{1,0:T(8,128)(2,1)} %param.7) | copy-start | bytes 41476
  2.2 12.5 %collective-permute-start.3 = (bf16[8,865]{1,0:T(8,128)(2,1)S(1)}, bf16[8,865]{1,0:T(8,128)(2,1)S(1)}, u32[]{:S(2)}, u32[]{:S(2)}) collective-permute-start(bf16[8,865]{1,0:T(8,128)(2,1)S(1)} %get-tuple-element.49), channel_id=1, source_target_pairs={{0,16},{8,24},{16,0},{24,8},{1,17},{9,25},{17,1},{25,9},{2,18},{10... | collective-permute-start | bytes 41528 | tf_op jit(solution)/shard_map/ppermute | solution.py:148
  5.1 9.5 %collective-permute-start.2 = (bf16[8,865]{1,0:T(8,128)(2,1)S(1)}, bf16[8,865]{1,0:T(8,128)(2,1)S(1)}, u32[]{:S(2)}, u32[]{:S(2)}) collective-permute-start(bf16[8,865]{1,0:T(8,128)(2,1)S(1)} %get-tuple-element.49), channel_id=1, source_target_pairs={{0,8},{8,0},{16,24},{24,16},{1,9},{9,1},{17,25},{25,17},{2,10},{10... | collective-permute-start | bytes 41528 | tf_op jit(solution)/shard_map/ppermute | solution.py:148
  6.6 8.0 %collective-permute-start.4 = (bf16[8,865]{1,0:T(8,128)(2,1)S(1)}, bf16[8,865]{1,0:T(8,128)(2,1)S(1)}, u32[]{:S(2)}, u32[]{:S(2)}) collective-permute-start(bf16[8,865]{1,0:T(8,128)(2,1)S(1)} %get-tuple-element.49), channel_id=1, source_target_pairs={{0,24},{8,16},{16,8},{24,0},{1,25},{9,17},{17,9},{25,1},{2,26},{10... | collective-permute-start | bytes 41528 | tf_op jit(solution)/shard_map/ppermute | solution.py:148
  6.7 5.5 %copy-start.5 = (bf16[1,32,2,32,128]{4,3,2,1,0:T(8,128)(2,1)S(1)}, bf16[1,32,2,32,128]{4,3,2,1,0:T(8,128)(2,1)}, u32[]{:S(2)}) copy-start(bf16[1,32,2,32,128]{4,3,2,1,0:T(8,128)(2,1)} %param.6) | copy-start | bytes 1572868
  7.8 8.7 %collective-permute-start.1 = (bf16[32,1,32,128]{3,2,1,0:T(8,128)(2,1)S(1)}, bf16[32,1,32,128]{3,2,1,0:T(8,128)(2,1)S(1)}, u32[]{:S(2)}, u32[]{:S(2)}) collective-permute-start(bf16[32,1,32,128]{3,2,1,0:T(8,128)(2,1)S(1)} %get-tuple-element.50), channel_id=1, source_target_pairs={{1,0},{2,1},{3,2},{4,3},{5,4},{6,5},{7,6},{9,8},{10,9},{11,10},{12... | collective-permute-start | bytes 786440 | tf_op jit(solution)/shard_map/ppermute | solution.py:143
  9.1 8.2 %collective-permute-start = (bf16[32,1,32,128]{3,2,1,0:T(8,128)(2,1)S(1)}, bf16[32,1,32,128]{3,2,1,0:T(8,128)(2,1)S(1)}, u32[]{:S(2)}, u32[]{:S(2)}) collective-permute-start(bf16[32,1,32,128]{3,2,1,0:T(8,128)(2,1)S(1)} %get-tuple-element.51), channel_id=1, source_target_pairs={{0,1},{1,2},{2,3},{3,4},{4,5},{5,6},{6,7},{8,9},{9,10},{10,11},{11... | collective-permute-start | bytes 786440 | tf_op jit(solution)/shard_map/ppermute | solution.py:143
  12.3 1.1 %copy-start = (bf16[1,32,2,32,128]{4,3,2,1,0:T(8,128)(2,1)S(1)}, bf16[1,32,2,32,128]{4,3,2,1,0:T(8,128)(2,1)}, u32[]{:S(2)}) copy-start(bf16[1,32,2,32,128]{4,3,2,1,0:T(8,128)(2,1)} %param.5) | copy-start | bytes 1572868
  23.2 9.8 %collective-permute-start.5 = (bf16[1,32,4096]{2,1,0:T(8,128)(2,1)}, bf16[1,32,4096]{2,1,0:T(8,128)(2,1)S(1)}, u32[]{:S(2)}, u32[]{:S(2)}) collective-permute-start(bf16[1,32,4096]{2,1,0:T(8,128)(2,1)} %get-tuple-element.29), channel_id=1, source_target_pairs={{0,1},{1,2},{2,3},{3,4},{4,5},{5,6},{6,7},{8,9},{9,10},{10,11},{11... | collective-permute-start | bytes 786440 | tf_op jit(solution)/shard_map/ppermute | solution.py:143
  26.7 6.3 %collective-permute-start.6 = (bf16[1,32,4096]{2,1,0:T(8,128)(2,1)}, bf16[1,32,4096]{2,1,0:T(8,128)(2,1)S(1)}, u32[]{:S(2)}, u32[]{:S(2)}) collective-permute-start(bf16[1,32,4096]{2,1,0:T(8,128)(2,1)} %get-tuple-element.30), channel_id=1, source_target_pairs={{1,0},{2,1},{3,2},{4,3},{5,4},{6,5},{7,6},{9,8},{10,9},{11,10},{12... | collective-permute-start | bytes 786440 | tf_op jit(solution)/shard_map/ppermute | solution.py:143
  33.0 1.6 %copy-start.1 = (bf16[1,32,4096]{2,1,0:T(8,128)(2,1)}, bf16[1,32,4096]{2,1,0:T(8,128)(2,1)S(1)}, u32[]{:S(2)}) copy-start(bf16[1,32,4096]{2,1,0:T(8,128)(2,1)S(1)} %collective-permute-done.5.lo) | copy-start | bytes 786436
  33.0 1.6 %copy-start.2 = (bf16[1,32,4096]{2,1,0:T(8,128)(2,1)}, bf16[1,32,4096]{2,1,0:T(8,128)(2,1)S(1)}, u32[]{:S(2)}) copy-start(bf16[1,32,4096]{2,1,0:T(8,128)(2,1)S(1)} %collective-permute-done.6.hi) | copy-start | bytes 786436
  33.0 4.6 %collective-permute-start.7 = (f32[16,865]{1,0:T(8,128)}, f32[16,865]{1,0:T(8,128)S(1)}, u32[]{:S(2)}, u32[]{:S(2)}) collective-permute-start(f32[16,865]{1,0:T(8,128)} %get-tuple-element.31), channel_id=1, source_target_pairs={{0,16},{8,24},{16,0},{24,8},{1,17},{9,25},{17,1},{25,9},{2,18},{10... | collective-permute-start | bytes 166088 | tf_op jit(solution)/shard_map/ppermute | solution.py:148
  34.6 3.0 %copy-start.7 = (f32[16,865]{1,0:T(8,128)S(1)}, f32[16,865]{1,0:T(8,128)}, u32[]{:S(2)}) copy-start(f32[16,865]{1,0:T(8,128)} %get-tuple-element.38) | copy-start | bytes 166084
  37.7 4.6 %collective-permute-start.8 = (f32[8,865]{1,0:T(8,128)S(1)}, f32[8,865]{1,0:T(8,128)S(1)}, u32[]{:S(2)}, u32[]{:S(2)}) collective-permute-start(f32[8,865]{1,0:T(8,128)S(1)} %constant_dynamic-slice_fusion), channel_id=1, source_target_pairs={{0,8},{8,0},{16,24},{24,16},{1,9},{9,1},{17,25},{25,17},{2,10},{10... | collective-permute-start | bytes 83048 | tf_op jit(solution)/shard_map/ppermute | solution.py:148
  39.2 7.4 %copy-start.6 = (bf16[2,32,4096]{2,1,0:T(8,128)(2,1)S(1)}, bf16[2,32,4096]{2,1,0:T(8,128)(2,1)}, u32[]{:S(2)}) copy-start(bf16[2,32,4096]{2,1,0:T(8,128)(2,1)} %get-tuple-element.26) | copy-start | bytes 1572868
  42.3 6.1 %collective-permute-start.9 = (f32[8,865]{1,0:T(8,128)S(1)}, f32[8,865]{1,0:T(8,128)S(1)}, u32[]{:S(2)}, u32[]{:S(2)}) collective-permute-start(f32[8,865]{1,0:T(8,128)S(1)} %dynamic-slice_add_fusion), channel_id=1, source_target_pairs={{0,4},{1,5},{2,6},{3,7},{4,0},{5,1},{6,2},{7,3},{8,12},{9,13},{10,... | collective-permute-start | bytes 83048 | tf_op jit(solution)/shard_map/ppermute | solution.py:148
  46.6 3.8 %copy-start.3 = (bf16[1,32,4096]{2,1,0:T(8,128)(2,1)S(1)}, bf16[1,32,4096]{2,1,0:T(8,128)(2,1)}, u32[]{:S(2)}) copy-start(bf16[1,32,4096]{2,1,0:T(8,128)(2,1)} %shard_map.86) | copy-start | bytes 786436
  46.6 3.8 %copy-start.4 = (bf16[1,32,4096]{2,1,0:T(8,128)(2,1)S(1)}, bf16[1,32,4096]{2,1,0:T(8,128)(2,1)}, u32[]{:S(2)}) copy-start(bf16[1,32,4096]{2,1,0:T(8,128)(2,1)} %shard_map.87) | copy-start | bytes 786436
  48.5 3.9 %collective-permute-start.10 = (f32[8,865]{1,0:T(8,128)S(1)}, f32[8,865]{1,0:T(8,128)S(1)}, u32[]{:S(2)}, u32[]{:S(2)}) collective-permute-start(f32[8,865]{1,0:T(8,128)S(1)} %add.53), channel_id=1, source_target_pairs={{0,2},{1,3},{2,0},{3,1},{4,6},{5,7},{6,4},{7,5},{8,10},{9,11},{10,... | collective-permute-start | bytes 83048 | tf_op jit(solution)/shard_map/ppermute | solution.py:148
  52.3 1.2 %collective-permute-start.11 = (f32[8,865]{1,0:T(8,128)S(1)}, f32[8,865]{1,0:T(8,128)S(1)}, u32[]{:S(2)}, u32[]{:S(2)}) collective-permute-start(f32[8,865]{1,0:T(8,128)S(1)} %add.54), channel_id=1, source_target_pairs={{0,1},{1,0},{2,3},{3,2},{4,5},{5,4},{6,7},{7,6},{8,9},{9,8},{10,11... | collective-permute-start | bytes 83048 | tf_op jit(solution)/shard_map/ppermute | solution.py:148
  53.5 0.7 %copy-start.8 = (f32[8,865]{1,0:T(8,128)}, f32[8,865]{1,0:T(8,128)S(1)}, u32[]{:S(2)}) copy-start(f32[8,865]{1,0:T(8,128)S(1)} %add_multiply_fusion) | copy-start | bytes 83044

commit v18 on v14

--- a/solution.py
+++ b/solution.py
@@ -184,8 +184,9 @@
             send = lax.dynamic_slice_in_dim(value, (1 - upper) * half, half, 0)
         else:
             keep, send = value, value
-        if k < len(work):
-            send, inputs = lax.optimization_barrier((send, work[k][1]))
+        if k < len(work) and work[k] is not None:
+            job_inputs = work[k][1](results) if callable(work[k][1]) else work[k][1]
+            send, inputs = lax.optimization_barrier((send, job_inputs))
             received = swap(send, axis, bit)
             result = work[k][0](*inputs)
             received, result = lax.optimization_barrier((received, result))
@@ -194,7 +195,7 @@
             received = swap(send, axis, bit)
         value = keep + received
     for job, inputs in work[len(rounds) :]:
-        results.append(job(*inputs))
+        results.append(job(*(inputs(results) if callable(inputs) else inputs)))
     return value, results
 
 
@@ -230,8 +231,9 @@
         (functools.partial(input_call, depth=depth, first=p, count=1), (dlo, dpre, dhi, backward_w, mask))
         for p in range(planes)
     ]
+    work += [None] * (3 - len(work)) + [(lambda *parts: unflat(jnp.concatenate(parts, axis=0)), lambda done: tuple(done))]
     owned, pieces = reduce_beside(local_grads, work)
-    grad_input = unflat(jnp.concatenate(pieces, axis=0))
+    grad_input = pieces[-1]
     cells = lax.axis_size("real") * lax.axis_size("strike") * planes * rows * depth
     factor = 1.0 / cells**0.5
     owned = owned * factor

time: 54.6 us -> 54.6 us (level)
  local copies, waits for them, and re-layouts: 11 us -> 11.6 us
  waiting for transfers between devices: 3.26 us -> 2.68 us
    transpose x0 -> x1, local copies, waits for them, and re-layouts: none -> 0.86 us  [unflat(): value.reshape(planes, value.shape[1], rows, depth).transpose(1, 0, 2, 3)]
    ppermute x8, waiting for transfers between devices: 3.25 us -> 2.67 us  [swap(): return lax.ppermute(value, axis, [(i, i ^ bit) for i in range(peers)])]
  transfers between devices with their start and end apart: 12 -> 12, of which waited for: 3 -> 3; matrix products, arithmetic and copies ran while one was open for 16% -> 17% of each run, Pallas kernels for 18% -> 18%
where the time goes in v18:
time: 54.6 us; the launch traced here: 54.2 us
  starting transfers between devices  23.4 us (43%)
  Pallas kernels  14.9 us (27%)
  local copies, waits for them, and re-layouts  11.6 us (21%)
  waiting for transfers between devices  2.68 us (5%)
  between operations  0.88 us (2%)
  other arithmetic  0.84 us (2%)
    ppermute x8, starting transfers between devices, swap(): return lax.ppermute(value, axis, [(i, i ^ bit) for i in range(peers)])  14.2 us
    ppermute x4, starting transfers between devices, neighbours(): return (lax.ppermute(last, axis, up), lax.ppermute(first, axis, down))  9.15 us
    pallas_call x2, Pallas kernels, input_call(): pl.pallas_call(functools.partial(_input_kernel, planes=planes, first=firs...  6.09 us
    pallas_call x1, Pallas kernels, forward_call(): pl.pallas_call(functools.partial(_forward_kernel, planes=planes, depth=de...  5.06 us
    pallas_call x1, Pallas kernels, weight_call(): pl.pallas_call(functools.partial(_weight_kernel, planes=planes, depth=dep...  3.73 us
    ppermute x8, waiting for transfers between devices, swap(): return lax.ppermute(value, axis, [(i, i ^ bit) for i in range(peers)])  2.67 us
    reshape x4, local copies, waits for them, and re-layouts, flat(): value.transpose(1, 0, 2, 3).reshape(value.shape[1], value.shape[0], lanes)  2.41 us
    another operation x2, local copies, waits for them, and re-layouts, flat(): value.transpose(1, 0, 2, 3).reshape(value.shape[1], value.shape[0], lanes)  1.62 us
  transfers between devices with their start and end apart: 12, of which 3 were waited for; matrix products, arithmetic and copies ran while one was open for 17% of the time, Pallas kernels for 18%

profile of v18, /device:TPU:0, one launch (start us, length us, event | category | flops | bytes accessed | tf_op | source)
XLA Modules:
  0.0 54.2 jit_solution(11991526100662204851)
XLA Ops:
  0.6 0.0 copy-start.10
  0.6 0.6 %copy-done.10 = bf16[8]{0:T(256)(128)(2,1)S(1)} copy-done((bf16[8]{0:T(256)(128)(2,1)S(1)}, bf16[8]{0:T(256)(128)(2,1)}, u32[]{:S(2)}) %copy-start.10) | copy-done | bytes 40
  1.3 0.1 copy.17
  1.4 0.7 %copy-done.9 = bf16[8,864]{1,0:T(8,128)(2,1)S(1)} copy-done((bf16[8,864]{1,0:T(8,128)(2,1)S(1)}, bf16[8,864]{1,0:T(8,128)(2,1)}, u32[]{:S(2)}) %copy-start.9) | copy-done | bytes 13848
  2.1 0.1 bitcast_dynamic-update-slice_fusion.3
  2.2 3.0 %collective-permute-start.3 = (bf16[8,865]{1,0:T(8,128)(2,1)S(1)}, bf16[8,865]{1,0:T(8,128)(2,1)S(1)}, u32[]{:S(2)}, u32[]{:S(2)}) collective-permute-start(bf16[8,865]{1,0:T(8,128)(2,1)S(1)} %get-tuple-element.59), channel_id=1, source_target_pairs={{0,16},{8,24},{16,0},{24,8},{1,17},{9,25},{17,1},{25,9},{2,18},{10... | collective-permute-start | bytes 41528 | tf_op jit(solution)/shard_map/ppermute | solution.py:148
  5.1 1.5 %collective-permute-start.2 = (bf16[8,865]{1,0:T(8,128)(2,1)S(1)}, bf16[8,865]{1,0:T(8,128)(2,1)S(1)}, u32[]{:S(2)}, u32[]{:S(2)}) collective-permute-start(bf16[8,865]{1,0:T(8,128)(2,1)S(1)} %get-tuple-element.59), channel_id=1, source_target_pairs={{0,8},{8,0},{16,24},{24,16},{1,9},{9,1},{17,25},{25,17},{2,10},{10... | collective-permute-start | bytes 41528 | tf_op jit(solution)/shard_map/ppermute | solution.py:148
  6.6 0.0 collective-permute-start.4
  6.7 1.1 %fusion = (bf16[32,1,32,128]{3,2,1,0:T(8,128)(2,1)S(1)}, bf16[32,1,32,128]{3,2,1,0:T(8,128)(2,1)S(1)}) fusion(bf16[32,2,32,128]{3,2,1,0:T(8,128)(2,1)} %bitcast.58), kind=kLoop, calls=%fused_computation.14 | loop fusion | bytes 1048576 | tf_op jit(solution)/shard_map/slice | solution.py:222
  7.8 1.3 %collective-permute-start.1 = (bf16[32,1,32,128]{3,2,1,0:T(8,128)(2,1)S(1)}, bf16[32,1,32,128]{3,2,1,0:T(8,128)(2,1)S(1)}, u32[]{:S(2)}, u32[]{:S(2)}) collective-permute-start(bf16[32,1,32,128]{3,2,1,0:T(8,128)(2,1)S(1)} %get-tuple-element.60), channel_id=1, source_target_pairs={{1,0},{2,1},{3,2},{4,3},{5,4},{6,5},{7,6},{9,8},{10,9},{11,10},{12... | collective-permute-start | bytes 786440 | tf_op jit(solution)/shard_map/ppermute | solution.py:143
  9.1 3.0 %collective-permute-start = (bf16[32,1,32,128]{3,2,1,0:T(8,128)(2,1)S(1)}, bf16[32,1,32,128]{3,2,1,0:T(8,128)(2,1)S(1)}, u32[]{:S(2)}, u32[]{:S(2)}) collective-permute-start(bf16[32,1,32,128]{3,2,1,0:T(8,128)(2,1)S(1)} %get-tuple-element.61), channel_id=1, source_target_pairs={{0,1},{1,2},{2,3},{3,4},{4,5},{5,6},{6,7},{8,9},{9,10},{10,11},{11... | collective-permute-start | bytes 786440 | tf_op jit(solution)/shard_map/ppermute | solution.py:143
  12.2 0.0 copy-done.5
  12.2 0.1 reshape.41
  12.3 0.0 copy-start
  12.3 1.1 %copy.24.cot = bf16[2,32,4096]{2,1,0:T(8,128)(2,1)} copy(bf16[2,32,4096]{2,0,1:T(2,128)(2,1)S(1)} %reshape.41) | data formatting | bytes 1048576 | tf_op jit(solution)/shard_map/reshape | solution.py:217
  13.4 0.0 copy-done
  13.4 0.1 reshape.40
  13.6 1.1 %copy.23.mid = bf16[2,32,4096]{2,1,0:T(8,128)(2,1)} copy(bf16[2,32,4096]{2,0,1:T(2,128)(2,1)S(1)} %reshape.40) | data formatting | bytes 1048576 | tf_op jit(solution)/shard_map/reshape | solution.py:217
  14.6 0.0 collective-permute-done.2
  14.6 0.0 collective-permute-done.3
  14.7 0.0 collective-permute-done.4
  14.7 0.2 reshape.34
  14.9 0.1 copy.18
  15.0 0.8 %reshape.35.wall = bf16[288,96]{1,0:T(8,128)(2,1)} reshape(bf16[3,3,32,3,32]{4,3,2,1,0:T(4,128)(2,1)S(1)} %copy.18) | data formatting | bytes 110592 | tf_op jit(solution)/shard_map/reshape | solution.py:212
  15.8 0.7 %slice_convert_fusion.bias = f32[32,1]{1,0:T(8,128)} fusion(bf16[32,865]{1,0:T(8,128)(2,1)S(1)} %bitcast.67), kind=kLoop, calls=%fused_computation.11 | loop fusion | flops 32 | bytes 192 | tf_op jit(solution)/shard_map/convert_element_type | solution.py:226
  16.5 0.0 collective-permute-done.1
  16.5 0.8 %reshape_transpose.7.hi = bf16[1,32,4096]{2,1,0:T(8,128)(2,1)} reshape(bf16[32,1,32,128]{3,2,1,0:T(8,128)(2,1)S(1)} %collective-permute-done.1) | data formatting | bytes 524288 | tf_op jit(solution)/shard_map/reshape;transpose | solution.py:217
  17.3 0.0 collective-permute-done
  17.3 0.8 %reshape_transpose.6.lo = bf16[1,32,4096]{2,1,0:T(8,128)(2,1)} reshape(bf16[32,1,32,128]{3,2,1,0:T(8,128)(2,1)S(1)} %collective-permute-done) | data formatting | bytes 524288 | tf_op jit(solution)/shard_map/reshape;transpose | solution.py:217
  18.1 5.1 %shard_map.84 = (bf16[2,32,4096]{2,1,0:T(8,128)(2,1)}, bf16[2,32,4096]{2,1,0:T(8,128)(2,1)}, bf16[1,32,4096]{2,1,0:T(8,128)(2,1)}, bf16[1,32,4096]{2,1,0:T(8,128)(2,1)}) custom-call(bf16[1,32,4096]{2,1,0:T(8,128)(2,1)} %reshape_transpose.6.lo, bf16[2,32,4096]{2,1,0:T(8,128)(2,1)} %copy.23.mid, bf16[1,32,4096]{2,1,0:T(8,128)(2,1)} %reshape_transpose.7.hi, ...), custom_call_target="tpu_custom_call" | custom-call | flops 452984832 | bytes 2621440 | tf_op jit(solution)/shard_map/pallas_call | solution.py:104
  23.2 3.5 %collective-permute-start.5 = (bf16[1,32,4096]{2,1,0:T(8,128)(2,1)}, bf16[1,32,4096]{2,1,0:T(8,128)(2,1)S(1)}, u32[]{:S(2)}, u32[]{:S(2)}) collective-permute-start(bf16[1,32,4096]{2,1,0:T(8,128)(2,1)} %get-tuple-element.35), channel_id=1, source_target_pairs={{0,1},{1,2},{2,3},{3,4},{4,5},{5,6},{6,7},{8,9},{9,10},{10,11},{11... | collective-permute-start | bytes 786440 | tf_op jit(solution)/shard_map/ppermute | solution.py:143
  26.7 1.3 %collective-permute-start.6 = (bf16[1,32,4096]{2,1,0:T(8,128)(2,1)}, bf16[1,32,4096]{2,1,0:T(8,128)(2,1)S(1)}, u32[]{:S(2)}, u32[]{:S(2)}) collective-permute-start(bf16[1,32,4096]{2,1,0:T(8,128)(2,1)} %get-tuple-element.36), channel_id=1, source_target_pairs={{1,0},{2,1},{3,2},{4,3},{5,4},{6,5},{7,6},{9,8},{10,9},{11,10},{12... | collective-permute-start | bytes 786440 | tf_op jit(solution)/shard_map/ppermute | solution.py:143
  28.1 0.1 reverse_bitcast_fusion
  28.2 0.3 copy.21
  28.5 0.8 %reshape.38.wall = bf16[288,96]{1,0:T(8,128)(2,1)} reshape(bf16[3,3,32,3,32]{4,3,2,1,0:T(4,128)(2,1)S(1)} %copy.21) | data formatting | bytes 110592 | tf_op jit(solution)/shard_map/reshape | solution.py:213
  29.3 3.7 %shard_map.85 = (f32[16,865]{1,0:T(8,128)}, f32[16,865]{1,0:T(8,128)}) custom-call(s32[1]{0:T(128)} %bitcast.13.upper, bf16[1,32,4096]{2,1,0:T(8,128)(2,1)} %reshape_transpose.6.lo, bf16[2,32,4096]{2,1,0:T(8,128)(2,1)} %copy.23.mid, bf16[1,32,4096]{2,1,0:T(8,128)(2,1)} %reshape_transpose.7.hi, bf16[2,32,4096]{2,1,0:T(8,128)(2,1)} %get-tuple-element.46.dpre.mid, ...), custom_call_target="tpu_custom_call" | custom-call | flops 452984832 | bytes 1572864 | tf_op jit(solution)/shard_map/pallas_call | solution.py:129
  33.0 0.0 collective-permute-done.5.lo
  33.0 0.0 collective-permute-done.6.hi
  33.0 0.0 copy-start.2
  33.0 1.6 %collective-permute-start.7 = (f32[16,865]{1,0:T(8,128)}, f32[16,865]{1,0:T(8,128)S(1)}, u32[]{:S(2)}, u32[]{:S(2)}) collective-permute-start(f32[16,865]{1,0:T(8,128)} %get-tuple-element.37), channel_id=1, source_target_pairs={{0,16},{8,24},{16,0},{24,8},{1,17},{9,25},{17,1},{25,9},{2,18},{10... | collective-permute-start | bytes 166088 | tf_op jit(solution)/shard_map/ppermute | solution.py:148
  34.6 0.0 copy-done.1
  34.6 0.0 copy-done.2
  34.6 3.0 %shard_map.86 = bf16[1,32,4096]{2,1,0:T(8,128)(2,1)} custom-call(bf16[1,32,4096]{2,1,0:T(8,128)(2,1)} %copy-done.1, bf16[2,32,4096]{2,1,0:T(8,128)(2,1)} %get-tuple-element.46.dpre.mid, bf16[1,32,4096]{2,1,0:T(8,128)(2,1)} %copy-done.2, bf16[288,96]{1,0:T(8,128)(2,1)} %reshape.38.wall, f32[9,1,4096]{2,1,0:T(1,128)} %constant.66.clone.mask), custom_call_target="tpu_custom_call" | custom-call | flops 226492416 | bytes 1572864 | tf_op jit(solution)/shard_map/pallas_call | solution.py:116
  37.6 0.0 collective-permute-done.7
  37.6 0.0 copy-done.7
  37.7 1.6 %collective-permute-start.8 = (f32[8,865]{1,0:T(8,128)S(1)}, f32[8,865]{1,0:T(8,128)S(1)}, u32[]{:S(2)}, u32[]{:S(2)}) collective-permute-start(f32[8,865]{1,0:T(8,128)S(1)} %constant_dynamic-slice_fusion), channel_id=1, source_target_pairs={{0,8},{8,0},{16,24},{24,16},{1,9},{9,1},{17,25},{25,17},{2,10},{10... | collective-permute-start | bytes 83048 | tf_op jit(solution)/shard_map/ppermute | solution.py:148
  39.2 3.1 %shard_map.87 = bf16[1,32,4096]{2,1,0:T(8,128)(2,1)} custom-call(bf16[1,32,4096]{2,1,0:T(8,128)(2,1)} %copy-done.1, bf16[2,32,4096]{2,1,0:T(8,128)(2,1)} %get-tuple-element.46.dpre.mid, bf16[1,32,4096]{2,1,0:T(8,128)(2,1)} %copy-done.2, bf16[288,96]{1,0:T(8,128)(2,1)} %reshape.38.wall, f32[9,1,4096]{2,1,0:T(1,128)} %constant.66.clone.mask), custom_call_target="tpu_custom_call" | custom-call | flops 226492416 | bytes 1572864 | tf_op jit(solution)/shard_map/pallas_call | solution.py:116
  42.3 0.0 collective-permute-done.8
  42.3 1.7 %collective-permute-start.9 = (f32[8,865]{1,0:T(8,128)S(1)}, f32[8,865]{1,0:T(8,128)S(1)}, u32[]{:S(2)}, u32[]{:S(2)}) collective-permute-start(f32[8,865]{1,0:T(8,128)S(1)} %dynamic-slice_add_fusion), channel_id=1, source_target_pairs={{0,1},{1,0},{2,3},{3,2},{4,5},{5,4},{6,7},{7,6},{8,9},{9,8},{10,11... | collective-permute-start | bytes 83048 | tf_op jit(solution)/shard_map/ppermute | solution.py:148
  44.0 0.0 copy-done.6
  44.0 0.1 copy.25
  44.1 0.8 %collective-permute-done.9 = f32[8,865]{1,0:T(8,128)S(1)} collective-permute-done((f32[8,865]{1,0:T(8,128)S(1)}, f32[8,865]{1,0:T(8,128)S(1)}, u32[]{:S(2)}, u32[]{:S(2)}) %collective-permute-start.9) | collective-permute-done | bytes 27712 | tf_op jit(solution)/shard_map/ppermute | solution.py:148
  44.9 1.9 %collective-permute-start.10 = (f32[8,865]{1,0:T(8,128)S(1)}, f32[8,865]{1,0:T(8,128)S(1)}, u32[]{:S(2)}, u32[]{:S(2)}) collective-permute-start(f32[8,865]{1,0:T(8,128)S(1)} %add.53), channel_id=1, source_target_pairs={{0,2},{1,3},{2,0},{3,1},{4,6},{5,7},{6,4},{7,5},{8,10},{9,11},{10,... | collective-permute-start | bytes 83048 | tf_op jit(solution)/shard_map/ppermute | solution.py:148
  46.8 0.0 copy-done.3
  46.8 0.0 copy-done.4
  46.8 0.1 pad_maximum_fusion
  46.9 0.1 copy.26
  47.0 0.9 %copy_bitcast_fusion = bf16[32,2,32,128]{3,2,1,0:T(8,128)(2,1)} fusion(bf16[2,32,32,128]{3,2,1,0:T(8,128)(2,1)S(1)} %bitcast.62), kind=kLoop, calls=%fused_computation.1 | loop fusion | bytes 1048576 | tf_op jit(solution)/shard_map/transpose | solution.py:220
  47.8 0.9 %collective-permute-done.10 = f32[8,865]{1,0:T(8,128)S(1)} collective-permute-done((f32[8,865]{1,0:T(8,128)S(1)}, f32[8,865]{1,0:T(8,128)S(1)}, u32[]{:S(2)}, u32[]{:S(2)}) %collective-permute-start.10) | collective-permute-done | bytes 27712 | tf_op jit(solution)/shard_map/ppermute | solution.py:148
  48.7 3.0 %collective-permute-start.11 = (f32[8,865]{1,0:T(8,128)S(1)}, f32[8,865]{1,0:T(8,128)S(1)}, u32[]{:S(2)}, u32[]{:S(2)}) collective-permute-start(f32[8,865]{1,0:T(8,128)S(1)} %add.54), channel_id=1, source_target_pairs={{0,4},{1,5},{2,6},{3,7},{4,0},{5,1},{6,2},{7,3},{8,12},{9,13},{10,... | collective-permute-start | bytes 83048 | tf_op jit(solution)/shard_map/ppermute | solution.py:148
  51.7 0.9 %copy_bitcast_fusion.1 = bf16[1,32,2,32,128]{4,3,2,1,0:T(8,128)(2,1)} fusion(bf16[2,32,32,128]{3,2,1,0:T(8,128)(2,1)S(1)} %bitcast.60), kind=kLoop, calls=%fused_computation.2 | loop fusion | bytes 1048576 | tf_op jit(solution)/shard_map/broadcast_in_dim | solution.py:240
  52.5 1.0 %collective-permute-done.11 = f32[8,865]{1,0:T(8,128)S(1)} collective-permute-done((f32[8,865]{1,0:T(8,128)S(1)}, f32[8,865]{1,0:T(8,128)S(1)}, u32[]{:S(2)}, u32[]{:S(2)}) %collective-permute-start.11) | collective-permute-done | bytes 27712 | tf_op jit(solution)/shard_map/ppermute | solution.py:148
  53.5 0.7 %slice_reduce_fusion = f32[8]{0:T(128)} fusion(f32[8,865]{1,0:T(8,128)S(1)} %add_multiply_fusion), kind=kLoop, calls=%fused_computation.12 | loop fusion | bytes 64 | tf_op jit(solution)/shard_map/slice | solution.py:240
  54.2 0.0 copy-done.8
  (18 shorter events, 0.1 us)
Async XLA Ops:
  0.6 0.7 %copy-start.10 = (bf16[8]{0:T(256)(128)(2,1)S(1)}, bf16[8]{0:T(256)(128)(2,1)}, u32[]{:S(2)}) copy-start(bf16[8]{0:T(256)(128)(2,1)} %param.8) | copy-start | bytes 52
  1.4 0.7 %copy-start.9 = (bf16[8,864]{1,0:T(8,128)(2,1)S(1)}, bf16[8,864]{1,0:T(8,128)(2,1)}, u32[]{:S(2)}) copy-start(bf16[8,864]{1,0:T(8,128)(2,1)} %param.7) | copy-start | bytes 41476
  2.2 12.5 %collective-permute-start.3 = (bf16[8,865]{1,0:T(8,128)(2,1)S(1)}, bf16[8,865]{1,0:T(8,128)(2,1)S(1)}, u32[]{:S(2)}, u32[]{:S(2)}) collective-permute-start(bf16[8,865]{1,0:T(8,128)(2,1)S(1)} %get-tuple-element.59), channel_id=1, source_target_pairs={{0,16},{8,24},{16,0},{24,8},{1,17},{9,25},{17,1},{25,9},{2,18},{10... | collective-permute-start | bytes 41528 | tf_op jit(solution)/shard_map/ppermute | solution.py:148
  5.1 9.5 %collective-permute-start.2 = (bf16[8,865]{1,0:T(8,128)(2,1)S(1)}, bf16[8,865]{1,0:T(8,128)(2,1)S(1)}, u32[]{:S(2)}, u32[]{:S(2)}) collective-permute-start(bf16[8,865]{1,0:T(8,128)(2,1)S(1)} %get-tuple-element.59), channel_id=1, source_target_pairs={{0,8},{8,0},{16,24},{24,16},{1,9},{9,1},{17,25},{25,17},{2,10},{10... | collective-permute-start | bytes 41528 | tf_op jit(solution)/shard_map/ppermute | solution.py:148
  6.6 8.0 %collective-permute-start.4 = (bf16[8,865]{1,0:T(8,128)(2,1)S(1)}, bf16[8,865]{1,0:T(8,128)(2,1)S(1)}, u32[]{:S(2)}, u32[]{:S(2)}) collective-permute-start(bf16[8,865]{1,0:T(8,128)(2,1)S(1)} %get-tuple-element.59), channel_id=1, source_target_pairs={{0,24},{8,16},{16,8},{24,0},{1,25},{9,17},{17,9},{25,1},{2,26},{10... | collective-permute-start | bytes 41528 | tf_op jit(solution)/shard_map/ppermute | solution.py:148
  6.7 5.5 %copy-start.5 = (bf16[1,32,2,32,128]{4,3,2,1,0:T(8,128)(2,1)S(1)}, bf16[1,32,2,32,128]{4,3,2,1,0:T(8,128)(2,1)}, u32[]{:S(2)}) copy-start(bf16[1,32,2,32,128]{4,3,2,1,0:T(8,128)(2,1)} %param.6) | copy-start | bytes 1572868
  7.8 8.7 %collective-permute-start.1 = (bf16[32,1,32,128]{3,2,1,0:T(8,128)(2,1)S(1)}, bf16[32,1,32,128]{3,2,1,0:T(8,128)(2,1)S(1)}, u32[]{:S(2)}, u32[]{:S(2)}) collective-permute-start(bf16[32,1,32,128]{3,2,1,0:T(8,128)(2,1)S(1)} %get-tuple-element.60), channel_id=1, source_target_pairs={{1,0},{2,1},{3,2},{4,3},{5,4},{6,5},{7,6},{9,8},{10,9},{11,10},{12... | collective-permute-start | bytes 786440 | tf_op jit(solution)/shard_map/ppermute | solution.py:143
  9.1 8.2 %collective-permute-start = (bf16[32,1,32,128]{3,2,1,0:T(8,128)(2,1)S(1)}, bf16[32,1,32,128]{3,2,1,0:T(8,128)(2,1)S(1)}, u32[]{:S(2)}, u32[]{:S(2)}) collective-permute-start(bf16[32,1,32,128]{3,2,1,0:T(8,128)(2,1)S(1)} %get-tuple-element.61), channel_id=1, source_target_pairs={{0,1},{1,2},{2,3},{3,4},{4,5},{5,6},{6,7},{8,9},{9,10},{10,11},{11... | collective-permute-start | bytes 786440 | tf_op jit(solution)/shard_map/ppermute | solution.py:143
  12.3 1.1 %copy-start = (bf16[1,32,2,32,128]{4,3,2,1,0:T(8,128)(2,1)S(1)}, bf16[1,32,2,32,128]{4,3,2,1,0:T(8,128)(2,1)}, u32[]{:S(2)}) copy-start(bf16[1,32,2,32,128]{4,3,2,1,0:T(8,128)(2,1)} %param.5) | copy-start | bytes 1572868
  23.2 9.8 %collective-permute-start.5 = (bf16[1,32,4096]{2,1,0:T(8,128)(2,1)}, bf16[1,32,4096]{2,1,0:T(8,128)(2,1)S(1)}, u32[]{:S(2)}, u32[]{:S(2)}) collective-permute-start(bf16[1,32,4096]{2,1,0:T(8,128)(2,1)} %get-tuple-element.35), channel_id=1, source_target_pairs={{0,1},{1,2},{2,3},{3,4},{4,5},{5,6},{6,7},{8,9},{9,10},{10,11},{11... | collective-permute-start | bytes 786440 | tf_op jit(solution)/shard_map/ppermute | solution.py:143
  26.7 6.3 %collective-permute-start.6 = (bf16[1,32,4096]{2,1,0:T(8,128)(2,1)}, bf16[1,32,4096]{2,1,0:T(8,128)(2,1)S(1)}, u32[]{:S(2)}, u32[]{:S(2)}) collective-permute-start(bf16[1,32,4096]{2,1,0:T(8,128)(2,1)} %get-tuple-element.36), channel_id=1, source_target_pairs={{1,0},{2,1},{3,2},{4,3},{5,4},{6,5},{7,6},{9,8},{10,9},{11,10},{12... | collective-permute-start | bytes 786440 | tf_op jit(solution)/shard_map/ppermute | solution.py:143
  33.0 1.6 %copy-start.1 = (bf16[1,32,4096]{2,1,0:T(8,128)(2,1)}, bf16[1,32,4096]{2,1,0:T(8,128)(2,1)S(1)}, u32[]{:S(2)}) copy-start(bf16[1,32,4096]{2,1,0:T(8,128)(2,1)S(1)} %collective-permute-done.5.lo) | copy-start | bytes 786436
  33.0 1.6 %copy-start.2 = (bf16[1,32,4096]{2,1,0:T(8,128)(2,1)}, bf16[1,32,4096]{2,1,0:T(8,128)(2,1)S(1)}, u32[]{:S(2)}) copy-start(bf16[1,32,4096]{2,1,0:T(8,128)(2,1)S(1)} %collective-permute-done.6.hi) | copy-start | bytes 786436
  33.0 4.6 %collective-permute-start.7 = (f32[16,865]{1,0:T(8,128)}, f32[16,865]{1,0:T(8,128)S(1)}, u32[]{:S(2)}, u32[]{:S(2)}) collective-permute-start(f32[16,865]{1,0:T(8,128)} %get-tuple-element.37), channel_id=1, source_target_pairs={{0,16},{8,24},{16,0},{24,8},{1,17},{9,25},{17,1},{25,9},{2,18},{10... | collective-permute-start | bytes 166088 | tf_op jit(solution)/shard_map/ppermute | solution.py:148
  34.6 3.0 %copy-start.7 = (f32[16,865]{1,0:T(8,128)S(1)}, f32[16,865]{1,0:T(8,128)}, u32[]{:S(2)}) copy-start(f32[16,865]{1,0:T(8,128)} %get-tuple-element.33) | copy-start | bytes 166084
  37.7 4.6 %collective-permute-start.8 = (f32[8,865]{1,0:T(8,128)S(1)}, f32[8,865]{1,0:T(8,128)S(1)}, u32[]{:S(2)}, u32[]{:S(2)}) collective-permute-start(f32[8,865]{1,0:T(8,128)S(1)} %constant_dynamic-slice_fusion), channel_id=1, source_target_pairs={{0,8},{8,0},{16,24},{24,16},{1,9},{9,1},{17,25},{25,17},{2,10},{10... | collective-permute-start | bytes 83048 | tf_op jit(solution)/shard_map/ppermute | solution.py:148
  39.2 4.8 %copy-start.6 = (bf16[2,32,4096]{2,1,0:T(8,128)(2,1)S(1)}, bf16[2,32,4096]{2,1,0:T(8,128)(2,1)}, u32[]{:S(2)}) copy-start(bf16[2,32,4096]{2,1,0:T(8,128)(2,1)} %get-tuple-element.31) | copy-start | bytes 1572868
  42.3 2.5 %collective-permute-start.9 = (f32[8,865]{1,0:T(8,128)S(1)}, f32[8,865]{1,0:T(8,128)S(1)}, u32[]{:S(2)}, u32[]{:S(2)}) collective-permute-start(f32[8,865]{1,0:T(8,128)S(1)} %dynamic-slice_add_fusion), channel_id=1, source_target_pairs={{0,1},{1,0},{2,3},{3,2},{4,5},{5,4},{6,7},{7,6},{8,9},{9,8},{10,11... | collective-permute-start | bytes 83048 | tf_op jit(solution)/shard_map/ppermute | solution.py:148
  44.0 2.8 %copy-start.3 = (bf16[1,32,4096]{2,1,0:T(8,128)(2,1)S(1)}, bf16[1,32,4096]{2,1,0:T(8,128)(2,1)}, u32[]{:S(2)}) copy-start(bf16[1,32,4096]{2,1,0:T(8,128)(2,1)} %shard_map.86) | copy-start | bytes 786436
  44.0 2.8 %copy-start.4 = (bf16[1,32,4096]{2,1,0:T(8,128)(2,1)S(1)}, bf16[1,32,4096]{2,1,0:T(8,128)(2,1)}, u32[]{:S(2)}) copy-start(bf16[1,32,4096]{2,1,0:T(8,128)(2,1)} %shard_map.87) | copy-start | bytes 786436
  44.9 3.9 %collective-permute-start.10 = (f32[8,865]{1,0:T(8,128)S(1)}, f32[8,865]{1,0:T(8,128)S(1)}, u32[]{:S(2)}, u32[]{:S(2)}) collective-permute-start(f32[8,865]{1,0:T(8,128)S(1)} %add.53), channel_id=1, source_target_pairs={{0,2},{1,3},{2,0},{3,1},{4,6},{5,7},{6,4},{7,5},{8,10},{9,11},{10,... | collective-permute-start | bytes 83048 | tf_op jit(solution)/shard_map/ppermute | solution.py:148
  48.7 4.8 %collective-permute-start.11 = (f32[8,865]{1,0:T(8,128)S(1)}, f32[8,865]{1,0:T(8,128)S(1)}, u32[]{:S(2)}, u32[]{:S(2)}) collective-permute-start(f32[8,865]{1,0:T(8,128)S(1)} %add.54), channel_id=1, source_target_pairs={{0,4},{1,5},{2,6},{3,7},{4,0},{5,1},{6,2},{7,3},{8,12},{9,13},{10,... | collective-permute-start | bytes 83048 | tf_op jit(solution)/shard_map/ppermute | solution.py:148
  53.5 0.7 %copy-start.8 = (f32[8,865]{1,0:T(8,128)}, f32[8,865]{1,0:T(8,128)S(1)}, u32[]{:S(2)}) copy-start(f32[8,865]{1,0:T(8,128)S(1)} %add_multiply_fusion) | copy-start | bytes 83044

commit v19 on v14

--- a/solution.py
+++ b/solution.py
@@ -45,7 +45,7 @@
     for p in range(planes):
         y = jnp.dot(wall[...], _stacked_parts(lo, mid, hi, p, planes), preferred_element_type=jnp.float32)
         pre = _shifted_sum(y, mask, chans, lanes, depth, 1) + bias[...]
-        sig = 1.0 / (1.0 + jnp.exp(-pre))
+        sig = 0.5 + 0.5 * jnp.tanh(0.5 * pre)
         act_out[p] = (pre * sig).astype(act_out.dtype)
         dpre = (cot[p].astype(jnp.float32) * sig * (1.0 + pre * (1.0 - sig))).astype(dpre_out.dtype)
         dpre_out[p] = dpre

time: 54.6 us -> 54.6 us (level)
  no operation moved by 1% of the time
where the time goes in v19:
time: 54.6 us; the launch traced here: 54.2 us
  starting transfers between devices  23.4 us (43%)
  Pallas kernels  14.8 us (27%)
  local copies, waits for them, and re-layouts  11 us (20%)
  waiting for transfers between devices  3.26 us (6%)
  between operations  0.88 us (2%)
  other arithmetic  0.84 us (2%)
    ppermute x8, starting transfers between devices, swap(): return lax.ppermute(value, axis, [(i, i ^ bit) for i in range(peers)])  14.2 us
    ppermute x4, starting transfers between devices, neighbours(): return (lax.ppermute(last, axis, up), lax.ppermute(first, axis, down))  9.15 us
    pallas_call x2, Pallas kernels, input_call(): pl.pallas_call(functools.partial(_input_kernel, planes=planes, first=firs...  6.09 us
    pallas_call x1, Pallas kernels, forward_call(): pl.pallas_call(functools.partial(_forward_kernel, planes=planes, depth=de...  5.02 us
    pallas_call x1, Pallas kernels, weight_call(): pl.pallas_call(functools.partial(_weight_kernel, planes=planes, depth=dep...  3.74 us
    ppermute x8, waiting for transfers between devices, swap(): return lax.ppermute(value, axis, [(i, i ^ bit) for i in range(peers)])  3.25 us
    reshape x4, local copies, waits for them, and re-layouts, flat(): value.transpose(1, 0, 2, 3).reshape(value.shape[1], value.shape[0], lanes)  2.41 us
    another operation x2, local copies, waits for them, and re-layouts, flat(): value.transpose(1, 0, 2, 3).reshape(value.shape[1], value.shape[0], lanes)  1.62 us
  transfers between devices with their start and end apart: 12, of which 3 were waited for; matrix products, arithmetic and copies ran while one was open for 16% of the time, Pallas kernels for 18%

profile of v19, /device:TPU:0, one launch (start us, length us, event | category | flops | bytes accessed | tf_op | source)
XLA Modules:
  0.0 54.2 jit_solution(18432348405627295059)
XLA Ops:
  0.6 0.0 copy-start.10
  0.6 0.6 %copy-done.10 = bf16[8]{0:T(256)(128)(2,1)S(1)} copy-done((bf16[8]{0:T(256)(128)(2,1)S(1)}, bf16[8]{0:T(256)(128)(2,1)}, u32[]{:S(2)}) %copy-start.10) | copy-done | bytes 40
  1.3 0.1 copy.17
  1.4 0.0 copy-start.9
  1.4 0.7 %copy-done.9 = bf16[8,864]{1,0:T(8,128)(2,1)S(1)} copy-done((bf16[8,864]{1,0:T(8,128)(2,1)S(1)}, bf16[8,864]{1,0:T(8,128)(2,1)}, u32[]{:S(2)}) %copy-start.9) | copy-done | bytes 13848
  2.1 0.1 bitcast_dynamic-update-slice_fusion.3
  2.2 3.0 %collective-permute-start.3 = (bf16[8,865]{1,0:T(8,128)(2,1)S(1)}, bf16[8,865]{1,0:T(8,128)(2,1)S(1)}, u32[]{:S(2)}, u32[]{:S(2)}) collective-permute-start(bf16[8,865]{1,0:T(8,128)(2,1)S(1)} %get-tuple-element.49), channel_id=1, source_target_pairs={{0,16},{8,24},{16,0},{24,8},{1,17},{9,25},{17,1},{25,9},{2,18},{10... | collective-permute-start | bytes 41528 | tf_op jit(solution)/shard_map/ppermute | solution.py:148
  5.1 1.5 %collective-permute-start.2 = (bf16[8,865]{1,0:T(8,128)(2,1)S(1)}, bf16[8,865]{1,0:T(8,128)(2,1)S(1)}, u32[]{:S(2)}, u32[]{:S(2)}) collective-permute-start(bf16[8,865]{1,0:T(8,128)(2,1)S(1)} %get-tuple-element.49), channel_id=1, source_target_pairs={{0,8},{8,0},{16,24},{24,16},{1,9},{9,1},{17,25},{25,17},{2,10},{10... | collective-permute-start | bytes 41528 | tf_op jit(solution)/shard_map/ppermute | solution.py:148
  6.6 0.0 collective-permute-start.4
  6.7 1.1 %fusion = (bf16[32,1,32,128]{3,2,1,0:T(8,128)(2,1)S(1)}, bf16[32,1,32,128]{3,2,1,0:T(8,128)(2,1)S(1)}) fusion(bf16[32,2,32,128]{3,2,1,0:T(8,128)(2,1)} %bitcast.59), kind=kLoop, calls=%fused_computation.14 | loop fusion | bytes 1048576 | tf_op jit(solution)/shard_map/slice | solution.py:221
  7.8 1.3 %collective-permute-start.1 = (bf16[32,1,32,128]{3,2,1,0:T(8,128)(2,1)S(1)}, bf16[32,1,32,128]{3,2,1,0:T(8,128)(2,1)S(1)}, u32[]{:S(2)}, u32[]{:S(2)}) collective-permute-start(bf16[32,1,32,128]{3,2,1,0:T(8,128)(2,1)S(1)} %get-tuple-element.50), channel_id=1, source_target_pairs={{1,0},{2,1},{3,2},{4,3},{5,4},{6,5},{7,6},{9,8},{10,9},{11,10},{12... | collective-permute-start | bytes 786440 | tf_op jit(solution)/shard_map/ppermute | solution.py:143
  9.1 3.0 %collective-permute-start = (bf16[32,1,32,128]{3,2,1,0:T(8,128)(2,1)S(1)}, bf16[32,1,32,128]{3,2,1,0:T(8,128)(2,1)S(1)}, u32[]{:S(2)}, u32[]{:S(2)}) collective-permute-start(bf16[32,1,32,128]{3,2,1,0:T(8,128)(2,1)S(1)} %get-tuple-element.51), channel_id=1, source_target_pairs={{0,1},{1,2},{2,3},{3,4},{4,5},{5,6},{6,7},{8,9},{9,10},{10,11},{11... | collective-permute-start | bytes 786440 | tf_op jit(solution)/shard_map/ppermute | solution.py:143
  12.2 0.0 copy-done.5
  12.2 0.1 reshape.41
  12.3 0.0 copy-start
  12.3 1.1 %copy.24.cot = bf16[2,32,4096]{2,1,0:T(8,128)(2,1)} copy(bf16[2,32,4096]{2,0,1:T(2,128)(2,1)S(1)} %reshape.41) | data formatting | bytes 1048576 | tf_op jit(solution)/shard_map/reshape | solution.py:216
  13.4 0.0 copy-done
  13.4 0.1 reshape.40
  13.6 1.1 %copy.23.mid = bf16[2,32,4096]{2,1,0:T(8,128)(2,1)} copy(bf16[2,32,4096]{2,0,1:T(2,128)(2,1)S(1)} %reshape.40) | data formatting | bytes 1048576 | tf_op jit(solution)/shard_map/reshape | solution.py:216
  14.6 0.0 collective-permute-done.2
  14.6 0.0 collective-permute-done.3
  14.7 0.0 collective-permute-done.4
  14.7 0.2 reshape.34
  14.9 0.1 copy.18
  15.0 0.8 %reshape.35.wall = bf16[288,96]{1,0:T(8,128)(2,1)} reshape(bf16[3,3,32,3,32]{4,3,2,1,0:T(4,128)(2,1)S(1)} %copy.18) | data formatting | bytes 110592 | tf_op jit(solution)/shard_map/reshape | solution.py:211
  15.8 0.7 %slice_convert_fusion.bias = f32[32,1]{1,0:T(8,128)} fusion(bf16[32,865]{1,0:T(8,128)(2,1)S(1)} %bitcast.67), kind=kLoop, calls=%fused_computation.11 | loop fusion | flops 32 | bytes 192 | tf_op jit(solution)/shard_map/convert_element_type | solution.py:225
  16.5 0.0 collective-permute-done.1
  16.5 0.8 %reshape_transpose.7.hi = bf16[1,32,4096]{2,1,0:T(8,128)(2,1)} reshape(bf16[32,1,32,128]{3,2,1,0:T(8,128)(2,1)S(1)} %collective-permute-done.1) | data formatting | bytes 524288 | tf_op jit(solution)/shard_map/reshape;transpose | solution.py:216
  17.3 0.0 collective-permute-done
  17.3 0.8 %reshape_transpose.6.lo = bf16[1,32,4096]{2,1,0:T(8,128)(2,1)} reshape(bf16[32,1,32,128]{3,2,1,0:T(8,128)(2,1)S(1)} %collective-permute-done) | data formatting | bytes 524288 | tf_op jit(solution)/shard_map/reshape;transpose | solution.py:216
  18.2 5.0 %shard_map.84 = (bf16[2,32,4096]{2,1,0:T(8,128)(2,1)}, bf16[2,32,4096]{2,1,0:T(8,128)(2,1)}, bf16[1,32,4096]{2,1,0:T(8,128)(2,1)}, bf16[1,32,4096]{2,1,0:T(8,128)(2,1)}) custom-call(bf16[1,32,4096]{2,1,0:T(8,128)(2,1)} %reshape_transpose.6.lo, bf16[2,32,4096]{2,1,0:T(8,128)(2,1)} %copy.23.mid, bf16[1,32,4096]{2,1,0:T(8,128)(2,1)} %reshape_transpose.7.hi, ...), custom_call_target="tpu_custom_call" | custom-call | flops 452984832 | bytes 2621440 | tf_op jit(solution)/shard_map/pallas_call | solution.py:104
  23.2 3.5 %collective-permute-start.5 = (bf16[1,32,4096]{2,1,0:T(8,128)(2,1)}, bf16[1,32,4096]{2,1,0:T(8,128)(2,1)S(1)}, u32[]{:S(2)}, u32[]{:S(2)}) collective-permute-start(bf16[1,32,4096]{2,1,0:T(8,128)(2,1)} %get-tuple-element.29), channel_id=1, source_target_pairs={{0,1},{1,2},{2,3},{3,4},{4,5},{5,6},{6,7},{8,9},{9,10},{10,11},{11... | collective-permute-start | bytes 786440 | tf_op jit(solution)/shard_map/ppermute | solution.py:143
  26.7 1.3 %collective-permute-start.6 = (bf16[1,32,4096]{2,1,0:T(8,128)(2,1)}, bf16[1,32,4096]{2,1,0:T(8,128)(2,1)S(1)}, u32[]{:S(2)}, u32[]{:S(2)}) collective-permute-start(bf16[1,32,4096]{2,1,0:T(8,128)(2,1)} %get-tuple-element.30), channel_id=1, source_target_pairs={{1,0},{2,1},{3,2},{4,3},{5,4},{6,5},{7,6},{9,8},{10,9},{11,10},{12... | collective-permute-start | bytes 786440 | tf_op jit(solution)/shard_map/ppermute | solution.py:143
  28.0 0.1 reverse_bitcast_fusion
  28.1 0.3 copy.21
  28.4 0.8 %reshape.38.wall = bf16[288,96]{1,0:T(8,128)(2,1)} reshape(bf16[3,3,32,3,32]{4,3,2,1,0:T(4,128)(2,1)S(1)} %copy.21) | data formatting | bytes 110592 | tf_op jit(solution)/shard_map/reshape | solution.py:212
  29.2 3.7 %shard_map.85 = (f32[16,865]{1,0:T(8,128)}, f32[16,865]{1,0:T(8,128)}) custom-call(s32[1]{0:T(128)} %bitcast.13.upper, bf16[1,32,4096]{2,1,0:T(8,128)(2,1)} %reshape_transpose.6.lo, bf16[2,32,4096]{2,1,0:T(8,128)(2,1)} %copy.23.mid, bf16[1,32,4096]{2,1,0:T(8,128)(2,1)} %reshape_transpose.7.hi, bf16[2,32,4096]{2,1,0:T(8,128)(2,1)} %get-tuple-element.42.dpre.mid, ...), custom_call_target="tpu_custom_call" | custom-call | flops 452984832 | bytes 1572864 | tf_op jit(solution)/shard_map/pallas_call | solution.py:129
  33.0 0.0 collective-permute-done.5.lo
  33.0 0.0 collective-permute-done.6.hi
  33.0 0.0 copy-start.2
  33.0 1.6 %collective-permute-start.7 = (f32[16,865]{1,0:T(8,128)}, f32[16,865]{1,0:T(8,128)S(1)}, u32[]{:S(2)}, u32[]{:S(2)}) collective-permute-start(f32[16,865]{1,0:T(8,128)} %get-tuple-element.31), channel_id=1, source_target_pairs={{0,16},{8,24},{16,0},{24,8},{1,17},{9,25},{17,1},{25,9},{2,18},{10... | collective-permute-start | bytes 166088 | tf_op jit(solution)/shard_map/ppermute | solution.py:148
  34.6 0.0 copy-done.1
  34.6 0.0 copy-done.2
  34.6 3.0 %shard_map.86 = bf16[1,32,4096]{2,1,0:T(8,128)(2,1)} custom-call(bf16[1,32,4096]{2,1,0:T(8,128)(2,1)} %copy-done.1, bf16[2,32,4096]{2,1,0:T(8,128)(2,1)} %get-tuple-element.42.dpre.mid, bf16[1,32,4096]{2,1,0:T(8,128)(2,1)} %copy-done.2, bf16[288,96]{1,0:T(8,128)(2,1)} %reshape.38.wall, f32[9,1,4096]{2,1,0:T(1,128)} %constant.66.clone.mask), custom_call_target="tpu_custom_call" | custom-call | flops 226492416 | bytes 1572864 | tf_op jit(solution)/shard_map/pallas_call | solution.py:116
  37.6 0.0 collective-permute-done.7
  37.6 0.0 copy-done.7
  37.6 1.6 %collective-permute-start.8 = (f32[8,865]{1,0:T(8,128)S(1)}, f32[8,865]{1,0:T(8,128)S(1)}, u32[]{:S(2)}, u32[]{:S(2)}) collective-permute-start(f32[8,865]{1,0:T(8,128)S(1)} %constant_dynamic-slice_fusion), channel_id=1, source_target_pairs={{0,8},{8,0},{16,24},{24,16},{1,9},{9,1},{17,25},{25,17},{2,10},{10... | collective-permute-start | bytes 83048 | tf_op jit(solution)/shard_map/ppermute | solution.py:148
  39.2 3.1 %shard_map.87 = bf16[1,32,4096]{2,1,0:T(8,128)(2,1)} custom-call(bf16[1,32,4096]{2,1,0:T(8,128)(2,1)} %copy-done.1, bf16[2,32,4096]{2,1,0:T(8,128)(2,1)} %get-tuple-element.42.dpre.mid, bf16[1,32,4096]{2,1,0:T(8,128)(2,1)} %copy-done.2, bf16[288,96]{1,0:T(8,128)(2,1)} %reshape.38.wall, f32[9,1,4096]{2,1,0:T(1,128)} %constant.66.clone.mask), custom_call_target="tpu_custom_call" | custom-call | flops 226492416 | bytes 1572864 | tf_op jit(solution)/shard_map/pallas_call | solution.py:116
  42.3 0.0 collective-permute-done.8
  42.3 1.6 %collective-permute-start.9 = (f32[8,865]{1,0:T(8,128)S(1)}, f32[8,865]{1,0:T(8,128)S(1)}, u32[]{:S(2)}, u32[]{:S(2)}) collective-permute-start(f32[8,865]{1,0:T(8,128)S(1)} %dynamic-slice_add_fusion), channel_id=1, source_target_pairs={{0,1},{1,0},{2,3},{3,2},{4,5},{5,4},{6,7},{7,6},{8,9},{9,8},{10,11... | collective-permute-start | bytes 83048 | tf_op jit(solution)/shard_map/ppermute | solution.py:148
  43.9 0.0 copy-done.6
  43.9 0.1 copy.25
  44.0 0.8 %collective-permute-done.9 = f32[8,865]{1,0:T(8,128)S(1)} collective-permute-done((f32[8,865]{1,0:T(8,128)S(1)}, f32[8,865]{1,0:T(8,128)S(1)}, u32[]{:S(2)}, u32[]{:S(2)}) %collective-permute-start.9) | collective-permute-done | bytes 27712 | tf_op jit(solution)/shard_map/ppermute | solution.py:148
  44.8 2.0 %collective-permute-start.10 = (f32[8,865]{1,0:T(8,128)S(1)}, f32[8,865]{1,0:T(8,128)S(1)}, u32[]{:S(2)}, u32[]{:S(2)}) collective-permute-start(f32[8,865]{1,0:T(8,128)S(1)} %add.53), channel_id=1, source_target_pairs={{0,2},{1,3},{2,0},{3,1},{4,6},{5,7},{6,4},{7,5},{8,10},{9,11},{10,... | collective-permute-start | bytes 83048 | tf_op jit(solution)/shard_map/ppermute | solution.py:148
  46.8 0.0 copy-done.3
  46.8 0.0 copy-done.4
  46.8 0.1 pad_maximum_fusion
  46.8 0.1 copy.26
  46.9 1.8 %collective-permute-done.10 = f32[8,865]{1,0:T(8,128)S(1)} collective-permute-done((f32[8,865]{1,0:T(8,128)S(1)}, f32[8,865]{1,0:T(8,128)S(1)}, u32[]{:S(2)}, u32[]{:S(2)}) %collective-permute-start.10) | collective-permute-done | bytes 27712 | tf_op jit(solution)/shard_map/ppermute | solution.py:148
  48.7 3.0 %collective-permute-start.11 = (f32[8,865]{1,0:T(8,128)S(1)}, f32[8,865]{1,0:T(8,128)S(1)}, u32[]{:S(2)}, u32[]{:S(2)}) collective-permute-start(f32[8,865]{1,0:T(8,128)S(1)} %add.54), channel_id=1, source_target_pairs={{0,4},{1,5},{2,6},{3,7},{4,0},{5,1},{6,2},{7,3},{8,12},{9,13},{10,... | collective-permute-start | bytes 83048 | tf_op jit(solution)/shard_map/ppermute | solution.py:148
  51.6 1.1 %copy_bitcast_fusion = (bf16[1,32,2,32,128]{4,3,2,1,0:T(8,128)(2,1)}, bf16[1,32,2,32,128]{4,3,2,1,0:T(8,128)(2,1)}) fusion(bf16[2,32,32,128]{3,2,1,0:T(8,128)(2,1)S(1)} %bitcast.62, bf16[2,32,32,128]{3,2,1,0:T(8,128)(2,1)S(1)} %bitcast.63), kind=kLoop, calls=%fused_computation.1 | loop fusion | bytes 2097152 | tf_op jit(solution)/shard_map/broadcast_in_dim | solution.py:238
  52.8 0.7 %collective-permute-done.11 = f32[8,865]{1,0:T(8,128)S(1)} collective-permute-done((f32[8,865]{1,0:T(8,128)S(1)}, f32[8,865]{1,0:T(8,128)S(1)}, u32[]{:S(2)}, u32[]{:S(2)}) %collective-permute-start.11) | collective-permute-done | bytes 27712 | tf_op jit(solution)/shard_map/ppermute | solution.py:148
  53.5 0.7 %slice_reduce_fusion = f32[8]{0:T(128)} fusion(f32[8,865]{1,0:T(8,128)S(1)} %add_multiply_fusion), kind=kLoop, calls=%fused_computation.12 | loop fusion | bytes 64 | tf_op jit(solution)/shard_map/slice | solution.py:238
  54.2 0.0 copy-done.8
  (17 shorter events, 0.1 us)
Async XLA Ops:
  0.6 0.7 %copy-start.10 = (bf16[8]{0:T(256)(128)(2,1)S(1)}, bf16[8]{0:T(256)(128)(2,1)}, u32[]{:S(2)}) copy-start(bf16[8]{0:T(256)(128)(2,1)} %param.8) | copy-start | bytes 52
  1.4 0.7 %copy-start.9 = (bf16[8,864]{1,0:T(8,128)(2,1)S(1)}, bf16[8,864]{1,0:T(8,128)(2,1)}, u32[]{:S(2)}) copy-start(bf16[8,864]{1,0:T(8,128)(2,1)} %param.7) | copy-start | bytes 41476
  2.2 12.5 %collective-permute-start.3 = (bf16[8,865]{1,0:T(8,128)(2,1)S(1)}, bf16[8,865]{1,0:T(8,128)(2,1)S(1)}, u32[]{:S(2)}, u32[]{:S(2)}) collective-permute-start(bf16[8,865]{1,0:T(8,128)(2,1)S(1)} %get-tuple-element.49), channel_id=1, source_target_pairs={{0,16},{8,24},{16,0},{24,8},{1,17},{9,25},{17,1},{25,9},{2,18},{10... | collective-permute-start | bytes 41528 | tf_op jit(solution)/shard_map/ppermute | solution.py:148
  5.1 9.5 %collective-permute-start.2 = (bf16[8,865]{1,0:T(8,128)(2,1)S(1)}, bf16[8,865]{1,0:T(8,128)(2,1)S(1)}, u32[]{:S(2)}, u32[]{:S(2)}) collective-permute-start(bf16[8,865]{1,0:T(8,128)(2,1)S(1)} %get-tuple-element.49), channel_id=1, source_target_pairs={{0,8},{8,0},{16,24},{24,16},{1,9},{9,1},{17,25},{25,17},{2,10},{10... | collective-permute-start | bytes 41528 | tf_op jit(solution)/shard_map/ppermute | solution.py:148
  6.6 8.0 %collective-permute-start.4 = (bf16[8,865]{1,0:T(8,128)(2,1)S(1)}, bf16[8,865]{1,0:T(8,128)(2,1)S(1)}, u32[]{:S(2)}, u32[]{:S(2)}) collective-permute-start(bf16[8,865]{1,0:T(8,128)(2,1)S(1)} %get-tuple-element.49), channel_id=1, source_target_pairs={{0,24},{8,16},{16,8},{24,0},{1,25},{9,17},{17,9},{25,1},{2,26},{10... | collective-permute-start | bytes 41528 | tf_op jit(solution)/shard_map/ppermute | solution.py:148
  6.7 5.5 %copy-start.5 = (bf16[1,32,2,32,128]{4,3,2,1,0:T(8,128)(2,1)S(1)}, bf16[1,32,2,32,128]{4,3,2,1,0:T(8,128)(2,1)}, u32[]{:S(2)}) copy-start(bf16[1,32,2,32,128]{4,3,2,1,0:T(8,128)(2,1)} %param.6) | copy-start | bytes 1572868
  7.8 8.7 %collective-permute-start.1 = (bf16[32,1,32,128]{3,2,1,0:T(8,128)(2,1)S(1)}, bf16[32,1,32,128]{3,2,1,0:T(8,128)(2,1)S(1)}, u32[]{:S(2)}, u32[]{:S(2)}) collective-permute-start(bf16[32,1,32,128]{3,2,1,0:T(8,128)(2,1)S(1)} %get-tuple-element.50), channel_id=1, source_target_pairs={{1,0},{2,1},{3,2},{4,3},{5,4},{6,5},{7,6},{9,8},{10,9},{11,10},{12... | collective-permute-start | bytes 786440 | tf_op jit(solution)/shard_map/ppermute | solution.py:143
  9.1 8.2 %collective-permute-start = (bf16[32,1,32,128]{3,2,1,0:T(8,128)(2,1)S(1)}, bf16[32,1,32,128]{3,2,1,0:T(8,128)(2,1)S(1)}, u32[]{:S(2)}, u32[]{:S(2)}) collective-permute-start(bf16[32,1,32,128]{3,2,1,0:T(8,128)(2,1)S(1)} %get-tuple-element.51), channel_id=1, source_target_pairs={{0,1},{1,2},{2,3},{3,4},{4,5},{5,6},{6,7},{8,9},{9,10},{10,11},{11... | collective-permute-start | bytes 786440 | tf_op jit(solution)/shard_map/ppermute | solution.py:143
  12.3 1.1 %copy-start = (bf16[1,32,2,32,128]{4,3,2,1,0:T(8,128)(2,1)S(1)}, bf16[1,32,2,32,128]{4,3,2,1,0:T(8,128)(2,1)}, u32[]{:S(2)}) copy-start(bf16[1,32,2,32,128]{4,3,2,1,0:T(8,128)(2,1)} %param.5) | copy-start | bytes 1572868
  23.2 9.8 %collective-permute-start.5 = (bf16[1,32,4096]{2,1,0:T(8,128)(2,1)}, bf16[1,32,4096]{2,1,0:T(8,128)(2,1)S(1)}, u32[]{:S(2)}, u32[]{:S(2)}) collective-permute-start(bf16[1,32,4096]{2,1,0:T(8,128)(2,1)} %get-tuple-element.29), channel_id=1, source_target_pairs={{0,1},{1,2},{2,3},{3,4},{4,5},{5,6},{6,7},{8,9},{9,10},{10,11},{11... | collective-permute-start | bytes 786440 | tf_op jit(solution)/shard_map/ppermute | solution.py:143
  26.7 6.3 %collective-permute-start.6 = (bf16[1,32,4096]{2,1,0:T(8,128)(2,1)}, bf16[1,32,4096]{2,1,0:T(8,128)(2,1)S(1)}, u32[]{:S(2)}, u32[]{:S(2)}) collective-permute-start(bf16[1,32,4096]{2,1,0:T(8,128)(2,1)} %get-tuple-element.30), channel_id=1, source_target_pairs={{1,0},{2,1},{3,2},{4,3},{5,4},{6,5},{7,6},{9,8},{10,9},{11,10},{12... | collective-permute-start | bytes 786440 | tf_op jit(solution)/shard_map/ppermute | solution.py:143
  33.0 1.6 %copy-start.1 = (bf16[1,32,4096]{2,1,0:T(8,128)(2,1)}, bf16[1,32,4096]{2,1,0:T(8,128)(2,1)S(1)}, u32[]{:S(2)}) copy-start(bf16[1,32,4096]{2,1,0:T(8,128)(2,1)S(1)} %collective-permute-done.5.lo) | copy-start | bytes 786436
  33.0 1.6 %copy-start.2 = (bf16[1,32,4096]{2,1,0:T(8,128)(2,1)}, bf16[1,32,4096]{2,1,0:T(8,128)(2,1)S(1)}, u32[]{:S(2)}) copy-start(bf16[1,32,4096]{2,1,0:T(8,128)(2,1)S(1)} %collective-permute-done.6.hi) | copy-start | bytes 786436
  33.0 4.6 %collective-permute-start.7 = (f32[16,865]{1,0:T(8,128)}, f32[16,865]{1,0:T(8,128)S(1)}, u32[]{:S(2)}, u32[]{:S(2)}) collective-permute-start(f32[16,865]{1,0:T(8,128)} %get-tuple-element.31), channel_id=1, source_target_pairs={{0,16},{8,24},{16,0},{24,8},{1,17},{9,25},{17,1},{25,9},{2,18},{10... | collective-permute-start | bytes 166088 | tf_op jit(solution)/shard_map/ppermute | solution.py:148
  34.6 3.0 %copy-start.7 = (f32[16,865]{1,0:T(8,128)S(1)}, f32[16,865]{1,0:T(8,128)}, u32[]{:S(2)}) copy-start(f32[16,865]{1,0:T(8,128)} %get-tuple-element.38) | copy-start | bytes 166084
  37.6 4.6 %collective-permute-start.8 = (f32[8,865]{1,0:T(8,128)S(1)}, f32[8,865]{1,0:T(8,128)S(1)}, u32[]{:S(2)}, u32[]{:S(2)}) collective-permute-start(f32[8,865]{1,0:T(8,128)S(1)} %constant_dynamic-slice_fusion), channel_id=1, source_target_pairs={{0,8},{8,0},{16,24},{24,16},{1,9},{9,1},{17,25},{25,17},{2,10},{10... | collective-permute-start | bytes 83048 | tf_op jit(solution)/shard_map/ppermute | solution.py:148
  39.2 4.7 %copy-start.6 = (bf16[2,32,4096]{2,1,0:T(8,128)(2,1)S(1)}, bf16[2,32,4096]{2,1,0:T(8,128)(2,1)}, u32[]{:S(2)}) copy-start(bf16[2,32,4096]{2,1,0:T(8,128)(2,1)} %get-tuple-element.26) | copy-start | bytes 1572868
  42.3 2.5 %collective-permute-start.9 = (f32[8,865]{1,0:T(8,128)S(1)}, f32[8,865]{1,0:T(8,128)S(1)}, u32[]{:S(2)}, u32[]{:S(2)}) collective-permute-start(f32[8,865]{1,0:T(8,128)S(1)} %dynamic-slice_add_fusion), channel_id=1, source_target_pairs={{0,1},{1,0},{2,3},{3,2},{4,5},{5,4},{6,7},{7,6},{8,9},{9,8},{10,11... | collective-permute-start | bytes 83048 | tf_op jit(solution)/shard_map/ppermute | solution.py:148
  43.9 2.8 %copy-start.3 = (bf16[1,32,4096]{2,1,0:T(8,128)(2,1)S(1)}, bf16[1,32,4096]{2,1,0:T(8,128)(2,1)}, u32[]{:S(2)}) copy-start(bf16[1,32,4096]{2,1,0:T(8,128)(2,1)} %shard_map.86) | copy-start | bytes 786436
  43.9 2.8 %copy-start.4 = (bf16[1,32,4096]{2,1,0:T(8,128)(2,1)S(1)}, bf16[1,32,4096]{2,1,0:T(8,128)(2,1)}, u32[]{:S(2)}) copy-start(bf16[1,32,4096]{2,1,0:T(8,128)(2,1)} %shard_map.87) | copy-start | bytes 786436
  44.8 3.9 %collective-permute-start.10 = (f32[8,865]{1,0:T(8,128)S(1)}, f32[8,865]{1,0:T(8,128)S(1)}, u32[]{:S(2)}, u32[]{:S(2)}) collective-permute-start(f32[8,865]{1,0:T(8,128)S(1)} %add.53), channel_id=1, source_target_pairs={{0,2},{1,3},{2,0},{3,1},{4,6},{5,7},{6,4},{7,5},{8,10},{9,11},{10,... | collective-permute-start | bytes 83048 | tf_op jit(solution)/shard_map/ppermute | solution.py:148
  48.7 4.8 %collective-permute-start.11 = (f32[8,865]{1,0:T(8,128)S(1)}, f32[8,865]{1,0:T(8,128)S(1)}, u32[]{:S(2)}, u32[]{:S(2)}) collective-permute-start(f32[8,865]{1,0:T(8,128)S(1)} %add.54), channel_id=1, source_target_pairs={{0,4},{1,5},{2,6},{3,7},{4,0},{5,1},{6,2},{7,3},{8,12},{9,13},{10,... | collective-permute-start | bytes 83048 | tf_op jit(solution)/shard_map/ppermute | solution.py:148
  53.5 0.7 %copy-start.8 = (f32[8,865]{1,0:T(8,128)}, f32[8,865]{1,0:T(8,128)S(1)}, u32[]{:S(2)}) copy-start(f32[8,865]{1,0:T(8,128)S(1)} %add_multiply_fusion) | copy-start | bytes 83044

commit v20 on v14

--- a/solution.py
+++ b/solution.py
@@ -204,6 +204,8 @@
     lanes = rows * depth
     taps_in = weight.shape[1]
     packed = jnp.concatenate([weight, bias[:, None]], axis=1)
+    below, above = neighbours(field[:, :1], field[:, planes - 1 :], "strike")
+    packed, below = lax.optimization_barrier((packed, below))
     whole = gather_rows(packed, "real")
     whole_weight, whole_bias = whole[:, :taps_in], whole[:, taps_in]
     out_chan = whole_weight.shape[0]
@@ -218,7 +220,6 @@
     def unflat(value):
         return value.reshape(planes, value.shape[1], rows, depth).transpose(1, 0, 2, 3)
 
-    below, above = neighbours(field[:, :1], field[:, planes - 1 :], "strike")
     mid = flat(field)
     lo, hi = flat(below), flat(above)
     act, dpre, first, last = forward_call(

time: 54.6 us -> 55.1 us (level)
  waiting for transfers between devices: 3.26 us -> 5.73 us
  local copies, waits for them, and re-layouts: 11 us -> 9.65 us
  starting transfers between devices: 23.4 us -> 22.8 us
    ppermute x8, waiting for transfers between devices: 3.25 us -> 5.4 us  [swap(): return lax.ppermute(value, axis, [(i, i ^ bit) for i in range(peers)])]
    ppermute x4, starting transfers between devices: 9.15 us -> 7.63 us  [neighbours(): return (lax.ppermute(last, axis, up), lax.ppermute(first, axis, down))]
    unnamed x24, local copies, waits for them, and re-layouts: 1.57 us -> 0.22 us
    ppermute x8, starting transfers between devices: 14.2 us -> 15.2 us  [swap(): return lax.ppermute(value, axis, [(i, i ^ bit) for i in range(peers)])]
  transfers between devices with their start and end apart: 12 -> 12, of which waited for: 3 -> 6; matrix products, arithmetic and copies ran while one was open for 16% -> 12% of each run, Pallas kernels for 18% -> 18%
where the time goes in v20:
time: 55.1 us; the launch traced here: 54.8 us
  starting transfers between devices  22.8 us (41%)
  Pallas kernels  14.9 us (27%)
  local copies, waits for them, and re-layouts  9.65 us (18%)
  waiting for transfers between devices  5.73 us (10%)
  between operations  0.86 us (2%)
  other arithmetic  0.84 us (2%)
    ppermute x8, starting transfers between devices, swap(): return lax.ppermute(value, axis, [(i, i ^ bit) for i in range(peers)])  15.2 us
    ppermute x4, starting transfers between devices, neighbours(): return (lax.ppermute(last, axis, up), lax.ppermute(first, axis, down))  7.63 us
    pallas_call x2, Pallas kernels, input_call(): pl.pallas_call(functools.partial(_input_kernel, planes=planes, first=firs...  6.09 us
    ppermute x8, waiting for transfers between devices, swap(): return lax.ppermute(value, axis, [(i, i ^ bit) for i in range(peers)])  5.4 us
    pallas_call x1, Pallas kernels, forward_call(): pl.pallas_call(functools.partial(_forward_kernel, planes=planes, depth=de...  5.06 us
    pallas_call x1, Pallas kernels, weight_call(): pl.pallas_call(functools.partial(_weight_kernel, planes=planes, depth=dep...  3.73 us
    reshape x4, local copies, waits for them, and re-layouts, flat(): value.transpose(1, 0, 2, 3).reshape(value.shape[1], value.shape[0], lanes)  2.41 us
    another operation x2, local copies, waits for them, and re-layouts, flat(): value.transpose(1, 0, 2, 3).reshape(value.shape[1], value.shape[0], lanes)  1.62 us
  transfers between devices with their start and end apart: 12, of which 6 were waited for; matrix products, arithmetic and copies ran while one was open for 12% of the time, Pallas kernels for 18%

profile of v20, /device:TPU:0, one launch (start us, length us, event | category | flops | bytes accessed | tf_op | source)
XLA Modules:
  0.0 54.8 jit_solution(255080455431890350)
XLA Ops:
  0.6 0.0 copy-start.9
  0.6 0.0 copy-start.5
  0.7 1.1 %fusion = (bf16[32,1,32,128]{3,2,1,0:T(8,128)(2,1)S(1)}, bf16[32,1,32,128]{3,2,1,0:T(8,128)(2,1)S(1)}) fusion(bf16[32,2,32,128]{3,2,1,0:T(8,128)(2,1)} %bitcast.59), kind=kLoop, calls=%fused_computation.14 | loop fusion | bytes 1048576 | tf_op jit(solution)/shard_map/slice | solution.py:207
  1.8 2.4 %collective-permute-start = (bf16[32,1,32,128]{3,2,1,0:T(8,128)(2,1)S(1)}, bf16[32,1,32,128]{3,2,1,0:T(8,128)(2,1)S(1)}, u32[]{:S(2)}, u32[]{:S(2)}) collective-permute-start(bf16[32,1,32,128]{3,2,1,0:T(8,128)(2,1)S(1)} %get-tuple-element.53), channel_id=1, source_target_pairs={{0,1},{1,2},{2,3},{3,4},{4,5},{5,6},{6,7},{8,9},{9,10},{10,11},{11... | collective-permute-start | bytes 786440 | tf_op jit(solution)/shard_map/ppermute | solution.py:143
  4.2 0.0 copy-start.10
  4.2 1.3 %collective-permute-start.1 = (bf16[32,1,32,128]{3,2,1,0:T(8,128)(2,1)S(1)}, bf16[32,1,32,128]{3,2,1,0:T(8,128)(2,1)S(1)}, u32[]{:S(2)}, u32[]{:S(2)}) collective-permute-start(bf16[32,1,32,128]{3,2,1,0:T(8,128)(2,1)S(1)} %get-tuple-element.52), channel_id=1, source_target_pairs={{1,0},{2,1},{3,2},{4,3},{5,4},{6,5},{7,6},{9,8},{10,9},{11,10},{12... | collective-permute-start | bytes 786440 | tf_op jit(solution)/shard_map/ppermute | solution.py:143
  5.5 0.0 copy-done.10
  5.5 0.1 copy.16
  5.6 0.0 copy-done.9
  5.6 0.1 pad_maximum_fusion.1
  5.7 0.0 copy-done.5
  5.7 0.1 reshape.41
  5.8 0.0 copy-start
  5.8 1.1 %copy.24.cot = bf16[2,32,4096]{2,1,0:T(8,128)(2,1)} copy(bf16[2,32,4096]{2,0,1:T(2,128)(2,1)S(1)} %reshape.41) | data formatting | bytes 1048576 | tf_op jit(solution)/shard_map/reshape | solution.py:218
  6.9 0.0 copy-done
  6.9 0.1 reshape.40
  7.0 1.1 %copy.23.mid = bf16[2,32,4096]{2,1,0:T(8,128)(2,1)} copy(bf16[2,32,4096]{2,0,1:T(2,128)(2,1)S(1)} %reshape.40) | data formatting | bytes 1048576 | tf_op jit(solution)/shard_map/reshape | solution.py:218
  8.1 0.0 collective-permute-done
  8.1 3.3 %collective-permute-start.4 = (bf16[8,865]{1,0:T(8,128)(2,1)S(1)}, bf16[8,865]{1,0:T(8,128)(2,1)S(1)}, u32[]{:S(2)}, u32[]{:S(2)}) collective-permute-start(bf16[8,865]{1,0:T(8,128)(2,1)S(1)} %pad_maximum_fusion.1), channel_id=1, source_target_pairs={{0,24},{8,16},{16,8},{24,0},{1,25},{9,17},{17,9},{25,1},{2,26},{10... | collective-permute-start | bytes 41528 | tf_op jit(solution)/shard_map/ppermute | solution.py:148
  11.4 0.5 collective-permute-start.3
  11.9 0.1 collective-permute-start.2
  12.0 0.8 %reshape_transpose.6.lo = bf16[1,32,4096]{2,1,0:T(8,128)(2,1)} reshape(bf16[32,1,32,128]{3,2,1,0:T(8,128)(2,1)S(1)} %collective-permute-done) | data formatting | bytes 524288 | tf_op jit(solution)/shard_map/reshape;transpose | solution.py:218
  12.8 0.0 collective-permute-done.1
  12.8 0.8 %reshape_transpose.7.hi = bf16[1,32,4096]{2,1,0:T(8,128)(2,1)} reshape(bf16[32,1,32,128]{3,2,1,0:T(8,128)(2,1)S(1)} %collective-permute-done.1) | data formatting | bytes 524288 | tf_op jit(solution)/shard_map/reshape;transpose | solution.py:218
  13.6 2.0 %collective-permute-done.2 = bf16[8,865]{1,0:T(8,128)(2,1)S(1)} collective-permute-done((bf16[8,865]{1,0:T(8,128)(2,1)S(1)}, bf16[8,865]{1,0:T(8,128)(2,1)S(1)}, u32[]{:S(2)}, u32[]{:S(2)}) %collective-permute-start.2) | collective-permute-done | bytes 13872 | tf_op jit(solution)/shard_map/ppermute | solution.py:148
  15.6 0.0 collective-permute-done.3
  15.6 0.0 collective-permute-done.4
  15.7 0.7 %slice_convert_fusion.bias = f32[32,1]{1,0:T(8,128)} fusion(bf16[32,865]{1,0:T(8,128)(2,1)S(1)} %bitcast.66), kind=kLoop, calls=%fused_computation.11 | loop fusion | flops 32 | bytes 192 | tf_op jit(solution)/shard_map/convert_element_type | solution.py:226
  16.3 0.2 reshape.34
  16.5 0.1 copy.18
  16.7 0.8 %reshape.35.wall = bf16[288,96]{1,0:T(8,128)(2,1)} reshape(bf16[3,3,32,3,32]{4,3,2,1,0:T(4,128)(2,1)S(1)} %copy.18) | data formatting | bytes 110592 | tf_op jit(solution)/shard_map/reshape | solution.py:213
  17.5 5.1 %shard_map.84 = (bf16[2,32,4096]{2,1,0:T(8,128)(2,1)}, bf16[2,32,4096]{2,1,0:T(8,128)(2,1)}, bf16[1,32,4096]{2,1,0:T(8,128)(2,1)}, bf16[1,32,4096]{2,1,0:T(8,128)(2,1)}) custom-call(bf16[1,32,4096]{2,1,0:T(8,128)(2,1)} %reshape_transpose.6.lo, bf16[2,32,4096]{2,1,0:T(8,128)(2,1)} %copy.23.mid, bf16[1,32,4096]{2,1,0:T(8,128)(2,1)} %reshape_transpose.7.hi, ...), custom_call_target="tpu_custom_call" | custom-call | flops 452984832 | bytes 2621440 | tf_op jit(solution)/shard_map/pallas_call | solution.py:104
  22.5 2.7 %collective-permute-start.5 = (bf16[1,32,4096]{2,1,0:T(8,128)(2,1)}, bf16[1,32,4096]{2,1,0:T(8,128)(2,1)S(1)}, u32[]{:S(2)}, u32[]{:S(2)}) collective-permute-start(bf16[1,32,4096]{2,1,0:T(8,128)(2,1)} %get-tuple-element.33), channel_id=1, source_target_pairs={{0,1},{1,2},{2,3},{3,4},{4,5},{5,6},{6,7},{8,9},{9,10},{10,11},{11... | collective-permute-start | bytes 786440 | tf_op jit(solution)/shard_map/ppermute | solution.py:143
  25.2 1.3 %collective-permute-start.6 = (bf16[1,32,4096]{2,1,0:T(8,128)(2,1)}, bf16[1,32,4096]{2,1,0:T(8,128)(2,1)S(1)}, u32[]{:S(2)}, u32[]{:S(2)}) collective-permute-start(bf16[1,32,4096]{2,1,0:T(8,128)(2,1)} %get-tuple-element.34), channel_id=1, source_target_pairs={{1,0},{2,1},{3,2},{4,3},{5,4},{6,5},{7,6},{9,8},{10,9},{11,10},{12... | collective-permute-start | bytes 786440 | tf_op jit(solution)/shard_map/ppermute | solution.py:143
  26.5 0.1 reverse_bitcast_fusion
  26.7 0.3 copy.21
  26.9 0.8 %reshape.38.wall = bf16[288,96]{1,0:T(8,128)(2,1)} reshape(bf16[3,3,32,3,32]{4,3,2,1,0:T(4,128)(2,1)S(1)} %copy.21) | data formatting | bytes 110592 | tf_op jit(solution)/shard_map/reshape | solution.py:214
  27.7 3.7 %shard_map.85 = (f32[16,865]{1,0:T(8,128)}, f32[16,865]{1,0:T(8,128)}) custom-call(s32[1]{0:T(128)} %bitcast.13.upper, bf16[1,32,4096]{2,1,0:T(8,128)(2,1)} %reshape_transpose.6.lo, bf16[2,32,4096]{2,1,0:T(8,128)(2,1)} %copy.23.mid, bf16[1,32,4096]{2,1,0:T(8,128)(2,1)} %reshape_transpose.7.hi, bf16[2,32,4096]{2,1,0:T(8,128)(2,1)} %get-tuple-element.46.dpre.mid, ...), custom_call_target="tpu_custom_call" | custom-call | flops 452984832 | bytes 1572864 | tf_op jit(solution)/shard_map/pallas_call | solution.py:129
  31.5 0.0 collective-permute-done.5.lo
  31.5 0.3 collective-permute-done.6.hi
  31.8 1.5 %collective-permute-start.7 = (f32[16,865]{1,0:T(8,128)}, f32[16,865]{1,0:T(8,128)S(1)}, u32[]{:S(2)}, u32[]{:S(2)}) collective-permute-start(f32[16,865]{1,0:T(8,128)} %get-tuple-element.35), channel_id=1, source_target_pairs={{0,16},{8,24},{16,0},{24,8},{1,17},{9,25},{17,1},{25,9},{2,18},{10... | collective-permute-start | bytes 166088 | tf_op jit(solution)/shard_map/ppermute | solution.py:148
  33.3 0.0 copy-done.1
  33.3 0.0 copy-done.2
  33.3 3.0 %shard_map.86 = bf16[1,32,4096]{2,1,0:T(8,128)(2,1)} custom-call(bf16[1,32,4096]{2,1,0:T(8,128)(2,1)} %copy-done.1, bf16[2,32,4096]{2,1,0:T(8,128)(2,1)} %get-tuple-element.46.dpre.mid, bf16[1,32,4096]{2,1,0:T(8,128)(2,1)} %copy-done.2, bf16[288,96]{1,0:T(8,128)(2,1)} %reshape.38.wall, f32[9,1,4096]{2,1,0:T(1,128)} %constant.66.clone.mask), custom_call_target="tpu_custom_call" | custom-call | flops 226492416 | bytes 1572864 | tf_op jit(solution)/shard_map/pallas_call | solution.py:116
  36.3 0.0 collective-permute-done.7
  36.4 0.0 copy-done.7
  36.4 0.7 %collective-permute-start.8 = (f32[8,865]{1,0:T(8,128)S(1)}, f32[8,865]{1,0:T(8,128)S(1)}, u32[]{:S(2)}, u32[]{:S(2)}) collective-permute-start(f32[8,865]{1,0:T(8,128)S(1)} %constant_dynamic-slice_fusion), channel_id=1, source_target_pairs={{0,8},{8,0},{16,24},{24,16},{1,9},{9,1},{17,25},{25,17},{2,10},{10... | collective-permute-start | bytes 83048 | tf_op jit(solution)/shard_map/ppermute | solution.py:148
  37.0 3.1 %shard_map.87 = bf16[1,32,4096]{2,1,0:T(8,128)(2,1)} custom-call(bf16[1,32,4096]{2,1,0:T(8,128)(2,1)} %copy-done.1, bf16[2,32,4096]{2,1,0:T(8,128)(2,1)} %get-tuple-element.46.dpre.mid, bf16[1,32,4096]{2,1,0:T(8,128)(2,1)} %copy-done.2, bf16[288,96]{1,0:T(8,128)(2,1)} %reshape.38.wall, f32[9,1,4096]{2,1,0:T(1,128)} %constant.66.clone.mask), custom_call_target="tpu_custom_call" | custom-call | flops 226492416 | bytes 1572864 | tf_op jit(solution)/shard_map/pallas_call | solution.py:116
  40.1 0.2 collective-permute-done.8
  40.3 4.0 %collective-permute-start.9 = (f32[8,865]{1,0:T(8,128)S(1)}, f32[8,865]{1,0:T(8,128)S(1)}, u32[]{:S(2)}, u32[]{:S(2)}) collective-permute-start(f32[8,865]{1,0:T(8,128)S(1)} %dynamic-slice_add_fusion), channel_id=1, source_target_pairs={{0,1},{1,0},{2,3},{3,2},{4,5},{5,4},{6,7},{7,6},{8,9},{9,8},{10,11... | collective-permute-start | bytes 83048 | tf_op jit(solution)/shard_map/ppermute | solution.py:148
  44.3 0.0 copy-done.6
  44.4 0.1 copy.25
  44.4 0.8 %collective-permute-done.9 = f32[8,865]{1,0:T(8,128)S(1)} collective-permute-done((f32[8,865]{1,0:T(8,128)S(1)}, f32[8,865]{1,0:T(8,128)S(1)}, u32[]{:S(2)}, u32[]{:S(2)}) %collective-permute-start.9) | collective-permute-done | bytes 27712 | tf_op jit(solution)/shard_map/ppermute | solution.py:148
  45.2 2.1 %collective-permute-start.10 = (f32[8,865]{1,0:T(8,128)S(1)}, f32[8,865]{1,0:T(8,128)S(1)}, u32[]{:S(2)}, u32[]{:S(2)}) collective-permute-start(f32[8,865]{1,0:T(8,128)S(1)} %add.53), channel_id=1, source_target_pairs={{0,2},{1,3},{2,0},{3,1},{4,6},{5,7},{6,4},{7,5},{8,10},{9,11},{10,... | collective-permute-start | bytes 83048 | tf_op jit(solution)/shard_map/ppermute | solution.py:148
  47.4 0.0 copy-done.3
  47.4 0.0 copy-done.4
  47.4 0.1 pad_maximum_fusion
  47.4 0.1 copy.26
  47.5 1.7 %collective-permute-done.10 = f32[8,865]{1,0:T(8,128)S(1)} collective-permute-done((f32[8,865]{1,0:T(8,128)S(1)}, f32[8,865]{1,0:T(8,128)S(1)}, u32[]{:S(2)}, u32[]{:S(2)}) %collective-permute-start.10) | collective-permute-done | bytes 27712 | tf_op jit(solution)/shard_map/ppermute | solution.py:148
  49.2 3.0 %collective-permute-start.11 = (f32[8,865]{1,0:T(8,128)S(1)}, f32[8,865]{1,0:T(8,128)S(1)}, u32[]{:S(2)}, u32[]{:S(2)}) collective-permute-start(f32[8,865]{1,0:T(8,128)S(1)} %add.54), channel_id=1, source_target_pairs={{0,4},{1,5},{2,6},{3,7},{4,0},{5,1},{6,2},{7,3},{8,12},{9,13},{10,... | collective-permute-start | bytes 83048 | tf_op jit(solution)/shard_map/ppermute | solution.py:148
  52.2 1.1 %copy_bitcast_fusion = (bf16[1,32,2,32,128]{4,3,2,1,0:T(8,128)(2,1)}, bf16[1,32,2,32,128]{4,3,2,1,0:T(8,128)(2,1)}) fusion(bf16[2,32,32,128]{3,2,1,0:T(8,128)(2,1)S(1)} %bitcast.62, bf16[2,32,32,128]{3,2,1,0:T(8,128)(2,1)S(1)} %bitcast.63), kind=kLoop, calls=%fused_computation.1 | loop fusion | bytes 2097152 | tf_op jit(solution)/shard_map/broadcast_in_dim | solution.py:239
  53.4 0.7 %collective-permute-done.11 = f32[8,865]{1,0:T(8,128)S(1)} collective-permute-done((f32[8,865]{1,0:T(8,128)S(1)}, f32[8,865]{1,0:T(8,128)S(1)}, u32[]{:S(2)}, u32[]{:S(2)}) %collective-permute-start.11) | collective-permute-done | bytes 27712 | tf_op jit(solution)/shard_map/ppermute | solution.py:148
  54.1 0.7 %slice_reduce_fusion = f32[8]{0:T(128)} fusion(f32[8,865]{1,0:T(8,128)S(1)} %add_multiply_fusion), kind=kLoop, calls=%fused_computation.12 | loop fusion | bytes 64 | tf_op jit(solution)/shard_map/slice | solution.py:239
  54.8 0.0 copy-done.8
  (18 shorter events, 0.1 us)
Async XLA Ops:
  0.6 5.0 %copy-start.9 = (bf16[8,864]{1,0:T(8,128)(2,1)S(1)}, bf16[8,864]{1,0:T(8,128)(2,1)}, u32[]{:S(2)}) copy-start(bf16[8,864]{1,0:T(8,128)(2,1)} %param.7) | copy-start | bytes 41476
  0.6 5.0 %copy-start.5 = (bf16[1,32,2,32,128]{4,3,2,1,0:T(8,128)(2,1)S(1)}, bf16[1,32,2,32,128]{4,3,2,1,0:T(8,128)(2,1)}, u32[]{:S(2)}) copy-start(bf16[1,32,2,32,128]{4,3,2,1,0:T(8,128)(2,1)} %param.6) | copy-start | bytes 1572868
  1.8 6.3 %collective-permute-start = (bf16[32,1,32,128]{3,2,1,0:T(8,128)(2,1)S(1)}, bf16[32,1,32,128]{3,2,1,0:T(8,128)(2,1)S(1)}, u32[]{:S(2)}, u32[]{:S(2)}) collective-permute-start(bf16[32,1,32,128]{3,2,1,0:T(8,128)(2,1)S(1)} %get-tuple-element.53), channel_id=1, source_target_pairs={{0,1},{1,2},{2,3},{3,4},{4,5},{5,6},{6,7},{8,9},{9,10},{10,11},{11... | collective-permute-start | bytes 786440 | tf_op jit(solution)/shard_map/ppermute | solution.py:143
  4.2 1.3 %copy-start.10 = (bf16[8]{0:T(256)(128)(2,1)S(1)}, bf16[8]{0:T(256)(128)(2,1)}, u32[]{:S(2)}) copy-start(bf16[8]{0:T(256)(128)(2,1)} %param.8) | copy-start | bytes 52
  4.2 8.6 %collective-permute-start.1 = (bf16[32,1,32,128]{3,2,1,0:T(8,128)(2,1)S(1)}, bf16[32,1,32,128]{3,2,1,0:T(8,128)(2,1)S(1)}, u32[]{:S(2)}, u32[]{:S(2)}) collective-permute-start(bf16[32,1,32,128]{3,2,1,0:T(8,128)(2,1)S(1)} %get-tuple-element.52), channel_id=1, source_target_pairs={{1,0},{2,1},{3,2},{4,3},{5,4},{6,5},{7,6},{9,8},{10,9},{11,10},{12... | collective-permute-start | bytes 786440 | tf_op jit(solution)/shard_map/ppermute | solution.py:143
  5.8 1.1 %copy-start = (bf16[1,32,2,32,128]{4,3,2,1,0:T(8,128)(2,1)S(1)}, bf16[1,32,2,32,128]{4,3,2,1,0:T(8,128)(2,1)}, u32[]{:S(2)}) copy-start(bf16[1,32,2,32,128]{4,3,2,1,0:T(8,128)(2,1)} %param.5) | copy-start | bytes 1572868
  8.1 7.5 %collective-permute-start.4 = (bf16[8,865]{1,0:T(8,128)(2,1)S(1)}, bf16[8,865]{1,0:T(8,128)(2,1)S(1)}, u32[]{:S(2)}, u32[]{:S(2)}) collective-permute-start(bf16[8,865]{1,0:T(8,128)(2,1)S(1)} %pad_maximum_fusion.1), channel_id=1, source_target_pairs={{0,24},{8,16},{16,8},{24,0},{1,25},{9,17},{17,9},{25,1},{2,26},{10... | collective-permute-start | bytes 41528 | tf_op jit(solution)/shard_map/ppermute | solution.py:148
  11.4 4.2 %collective-permute-start.3 = (bf16[8,865]{1,0:T(8,128)(2,1)S(1)}, bf16[8,865]{1,0:T(8,128)(2,1)S(1)}, u32[]{:S(2)}, u32[]{:S(2)}) collective-permute-start(bf16[8,865]{1,0:T(8,128)(2,1)S(1)} %pad_maximum_fusion.1), channel_id=1, source_target_pairs={{0,16},{8,24},{16,0},{24,8},{1,17},{9,25},{17,1},{25,9},{2,18},{10... | collective-permute-start | bytes 41528 | tf_op jit(solution)/shard_map/ppermute | solution.py:148
  11.9 3.7 %collective-permute-start.2 = (bf16[8,865]{1,0:T(8,128)(2,1)S(1)}, bf16[8,865]{1,0:T(8,128)(2,1)S(1)}, u32[]{:S(2)}, u32[]{:S(2)}) collective-permute-start(bf16[8,865]{1,0:T(8,128)(2,1)S(1)} %pad_maximum_fusion.1), channel_id=1, source_target_pairs={{0,8},{8,0},{16,24},{24,16},{1,9},{9,1},{17,25},{25,17},{2,10},{10... | collective-permute-start | bytes 41528 | tf_op jit(solution)/shard_map/ppermute | solution.py:148
  22.5 8.9 %collective-permute-start.5 = (bf16[1,32,4096]{2,1,0:T(8,128)(2,1)}, bf16[1,32,4096]{2,1,0:T(8,128)(2,1)S(1)}, u32[]{:S(2)}, u32[]{:S(2)}) collective-permute-start(bf16[1,32,4096]{2,1,0:T(8,128)(2,1)} %get-tuple-element.33), channel_id=1, source_target_pairs={{0,1},{1,2},{2,3},{3,4},{4,5},{5,6},{6,7},{8,9},{9,10},{10,11},{11... | collective-permute-start | bytes 786440 | tf_op jit(solution)/shard_map/ppermute | solution.py:143
  25.2 6.6 %collective-permute-start.6 = (bf16[1,32,4096]{2,1,0:T(8,128)(2,1)}, bf16[1,32,4096]{2,1,0:T(8,128)(2,1)S(1)}, u32[]{:S(2)}, u32[]{:S(2)}) collective-permute-start(bf16[1,32,4096]{2,1,0:T(8,128)(2,1)} %get-tuple-element.34), channel_id=1, source_target_pairs={{1,0},{2,1},{3,2},{4,3},{5,4},{6,5},{7,6},{9,8},{10,9},{11,10},{12... | collective-permute-start | bytes 786440 | tf_op jit(solution)/shard_map/ppermute | solution.py:143
  31.5 1.8 %copy-start.1 = (bf16[1,32,4096]{2,1,0:T(8,128)(2,1)}, bf16[1,32,4096]{2,1,0:T(8,128)(2,1)S(1)}, u32[]{:S(2)}) copy-start(bf16[1,32,4096]{2,1,0:T(8,128)(2,1)S(1)} %collective-permute-done.5.lo) | copy-start | bytes 786436
  31.8 1.5 %copy-start.2 = (bf16[1,32,4096]{2,1,0:T(8,128)(2,1)}, bf16[1,32,4096]{2,1,0:T(8,128)(2,1)S(1)}, u32[]{:S(2)}) copy-start(bf16[1,32,4096]{2,1,0:T(8,128)(2,1)S(1)} %collective-permute-done.6.hi) | copy-start | bytes 786436
  31.8 4.6 %collective-permute-start.7 = (f32[16,865]{1,0:T(8,128)}, f32[16,865]{1,0:T(8,128)S(1)}, u32[]{:S(2)}, u32[]{:S(2)}) collective-permute-start(f32[16,865]{1,0:T(8,128)} %get-tuple-element.35), channel_id=1, source_target_pairs={{0,16},{8,24},{16,0},{24,8},{1,17},{9,25},{17,1},{25,9},{2,18},{10... | collective-permute-start | bytes 166088 | tf_op jit(solution)/shard_map/ppermute | solution.py:148
  33.3 3.0 %copy-start.7 = (f32[16,865]{1,0:T(8,128)S(1)}, f32[16,865]{1,0:T(8,128)}, u32[]{:S(2)}) copy-start(f32[16,865]{1,0:T(8,128)} %get-tuple-element.42) | copy-start | bytes 166084
  36.4 3.9 %collective-permute-start.8 = (f32[8,865]{1,0:T(8,128)S(1)}, f32[8,865]{1,0:T(8,128)S(1)}, u32[]{:S(2)}, u32[]{:S(2)}) collective-permute-start(f32[8,865]{1,0:T(8,128)S(1)} %constant_dynamic-slice_fusion), channel_id=1, source_target_pairs={{0,8},{8,0},{16,24},{24,16},{1,9},{9,1},{17,25},{25,17},{2,10},{10... | collective-permute-start | bytes 83048 | tf_op jit(solution)/shard_map/ppermute | solution.py:148
  37.0 7.3 %copy-start.6 = (bf16[2,32,4096]{2,1,0:T(8,128)(2,1)S(1)}, bf16[2,32,4096]{2,1,0:T(8,128)(2,1)}, u32[]{:S(2)}) copy-start(bf16[2,32,4096]{2,1,0:T(8,128)(2,1)} %get-tuple-element.30) | copy-start | bytes 1572868
  40.3 4.9 %collective-permute-start.9 = (f32[8,865]{1,0:T(8,128)S(1)}, f32[8,865]{1,0:T(8,128)S(1)}, u32[]{:S(2)}, u32[]{:S(2)}) collective-permute-start(f32[8,865]{1,0:T(8,128)S(1)} %dynamic-slice_add_fusion), channel_id=1, source_target_pairs={{0,1},{1,0},{2,3},{3,2},{4,5},{5,4},{6,7},{7,6},{8,9},{9,8},{10,11... | collective-permute-start | bytes 83048 | tf_op jit(solution)/shard_map/ppermute | solution.py:148
  44.3 3.0 %copy-start.3 = (bf16[1,32,4096]{2,1,0:T(8,128)(2,1)S(1)}, bf16[1,32,4096]{2,1,0:T(8,128)(2,1)}, u32[]{:S(2)}) copy-start(bf16[1,32,4096]{2,1,0:T(8,128)(2,1)} %shard_map.86) | copy-start | bytes 786436
  44.3 3.0 %copy-start.4 = (bf16[1,32,4096]{2,1,0:T(8,128)(2,1)S(1)}, bf16[1,32,4096]{2,1,0:T(8,128)(2,1)}, u32[]{:S(2)}) copy-start(bf16[1,32,4096]{2,1,0:T(8,128)(2,1)} %shard_map.87) | copy-start | bytes 786436
  45.2 4.0 %collective-permute-start.10 = (f32[8,865]{1,0:T(8,128)S(1)}, f32[8,865]{1,0:T(8,128)S(1)}, u32[]{:S(2)}, u32[]{:S(2)}) collective-permute-start(f32[8,865]{1,0:T(8,128)S(1)} %add.53), channel_id=1, source_target_pairs={{0,2},{1,3},{2,0},{3,1},{4,6},{5,7},{6,4},{7,5},{8,10},{9,11},{10,... | collective-permute-start | bytes 83048 | tf_op jit(solution)/shard_map/ppermute | solution.py:148
  49.2 4.9 %collective-permute-start.11 = (f32[8,865]{1,0:T(8,128)S(1)}, f32[8,865]{1,0:T(8,128)S(1)}, u32[]{:S(2)}, u32[]{:S(2)}) collective-permute-start(f32[8,865]{1,0:T(8,128)S(1)} %add.54), channel_id=1, source_target_pairs={{0,4},{1,5},{2,6},{3,7},{4,0},{5,1},{6,2},{7,3},{8,12},{9,13},{10,... | collective-permute-start | bytes 83048 | tf_op jit(solution)/shard_map/ppermute | solution.py:148
  54.1 0.7 %copy-start.8 = (f32[8,865]{1,0:T(8,128)}, f32[8,865]{1,0:T(8,128)S(1)}, u32[]{:S(2)}) copy-start(f32[8,865]{1,0:T(8,128)S(1)} %add_multiply_fusion) | copy-start | bytes 83044

commit v21 on v14

--- a/solution.py
+++ b/solution.py
@@ -218,9 +218,8 @@
     def unflat(value):
         return value.reshape(planes, value.shape[1], rows, depth).transpose(1, 0, 2, 3)
 
-    below, above = neighbours(field[:, :1], field[:, planes - 1 :], "strike")
+    lo, hi = neighbours(flat(field[:, :1]), flat(field[:, planes - 1 :]), "strike")
     mid = flat(field)
-    lo, hi = flat(below), flat(above)
     act, dpre, first, last = forward_call(
         lo, mid, hi, forward_w, whole_bias.astype(jnp.float32)[:, None], flat(cotangent[0]), mask, depth
     )

time: 54.6 us -> 55.9 us (1.024)
  starting transfers between devices: 23.4 us -> 24.7 us
    another operation x2, local copies, waits for them, and re-layouts: 1.62 us -> 0.23 us  [flat(): value.transpose(1, 0, 2, 3).reshape(value.shape[1], value.shape[0], lanes)]
    unnamed x24 -> x28, local copies, waits for them, and re-layouts: 1.57 us -> 2.95 us
    ppermute x4, starting transfers between devices: 9.15 us -> 10 us  [neighbours(): return (lax.ppermute(last, axis, up), lax.ppermute(first, axis, down))]
  transfers between devices with their start and end apart: 12 -> 12, of which waited for: 3 -> 3; matrix products, arithmetic and copies ran while one was open for 16% -> 15% of each run, Pallas kernels for 18% -> 18%
where the time goes in v21:
time: 55.9 us; the launch traced here: 55.5 us
  starting transfers between devices  24.7 us (44%)
  Pallas kernels  14.9 us (27%)
  local copies, waits for them, and re-layouts  10.9 us (19%)
  waiting for transfers between devices  3.25 us (6%)
  between operations  0.9 us (2%)
  other arithmetic  0.84 us (2%)
    ppermute x8, starting transfers between devices, swap(): return lax.ppermute(value, axis, [(i, i ^ bit) for i in range(peers)])  14.7 us
    ppermute x4, starting transfers between devices, neighbours(): return (lax.ppermute(last, axis, up), lax.ppermute(first, axis, down))  10 us
    pallas_call x2, Pallas kernels, input_call(): pl.pallas_call(functools.partial(_input_kernel, planes=planes, first=firs...  6.09 us
    pallas_call x1, Pallas kernels, forward_call(): pl.pallas_call(functools.partial(_forward_kernel, planes=planes, depth=de...  5.06 us
    pallas_call x1, Pallas kernels, weight_call(): pl.pallas_call(functools.partial(_weight_kernel, planes=planes, depth=dep...  3.74 us
    ppermute x8, waiting for transfers between devices, swap(): return lax.ppermute(value, axis, [(i, i ^ bit) for i in range(peers)])  3.23 us
    unnamed x28, local copies, waits for them, and re-layouts  2.95 us
    reshape x4, local copies, waits for them, and re-layouts, flat(): value.transpose(1, 0, 2, 3).reshape(value.shape[1], value.shape[0], lanes)  2.41 us
  transfers between devices with their start and end apart: 12, of which 3 were waited for; matrix products, arithmetic and copies ran while one was open for 15% of the time, Pallas kernels for 18%

profile of v21, /device:TPU:0, one launch (start us, length us, event | category | flops | bytes accessed | tf_op | source)
XLA Modules:
  0.0 55.5 jit_solution(5285405261942263605)
XLA Ops:
  0.6 0.0 copy-start.12
  0.6 0.6 %copy-done.12 = bf16[8]{0:T(256)(128)(2,1)S(1)} copy-done((bf16[8]{0:T(256)(128)(2,1)S(1)}, bf16[8]{0:T(256)(128)(2,1)}, u32[]{:S(2)}) %copy-start.12) | copy-done | bytes 40
  1.3 0.1 copy.17
  1.4 0.7 %copy-done.11 = bf16[8,864]{1,0:T(8,128)(2,1)S(1)} copy-done((bf16[8,864]{1,0:T(8,128)(2,1)S(1)}, bf16[8,864]{1,0:T(8,128)(2,1)}, u32[]{:S(2)}) %copy-start.11) | copy-done | bytes 13848
  2.1 0.1 bitcast_dynamic-update-slice_fusion.3
  2.2 3.0 %collective-permute-start.3 = (bf16[8,865]{1,0:T(8,128)(2,1)S(1)}, bf16[8,865]{1,0:T(8,128)(2,1)S(1)}, u32[]{:S(2)}, u32[]{:S(2)}) collective-permute-start(bf16[8,865]{1,0:T(8,128)(2,1)S(1)} %get-tuple-element.49), channel_id=1, source_target_pairs={{0,16},{8,24},{16,0},{24,8},{1,17},{9,25},{17,1},{25,9},{2,18},{10... | collective-permute-start | bytes 41528 | tf_op jit(solution)/shard_map/ppermute | solution.py:148
  5.1 1.5 %collective-permute-start.2 = (bf16[8,865]{1,0:T(8,128)(2,1)S(1)}, bf16[8,865]{1,0:T(8,128)(2,1)S(1)}, u32[]{:S(2)}, u32[]{:S(2)}) collective-permute-start(bf16[8,865]{1,0:T(8,128)(2,1)S(1)} %get-tuple-element.49), channel_id=1, source_target_pairs={{0,8},{8,0},{16,24},{24,16},{1,9},{9,1},{17,25},{25,17},{2,10},{10... | collective-permute-start | bytes 41528 | tf_op jit(solution)/shard_map/ppermute | solution.py:148
  6.6 0.0 collective-permute-start.4
  6.7 1.1 %fusion = (bf16[32,1,32,128]{3,2,1,0:T(8,128)(2,1)S(1)}, bf16[32,1,32,128]{3,2,1,0:T(8,128)(2,1)S(1)}) fusion(bf16[32,2,32,128]{3,2,1,0:T(8,128)(2,1)} %bitcast.59), kind=kLoop, calls=%fused_computation.14 | loop fusion | bytes 1048576 | tf_op jit(solution)/shard_map/slice | solution.py:221
  7.8 0.0 copy-start.7
  7.8 0.1 reshape_transpose.6
  7.9 1.4 %collective-permute-start = (bf16[1,32,4096]{2,1,0:T(8,128)(2,1)S(1)}, bf16[1,32,4096]{2,1,0:T(8,128)(2,1)S(1)}, u32[]{:S(2)}, u32[]{:S(2)}) collective-permute-start(bf16[1,32,4096]{2,1,0:T(8,128)(2,1)S(1)} %reshape_transpose.6), channel_id=1, source_target_pairs={{0,1},{1,2},{2,3},{3,4},{4,5},{5,6},{6,7},{8,9},{9,10},{10,11},{11... | collective-permute-start | bytes 786440 | tf_op jit(solution)/shard_map/ppermute | solution.py:143
  9.3 0.1 reshape_transpose.7
  9.5 1.3 %collective-permute-start.1 = (bf16[1,32,4096]{2,1,0:T(8,128)(2,1)S(1)}, bf16[1,32,4096]{2,1,0:T(8,128)(2,1)S(1)}, u32[]{:S(2)}, u32[]{:S(2)}) collective-permute-start(bf16[1,32,4096]{2,1,0:T(8,128)(2,1)S(1)} %reshape_transpose.7), channel_id=1, source_target_pairs={{1,0},{2,1},{3,2},{4,3},{5,4},{6,5},{7,6},{9,8},{10,9},{11,10},{12... | collective-permute-start | bytes 786440 | tf_op jit(solution)/shard_map/ppermute | solution.py:143
  10.8 0.0 copy-done.7
  10.8 0.1 reshape.41
  10.9 0.0 copy-start
  10.9 1.1 %copy.24.cot = bf16[2,32,4096]{2,1,0:T(8,128)(2,1)} copy(bf16[2,32,4096]{2,0,1:T(2,128)(2,1)S(1)} %reshape.41) | data formatting | bytes 1048576 | tf_op jit(solution)/shard_map/reshape | solution.py:216
  12.0 0.0 copy-done
  12.0 0.1 reshape.40
  12.1 1.1 %copy.23.mid = bf16[2,32,4096]{2,1,0:T(8,128)(2,1)} copy(bf16[2,32,4096]{2,0,1:T(2,128)(2,1)S(1)} %reshape.40) | data formatting | bytes 1048576 | tf_op jit(solution)/shard_map/reshape | solution.py:216
  13.2 0.0 collective-permute-done.2
  13.2 0.0 collective-permute-done.3
  13.3 0.0 collective-permute-done.4
  13.3 0.2 reshape.34
  13.5 0.1 copy.18
  13.6 0.8 %reshape.35.wall = bf16[288,96]{1,0:T(8,128)(2,1)} reshape(bf16[3,3,32,3,32]{4,3,2,1,0:T(4,128)(2,1)S(1)} %copy.18) | data formatting | bytes 110592 | tf_op jit(solution)/shard_map/reshape | solution.py:211
  14.4 0.7 %slice_convert_fusion.bias = f32[32,1]{1,0:T(8,128)} fusion(bf16[32,865]{1,0:T(8,128)(2,1)S(1)} %bitcast.67), kind=kLoop, calls=%fused_computation.11 | loop fusion | flops 32 | bytes 192 | tf_op jit(solution)/shard_map/convert_element_type | solution.py:224
  15.1 0.0 collective-permute-done.lo
  15.1 0.0 collective-permute-done.1.hi
  15.1 0.7 %copy-done.1 = bf16[1,32,4096]{2,1,0:T(8,128)(2,1)} copy-done((bf16[1,32,4096]{2,1,0:T(8,128)(2,1)}, bf16[1,32,4096]{2,1,0:T(8,128)(2,1)S(1)}, u32[]{:S(2)}) %copy-start.1) | copy-done | bytes 262168
  15.8 0.7 %copy-done.2 = bf16[1,32,4096]{2,1,0:T(8,128)(2,1)} copy-done((bf16[1,32,4096]{2,1,0:T(8,128)(2,1)}, bf16[1,32,4096]{2,1,0:T(8,128)(2,1)S(1)}, u32[]{:S(2)}) %copy-start.2) | copy-done | bytes 262168
  16.5 5.1 %shard_map.84 = (bf16[2,32,4096]{2,1,0:T(8,128)(2,1)}, bf16[2,32,4096]{2,1,0:T(8,128)(2,1)}, bf16[1,32,4096]{2,1,0:T(8,128)(2,1)}, bf16[1,32,4096]{2,1,0:T(8,128)(2,1)}) custom-call(bf16[1,32,4096]{2,1,0:T(8,128)(2,1)} %copy-done.1, bf16[2,32,4096]{2,1,0:T(8,128)(2,1)} %copy.23.mid, bf16[1,32,4096]{2,1,0:T(8,128)(2,1)} %copy-done.2, ...), custom_call_target="tpu_custom_call" | custom-call | flops 452984832 | bytes 2621440 | tf_op jit(solution)/shard_map/pallas_call | solution.py:104
  21.6 6.0 %collective-permute-start.5 = (bf16[1,32,4096]{2,1,0:T(8,128)(2,1)}, bf16[1,32,4096]{2,1,0:T(8,128)(2,1)S(1)}, u32[]{:S(2)}, u32[]{:S(2)}) collective-permute-start(bf16[1,32,4096]{2,1,0:T(8,128)(2,1)} %get-tuple-element.29), channel_id=1, source_target_pairs={{0,1},{1,2},{2,3},{3,4},{4,5},{5,6},{6,7},{8,9},{9,10},{10,11},{11... | collective-permute-start | bytes 786440 | tf_op jit(solution)/shard_map/ppermute | solution.py:143
  27.6 1.3 %collective-permute-start.6 = (bf16[1,32,4096]{2,1,0:T(8,128)(2,1)}, bf16[1,32,4096]{2,1,0:T(8,128)(2,1)S(1)}, u32[]{:S(2)}, u32[]{:S(2)}) collective-permute-start(bf16[1,32,4096]{2,1,0:T(8,128)(2,1)} %get-tuple-element.30), channel_id=1, source_target_pairs={{1,0},{2,1},{3,2},{4,3},{5,4},{6,5},{7,6},{9,8},{10,9},{11,10},{12... | collective-permute-start | bytes 786440 | tf_op jit(solution)/shard_map/ppermute | solution.py:143
  28.9 0.1 reverse_bitcast_fusion
  29.0 0.3 copy.21
  29.3 0.8 %reshape.38.wall = bf16[288,96]{1,0:T(8,128)(2,1)} reshape(bf16[3,3,32,3,32]{4,3,2,1,0:T(4,128)(2,1)S(1)} %copy.21) | data formatting | bytes 110592 | tf_op jit(solution)/shard_map/reshape | solution.py:212
  30.1 3.7 %shard_map.85 = (f32[16,865]{1,0:T(8,128)}, f32[16,865]{1,0:T(8,128)}) custom-call(s32[1]{0:T(128)} %bitcast.13.upper, bf16[1,32,4096]{2,1,0:T(8,128)(2,1)} %copy-done.1, bf16[2,32,4096]{2,1,0:T(8,128)(2,1)} %copy.23.mid, bf16[1,32,4096]{2,1,0:T(8,128)(2,1)} %copy-done.2, bf16[2,32,4096]{2,1,0:T(8,128)(2,1)} %get-tuple-element.42.dpre.mid, ...), custom_call_target="tpu_custom_call" | custom-call | flops 452984832 | bytes 1572864 | tf_op jit(solution)/shard_map/pallas_call | solution.py:129
  33.8 0.0 collective-permute-done.5.lo
  33.8 0.0 collective-permute-done.6.hi
  33.8 0.0 copy-start.4
  33.8 1.6 %collective-permute-start.7 = (f32[16,865]{1,0:T(8,128)}, f32[16,865]{1,0:T(8,128)S(1)}, u32[]{:S(2)}, u32[]{:S(2)}) collective-permute-start(f32[16,865]{1,0:T(8,128)} %get-tuple-element.31), channel_id=1, source_target_pairs={{0,16},{8,24},{16,0},{24,8},{1,17},{9,25},{17,1},{25,9},{2,18},{10... | collective-permute-start | bytes 166088 | tf_op jit(solution)/shard_map/ppermute | solution.py:148
  35.4 0.0 copy-done.3
  35.4 0.0 copy-done.4
  35.4 3.0 %shard_map.86 = bf16[1,32,4096]{2,1,0:T(8,128)(2,1)} custom-call(bf16[1,32,4096]{2,1,0:T(8,128)(2,1)} %copy-done.3, bf16[2,32,4096]{2,1,0:T(8,128)(2,1)} %get-tuple-element.42.dpre.mid, bf16[1,32,4096]{2,1,0:T(8,128)(2,1)} %copy-done.4, bf16[288,96]{1,0:T(8,128)(2,1)} %reshape.38.wall, f32[9,1,4096]{2,1,0:T(1,128)} %constant.66.clone.mask), custom_call_target="tpu_custom_call" | custom-call | flops 226492416 | bytes 1572864 | tf_op jit(solution)/shard_map/pallas_call | solution.py:116
  38.5 0.0 collective-permute-done.7
  38.5 0.0 copy-done.9
  38.5 1.6 %collective-permute-start.8 = (f32[8,865]{1,0:T(8,128)S(1)}, f32[8,865]{1,0:T(8,128)S(1)}, u32[]{:S(2)}, u32[]{:S(2)}) collective-permute-start(f32[8,865]{1,0:T(8,128)S(1)} %constant_dynamic-slice_fusion), channel_id=1, source_target_pairs={{0,8},{8,0},{16,24},{24,16},{1,9},{9,1},{17,25},{25,17},{2,10},{10... | collective-permute-start | bytes 83048 | tf_op jit(solution)/shard_map/ppermute | solution.py:148
  40.0 3.1 %shard_map.87 = bf16[1,32,4096]{2,1,0:T(8,128)(2,1)} custom-call(bf16[1,32,4096]{2,1,0:T(8,128)(2,1)} %copy-done.3, bf16[2,32,4096]{2,1,0:T(8,128)(2,1)} %get-tuple-element.42.dpre.mid, bf16[1,32,4096]{2,1,0:T(8,128)(2,1)} %copy-done.4, bf16[288,96]{1,0:T(8,128)(2,1)} %reshape.38.wall, f32[9,1,4096]{2,1,0:T(1,128)} %constant.66.clone.mask), custom_call_target="tpu_custom_call" | custom-call | flops 226492416 | bytes 1572864 | tf_op jit(solution)/shard_map/pallas_call | solution.py:116
  43.1 0.0 collective-permute-done.8
  43.1 2.1 %collective-permute-start.9 = (f32[8,865]{1,0:T(8,128)S(1)}, f32[8,865]{1,0:T(8,128)S(1)}, u32[]{:S(2)}, u32[]{:S(2)}) collective-permute-start(f32[8,865]{1,0:T(8,128)S(1)} %dynamic-slice_add_fusion), channel_id=1, source_target_pairs={{0,1},{1,0},{2,3},{3,2},{4,5},{5,4},{6,7},{7,6},{8,9},{9,8},{10,11... | collective-permute-start | bytes 83048 | tf_op jit(solution)/shard_map/ppermute | solution.py:148
  45.2 0.0 copy-done.8
  45.2 0.1 copy.25
  45.3 0.8 %collective-permute-done.9 = f32[8,865]{1,0:T(8,128)S(1)} collective-permute-done((f32[8,865]{1,0:T(8,128)S(1)}, f32[8,865]{1,0:T(8,128)S(1)}, u32[]{:S(2)}, u32[]{:S(2)}) %collective-permute-start.9) | collective-permute-done | bytes 27712 | tf_op jit(solution)/shard_map/ppermute | solution.py:148
  46.1 2.0 %collective-permute-start.10 = (f32[8,865]{1,0:T(8,128)S(1)}, f32[8,865]{1,0:T(8,128)S(1)}, u32[]{:S(2)}, u32[]{:S(2)}) collective-permute-start(f32[8,865]{1,0:T(8,128)S(1)} %add.53), channel_id=1, source_target_pairs={{0,2},{1,3},{2,0},{3,1},{4,6},{5,7},{6,4},{7,5},{8,10},{9,11},{10,... | collective-permute-start | bytes 83048 | tf_op jit(solution)/shard_map/ppermute | solution.py:148
  48.0 0.0 copy-done.5
  48.0 0.1 pad_maximum_fusion
  48.1 0.1 copy.26
  48.2 1.7 %collective-permute-done.10 = f32[8,865]{1,0:T(8,128)S(1)} collective-permute-done((f32[8,865]{1,0:T(8,128)S(1)}, f32[8,865]{1,0:T(8,128)S(1)}, u32[]{:S(2)}, u32[]{:S(2)}) %collective-permute-start.10) | collective-permute-done | bytes 27712 | tf_op jit(solution)/shard_map/ppermute | solution.py:148
  49.9 3.0 %collective-permute-start.11 = (f32[8,865]{1,0:T(8,128)S(1)}, f32[8,865]{1,0:T(8,128)S(1)}, u32[]{:S(2)}, u32[]{:S(2)}) collective-permute-start(f32[8,865]{1,0:T(8,128)S(1)} %add.54), channel_id=1, source_target_pairs={{0,4},{1,5},{2,6},{3,7},{4,0},{5,1},{6,2},{7,3},{8,12},{9,13},{10,... | collective-permute-start | bytes 83048 | tf_op jit(solution)/shard_map/ppermute | solution.py:148
  52.9 1.1 %copy_bitcast_fusion = (bf16[1,32,2,32,128]{4,3,2,1,0:T(8,128)(2,1)}, bf16[1,32,2,32,128]{4,3,2,1,0:T(8,128)(2,1)}) fusion(bf16[2,32,32,128]{3,2,1,0:T(8,128)(2,1)S(1)} %bitcast.62, bf16[2,32,32,128]{3,2,1,0:T(8,128)(2,1)S(1)} %bitcast.63), kind=kLoop, calls=%fused_computation.1 | loop fusion | bytes 2097152 | tf_op jit(solution)/shard_map/broadcast_in_dim | solution.py:237
  54.0 0.7 %collective-permute-done.11 = f32[8,865]{1,0:T(8,128)S(1)} collective-permute-done((f32[8,865]{1,0:T(8,128)S(1)}, f32[8,865]{1,0:T(8,128)S(1)}, u32[]{:S(2)}, u32[]{:S(2)}) %collective-permute-start.11) | collective-permute-done | bytes 27712 | tf_op jit(solution)/shard_map/ppermute | solution.py:148
  54.8 0.7 %slice_reduce_fusion = f32[8]{0:T(128)} fusion(f32[8,865]{1,0:T(8,128)S(1)} %add_multiply_fusion), kind=kLoop, calls=%fused_computation.12 | loop fusion | bytes 64 | tf_op jit(solution)/shard_map/slice | solution.py:237
  (21 shorter events, 0.1 us)
Async XLA Ops:
  0.6 0.7 %copy-start.12 = (bf16[8]{0:T(256)(128)(2,1)S(1)}, bf16[8]{0:T(256)(128)(2,1)}, u32[]{:S(2)}) copy-start(bf16[8]{0:T(256)(128)(2,1)} %param.8) | copy-start | bytes 52
  1.4 0.7 %copy-start.11 = (bf16[8,864]{1,0:T(8,128)(2,1)S(1)}, bf16[8,864]{1,0:T(8,128)(2,1)}, u32[]{:S(2)}) copy-start(bf16[8,864]{1,0:T(8,128)(2,1)} %param.7) | copy-start | bytes 41476
  2.2 11.1 %collective-permute-start.3 = (bf16[8,865]{1,0:T(8,128)(2,1)S(1)}, bf16[8,865]{1,0:T(8,128)(2,1)S(1)}, u32[]{:S(2)}, u32[]{:S(2)}) collective-permute-start(bf16[8,865]{1,0:T(8,128)(2,1)S(1)} %get-tuple-element.49), channel_id=1, source_target_pairs={{0,16},{8,24},{16,0},{24,8},{1,17},{9,25},{17,1},{25,9},{2,18},{10... | collective-permute-start | bytes 41528 | tf_op jit(solution)/shard_map/ppermute | solution.py:148
  5.1 8.1 %collective-permute-start.2 = (bf16[8,865]{1,0:T(8,128)(2,1)S(1)}, bf16[8,865]{1,0:T(8,128)(2,1)S(1)}, u32[]{:S(2)}, u32[]{:S(2)}) collective-permute-start(bf16[8,865]{1,0:T(8,128)(2,1)S(1)} %get-tuple-element.49), channel_id=1, source_target_pairs={{0,8},{8,0},{16,24},{24,16},{1,9},{9,1},{17,25},{25,17},{2,10},{10... | collective-permute-start | bytes 41528 | tf_op jit(solution)/shard_map/ppermute | solution.py:148
  6.6 6.6 %collective-permute-start.4 = (bf16[8,865]{1,0:T(8,128)(2,1)S(1)}, bf16[8,865]{1,0:T(8,128)(2,1)S(1)}, u32[]{:S(2)}, u32[]{:S(2)}) collective-permute-start(bf16[8,865]{1,0:T(8,128)(2,1)S(1)} %get-tuple-element.49), channel_id=1, source_target_pairs={{0,24},{8,16},{16,8},{24,0},{1,25},{9,17},{17,9},{25,1},{2,26},{10... | collective-permute-start | bytes 41528 | tf_op jit(solution)/shard_map/ppermute | solution.py:148
  7.8 3.0 %copy-start.7 = (bf16[1,32,2,32,128]{4,3,2,1,0:T(8,128)(2,1)S(1)}, bf16[1,32,2,32,128]{4,3,2,1,0:T(8,128)(2,1)}, u32[]{:S(2)}) copy-start(bf16[1,32,2,32,128]{4,3,2,1,0:T(8,128)(2,1)} %param.6) | copy-start | bytes 1572868
  7.9 7.2 %collective-permute-start = (bf16[1,32,4096]{2,1,0:T(8,128)(2,1)S(1)}, bf16[1,32,4096]{2,1,0:T(8,128)(2,1)S(1)}, u32[]{:S(2)}, u32[]{:S(2)}) collective-permute-start(bf16[1,32,4096]{2,1,0:T(8,128)(2,1)S(1)} %reshape_transpose.6), channel_id=1, source_target_pairs={{0,1},{1,2},{2,3},{3,4},{4,5},{5,6},{6,7},{8,9},{9,10},{10,11},{11... | collective-permute-start | bytes 786440 | tf_op jit(solution)/shard_map/ppermute | solution.py:143
  9.5 5.7 %collective-permute-start.1 = (bf16[1,32,4096]{2,1,0:T(8,128)(2,1)S(1)}, bf16[1,32,4096]{2,1,0:T(8,128)(2,1)S(1)}, u32[]{:S(2)}, u32[]{:S(2)}) collective-permute-start(bf16[1,32,4096]{2,1,0:T(8,128)(2,1)S(1)} %reshape_transpose.7), channel_id=1, source_target_pairs={{1,0},{2,1},{3,2},{4,3},{5,4},{6,5},{7,6},{9,8},{10,9},{11,10},{12... | collective-permute-start | bytes 786440 | tf_op jit(solution)/shard_map/ppermute | solution.py:143
  10.9 1.1 %copy-start = (bf16[1,32,2,32,128]{4,3,2,1,0:T(8,128)(2,1)S(1)}, bf16[1,32,2,32,128]{4,3,2,1,0:T(8,128)(2,1)}, u32[]{:S(2)}) copy-start(bf16[1,32,2,32,128]{4,3,2,1,0:T(8,128)(2,1)} %param.5) | copy-start | bytes 1572868
  15.1 0.7 %copy-start.1 = (bf16[1,32,4096]{2,1,0:T(8,128)(2,1)}, bf16[1,32,4096]{2,1,0:T(8,128)(2,1)S(1)}, u32[]{:S(2)}) copy-start(bf16[1,32,4096]{2,1,0:T(8,128)(2,1)S(1)} %collective-permute-done.lo) | copy-start | bytes 786436
  15.8 0.7 %copy-start.2 = (bf16[1,32,4096]{2,1,0:T(8,128)(2,1)}, bf16[1,32,4096]{2,1,0:T(8,128)(2,1)S(1)}, u32[]{:S(2)}) copy-start(bf16[1,32,4096]{2,1,0:T(8,128)(2,1)S(1)} %collective-permute-done.1.hi) | copy-start | bytes 786436
  21.6 12.3 %collective-permute-start.5 = (bf16[1,32,4096]{2,1,0:T(8,128)(2,1)}, bf16[1,32,4096]{2,1,0:T(8,128)(2,1)S(1)}, u32[]{:S(2)}, u32[]{:S(2)}) collective-permute-start(bf16[1,32,4096]{2,1,0:T(8,128)(2,1)} %get-tuple-element.29), channel_id=1, source_target_pairs={{0,1},{1,2},{2,3},{3,4},{4,5},{5,6},{6,7},{8,9},{9,10},{10,11},{11... | collective-permute-start | bytes 786440 | tf_op jit(solution)/shard_map/ppermute | solution.py:143
  27.6 6.3 %collective-permute-start.6 = (bf16[1,32,4096]{2,1,0:T(8,128)(2,1)}, bf16[1,32,4096]{2,1,0:T(8,128)(2,1)S(1)}, u32[]{:S(2)}, u32[]{:S(2)}) collective-permute-start(bf16[1,32,4096]{2,1,0:T(8,128)(2,1)} %get-tuple-element.30), channel_id=1, source_target_pairs={{1,0},{2,1},{3,2},{4,3},{5,4},{6,5},{7,6},{9,8},{10,9},{11,10},{12... | collective-permute-start | bytes 786440 | tf_op jit(solution)/shard_map/ppermute | solution.py:143
  33.8 1.6 %copy-start.3 = (bf16[1,32,4096]{2,1,0:T(8,128)(2,1)}, bf16[1,32,4096]{2,1,0:T(8,128)(2,1)S(1)}, u32[]{:S(2)}) copy-start(bf16[1,32,4096]{2,1,0:T(8,128)(2,1)S(1)} %collective-permute-done.5.lo) | copy-start | bytes 786436
  33.8 1.6 %copy-start.4 = (bf16[1,32,4096]{2,1,0:T(8,128)(2,1)}, bf16[1,32,4096]{2,1,0:T(8,128)(2,1)S(1)}, u32[]{:S(2)}) copy-start(bf16[1,32,4096]{2,1,0:T(8,128)(2,1)S(1)} %collective-permute-done.6.hi) | copy-start | bytes 786436
  33.8 4.6 %collective-permute-start.7 = (f32[16,865]{1,0:T(8,128)}, f32[16,865]{1,0:T(8,128)S(1)}, u32[]{:S(2)}, u32[]{:S(2)}) collective-permute-start(f32[16,865]{1,0:T(8,128)} %get-tuple-element.31), channel_id=1, source_target_pairs={{0,16},{8,24},{16,0},{24,8},{1,17},{9,25},{17,1},{25,9},{2,18},{10... | collective-permute-start | bytes 166088 | tf_op jit(solution)/shard_map/ppermute | solution.py:148
  35.4 3.0 %copy-start.9 = (f32[16,865]{1,0:T(8,128)S(1)}, f32[16,865]{1,0:T(8,128)}, u32[]{:S(2)}) copy-start(f32[16,865]{1,0:T(8,128)} %get-tuple-element.38) | copy-start | bytes 166084
  38.5 4.6 %collective-permute-start.8 = (f32[8,865]{1,0:T(8,128)S(1)}, f32[8,865]{1,0:T(8,128)S(1)}, u32[]{:S(2)}, u32[]{:S(2)}) collective-permute-start(f32[8,865]{1,0:T(8,128)S(1)} %constant_dynamic-slice_fusion), channel_id=1, source_target_pairs={{0,8},{8,0},{16,24},{24,16},{1,9},{9,1},{17,25},{25,17},{2,10},{10... | collective-permute-start | bytes 83048 | tf_op jit(solution)/shard_map/ppermute | solution.py:148
  40.0 5.2 %copy-start.8 = (bf16[2,32,4096]{2,1,0:T(8,128)(2,1)S(1)}, bf16[2,32,4096]{2,1,0:T(8,128)(2,1)}, u32[]{:S(2)}) copy-start(bf16[2,32,4096]{2,1,0:T(8,128)(2,1)} %get-tuple-element.26) | copy-start | bytes 1572868
  43.1 2.9 %collective-permute-start.9 = (f32[8,865]{1,0:T(8,128)S(1)}, f32[8,865]{1,0:T(8,128)S(1)}, u32[]{:S(2)}, u32[]{:S(2)}) collective-permute-start(f32[8,865]{1,0:T(8,128)S(1)} %dynamic-slice_add_fusion), channel_id=1, source_target_pairs={{0,1},{1,0},{2,3},{3,2},{4,5},{5,4},{6,7},{7,6},{8,9},{9,8},{10,11... | collective-permute-start | bytes 83048 | tf_op jit(solution)/shard_map/ppermute | solution.py:148
  45.2 2.8 %copy-start.5 = (bf16[1,32,4096]{2,1,0:T(8,128)(2,1)S(1)}, bf16[1,32,4096]{2,1,0:T(8,128)(2,1)}, u32[]{:S(2)}) copy-start(bf16[1,32,4096]{2,1,0:T(8,128)(2,1)} %shard_map.86) | copy-start | bytes 786436
  45.2 2.8 %copy-start.6 = (bf16[1,32,4096]{2,1,0:T(8,128)(2,1)S(1)}, bf16[1,32,4096]{2,1,0:T(8,128)(2,1)}, u32[]{:S(2)}) copy-start(bf16[1,32,4096]{2,1,0:T(8,128)(2,1)} %shard_map.87) | copy-start | bytes 786436
  46.1 3.9 %collective-permute-start.10 = (f32[8,865]{1,0:T(8,128)S(1)}, f32[8,865]{1,0:T(8,128)S(1)}, u32[]{:S(2)}, u32[]{:S(2)}) collective-permute-start(f32[8,865]{1,0:T(8,128)S(1)} %add.53), channel_id=1, source_target_pairs={{0,2},{1,3},{2,0},{3,1},{4,6},{5,7},{6,4},{7,5},{8,10},{9,11},{10,... | collective-permute-start | bytes 83048 | tf_op jit(solution)/shard_map/ppermute | solution.py:148
  49.9 4.8 %collective-permute-start.11 = (f32[8,865]{1,0:T(8,128)S(1)}, f32[8,865]{1,0:T(8,128)S(1)}, u32[]{:S(2)}, u32[]{:S(2)}) collective-permute-start(f32[8,865]{1,0:T(8,128)S(1)} %add.54), channel_id=1, source_target_pairs={{0,4},{1,5},{2,6},{3,7},{4,0},{5,1},{6,2},{7,3},{8,12},{9,13},{10,... | collective-permute-start | bytes 83048 | tf_op jit(solution)/shard_map/ppermute | solution.py:148
  54.8 0.7 %copy-start.10 = (f32[8,865]{1,0:T(8,128)}, f32[8,865]{1,0:T(8,128)S(1)}, u32[]{:S(2)}) copy-start(f32[8,865]{1,0:T(8,128)S(1)} %add_multiply_fusion) | copy-start | bytes 83044

commit v22 on v14

--- a/solution.py
+++ b/solution.py
@@ -227,8 +227,7 @@
     dlo, dhi = neighbours(first, last, "strike")
     local_grads = weight_call(first_upper().astype(jnp.int32)[None], lo, mid, hi, dpre, mask, depth)
     work = [
-        (functools.partial(input_call, depth=depth, first=p, count=1), (dlo, dpre, dhi, backward_w, mask))
-        for p in range(planes)
+        (functools.partial(input_call, depth=depth, first=0, count=planes), (dlo, dpre, dhi, backward_w, mask))
     ]
     owned, pieces = reduce_beside(local_grads, work)
     grad_input = unflat(jnp.concatenate(pieces, axis=0))

time: 54.6 us -> 54.6 us (level)
  Pallas kernels: 14.9 us -> 12.9 us
  waiting for transfers between devices: 3.26 us -> 4.69 us
  local copies, waits for them, and re-layouts: 11 us -> 11.9 us
    pallas_call x2 -> x1, Pallas kernels: 6.08 us -> 4.07 us  [input_call(): pl.pallas_call(functools.partial(_input_kernel, planes=planes, first=firs...]
    ppermute x8, waiting for transfers between devices: 3.25 us -> 4.68 us  [swap(): return lax.ppermute(value, axis, [(i, i ^ bit) for i in range(peers)])]
    unnamed x24 -> x22, local copies, waits for them, and re-layouts: 1.57 us -> 2.5 us
  transfers between devices with their start and end apart: 12 -> 12, of which waited for: 3 -> 4; matrix products, arithmetic and copies ran while one was open for 16% -> 16% of each run, Pallas kernels for 18% -> 14%
where the time goes in v22:
time: 54.6 us; the launch traced here: 54.2 us
  starting transfers between devices  23 us (42%)
  Pallas kernels  12.9 us (24%)
  local copies, waits for them, and re-layouts  11.9 us (22%)
  waiting for transfers between devices  4.69 us (9%)
  between operations  0.87 us (2%)
  other arithmetic  0.79 us (1%)
    ppermute x8, starting transfers between devices, swap(): return lax.ppermute(value, axis, [(i, i ^ bit) for i in range(peers)])  13.9 us
    ppermute x4, starting transfers between devices, neighbours(): return (lax.ppermute(last, axis, up), lax.ppermute(first, axis, down))  9.15 us
    pallas_call x1, Pallas kernels, forward_call(): pl.pallas_call(functools.partial(_forward_kernel, planes=planes, depth=de...  5.06 us
    ppermute x8, waiting for transfers between devices, swap(): return lax.ppermute(value, axis, [(i, i ^ bit) for i in range(peers)])  4.68 us
    pallas_call x1, Pallas kernels, input_call(): pl.pallas_call(functools.partial(_input_kernel, planes=planes, first=firs...  4.07 us
    pallas_call x1, Pallas kernels, weight_call(): pl.pallas_call(functools.partial(_weight_kernel, planes=planes, depth=dep...  3.73 us
    unnamed x22, local copies, waits for them, and re-layouts  2.5 us
    reshape x4, local copies, waits for them, and re-layouts, flat(): value.transpose(1, 0, 2, 3).reshape(value.shape[1], value.shape[0], lanes)  2.41 us
  transfers between devices with their start and end apart: 12, of which 4 were waited for; matrix products, arithmetic and copies ran while one was open for 16% of the time, Pallas kernels for 14%

profile of v22, /device:TPU:0, one launch (start us, length us, event | category | flops | bytes accessed | tf_op | source)
XLA Modules:
  0.0 54.2 jit_solution(8336481208046776605)
XLA Ops:
  0.6 0.0 copy-start.9
  0.6 0.6 %copy-done.9 = bf16[8]{0:T(256)(128)(2,1)S(1)} copy-done((bf16[8]{0:T(256)(128)(2,1)S(1)}, bf16[8]{0:T(256)(128)(2,1)}, u32[]{:S(2)}) %copy-start.9) | copy-done | bytes 40
  1.3 0.1 copy.17
  1.4 0.0 copy-start.8
  1.4 0.7 %copy-done.8 = bf16[8,864]{1,0:T(8,128)(2,1)S(1)} copy-done((bf16[8,864]{1,0:T(8,128)(2,1)S(1)}, bf16[8,864]{1,0:T(8,128)(2,1)}, u32[]{:S(2)}) %copy-start.8) | copy-done | bytes 13848
  2.1 0.1 bitcast_dynamic-update-slice_fusion.3
  2.2 3.0 %collective-permute-start.3 = (bf16[8,865]{1,0:T(8,128)(2,1)S(1)}, bf16[8,865]{1,0:T(8,128)(2,1)S(1)}, u32[]{:S(2)}, u32[]{:S(2)}) collective-permute-start(bf16[8,865]{1,0:T(8,128)(2,1)S(1)} %get-tuple-element.33), channel_id=1, source_target_pairs={{0,16},{8,24},{16,0},{24,8},{1,17},{9,25},{17,1},{25,9},{2,18},{10... | collective-permute-start | bytes 41528 | tf_op jit(solution)/shard_map/ppermute | solution.py:148
  5.1 1.5 %collective-permute-start.2 = (bf16[8,865]{1,0:T(8,128)(2,1)S(1)}, bf16[8,865]{1,0:T(8,128)(2,1)S(1)}, u32[]{:S(2)}, u32[]{:S(2)}) collective-permute-start(bf16[8,865]{1,0:T(8,128)(2,1)S(1)} %get-tuple-element.33), channel_id=1, source_target_pairs={{0,8},{8,0},{16,24},{24,16},{1,9},{9,1},{17,25},{25,17},{2,10},{10... | collective-permute-start | bytes 41528 | tf_op jit(solution)/shard_map/ppermute | solution.py:148
  6.6 0.0 collective-permute-start.4
  6.7 0.0 copy-start.2
  6.7 1.1 %fusion = (bf16[32,1,32,128]{3,2,1,0:T(8,128)(2,1)S(1)}, bf16[32,1,32,128]{3,2,1,0:T(8,128)(2,1)S(1)}) fusion(bf16[32,2,32,128]{3,2,1,0:T(8,128)(2,1)} %bitcast.60), kind=kLoop, calls=%fused_computation.13 | loop fusion | bytes 1048576 | tf_op jit(solution)/shard_map/slice | solution.py:221
  7.8 1.3 %collective-permute-start.1 = (bf16[32,1,32,128]{3,2,1,0:T(8,128)(2,1)S(1)}, bf16[32,1,32,128]{3,2,1,0:T(8,128)(2,1)S(1)}, u32[]{:S(2)}, u32[]{:S(2)}) collective-permute-start(bf16[32,1,32,128]{3,2,1,0:T(8,128)(2,1)S(1)} %get-tuple-element.34), channel_id=1, source_target_pairs={{1,0},{2,1},{3,2},{4,3},{5,4},{6,5},{7,6},{9,8},{10,9},{11,10},{12... | collective-permute-start | bytes 786440 | tf_op jit(solution)/shard_map/ppermute | solution.py:143
  9.1 3.0 %collective-permute-start = (bf16[32,1,32,128]{3,2,1,0:T(8,128)(2,1)S(1)}, bf16[32,1,32,128]{3,2,1,0:T(8,128)(2,1)S(1)}, u32[]{:S(2)}, u32[]{:S(2)}) collective-permute-start(bf16[32,1,32,128]{3,2,1,0:T(8,128)(2,1)S(1)} %get-tuple-element.35), channel_id=1, source_target_pairs={{0,1},{1,2},{2,3},{3,4},{4,5},{5,6},{6,7},{8,9},{9,10},{10,11},{11... | collective-permute-start | bytes 786440 | tf_op jit(solution)/shard_map/ppermute | solution.py:143
  12.2 0.0 copy-done.2
  12.2 0.1 reshape.41
  12.3 0.0 copy-start.1
  12.3 1.1 %copy.24.cot = bf16[2,32,4096]{2,1,0:T(8,128)(2,1)} copy(bf16[2,32,4096]{2,0,1:T(2,128)(2,1)S(1)} %reshape.41) | data formatting | bytes 1048576 | tf_op jit(solution)/shard_map/reshape | solution.py:216
  13.4 0.0 copy-done.1
  13.4 0.1 reshape.40
  13.6 1.1 %copy.23.mid = bf16[2,32,4096]{2,1,0:T(8,128)(2,1)} copy(bf16[2,32,4096]{2,0,1:T(2,128)(2,1)S(1)} %reshape.40) | data formatting | bytes 1048576 | tf_op jit(solution)/shard_map/reshape | solution.py:216
  14.6 0.0 collective-permute-done.2
  14.6 0.0 collective-permute-done.3
  14.7 0.0 collective-permute-done.4
  14.7 0.2 reshape.34
  14.9 0.1 copy.18
  15.0 0.8 %reshape.35.wall = bf16[288,96]{1,0:T(8,128)(2,1)} reshape(bf16[3,3,32,3,32]{4,3,2,1,0:T(4,128)(2,1)S(1)} %copy.18) | data formatting | bytes 110592 | tf_op jit(solution)/shard_map/reshape | solution.py:211
  15.8 0.7 %slice_convert_fusion.bias = f32[32,1]{1,0:T(8,128)} fusion(bf16[32,865]{1,0:T(8,128)(2,1)S(1)} %bitcast.67), kind=kLoop, calls=%fused_computation.10 | loop fusion | flops 32 | bytes 192 | tf_op jit(solution)/shard_map/convert_element_type | solution.py:225
  16.5 0.0 collective-permute-done.1
  16.5 0.8 %reshape_transpose.7.hi = bf16[1,32,4096]{2,1,0:T(8,128)(2,1)} reshape(bf16[32,1,32,128]{3,2,1,0:T(8,128)(2,1)S(1)} %collective-permute-done.1) | data formatting | bytes 524288 | tf_op jit(solution)/shard_map/reshape;transpose | solution.py:216
  17.3 0.0 collective-permute-done
  17.3 0.8 %reshape_transpose.6.lo = bf16[1,32,4096]{2,1,0:T(8,128)(2,1)} reshape(bf16[32,1,32,128]{3,2,1,0:T(8,128)(2,1)S(1)} %collective-permute-done) | data formatting | bytes 524288 | tf_op jit(solution)/shard_map/reshape;transpose | solution.py:216
  18.1 5.1 %shard_map.84 = (bf16[2,32,4096]{2,1,0:T(8,128)(2,1)}, bf16[2,32,4096]{2,1,0:T(8,128)(2,1)}, bf16[1,32,4096]{2,1,0:T(8,128)(2,1)}, bf16[1,32,4096]{2,1,0:T(8,128)(2,1)}) custom-call(bf16[1,32,4096]{2,1,0:T(8,128)(2,1)} %reshape_transpose.6.lo, bf16[2,32,4096]{2,1,0:T(8,128)(2,1)} %copy.23.mid, bf16[1,32,4096]{2,1,0:T(8,128)(2,1)} %reshape_transpose.7.hi, ...), custom_call_target="tpu_custom_call" | custom-call | flops 452984832 | bytes 2621440 | tf_op jit(solution)/shard_map/pallas_call | solution.py:104
  23.2 3.5 %collective-permute-start.5 = (bf16[1,32,4096]{2,1,0:T(8,128)(2,1)}, bf16[1,32,4096]{2,1,0:T(8,128)(2,1)S(1)}, u32[]{:S(2)}, u32[]{:S(2)}) collective-permute-start(bf16[1,32,4096]{2,1,0:T(8,128)(2,1)} %get-tuple-element.21), channel_id=1, source_target_pairs={{0,1},{1,2},{2,3},{3,4},{4,5},{5,6},{6,7},{8,9},{9,10},{10,11},{11... | collective-permute-start | bytes 786440 | tf_op jit(solution)/shard_map/ppermute | solution.py:143
  26.7 1.3 %collective-permute-start.6 = (bf16[1,32,4096]{2,1,0:T(8,128)(2,1)}, bf16[1,32,4096]{2,1,0:T(8,128)(2,1)S(1)}, u32[]{:S(2)}, u32[]{:S(2)}) collective-permute-start(bf16[1,32,4096]{2,1,0:T(8,128)(2,1)} %get-tuple-element.22), channel_id=1, source_target_pairs={{1,0},{2,1},{3,2},{4,3},{5,4},{6,5},{7,6},{9,8},{10,9},{11,10},{12... | collective-permute-start | bytes 786440 | tf_op jit(solution)/shard_map/ppermute | solution.py:143
  28.1 0.1 reverse_bitcast_fusion
  28.2 0.3 copy.21
  28.5 0.8 %reshape.38.wall = bf16[288,96]{1,0:T(8,128)(2,1)} reshape(bf16[3,3,32,3,32]{4,3,2,1,0:T(4,128)(2,1)S(1)} %copy.21) | data formatting | bytes 110592 | tf_op jit(solution)/shard_map/reshape | solution.py:212
  29.3 3.7 %shard_map.85 = (f32[16,865]{1,0:T(8,128)}, f32[16,865]{1,0:T(8,128)}) custom-call(s32[1]{0:T(128)} %bitcast.13.upper, bf16[1,32,4096]{2,1,0:T(8,128)(2,1)} %reshape_transpose.6.lo, bf16[2,32,4096]{2,1,0:T(8,128)(2,1)} %copy.23.mid, bf16[1,32,4096]{2,1,0:T(8,128)(2,1)} %reshape_transpose.7.hi, bf16[2,32,4096]{2,1,0:T(8,128)(2,1)} %get-tuple-element.25.dpre.mid, ...), custom_call_target="tpu_custom_call" | custom-call | flops 452984832 | bytes 1572864 | tf_op jit(solution)/shard_map/pallas_call | solution.py:129
  33.0 0.0 collective-permute-done.5.lo
  33.0 0.0 copy-start.4
  33.0 0.0 collective-permute-done.6.hi
  33.0 0.0 copy-start.5
  33.0 1.6 %collective-permute-start.7 = (f32[16,865]{1,0:T(8,128)}, f32[16,865]{1,0:T(8,128)S(1)}, u32[]{:S(2)}, u32[]{:S(2)}) collective-permute-start(f32[16,865]{1,0:T(8,128)} %get-tuple-element.23), channel_id=1, source_target_pairs={{0,16},{8,24},{16,0},{24,8},{1,17},{9,25},{17,1},{25,9},{2,18},{10... | collective-permute-start | bytes 166088 | tf_op jit(solution)/shard_map/ppermute | solution.py:148
  34.6 0.0 copy-done.4
  34.6 0.0 copy-done.5
  34.6 0.0 copy-start.6
  34.6 4.1 %shard_map.86 = bf16[2,32,4096]{2,1,0:T(8,128)(2,1)} custom-call(bf16[1,32,4096]{2,1,0:T(8,128)(2,1)} %copy-done.4, bf16[2,32,4096]{2,1,0:T(8,128)(2,1)} %get-tuple-element.25.dpre.mid, bf16[1,32,4096]{2,1,0:T(8,128)(2,1)} %copy-done.5, bf16[288,96]{1,0:T(8,128)(2,1)} %reshape.38.wall, f32[9,1,4096]{2,1,0:T(1,128)} %constant.66.clone.mask), custom_call_target="tpu_custom_call" | custom-call | flops 452984832 | bytes 1572864 | tf_op jit(solution)/shard_map/pallas_call | solution.py:116
  38.7 0.0 collective-permute-done.7
  38.7 0.0 copy-done.6
  38.7 1.6 %collective-permute-start.8 = (f32[8,865]{1,0:T(8,128)S(1)}, f32[8,865]{1,0:T(8,128)S(1)}, u32[]{:S(2)}, u32[]{:S(2)}) collective-permute-start(f32[8,865]{1,0:T(8,128)S(1)} %constant_dynamic-slice_fusion), channel_id=1, source_target_pairs={{0,8},{8,0},{16,24},{24,16},{1,9},{9,1},{17,25},{25,17},{2,10},{10... | collective-permute-start | bytes 83048 | tf_op jit(solution)/shard_map/ppermute | solution.py:148
  40.3 2.4 %collective-permute-done.8 = f32[8,865]{1,0:T(8,128)S(1)} collective-permute-done((f32[8,865]{1,0:T(8,128)S(1)}, f32[8,865]{1,0:T(8,128)S(1)}, u32[]{:S(2)}, u32[]{:S(2)}) %collective-permute-start.8) | collective-permute-done | bytes 27712 | tf_op jit(solution)/shard_map/ppermute | solution.py:148
  42.7 0.7 %collective-permute-start.9 = (f32[8,865]{1,0:T(8,128)S(1)}, f32[8,865]{1,0:T(8,128)S(1)}, u32[]{:S(2)}, u32[]{:S(2)}) collective-permute-start(f32[8,865]{1,0:T(8,128)S(1)} %dynamic-slice_add_fusion), channel_id=1, source_target_pairs={{0,1},{1,0},{2,3},{3,2},{4,5},{5,4},{6,7},{7,6},{8,9},{9,8},{10,11... | collective-permute-start | bytes 83048 | tf_op jit(solution)/shard_map/ppermute | solution.py:148
  43.4 0.9 %collective-permute-done.9 = f32[8,865]{1,0:T(8,128)S(1)} collective-permute-done((f32[8,865]{1,0:T(8,128)S(1)}, f32[8,865]{1,0:T(8,128)S(1)}, u32[]{:S(2)}, u32[]{:S(2)}) %collective-permute-start.9) | collective-permute-done | bytes 27712 | tf_op jit(solution)/shard_map/ppermute | solution.py:148
  44.3 2.5 %collective-permute-start.10 = (f32[8,865]{1,0:T(8,128)S(1)}, f32[8,865]{1,0:T(8,128)S(1)}, u32[]{:S(2)}, u32[]{:S(2)}) collective-permute-start(f32[8,865]{1,0:T(8,128)S(1)} %add.53), channel_id=1, source_target_pairs={{0,2},{1,3},{2,0},{3,1},{4,6},{5,7},{6,4},{7,5},{8,10},{9,11},{10,... | collective-permute-start | bytes 83048 | tf_op jit(solution)/shard_map/ppermute | solution.py:148
  46.7 0.0 copy-done.3
  46.7 0.1 copy.25
  46.8 0.9 %copy-done = bf16[2,32,4096]{2,1,0:T(8,128)(2,1)S(1)} copy-done((bf16[2,32,4096]{2,1,0:T(8,128)(2,1)S(1)}, bf16[2,32,4096]{2,1,0:T(8,128)(2,1)}, u32[]{:S(2)}) %copy-start) | copy-done | bytes 524312
  47.8 0.1 copy.26
  47.9 0.7 %collective-permute-done.10 = f32[8,865]{1,0:T(8,128)S(1)} collective-permute-done((f32[8,865]{1,0:T(8,128)S(1)}, f32[8,865]{1,0:T(8,128)S(1)}, u32[]{:S(2)}, u32[]{:S(2)}) %collective-permute-start.10) | collective-permute-done | bytes 27712 | tf_op jit(solution)/shard_map/ppermute | solution.py:148
  48.6 3.0 %collective-permute-start.11 = (f32[8,865]{1,0:T(8,128)S(1)}, f32[8,865]{1,0:T(8,128)S(1)}, u32[]{:S(2)}, u32[]{:S(2)}) collective-permute-start(f32[8,865]{1,0:T(8,128)S(1)} %add.54), channel_id=1, source_target_pairs={{0,4},{1,5},{2,6},{3,7},{4,0},{5,1},{6,2},{7,3},{8,12},{9,13},{10,... | collective-permute-start | bytes 83048 | tf_op jit(solution)/shard_map/ppermute | solution.py:148
  51.6 1.1 %copy_bitcast_fusion = (bf16[1,32,2,32,128]{4,3,2,1,0:T(8,128)(2,1)}, bf16[1,32,2,32,128]{4,3,2,1,0:T(8,128)(2,1)}) fusion(bf16[2,32,32,128]{3,2,1,0:T(8,128)(2,1)S(1)} %bitcast.62, bf16[2,32,32,128]{3,2,1,0:T(8,128)(2,1)S(1)} %bitcast.63), kind=kLoop, calls=%fused_computation | loop fusion | bytes 2097152 | tf_op jit(solution)/shard_map/broadcast_in_dim | solution.py:237
  52.7 0.7 %collective-permute-done.11 = f32[8,865]{1,0:T(8,128)S(1)} collective-permute-done((f32[8,865]{1,0:T(8,128)S(1)}, f32[8,865]{1,0:T(8,128)S(1)}, u32[]{:S(2)}, u32[]{:S(2)}) %collective-permute-start.11) | collective-permute-done | bytes 27712 | tf_op jit(solution)/shard_map/ppermute | solution.py:148
  53.5 0.7 %slice_reduce_fusion = f32[8]{0:T(128)} fusion(f32[8,865]{1,0:T(8,128)S(1)} %add_multiply_fusion), kind=kLoop, calls=%fused_computation.11 | loop fusion | bytes 64 | tf_op jit(solution)/shard_map/slice | solution.py:237
  54.2 0.0 copy-done.7
  (13 shorter events, 0.1 us)
Async XLA Ops:
  0.6 0.7 %copy-start.9 = (bf16[8]{0:T(256)(128)(2,1)S(1)}, bf16[8]{0:T(256)(128)(2,1)}, u32[]{:S(2)}) copy-start(bf16[8]{0:T(256)(128)(2,1)} %param.8) | copy-start | bytes 52
  1.4 0.7 %copy-start.8 = (bf16[8,864]{1,0:T(8,128)(2,1)S(1)}, bf16[8,864]{1,0:T(8,128)(2,1)}, u32[]{:S(2)}) copy-start(bf16[8,864]{1,0:T(8,128)(2,1)} %param.7) | copy-start | bytes 41476
  2.2 12.5 %collective-permute-start.3 = (bf16[8,865]{1,0:T(8,128)(2,1)S(1)}, bf16[8,865]{1,0:T(8,128)(2,1)S(1)}, u32[]{:S(2)}, u32[]{:S(2)}) collective-permute-start(bf16[8,865]{1,0:T(8,128)(2,1)S(1)} %get-tuple-element.33), channel_id=1, source_target_pairs={{0,16},{8,24},{16,0},{24,8},{1,17},{9,25},{17,1},{25,9},{2,18},{10... | collective-permute-start | bytes 41528 | tf_op jit(solution)/shard_map/ppermute | solution.py:148
  5.1 9.5 %collective-permute-start.2 = (bf16[8,865]{1,0:T(8,128)(2,1)S(1)}, bf16[8,865]{1,0:T(8,128)(2,1)S(1)}, u32[]{:S(2)}, u32[]{:S(2)}) collective-permute-start(bf16[8,865]{1,0:T(8,128)(2,1)S(1)} %get-tuple-element.33), channel_id=1, source_target_pairs={{0,8},{8,0},{16,24},{24,16},{1,9},{9,1},{17,25},{25,17},{2,10},{10... | collective-permute-start | bytes 41528 | tf_op jit(solution)/shard_map/ppermute | solution.py:148
  6.6 8.0 %collective-permute-start.4 = (bf16[8,865]{1,0:T(8,128)(2,1)S(1)}, bf16[8,865]{1,0:T(8,128)(2,1)S(1)}, u32[]{:S(2)}, u32[]{:S(2)}) collective-permute-start(bf16[8,865]{1,0:T(8,128)(2,1)S(1)} %get-tuple-element.33), channel_id=1, source_target_pairs={{0,24},{8,16},{16,8},{24,0},{1,25},{9,17},{17,9},{25,1},{2,26},{10... | collective-permute-start | bytes 41528 | tf_op jit(solution)/shard_map/ppermute | solution.py:148
  6.7 5.5 %copy-start.2 = (bf16[1,32,2,32,128]{4,3,2,1,0:T(8,128)(2,1)S(1)}, bf16[1,32,2,32,128]{4,3,2,1,0:T(8,128)(2,1)}, u32[]{:S(2)}) copy-start(bf16[1,32,2,32,128]{4,3,2,1,0:T(8,128)(2,1)} %param.6) | copy-start | bytes 1572868
  7.8 8.7 %collective-permute-start.1 = (bf16[32,1,32,128]{3,2,1,0:T(8,128)(2,1)S(1)}, bf16[32,1,32,128]{3,2,1,0:T(8,128)(2,1)S(1)}, u32[]{:S(2)}, u32[]{:S(2)}) collective-permute-start(bf16[32,1,32,128]{3,2,1,0:T(8,128)(2,1)S(1)} %get-tuple-element.34), channel_id=1, source_target_pairs={{1,0},{2,1},{3,2},{4,3},{5,4},{6,5},{7,6},{9,8},{10,9},{11,10},{12... | collective-permute-start | bytes 786440 | tf_op jit(solution)/shard_map/ppermute | solution.py:143
  9.1 8.2 %collective-permute-start = (bf16[32,1,32,128]{3,2,1,0:T(8,128)(2,1)S(1)}, bf16[32,1,32,128]{3,2,1,0:T(8,128)(2,1)S(1)}, u32[]{:S(2)}, u32[]{:S(2)}) collective-permute-start(bf16[32,1,32,128]{3,2,1,0:T(8,128)(2,1)S(1)} %get-tuple-element.35), channel_id=1, source_target_pairs={{0,1},{1,2},{2,3},{3,4},{4,5},{5,6},{6,7},{8,9},{9,10},{10,11},{11... | collective-permute-start | bytes 786440 | tf_op jit(solution)/shard_map/ppermute | solution.py:143
  12.3 1.1 %copy-start.1 = (bf16[1,32,2,32,128]{4,3,2,1,0:T(8,128)(2,1)S(1)}, bf16[1,32,2,32,128]{4,3,2,1,0:T(8,128)(2,1)}, u32[]{:S(2)}) copy-start(bf16[1,32,2,32,128]{4,3,2,1,0:T(8,128)(2,1)} %param.5) | copy-start | bytes 1572868
  23.2 9.8 %collective-permute-start.5 = (bf16[1,32,4096]{2,1,0:T(8,128)(2,1)}, bf16[1,32,4096]{2,1,0:T(8,128)(2,1)S(1)}, u32[]{:S(2)}, u32[]{:S(2)}) collective-permute-start(bf16[1,32,4096]{2,1,0:T(8,128)(2,1)} %get-tuple-element.21), channel_id=1, source_target_pairs={{0,1},{1,2},{2,3},{3,4},{4,5},{5,6},{6,7},{8,9},{9,10},{10,11},{11... | collective-permute-start | bytes 786440 | tf_op jit(solution)/shard_map/ppermute | solution.py:143
  26.7 6.3 %collective-permute-start.6 = (bf16[1,32,4096]{2,1,0:T(8,128)(2,1)}, bf16[1,32,4096]{2,1,0:T(8,128)(2,1)S(1)}, u32[]{:S(2)}, u32[]{:S(2)}) collective-permute-start(bf16[1,32,4096]{2,1,0:T(8,128)(2,1)} %get-tuple-element.22), channel_id=1, source_target_pairs={{1,0},{2,1},{3,2},{4,3},{5,4},{6,5},{7,6},{9,8},{10,9},{11,10},{12... | collective-permute-start | bytes 786440 | tf_op jit(solution)/shard_map/ppermute | solution.py:143
  33.0 1.6 %copy-start.4 = (bf16[1,32,4096]{2,1,0:T(8,128)(2,1)}, bf16[1,32,4096]{2,1,0:T(8,128)(2,1)S(1)}, u32[]{:S(2)}) copy-start(bf16[1,32,4096]{2,1,0:T(8,128)(2,1)S(1)} %collective-permute-done.5.lo) | copy-start | bytes 786436
  33.0 1.6 %copy-start.5 = (bf16[1,32,4096]{2,1,0:T(8,128)(2,1)}, bf16[1,32,4096]{2,1,0:T(8,128)(2,1)S(1)}, u32[]{:S(2)}) copy-start(bf16[1,32,4096]{2,1,0:T(8,128)(2,1)S(1)} %collective-permute-done.6.hi) | copy-start | bytes 786436
  33.0 5.7 %collective-permute-start.7 = (f32[16,865]{1,0:T(8,128)}, f32[16,865]{1,0:T(8,128)S(1)}, u32[]{:S(2)}, u32[]{:S(2)}) collective-permute-start(f32[16,865]{1,0:T(8,128)} %get-tuple-element.23), channel_id=1, source_target_pairs={{0,16},{8,24},{16,0},{24,8},{1,17},{9,25},{17,1},{25,9},{2,18},{10... | collective-permute-start | bytes 166088 | tf_op jit(solution)/shard_map/ppermute | solution.py:148
  34.6 4.1 %copy-start.6 = (f32[16,865]{1,0:T(8,128)S(1)}, f32[16,865]{1,0:T(8,128)}, u32[]{:S(2)}) copy-start(f32[16,865]{1,0:T(8,128)} %get-tuple-element.30) | copy-start | bytes 166084
  34.6 12.1 %copy-start.3 = (bf16[2,32,4096]{2,1,0:T(8,128)(2,1)S(1)}, bf16[2,32,4096]{2,1,0:T(8,128)(2,1)}, u32[]{:S(2)}) copy-start(bf16[2,32,4096]{2,1,0:T(8,128)(2,1)} %get-tuple-element.18) | copy-start | bytes 1572868
  38.7 3.9 %collective-permute-start.8 = (f32[8,865]{1,0:T(8,128)S(1)}, f32[8,865]{1,0:T(8,128)S(1)}, u32[]{:S(2)}, u32[]{:S(2)}) collective-permute-start(f32[8,865]{1,0:T(8,128)S(1)} %constant_dynamic-slice_fusion), channel_id=1, source_target_pairs={{0,8},{8,0},{16,24},{24,16},{1,9},{9,1},{17,25},{25,17},{2,10},{10... | collective-permute-start | bytes 83048 | tf_op jit(solution)/shard_map/ppermute | solution.py:148
  42.7 1.6 %collective-permute-start.9 = (f32[8,865]{1,0:T(8,128)S(1)}, f32[8,865]{1,0:T(8,128)S(1)}, u32[]{:S(2)}, u32[]{:S(2)}) collective-permute-start(f32[8,865]{1,0:T(8,128)S(1)} %dynamic-slice_add_fusion), channel_id=1, source_target_pairs={{0,1},{1,0},{2,3},{3,2},{4,5},{5,4},{6,7},{7,6},{8,9},{9,8},{10,11... | collective-permute-start | bytes 83048 | tf_op jit(solution)/shard_map/ppermute | solution.py:148
  44.3 4.3 %collective-permute-start.10 = (f32[8,865]{1,0:T(8,128)S(1)}, f32[8,865]{1,0:T(8,128)S(1)}, u32[]{:S(2)}, u32[]{:S(2)}) collective-permute-start(f32[8,865]{1,0:T(8,128)S(1)} %add.53), channel_id=1, source_target_pairs={{0,2},{1,3},{2,0},{3,1},{4,6},{5,7},{6,4},{7,5},{8,10},{9,11},{10,... | collective-permute-start | bytes 83048 | tf_op jit(solution)/shard_map/ppermute | solution.py:148
  46.7 1.0 %copy-start = (bf16[2,32,4096]{2,1,0:T(8,128)(2,1)S(1)}, bf16[2,32,4096]{2,1,0:T(8,128)(2,1)}, u32[]{:S(2)}) copy-start(bf16[2,32,4096]{2,1,0:T(8,128)(2,1)} %shard_map.86) | copy-start | bytes 1572868
  48.6 4.9 %collective-permute-start.11 = (f32[8,865]{1,0:T(8,128)S(1)}, f32[8,865]{1,0:T(8,128)S(1)}, u32[]{:S(2)}, u32[]{:S(2)}) collective-permute-start(f32[8,865]{1,0:T(8,128)S(1)} %add.54), channel_id=1, source_target_pairs={{0,4},{1,5},{2,6},{3,7},{4,0},{5,1},{6,2},{7,3},{8,12},{9,13},{10,... | collective-permute-start | bytes 83048 | tf_op jit(solution)/shard_map/ppermute | solution.py:148
  53.5 0.7 %copy-start.7 = (f32[8,865]{1,0:T(8,128)}, f32[8,865]{1,0:T(8,128)S(1)}, u32[]{:S(2)}) copy-start(f32[8,865]{1,0:T(8,128)S(1)} %add_multiply_fusion) | copy-start | bytes 83044
